TPU v7x, 128 devices: a whole 4x4x4 slice. The times are simulated.
128 devices in a mesh: section: 2 (over x_lo), tok: 8 (over x_hi, z), mdl: 8 (over y, core).
Axes of the slice: x: 4 (x_hi: 2, x_lo: 2; x = x_hi * 2 + x_lo), y: 4, z: 4, core: 2. Of those that a mesh axis runs over, the one named last changes fastest.
Arguments:
- layer_input: bfloat16 [2, 2048, 2048], P(None, 'tok'), may hold values from -6 to 6
- segment_ids: int32 [2, 2048], replicated, may hold values from 0 to 3, as said below
- route_ids: int32 [2, 2048, 6], P(None, ('tok', 'mdl')), may hold values from 0 to 63, all different within a row; in each aligned block of 32 rows (0 to 31, 32 to 63, ..., all dimensions but the last counted through in order) at most 4 rows name the same one
- route_weights: float32 [2, 2048, 6], P(None, ('tok', 'mdl')), may hold values from 0.1 to 0.5
- attn_gain: float32 [2048], replicated, may hold values from 0.5 to 1.5
- w_query: bfloat16 [2048, 3072], P(None, 'mdl'), may hold values from -6.629126 to 6.629126
- w_kv_down: bfloat16 [2048, 576], replicated, may hold values from -0.13258252 to 0.13258252
- latent_gain: float32 [512], replicated, may hold values from 0.5 to 1.5
- w_kv_up: bfloat16 [512, 4096], P(None, 'mdl'), may hold values from -0.25 to 0.25
- w_out: bfloat16 [2048, 2048], P('mdl'), may hold values from -0.125 to 0.125
- ffn_gain: float32 [2048], replicated, may hold values from 0.5 to 1.5
- w_shared_gate: bfloat16 [2048, 2048], P(None, 'mdl'), may hold values from -0.125 to 0.125
- w_shared_up: bfloat16 [2048, 2048], P(None, 'mdl'), may hold values from -0.125 to 0.125
- w_shared_down: bfloat16 [2048, 2048], P('mdl'), may hold values from -0.125 to 0.125
- w_expert_gate: bfloat16 [64, 2048, 768], P(('tok', 'mdl')), may hold values from -0.125 to 0.125
- w_expert_up: bfloat16 [64, 2048, 768], P(('tok', 'mdl')), may hold values from -0.125 to 0.125
- w_expert_down: bfloat16 [64, 768, 2048], P(('tok', 'mdl')), may hold values from -0.21875 to 0.21875
Outputs:
- layer_output: bfloat16 [2, 2048, 2048], P('section', ('tok', 'mdl'))
Inputs may be any that keep to these rules, and one draw needn't show every extreme that they name: `segment_ids`: segment numbers never fall along a pack; each segment has 1 to 1024 tokens and one has exactly 1024. `route_ids`: each token names 6 different experts. In each aligned block of 32 tokens of a pack (the tokens of one device), no expert is named by more than 4 tokens, a bound that some block reaches.
All inputs are finite; a program needn't handle non-finite values.
Results may differ from a plain program's by a relative error of at most 0.02.
Values may be sent and summed in bfloat16 or wider, within the bound.
No kernel may reach another device: no remote copies, remote signals or barrier semaphores. Data moves between devices by JAX's collectives and lax.ppermute only.
A program may use at most 128 MiB of HBM per device.

v0:
```python
import math

import jax
import jax.numpy as jnp
from jax import lax
from jax.sharding import PartitionSpec as P

NOPE = 128
ROPE = 64
VDIM = 128
LATENT = 512
SEGS = 4


EPS = 1e-06


def passed_along(value, axis, steps):
    count = lax.axis_size(axis)
    initial, last = (max(0, -steps), min(count, count - steps))
    return lax.ppermute(value, axis, [(source, source + steps) for source in range(initial, last)])


def rms_scale(values, gain_vec):
    values = values.astype(jnp.float32)
    return values * lax.rsqrt(jnp.mean(values * values, axis=-1, keepdims=True) + EPS) * gain_vec


def rotary(values, positions):
    half_width = values.shape[-1] // 2
    frequency = 10000.0 ** (-jnp.arange(half_width, dtype=jnp.float32) / half_width)
    angles = positions.astype(jnp.float32)[:, None] * frequency[None, :]
    if values.ndim == 3:
        angles = angles[:, None, :]
    cosine = jnp.cos(angles)
    sine_part = jnp.sin(angles)
    lead_half = values[..., :half_width]
    tail_half = values[..., half_width:]
    return jnp.concatenate(
        [lead_half * cosine - tail_half * sine_part, lead_half * sine_part + tail_half * cosine],
        axis=-1,
    )


def positions_of(segment_row, segment_count):
    labels = jnp.arange(segment_count, dtype=jnp.int32)
    starts = jnp.sum((segment_row[None, :] < labels[:, None]).astype(jnp.int32), axis=1)
    member = (segment_row[:, None] == labels[None, :]).astype(jnp.int32)
    return jnp.arange(segment_row.shape[0], dtype=jnp.int32) - jnp.sum(
        member * starts[None, :], axis=1
    )


def shards(
    layer_input,
    segment_ids,
    route_ids,
    route_weights,
    attn_gain,
    w_query,
    w_kv_down,
    latent_gain,
    w_kv_up,
    w_out,
    ffn_gain,
    w_shared_gate,
    w_shared_up,
    w_shared_down,
    w_expert_gate,
    w_expert_up,
    w_expert_down,
):
    n_mdl = lax.axis_size("mdl")
    n_wide = lax.axis_size(("tok", "mdl"))
    section_id = lax.axis_index("section")
    attending = section_id == 0
    expert_side = section_id == 1
    tok_rank = lax.axis_index("tok")
    mdl_rank = lax.axis_index("mdl")
    micro_count, tok_dev, model_width = layer_input.shape
    row_dev = tok_dev // n_mdl
    top_count = route_ids.shape[2]
    local_heads = w_out.shape[0] // VDIM
    qk_width = NOPE + ROPE
    score_scale = 1.0 / math.sqrt(qk_width)
    expert_dev = w_expert_gate.shape[0]
    expert_total = expert_dev * n_wide
    capacity = max(2, 3 * row_dev * top_count // (2 * expert_total))
    slot_total = expert_total * capacity
    slot_ids = jnp.arange(slot_total, dtype=jnp.int32)
    expert_labels = jnp.arange(expert_total, dtype=jnp.int32)
    results = []
    for batch_idx in range(micro_count):
        segment_row = segment_ids[batch_idx]
        positions = positions_of(segment_row, SEGS)
        query_start = tok_rank * tok_dev
        own_start = query_start + mdl_rank * row_dev
        query_pos = lax.dynamic_slice_in_dim(positions, query_start, tok_dev)
        own_pos = lax.dynamic_slice_in_dim(positions, own_start, row_dev)
        query_seg = lax.dynamic_slice_in_dim(segment_row, query_start, tok_dev)
        query_index = query_start + jnp.arange(tok_dev, dtype=jnp.int32)
        rows_in = layer_input[batch_idx]

        def project():
            normed = rms_scale(rows_in, attn_gain).astype(jnp.bfloat16)
            queries = jnp.dot(normed, w_query, preferred_element_type=jnp.float32).reshape(
                tok_dev, local_heads, qk_width
            )
            queries = jnp.concatenate(
                [queries[..., :NOPE], rotary(queries[..., NOPE:], query_pos)], axis=-1
            ).astype(jnp.bfloat16)
            own_normed = lax.dynamic_slice_in_dim(normed, mdl_rank * row_dev, row_dev)
            compressed = jnp.dot(own_normed, w_kv_down, preferred_element_type=jnp.float32)
            latent = rms_scale(compressed[:, :LATENT], latent_gain).astype(jnp.bfloat16)
            key_rope = rotary(compressed[:, LATENT:], own_pos).astype(jnp.bfloat16)
            return (queries, latent, key_rope)

        def no_project():
            return (
                jnp.zeros((tok_dev, local_heads, qk_width), jnp.bfloat16),
                jnp.zeros((row_dev, LATENT), jnp.bfloat16),
                jnp.zeros((row_dev, ROPE), jnp.bfloat16),
            )

        queries, latent, key_rope = lax.cond(attending, project, no_project)
        initial = (
            jnp.full((tok_dev, local_heads), -1e30, jnp.float32),
            jnp.zeros((tok_dev, local_heads), jnp.float32),
            jnp.zeros((tok_dev, local_heads, VDIM), jnp.float32),
        )
        latent_rows, rope_rows = (
            lax.all_gather(latent, "mdl", axis=0, tiled=True),
            lax.all_gather(key_rope, "mdl", axis=0, tiled=True),
        )
        expanded_here = (
            jnp.dot(latent_rows, w_kv_up, preferred_element_type=jnp.float32)
            .astype(jnp.bfloat16)
            .reshape(tok_dev, local_heads, NOPE + VDIM)
        )
        carried = initial
        expanded = lax.all_gather(expanded_here, "tok", axis=0, tiled=True)
        rope_keys = lax.all_gather(rope_rows, "tok", axis=0, tiled=True)
        key_count = expanded.shape[0]
        block_len = math.gcd(key_count, 512)
        block_count = key_count // block_len
        expanded_blocks = expanded.reshape(block_count, block_len, local_heads, NOPE + VDIM)
        rope_blocks = rope_keys.reshape(block_count, block_len, ROPE)

        def one_block(state_now, inputs):
            block_idx, kv_block, rope_block = inputs
            key_start = block_idx * block_len
            key_seg = lax.dynamic_slice_in_dim(segment_row, key_start, block_len)

            def update(state_old):
                running_max, totals, weighted = state_old
                scores = jnp.einsum(
                    "qhd,khd->qhk",
                    queries[..., :NOPE],
                    kv_block[..., :NOPE],
                    preferred_element_type=jnp.float32,
                )
                scores = scores + jnp.einsum(
                    "qhd,kd->qhk",
                    queries[..., NOPE:],
                    rope_block,
                    preferred_element_type=jnp.float32,
                )
                scores = scores * score_scale
                key_index = key_start + jnp.arange(block_len, dtype=jnp.int32)
                allowed = (key_seg[None, :] == query_seg[:, None]) & (
                    key_index[None, :] <= query_index[:, None]
                )
                allowed = allowed[:, None, :]
                masked = jnp.where(allowed, scores, -1e30)
                new_max = jnp.maximum(running_max, jnp.max(masked, axis=-1))
                weights = jnp.where(allowed, jnp.exp(scores - new_max[..., None]), 0.0)
                factor = jnp.exp(running_max - new_max)
                totals = totals * factor + jnp.sum(weights, axis=-1)
                weighted = weighted * factor[..., None] + jnp.einsum(
                    "qhk,khd->qhd",
                    weights.astype(jnp.bfloat16),
                    kv_block[..., NOPE:],
                    preferred_element_type=jnp.float32,
                )
                return (new_max, totals, weighted)

            def keep_state(state_old):
                return state_old

            return (lax.cond(attending, update, keep_state, state_now), None)

        carried, unused = lax.scan(
            one_block,
            carried,
            (jnp.arange(block_count, dtype=jnp.int32), expanded_blocks, rope_blocks),
        )
        running_max, totals, weighted = carried
        safe_totals = jnp.where(attending, totals, 1.0)
        attended = (
            (weighted / safe_totals[..., None])
            .astype(jnp.bfloat16)
            .reshape(tok_dev, local_heads * VDIM)
        )
        mixed_heads = lax.psum_scatter(
            jnp.dot(attended, w_out, preferred_element_type=jnp.float32).astype(jnp.bfloat16),
            "mdl",
            scatter_dimension=0,
            tiled=True,
        ).astype(jnp.float32)
        own_input = lax.dynamic_slice_in_dim(rows_in, mdl_rank * row_dev, row_dev)
        residual = (own_input.astype(jnp.float32) + mixed_heads).astype(jnp.bfloat16)
        arrived = passed_along(residual, "section", 1)
        normed_ffn = rms_scale(arrived, ffn_gain).astype(jnp.bfloat16)
        shard_rows = lax.all_gather(normed_ffn, "mdl", axis=0, tiled=True)

        def shared_compute():
            gate_proj = jnp.dot(shard_rows, w_shared_gate, preferred_element_type=jnp.float32)
            up_proj = jnp.dot(shard_rows, w_shared_up, preferred_element_type=jnp.float32)
            return (jax.nn.silu(gate_proj) * up_proj).astype(jnp.bfloat16)

        def shared_no_compute():
            return jnp.zeros((shard_rows.shape[0], w_shared_gate.shape[1]), jnp.bfloat16)

        shared_act = lax.cond(expert_side, shared_compute, shared_no_compute)
        shared_out = lax.psum_scatter(
            jnp.dot(shared_act, w_shared_down, preferred_element_type=jnp.float32).astype(
                jnp.bfloat16
            ),
            "mdl",
            scatter_dimension=0,
            tiled=True,
        ).astype(jnp.float32)
        expert_ids = route_ids[batch_idx].reshape(-1)
        onehot = (expert_ids[:, None] == expert_labels[None, :]).astype(jnp.int32)
        earlier = jnp.cumsum(onehot, axis=0) - onehot
        slot_index = jnp.sum(earlier * onehot, axis=1)
        target = expert_ids * capacity + slot_index
        placing = (
            (slot_ids[:, None] == target[None, :])
            .astype(jnp.int32)
            .reshape(slot_total, row_dev, top_count)
        )
        placing = jnp.sum(placing, axis=2).astype(jnp.bfloat16)
        outgoing = (
            jnp.dot(placing, normed_ffn, preferred_element_type=jnp.float32)
            .astype(jnp.bfloat16)
            .reshape(expert_total, capacity, model_width)
        )
        buffer = lax.all_to_all(outgoing, ("tok", "mdl"), split_axis=0, concat_axis=0, tiled=True)
        item_count = buffer.shape[1]
        grouped = (
            buffer.reshape(n_wide, expert_dev, item_count, model_width)
            .transpose(1, 0, 2, 3)
            .reshape(expert_dev, n_wide * item_count, model_width)
        )

        def run_compute():
            gate_proj = jnp.einsum(
                "erd,edf->erf", grouped, w_expert_gate, preferred_element_type=jnp.float32
            )
            up_proj = jnp.einsum(
                "erd,edf->erf", grouped, w_expert_up, preferred_element_type=jnp.float32
            )
            expert_act = (jax.nn.silu(gate_proj) * up_proj).astype(jnp.bfloat16)
            return jnp.einsum(
                "erf,efd->erd", expert_act, w_expert_down, preferred_element_type=jnp.float32
            ).astype(jnp.bfloat16)

        def run_no_compute():
            return jnp.zeros_like(grouped)

        produced = lax.cond(expert_side, run_compute, run_no_compute)
        processed = (
            produced.reshape(expert_dev, n_wide, item_count, model_width)
            .transpose(1, 0, 2, 3)
            .reshape(n_wide * expert_dev, item_count, model_width)
        )
        returned = lax.all_to_all(
            processed, ("tok", "mdl"), split_axis=0, concat_axis=0, tiled=True
        )
        weight_rows = route_weights[batch_idx]
        matched = target.reshape(row_dev, top_count)[:, :, None] == slot_ids[None, None, :]
        combining = jnp.sum(jnp.where(matched, weight_rows[:, :, None], 0.0), axis=1)
        routed = jnp.dot(
            combining,
            returned.reshape(slot_total, model_width).astype(jnp.float32),
            precision=lax.Precision.HIGHEST,
        )
        finished = (arrived.astype(jnp.float32) + shared_out + routed).astype(jnp.bfloat16)
        results.append(finished)
    half_count = micro_count // 2
    early_out = jnp.stack(results[:half_count])
    late_out = jnp.stack(results[half_count:])
    sent_back = passed_along(early_out, "section", -1)
    return jnp.where(attending, sent_back, late_out)


def solution(mesh):
    in_specs = (
        P(None, "tok", None),
        P(),
        P(None, ("tok", "mdl"), None),
        P(None, ("tok", "mdl"), None),
        P(),
        P(None, "mdl"),
        P(),
        P(),
        P(None, "mdl"),
        P("mdl", None),
        P(),
        P(None, "mdl"),
        P(None, "mdl"),
        P("mdl", None),
        P(("tok", "mdl"), None, None),
        P(("tok", "mdl"), None, None),
        P(("tok", "mdl"), None, None),
    )
    out_specs = P("section", ("tok", "mdl"), None)
    return jax.shard_map(shards, mesh=mesh, in_specs=in_specs, out_specs=out_specs, check_vma=False)
```

profile of v0, /device:TPU:1, one launch (start us, length us, event | category | flops | bytes accessed | tf_op | source)
XLA Modules:
  0.0 414.1 jit_solution(3455496598058938903)
XLA Ops:
  11.5 11.3 %conditional.8 = (bf16[32,512]{1,0:T(8,128)(2,1)S(1)}, bf16[32,64]{1,0:T(8,128)(2,1)S(1)}, bf16[256,2,192]{2,0,1:T(8,128)(2,1)S(1)}) conditional(s32[]{:T(128)} %convert_element_type.240, () %tuple.95, (bf16[1,256,2048]{2,1,0:T(8,128)(2,1)}, f32[2048]{0:T(1024)S(1)}, bf16[2048,384]{1,0:T(8,128)(2,1)}, s32[2048]{0:T(1024)}, s32[2048,4]{0,1:T(4,128)S(1)}, ...), branch_computations={%region_0.0_spmd, %region_1.6_spmd} | conditional | flops 483403392 | bytes 24214678 | solution.py:125
  22.8 14.7 %all_gather.30 = bf16[256,512]{1,0:T(8,128)(2,1)S(1)} all-gather(bf16[32,512]{1,0:T(8,128)(2,1)S(1)} %get-tuple-element.591), channel_id=1, replica_groups=mesh['section'=2,'tok'=8,'mdl'=8] {'mdl'}, dimensions={0}, use_global_device_ids=true | all-gather | bytes 294912 | tf_op jit(solution)/shard_map/all_gather | solution.py:132
  38.6 8.5 %conditional.11 = (bf16[32,512]{1,0:T(8,128)(2,1)S(1)}, bf16[32,64]{1,0:T(8,128)(2,1)S(1)}, bf16[256,2,192]{2,0,1:T(8,128)(2,1)S(1)}) conditional(s32[]{:T(128)} %convert_element_type.240, () %tuple.102, (bf16[1,256,2048]{2,1,0:T(8,128)(2,1)S(1)}, f32[2048]{0:T(1024)S(1)}, bf16[2048,384]{1,0:T(8,128)(2,1)}, s32[2048]{0:T(1024)S(1)}, ...), branch_computations={%region_24.25_spmd, %region_25.30_spmd} | conditional | flops 483403392 | bytes 24214678 | solution.py:125
  47.1 12.8 %all_gather.35 = bf16[256,512]{1,0:T(8,128)(2,1)S(1)} all-gather(bf16[32,512]{1,0:T(8,128)(2,1)S(1)} %get-tuple-element.596), channel_id=1, replica_groups=mesh['section'=2,'tok'=8,'mdl'=8] {'mdl'}, dimensions={0}, use_global_device_ids=true | all-gather | bytes 294912 | tf_op jit(solution)/shard_map/all_gather | solution.py:132
  61.0 12.8 %all_gather.32 = bf16[256,64]{1,0:T(8,128)(2,1)S(1)} all-gather(bf16[32,64]{1,0:T(8,128)(2,1)S(1)} %get-tuple-element.593), channel_id=1, replica_groups=mesh['section'=2,'tok'=8,'mdl'=8] {'mdl'}, dimensions={0}, use_global_device_ids=true | all-gather | bytes 36864 | tf_op jit(solution)/shard_map/all_gather | solution.py:133
  73.8 32.3 %all_gather.33 = bf16[2048,64]{1,0:T(8,128)(2,1)S(1)} all-gather(bf16[256,64]{1,0:T(8,128)(2,1)S(1)} %all_gather.32), channel_id=1, replica_groups=mesh['section'=2,'tok'=8,'mdl'=8] {'tok'}, dimensions={0}, use_global_device_ids=true | all-gather | bytes 294912 | tf_op jit(solution)/shard_map/all_gather | solution.py:142
  111.3 28.6 %while.30 = (s32[]{:T(128)}, f32[256,2]{0,1:T(2,128)S(1)}, f32[256,2]{0,1:T(2,128)S(1)}, f32[256,2,128]{2,0,1:T(8,128)S(1)}, pred[]{:T(512)}, /*index=5*/s32[204...) while((s32[]{:T(128)}, f32[256,2]{0,1:T(2,128)S(1)}, ...), condition=%wide.region_11.12_spmd.clone, body=%wide.region_6.11_spmd.clone.sunk | while | flops 170919680 | bytes 8568684 | solution.py:192
  111.3 7.1 %conditional.18 = ((f32[256,2]{0,1:T(2,128)S(1)}, f32[256,2]{0,1:T(2,128)S(1)}, f32[256,2,128]{2,0,1:T(8,128)S(1)})) conditional(s32[]{:T(128)} %convert_element_type.414, (f32[256,2]{0,1:T(2,128)S(1)}, f32[256,2]{0,1:T(2,128)S(1)}, f32[256,2,128]{2,0,1:T(8,128)S(1)}) %tuple.170, (s32[4]{0:T(128)S(1)}, s32[]{:T(128)}, s32[2048]{0:T(1024)}, ...), branch_computations={%region_7.7_spmd, %region_8.10_spmd} | conditional | flops 170919680 | bytes 8567402 | solution.py:190
  118.5 7.1 %conditional.18 = ((f32[256,2]{0,1:T(2,128)S(1)}, f32[256,2]{0,1:T(2,128)S(1)}, f32[256,2,128]{2,0,1:T(8,128)S(1)})) conditional(s32[]{:T(128)} %convert_element_type.414, (f32[256,2]{0,1:T(2,128)S(1)}, f32[256,2]{0,1:T(2,128)S(1)}, f32[256,2,128]{2,0,1:T(8,128)S(1)}) %tuple.170, (s32[4]{0:T(128)S(1)}, s32[]{:T(128)}, s32[2048]{0:T(1024)}, ...), branch_computations={%region_7.7_spmd, %region_8.10_spmd} | conditional | flops 170919680 | bytes 8567402 | solution.py:190
  125.6 7.1 %conditional.18 = ((f32[256,2]{0,1:T(2,128)S(1)}, f32[256,2]{0,1:T(2,128)S(1)}, f32[256,2,128]{2,0,1:T(8,128)S(1)})) conditional(s32[]{:T(128)} %convert_element_type.414, (f32[256,2]{0,1:T(2,128)S(1)}, f32[256,2]{0,1:T(2,128)S(1)}, f32[256,2,128]{2,0,1:T(8,128)S(1)}) %tuple.170, (s32[4]{0:T(128)S(1)}, s32[]{:T(128)}, s32[2048]{0:T(1024)}, ...), branch_computations={%region_7.7_spmd, %region_8.10_spmd} | conditional | flops 170919680 | bytes 8567402 | solution.py:190
  132.8 7.1 %conditional.18 = ((f32[256,2]{0,1:T(2,128)S(1)}, f32[256,2]{0,1:T(2,128)S(1)}, f32[256,2,128]{2,0,1:T(8,128)S(1)})) conditional(s32[]{:T(128)} %convert_element_type.414, (f32[256,2]{0,1:T(2,128)S(1)}, f32[256,2]{0,1:T(2,128)S(1)}, f32[256,2,128]{2,0,1:T(8,128)S(1)}) %tuple.170, (s32[4]{0:T(128)S(1)}, s32[]{:T(128)}, s32[2048]{0:T(1024)}, ...), branch_computations={%region_7.7_spmd, %region_8.10_spmd} | conditional | flops 170919680 | bytes 8567402 | solution.py:190
  141.6 17.5 %all_gather.37 = bf16[256,64]{1,0:T(8,128)(2,1)S(1)} all-gather(bf16[32,64]{1,0:T(8,128)(2,1)S(1)} %copy-done.12), channel_id=1, replica_groups=mesh['section'=2,'tok'=8,'mdl'=8] {'mdl'}, dimensions={0}, use_global_device_ids=true | all-gather | bytes 36864 | tf_op jit(solution)/shard_map/all_gather | solution.py:133
  159.1 29.4 %all_gather.38 = bf16[2048,64]{1,0:T(8,128)(2,1)S(1)} all-gather(bf16[256,64]{1,0:T(8,128)(2,1)S(1)} %all_gather.37), channel_id=1, replica_groups=mesh['section'=2,'tok'=8,'mdl'=8] {'tok'}, dimensions={0}, use_global_device_ids=true | all-gather | bytes 294912 | tf_op jit(solution)/shard_map/all_gather | solution.py:142
  192.5 20.1 %while.31 = (s32[]{:T(128)}, f32[256,2]{0,1:T(2,128)S(1)}, f32[256,2]{0,1:T(2,128)S(1)}, f32[256,2,128]{2,0,1:T(8,128)S(1)}, pred[]{:T(512)}, /*index=5*/s32[204...) while((s32[]{:T(128)}, f32[256,2]{0,1:T(2,128)S(1)}, ...), condition=%wide.region_35.36_spmd.clone, body=%wide.region_30.35_spmd.clone.sunk | while | flops 170919680 | bytes 8568684 | solution.py:192
  216.7 33.5 %reduce-scatter.9.cloned.1.call-done = bf16[32,2048]{1,0:T(8,128)(2,1)} async-done(((bf16[256,2048]{1,0:T(8,128)(2,1)}), bf16[32,2048]{1,0:T(8,128)(2,1)}) %reduce-scatter.9.cloned.1.call-update) | async-done | bytes 131088 | tf_op jit(solution)/shard_map/reduce_scatter | solution.py:204
  262.9 11.6 %all-to-all-start.2 = ((bf16[64,4,2048]{2,1,0:T(4,128)(2,1)}), bf16[64,4,2048]{2,1,0:T(4,128)(2,1)}, u32[]{:S(2)}, u32[]{:S(2)}) async-start(bf16[64,4,2048]{2,1,0:T(4,128)(2,1)} %reshape.509), calls=%async_computation.6 | async-start | bytes 2097152 | tf_op jit(solution)/shard_map/all_to_all | solution.py:249
  274.7 16.2 %all-gather.7.cloned.1.call-done = bf16[256,2048]{1,0:T(8,128)(2,1)} async-done(((bf16[32,2048]{1,0:T(8,128)(2,1)}), bf16[256,2048]{1,0:T(8,128)(2,1)}) %all-gather.7.cloned.1.call-update) | async-done | bytes 1048592 | tf_op jit(solution)/shard_map/all_gather | solution.py:214
  298.3 10.5 %all-to-all-start = ((bf16[64,4,2048]{2,1,0:T(4,128)(2,1)}), bf16[64,4,2048]{2,1,0:T(4,128)(2,1)}, u32[]{:S(2)}, u32[]{:S(2)}) async-start(bf16[64,4,2048]{2,1,0:T(4,128)(2,1)} %reshape.501), calls=%async_computation.2 | async-start | bytes 2097152 | tf_op jit(solution)/shard_map/all_to_all | solution.py:249
  312.3 15.0 %all-to-all-done = bf16[64,4,2048]{2,1,0:T(4,128)(2,1)} async-done(((bf16[64,4,2048]{2,1,0:T(4,128)(2,1)}), bf16[64,4,2048]{2,1,0:T(4,128)(2,1)}, u32[]{:S(2)}, u32[]{:S(2)}) %all-to-all-start) | async-done | bytes 1048608 | tf_op jit(solution)/shard_map/all_to_all | solution.py:249
  327.3 7.2 %all-to-all-start.3 = ((bf16[64,4,2048]{2,1,0:T(4,128)(2,1)}), bf16[64,4,2048]{2,1,0:T(4,128)(2,1)}, u32[]{:S(2)}, u32[]{:S(2)}) async-start(bf16[64,4,2048]{2,1,0:T(4,128)(2,1)} %reshape_transpose_reshape.11), calls=%async_computation.7 | async-start | bytes 2097152 | tf_op jit(solution)/shard_map/all_to_all | solution.py:278
  337.5 15.5 %all-to-all-done.3 = bf16[64,4,2048]{2,1,0:T(4,128)(2,1)} async-done(((bf16[64,4,2048]{2,1,0:T(4,128)(2,1)}), bf16[64,4,2048]{2,1,0:T(4,128)(2,1)}, u32[]{:S(2)}, u32[]{:S(2)}) %all-to-all-start.3) | async-done | bytes 1048608 | tf_op jit(solution)/shard_map/all_to_all | solution.py:278
  353.0 7.0 %all-to-all-start.1 = ((bf16[64,4,2048]{2,1,0:T(4,128)(2,1)}), bf16[64,4,2048]{2,1,0:T(4,128)(2,1)S(1)}, u32[]{:S(2)}, u32[]{:S(2)}) async-start(bf16[64,4,2048]{2,1,0:T(4,128)(2,1)} %reshape_transpose_reshape.10), calls=%async_computation.3 | async-start | bytes 2097152 | tf_op jit(solution)/shard_map/all_to_all | solution.py:278
  362.2 16.3 %all-to-all-done.1 = bf16[64,4,2048]{2,1,0:T(4,128)(2,1)S(1)} async-done(((bf16[64,4,2048]{2,1,0:T(4,128)(2,1)}), bf16[64,4,2048]{2,1,0:T(4,128)(2,1)S(1)}, u32[]{:S(2)}, u32[]{:S(2)}) %all-to-all-start.1) | async-done | bytes 1048608 | tf_op jit(solution)/shard_map/all_to_all | solution.py:278
  384.1 21.5 %reduce-scatter.11.cloned.1.call-done = bf16[32,2048]{1,0:T(8,128)(2,1)} async-done(((bf16[256,2048]{1,0:T(8,128)(2,1)}), bf16[32,2048]{1,0:T(8,128)(2,1)}) %reduce-scatter.11.cloned.1.call-update) | async-done | bytes 131088 | tf_op jit(solution)/shard_map/reduce_scatter | solution.py:225
  (330 shorter events, 142.1 us)
Async XLA Ops:
  6.5 133.5 %copy-start = (bf16[256,2048]{1,0:T(8,128)(2,1)S(1)}, bf16[256,2048]{1,0:T(8,128)(2,1)}, u32[]{:S(2)}) copy-start(bf16[256,2048]{1,0:T(8,128)(2,1)} %param.46) | copy-start | bytes 3145732
  6.5 101.7 %all-gather.5.cloned.1.call-start = ((), (), s32[]{:S(2)}) async-start(), calls=%async_computation.8 | async-start | bytes 2359296 | tf_op jit(solution)/shard_map/all_gather | solution.py:141
  11.4 27.2 %copy-start.1 = (bf16[1,256,2048]{2,1,0:T(8,128)(2,1)}, bf16[1,256,2048]{2,1,0:T(8,128)(2,1)S(1)}, u32[]{:S(2)}) copy-start(bf16[1,256,2048]{2,1,0:T(8,128)(2,1)S(1)} %get-tuple-element.875) | copy-start | bytes 3145732
  11.5 26.0 %copy-start.6 = (bf16[512,512]{1,0:T(8,128)(2,1)S(1)}, bf16[512,512]{1,0:T(8,128)(2,1)}, u32[]{:S(2)}) copy-start(bf16[512,512]{1,0:T(8,128)(2,1)} %param.45) | copy-start | bytes 1572868
  11.5 3.5 copy-start.2
  38.5 150.9 %all-gather.9.cloned.1.call-start = ((), (), s32[]{:S(2)}) async-start(), calls=%async_computation.12 | async-start | bytes 2359296 | tf_op jit(solution)/shard_map/all_gather | solution.py:141
  47.1 64.2 %copy-start.11 = (bf16[32,64]{1,0:T(8,128)(2,1)}, bf16[32,64]{1,0:T(8,128)(2,1)S(1)}, u32[]{:S(2)}) copy-start(bf16[32,64]{1,0:T(8,128)(2,1)S(1)} %get-tuple-element.598) | copy-start | bytes 12292
  61.0 153.4 %reduce-scatter.5.cloned.1.call-start = ((), (), s32[]{:S(2)}) async-start(), calls=%async_computation.9 | async-start | bytes 1179648 | tf_op jit(solution)/shard_map/reduce_scatter | solution.py:204
  141.5 108.7 %reduce-scatter.9.cloned.1.call-start = ((), (), s32[]{:S(2)}) async-start(), calls=%async_computation.13 | async-start | bytes 1179648 | tf_op jit(solution)/shard_map/reduce_scatter | solution.py:204
  212.8 43.7 %copy-start.13 = (f32[2048]{0:T(1024)S(1)}, f32[2048]{0:T(1024)}, u32[]{:S(2)}) copy-start(f32[2048]{0:T(1024)} %param.47) | copy-start | bytes 24580
  212.8 44.6 %copy-start.15 = (s32[2,32,6]{1,0,2:T(2,128)S(1)}, s32[2,32,6]{1,0,2:T(2,128)}, u32[]{:S(2)}) copy-start(s32[2,32,6]{1,0,2:T(2,128)} %param.39) | copy-start | bytes 4612
  214.3 76.5 %all-gather.7.cloned.1.call-start = ((), (), s32[]{:S(2)}) async-start(), calls=%async_computation.10 | async-start | bytes 1179648 | tf_op jit(solution)/shard_map/all_gather | solution.py:214
  215.4 39.0 %collective-permute-start = (bf16[32,2048]{1,0:T(8,128)(2,1)S(1)}, bf16[32,2048]{1,0:T(8,128)(2,1)S(1)}, u32[]{:S(2)}, u32[]{:S(2)}) collective-permute-start(bf16[32,2048]{1,0:T(8,128)(2,1)S(1)} %fusion.143), channel_id=1, source_target_pairs={{0,64},{1,65},{2,66},{3,67},{4,68},{5,69},{6,70},{7,71},{8,72},{9,... | collective-permute-start | bytes 393224 | tf_op jit(solution)/shard_map/ppermute | solution.py:21
  251.2 5.1 %collective-permute-start.2 = (bf16[32,2048]{1,0:T(8,128)(2,1)S(1)}, bf16[32,2048]{1,0:T(8,128)(2,1)S(1)}, u32[]{:S(2)}, u32[]{:S(2)}) collective-permute-start(bf16[32,2048]{1,0:T(8,128)(2,1)S(1)} %fusion.142), channel_id=1, source_target_pairs={{0,64},{1,65},{2,66},{3,67},{4,68},{5,69},{6,70},{7,71},{8,72},{9,... | collective-permute-start | bytes 393224 | tf_op jit(solution)/shard_map/ppermute | solution.py:21
  257.3 77.2 %all-gather.11.cloned.1.call-start = ((), (), s32[]{:S(2)}) async-start(), calls=%async_computation.14 | async-start | bytes 1179648 | tf_op jit(solution)/shard_map/all_gather | solution.py:214
  261.7 29.1 %copy-start.4 = (bf16[2048,256]{1,0:T(8,128)(2,1)S(1)}, bf16[2048,256]{1,0:T(8,128)(2,1)}, u32[]{:S(2)}) copy-start(bf16[2048,256]{1,0:T(8,128)(2,1)} %param.48) | copy-start | bytes 3145732
  262.9 35.4 %all-to-all-start.2 = ((bf16[64,4,2048]{2,1,0:T(4,128)(2,1)}), bf16[64,4,2048]{2,1,0:T(4,128)(2,1)}, u32[]{:S(2)}, u32[]{:S(2)}) async-start(bf16[64,4,2048]{2,1,0:T(4,128)(2,1)} %reshape.509), calls=%async_computation.6 | async-start | bytes 2097152 | tf_op jit(solution)/shard_map/all_to_all | solution.py:249
  274.6 105.0 %reduce-scatter.7.cloned.1.call-start = ((), (), s32[]{:S(2)}) async-start(), calls=%async_computation.11 | async-start | bytes 1179648 | tf_op jit(solution)/shard_map/reduce_scatter | solution.py:225
  298.3 29.0 %all-to-all-start = ((bf16[64,4,2048]{2,1,0:T(4,128)(2,1)}), bf16[64,4,2048]{2,1,0:T(4,128)(2,1)}, u32[]{:S(2)}, u32[]{:S(2)}) async-start(bf16[64,4,2048]{2,1,0:T(4,128)(2,1)} %reshape.501), calls=%async_computation.2 | async-start | bytes 2097152 | tf_op jit(solution)/shard_map/all_to_all | solution.py:249
  327.3 25.7 %all-to-all-start.3 = ((bf16[64,4,2048]{2,1,0:T(4,128)(2,1)}), bf16[64,4,2048]{2,1,0:T(4,128)(2,1)}, u32[]{:S(2)}, u32[]{:S(2)}) async-start(bf16[64,4,2048]{2,1,0:T(4,128)(2,1)} %reshape_transpose_reshape.11), calls=%async_computation.7 | async-start | bytes 2097152 | tf_op jit(solution)/shard_map/all_to_all | solution.py:278
  334.5 71.2 %reduce-scatter.11.cloned.1.call-start = ((), (), s32[]{:S(2)}) async-start(), calls=%async_computation.15 | async-start | bytes 1179648 | tf_op jit(solution)/shard_map/reduce_scatter | solution.py:225
  336.2 23.7 %copy-start.16 = (f32[2,32,6]{1,0,2:T(2,128)S(1)}, f32[2,32,6]{1,0,2:T(2,128)}, u32[]{:S(2)}) copy-start(f32[2,32,6]{1,0,2:T(2,128)} %param.40) | copy-start | bytes 4612
  353.0 25.5 %all-to-all-start.1 = ((bf16[64,4,2048]{2,1,0:T(4,128)(2,1)}), bf16[64,4,2048]{2,1,0:T(4,128)(2,1)S(1)}, u32[]{:S(2)}, u32[]{:S(2)}) async-start(bf16[64,4,2048]{2,1,0:T(4,128)(2,1)} %reshape_transpose_reshape.10), calls=%async_computation.3 | async-start | bytes 2097152 | tf_op jit(solution)/shard_map/all_to_all | solution.py:278
  381.5 24.2 %collective-permute-start.1 = (bf16[1,32,2048]{2,1,0:T(8,128)(2,1)S(1)}, bf16[1,32,2048]{2,1,0:T(8,128)(2,1)S(1)}, u32[]{:S(2)}, u32[]{:S(2)}) collective-permute-start(bf16[1,32,2048]{2,1,0:T(8,128)(2,1)S(1)} %fusion.146), channel_id=1, source_target_pairs={{64,0},{65,1},{66,2},{67,3},{68,4},{69,5},{70,6},{71,7},{72,8},{73... | collective-permute-start | bytes 393224 | tf_op jit(solution)/shard_map/ppermute | solution.py:21
  (6 other events, 13.3 us)
Sparse Core Ops, SparseCore 0:
  38.7 56.3 all-gather.4
  97.3 52.0 all-gather.8
  151.8 30.2 reduce-scatter.4
  214.5 35.7 reduce-scatter.8
  257.5 33.3 all-gather.6
  292.4 31.1 all-gather.10
  326.0 38.6 reduce-scatter.6
  367.1 38.5 reduce-scatter.10
where the time goes:
time: 418 us; the launch traced here: 414 us
  blocking collectives  120 us (29%)
  waiting for transfers between devices  120 us (29%)
  local copies, waits for them, and re-layouts  55.5 us (13%)
  starting transfers between devices  42.4 us (10%)
  matrix products  35.6 us (9%)
  other arithmetic  21.1 us (5%)
  between operations  14.1 us (3%)
  loops' own time  5.92 us (1%)
    all_gather x2, blocking collectives, shards(): rope_keys = lax.all_gather(rope_rows, 'tok', axis=0, tiled=True)  61.7 us
    reduce_scatter x2, waiting for transfers between devices, shards(): lax.psum_scatter(jnp.dot(attended, w_out, preferred_element_type=jnp.floa...  33.5 us
    all_to_all x2, waiting for transfers between devices, shards(): lax.all_to_all(processed, ('tok', 'mdl'), split_axis=0, concat_axis=0, ti...  31.8 us
    all_gather x2, blocking collectives, shards(): lax.all_gather(key_rope, 'mdl', axis=0, tiled=True)  30.3 us
    all_gather x2, blocking collectives, shards(): lax.all_gather(latent, 'mdl', axis=0, tiled=True)  27.5 us
    all_to_all x2, starting transfers between devices, shards(): lax.all_to_all(outgoing, ('tok', 'mdl'), split_axis=0, concat_axis=0, til...  22.2 us
    reduce_scatter x2, waiting for transfers between devices, shards(): lax.psum_scatter(jnp.dot(shared_act, w_shared_down, preferred_element_typ...  21.5 us
    all_gather x2, waiting for transfers between devices, shards(): shard_rows = lax.all_gather(normed_ffn, 'mdl', axis=0, tiled=True)  16.2 us
  transfers between devices with their start and end apart: 15, of which 7 were waited for; matrix products, arithmetic and copies ran while one was open for 22% of the time, Pallas kernels for 0%

commit v1 on v0

v1 whole, which is shorter than its diff:
```python
import math

import jax
import jax.numpy as jnp
from jax import lax
from jax.sharding import PartitionSpec as P

NOPE = 128
ROPE = 64
VDIM = 128
LATENT = 512
SEGS = 4


EPS = 1e-06


def passed_along(value, axis, steps):
    count = lax.axis_size(axis)
    initial, last = (max(0, -steps), min(count, count - steps))
    return lax.ppermute(value, axis, [(source, source + steps) for source in range(initial, last)])


def rms_scale(values, gain_vec):
    values = values.astype(jnp.float32)
    return values * lax.rsqrt(jnp.mean(values * values, axis=-1, keepdims=True) + EPS) * gain_vec


def rotary(values, positions):
    half_width = values.shape[-1] // 2
    frequency = 10000.0 ** (-jnp.arange(half_width, dtype=jnp.float32) / half_width)
    angles = positions.astype(jnp.float32)[:, None] * frequency[None, :]
    if values.ndim == 3:
        angles = angles[:, None, :]
    cosine = jnp.cos(angles)
    sine_part = jnp.sin(angles)
    lead_half = values[..., :half_width]
    tail_half = values[..., half_width:]
    return jnp.concatenate(
        [lead_half * cosine - tail_half * sine_part, lead_half * sine_part + tail_half * cosine],
        axis=-1,
    )


def positions_of(segment_row, segment_count):
    labels = jnp.arange(segment_count, dtype=jnp.int32)
    starts = jnp.sum((segment_row[None, :] < labels[:, None]).astype(jnp.int32), axis=1)
    member = (segment_row[:, None] == labels[None, :]).astype(jnp.int32)
    return jnp.arange(segment_row.shape[0], dtype=jnp.int32) - jnp.sum(
        member * starts[None, :], axis=1
    )


def shards(
    layer_input,
    segment_ids,
    route_ids,
    route_weights,
    attn_gain,
    w_query,
    w_kv_down,
    latent_gain,
    w_kv_up,
    w_out,
    ffn_gain,
    w_shared_gate,
    w_shared_up,
    w_shared_down,
    w_expert_gate,
    w_expert_up,
    w_expert_down,
):
    n_mdl = lax.axis_size("mdl")
    n_wide = lax.axis_size(("tok", "mdl"))
    section_id = lax.axis_index("section")
    tok_rank = lax.axis_index("tok")
    mdl_rank = lax.axis_index("mdl")
    micro_count, tok_dev, model_width = layer_input.shape
    row_dev = tok_dev // n_mdl
    top_count = route_ids.shape[2]
    local_heads = w_out.shape[0] // VDIM
    qk_width = NOPE + ROPE
    score_scale = 1.0 / math.sqrt(qk_width)
    expert_dev = w_expert_gate.shape[0]
    expert_total = expert_dev * n_wide
    capacity = max(2, 3 * row_dev * top_count // (2 * expert_total))
    slot_total = expert_total * capacity
    slot_ids = jnp.arange(slot_total, dtype=jnp.int32)
    expert_labels = jnp.arange(expert_total, dtype=jnp.int32)

    segment_row = lax.dynamic_index_in_dim(segment_ids, section_id, 0, keepdims=False)
    rows_in = lax.dynamic_index_in_dim(layer_input, section_id, 0, keepdims=False)
    expert_ids = lax.dynamic_index_in_dim(route_ids, section_id, 0, keepdims=False).reshape(-1)
    weight_rows = lax.dynamic_index_in_dim(route_weights, section_id, 0, keepdims=False)

    positions = positions_of(segment_row, SEGS)
    query_start = tok_rank * tok_dev
    query_pos = lax.dynamic_slice_in_dim(positions, query_start, tok_dev)
    query_seg = lax.dynamic_slice_in_dim(segment_row, query_start, tok_dev)
    query_index = query_start + jnp.arange(tok_dev, dtype=jnp.int32)

    normed = rms_scale(rows_in, attn_gain).astype(jnp.bfloat16)
    queries = jnp.dot(normed, w_query, preferred_element_type=jnp.float32).reshape(
        tok_dev, local_heads, qk_width
    )
    queries = jnp.concatenate(
        [queries[..., :NOPE], rotary(queries[..., NOPE:], query_pos)], axis=-1
    ).astype(jnp.bfloat16)
    compressed = jnp.dot(normed, w_kv_down, preferred_element_type=jnp.float32)
    latent = rms_scale(compressed[:, :LATENT], latent_gain).astype(jnp.bfloat16)
    key_rope = rotary(compressed[:, LATENT:], query_pos).astype(jnp.bfloat16)
    kv_rows = lax.all_gather(
        jnp.concatenate([latent, key_rope], axis=-1), "tok", axis=0, tiled=True
    )
    key_count = kv_rows.shape[0]
    expanded = (
        jnp.dot(kv_rows[:, :LATENT], w_kv_up, preferred_element_type=jnp.float32)
        .astype(jnp.bfloat16)
        .reshape(key_count, local_heads, NOPE + VDIM)
    )
    rope_keys = kv_rows[:, LATENT:]
    scores = jnp.einsum(
        "qhd,khd->hqk", queries[..., :NOPE], expanded[..., :NOPE],
        preferred_element_type=jnp.float32,
    )
    scores = scores + jnp.einsum(
        "qhd,kd->hqk", queries[..., NOPE:], rope_keys, preferred_element_type=jnp.float32
    )
    scores = scores * score_scale
    key_index = jnp.arange(key_count, dtype=jnp.int32)
    allowed = (segment_row[None, :] == query_seg[:, None]) & (
        key_index[None, :] <= query_index[:, None]
    )
    allowed = allowed[None, :, :]
    masked = jnp.where(allowed, scores, -1e30)
    row_max = jnp.max(masked, axis=-1, keepdims=True)
    weights = jnp.where(allowed, jnp.exp(scores - row_max), 0.0)
    totals = jnp.sum(weights, axis=-1, keepdims=True)
    weighted = jnp.einsum(
        "hqk,khd->hqd", weights.astype(jnp.bfloat16), expanded[..., NOPE:],
        preferred_element_type=jnp.float32,
    )
    attended = (
        (weighted / totals).astype(jnp.bfloat16).transpose(1, 0, 2).reshape(tok_dev, local_heads * VDIM)
    )
    mixed_heads = lax.psum(
        jnp.dot(attended, w_out, preferred_element_type=jnp.float32).astype(jnp.bfloat16), "mdl"
    ).astype(jnp.float32)
    residual = (rows_in.astype(jnp.float32) + mixed_heads).astype(jnp.bfloat16)
    normed_ffn_all = rms_scale(residual, ffn_gain).astype(jnp.bfloat16)
    own_residual = lax.dynamic_slice_in_dim(residual, mdl_rank * row_dev, row_dev)
    normed_ffn = lax.dynamic_slice_in_dim(normed_ffn_all, mdl_rank * row_dev, row_dev)

    gate_proj = jnp.dot(normed_ffn_all, w_shared_gate, preferred_element_type=jnp.float32)
    up_proj = jnp.dot(normed_ffn_all, w_shared_up, preferred_element_type=jnp.float32)
    shared_act = (jax.nn.silu(gate_proj) * up_proj).astype(jnp.bfloat16)
    shared_out = lax.psum_scatter(
        jnp.dot(shared_act, w_shared_down, preferred_element_type=jnp.float32).astype(jnp.bfloat16),
        "mdl",
        scatter_dimension=0,
        tiled=True,
    ).astype(jnp.float32)

    onehot = (expert_ids[:, None] == expert_labels[None, :]).astype(jnp.int32)
    earlier = jnp.cumsum(onehot, axis=0) - onehot
    slot_index = jnp.sum(earlier * onehot, axis=1)
    target = expert_ids * capacity + slot_index
    placing = (
        (slot_ids[:, None] == target[None, :])
        .astype(jnp.int32)
        .reshape(slot_total, row_dev, top_count)
    )
    placing = jnp.sum(placing, axis=2).astype(jnp.bfloat16)
    outgoing = (
        jnp.dot(placing, normed_ffn, preferred_element_type=jnp.float32)
        .astype(jnp.bfloat16)
        .reshape(expert_total, capacity, model_width)
    )
    buffer = lax.all_to_all(outgoing, ("tok", "mdl"), split_axis=0, concat_axis=0, tiled=True)
    item_count = buffer.shape[1]
    grouped = (
        buffer.reshape(n_wide, expert_dev, item_count, model_width)
        .transpose(1, 0, 2, 3)
        .reshape(expert_dev, n_wide * item_count, model_width)
    )
    e_gate = jnp.einsum("erd,edf->erf", grouped, w_expert_gate, preferred_element_type=jnp.float32)
    e_up = jnp.einsum("erd,edf->erf", grouped, w_expert_up, preferred_element_type=jnp.float32)
    expert_act = (jax.nn.silu(e_gate) * e_up).astype(jnp.bfloat16)
    produced = jnp.einsum(
        "erf,efd->erd", expert_act, w_expert_down, preferred_element_type=jnp.float32
    ).astype(jnp.bfloat16)
    processed = (
        produced.reshape(expert_dev, n_wide, item_count, model_width)
        .transpose(1, 0, 2, 3)
        .reshape(n_wide * expert_dev, item_count, model_width)
    )
    returned = lax.all_to_all(processed, ("tok", "mdl"), split_axis=0, concat_axis=0, tiled=True)
    matched = target.reshape(row_dev, top_count)[:, :, None] == slot_ids[None, None, :]
    combining = jnp.sum(jnp.where(matched, weight_rows[:, :, None], 0.0), axis=1)
    routed = jnp.dot(
        combining,
        returned.reshape(slot_total, model_width).astype(jnp.float32),
        precision=lax.Precision.HIGHEST,
    )
    finished = (own_residual.astype(jnp.float32) + shared_out + routed).astype(jnp.bfloat16)
    return finished[None]


def solution(mesh):
    in_specs = (
        P(None, "tok", None),
        P(),
        P(None, ("tok", "mdl"), None),
        P(None, ("tok", "mdl"), None),
        P(),
        P(None, "mdl"),
        P(),
        P(),
        P(None, "mdl"),
        P("mdl", None),
        P(),
        P(None, "mdl"),
        P(None, "mdl"),
        P("mdl", None),
        P(("tok", "mdl"), None, None),
        P(("tok", "mdl"), None, None),
        P(("tok", "mdl"), None, None),
    )
    out_specs = P("section", ("tok", "mdl"), None)
    return jax.shard_map(shards, mesh=mesh, in_specs=in_specs, out_specs=out_specs, check_vma=False)
```

time: 418 us -> 238 us (0.57)
  blocking collectives: 120 us -> 0 us
  local copies, waits for them, and re-layouts: 55.5 us -> 18 us
  starting transfers between devices: 42.4 us -> 16.2 us
  waiting for transfers between devices: 120 us -> 139 us
  other arithmetic: 21.1 us -> 11.5 us
  loops' own time: 5.92 us -> 0 us
    all_gather x6 -> x0, blocking collectives: 120 us -> none  [the longest x2 61.7 us: shards(): rope_keys = lax.all_gather(rope_rows, 'tok', axis=0, tiled=True)]
    psum x0 -> x1, waiting for transfers between devices: none -> 59 us  [shards(): lax.psum(jnp.dot(attended, w_out, preferred_element_type=jnp.float32).ast...]
    all_gather x4 -> x1, waiting for transfers between devices: 16.2 us -> 49.9 us  [shards(): lax.all_gather(jnp.concatenate([latent, key_rope], axis=-1), 'tok', axis=...]
    reduce_scatter x2 -> x0, waiting for transfers between devices: 33.5 us -> none  [shards(): lax.psum_scatter(jnp.dot(attended, w_out, preferred_element_type=jnp.floa...]
    reduce_scatter x2 -> x1, waiting for transfers between devices: 21.5 us -> 0.01 us  [shards(): lax.psum_scatter(jnp.dot(shared_act, w_shared_down, preferred_element_typ...]
    all_to_all x2 -> x1, waiting for transfers between devices: 31.8 us -> 18.3 us  [shards(): lax.all_to_all(processed, ('tok', 'mdl'), split_axis=0, concat_axis=0, ti...]
    all_to_all x2 -> x1, starting transfers between devices: 22.2 us -> 10.7 us  [shards(): lax.all_to_all(outgoing, ('tok', 'mdl'), split_axis=0, concat_axis=0, til...]
    another operation x24 -> x3, local copies, waits for them, and re-layouts: 11.1 us -> 2.15 us
  transfers between devices with their start and end apart: 15 -> 5, of which waited for: 7 -> 4; matrix products, arithmetic and copies ran while one was open for 22% -> 13% of each run, Pallas kernels for 0% -> 0%
where the time goes in v1:
time: 238 us; the launch traced here: 237 us
  waiting for transfers between devices  139 us (58%)
  matrix products  38.8 us (16%)
  local copies, waits for them, and re-layouts  18 us (8%)
  starting transfers between devices  16.2 us (7%)
  between operations  13.4 us (6%)
  other arithmetic  11.5 us (5%)
    psum x1, waiting for transfers between devices, shards(): lax.psum(jnp.dot(attended, w_out, preferred_element_type=jnp.float32).ast...  59 us
    all_gather x1, waiting for transfers between devices, shards(): lax.all_gather(jnp.concatenate([latent, key_rope], axis=-1), 'tok', axis=...  49.9 us
    all_to_all x1, waiting for transfers between devices, shards(): lax.all_to_all(processed, ('tok', 'mdl'), split_axis=0, concat_axis=0, ti...  18.3 us
    all_to_all x1, waiting for transfers between devices, shards(): lax.all_to_all(outgoing, ('tok', 'mdl'), split_axis=0, concat_axis=0, til...  12.2 us
    all_to_all x1, starting transfers between devices, shards(): lax.all_to_all(outgoing, ('tok', 'mdl'), split_axis=0, concat_axis=0, til...  10.7 us
    unnamed x32, local copies, waits for them, and re-layouts  6.91 us
    dot_general x1, matrix products, shards(): jnp.einsum('erf,efd->erd', expert_act, w_expert_down, preferred_element_t...  5.54 us
    dot_general x1, matrix products, shards(): jnp.einsum('hqk,khd->hqd', weights.astype(jnp.bfloat16), expanded[..., NO...  5.43 us
  transfers between devices with their start and end apart: 5, of which 4 were waited for; matrix products, arithmetic and copies ran while one was open for 13% of the time, Pallas kernels for 0%

profile of v1, /device:TPU:1, one launch (start us, length us, event | category | flops | bytes accessed | tf_op | source)
XLA Modules:
  0.0 237.3 jit_solution(6687160402400603476)
XLA Ops:
  9.2 2.9 %fusion.53 = f32[256,576]{0,1:T(8,128)S(1)} fusion(bf16[2048,576]{0,1:T(8,128)(2,1)} %param.23, f32[2048]{0:T(1024)} %param.21, f32[256]{0:T(256)S(1)} %add_rsqrt_fusion.2, bf16[2,256,2048]{2,1,0:T(8,128)(2,1)} %param.17, s32[]{:T(128)S(6)} %select_n.33), kind=kOutput, calls=%fused_computation.52 | convolution fusion | flops 606076928 | bytes 4006916 | tf_op jit(solution)/shard_map/dot_general | solution.py:109
  16.1 2.6 %copy.37 = bf16[2048,384]{0,1:T(8,128)(2,1)} copy(bf16[2048,384]{1,0:T(8,128)(2,1)} %param.22) | data formatting | bytes 3145728 | tf_op args[5]
  20.6 2.4 %fusion.51 = f32[256,2,192]{0,2,1:T(8,128)S(1)} fusion(bf16[2,192,2048]{2,1,0:T(8,128)(2,1)} %bitcast.95, f32[2048]{0:T(1024)S(1)} %copy-done.14, f32[256]{0:T(256)S(1)} %add_rsqrt_fusion.2, bf16[2,256,2048]{2,1,0:T(8,128)(2,1)} %param.17, s32[]{:T(128)S(6)} %select_n.33), kind=kOutput, calls=%fused_computation.51 | convolution fusion | flops 404750336 | bytes 3023876 | tf_op jit(solution)/shard_map/dot_general | solution.py:103
  25.3 49.9 %all-gather.2.cloned.1.call-done = bf16[2048,576]{0,1:T(8,128)(2,1)} async-done(((bf16[256,576]{0,1:T(8,128)(2,1)}), bf16[2048,576]{0,1:T(8,128)(2,1)}) %all-gather.2.cloned.1.call-update) | async-done | bytes 2359312 | tf_op jit(solution)/shard_map/all_gather | solution.py:112
  75.3 3.0 %convolution_convert_fusion = bf16[2048,512]{0,1:T(8,128)(2,1)S(1)} fusion(bf16[512,512]{1,0:T(8,128)(2,1)} %param.25, bf16[2048,576]{0,1:T(8,128)(2,1)} %all-gather.2.cloned.1.call-done), kind=kOutput, calls=%fused_computation.12 | convolution fusion | flops 1074790400 | bytes 4718592 | tf_op jit(solution)/shard_map/dot_general | solution.py:117
  79.6 1.8 fusion.1
  81.4 1.7 fusion.99
  83.3 5.4 %fusion.47 = bf16[256,2,128]{0,2,1:T(8,128)(2,1)S(1)} fusion(bf16[2048,2,256]{0,2,1:T(8,128)(2,1)} %bitcast.97, f32[256,2]{0,1:T(2,128)S(1)} %bitcast.104, f32[2,256,2048]{2,1,0:T(8,128)} %copy-done.3, pred[256,2048]{1,0:T(8,128)(4,1)} %fusion.32), kind=kOutput, calls=%fused_computation.49 | convolution fusion | flops 272763392 | bytes 10618880 | tf_op jit(solution)/shard_map/hqk,khd->hqd/dot_general | solution.py:139
  88.8 2.7 %convolution_convert_fusion.2 = bf16[256,2048]{1,0:T(8,128)(2,1)} fusion(bf16[256,256]{0,1:T(8,128)(2,1)S(1)} %bitcast.101, bf16[256,2048]{1,0:T(8,128)(2,1)} %param.26), kind=kOutput, calls=%fused_computation.21 | convolution fusion | flops 268959744 | bytes 2228224 | tf_op jit(solution)/shard_map/dot_general | solution.py:147
  92.0 59.0 %all-reduce.3.cloned.1.call-done = bf16[256,2048]{1,0:T(8,128)(2,1)} async-done(((bf16[256,2048]{1,0:T(8,128)(2,1)}), bf16[256,2048]{1,0:T(8,128)(2,1)}) %all-reduce.3.cloned.1.call-update) | async-done | bytes 1048592 | tf_op jit(solution)/shard_map/psum | solution.py:146
  150.9 2.0 fusion.19
  156.7 2.3 reshape.251
  159.0 10.7 %all-to-all-start = ((bf16[64,4,2048]{2,1,0:T(4,128)(2,1)}), bf16[64,4,2048]{2,1,0:T(4,128)(2,1)}, u32[]{:S(2)}, u32[]{:S(2)}) async-start(bf16[64,4,2048]{2,1,0:T(4,128)(2,1)} %reshape.251), calls=%async_computation.1 | async-start | bytes 2097152 | tf_op jit(solution)/shard_map/all_to_all | solution.py:179
  169.8 2.0 fusion.100
  171.8 4.2 %convolution_convert_fusion.1 = bf16[256,2048]{1,0:T(8,128)(2,1)} fusion(bf16[256,2048]{1,0:T(8,128)(2,1)} %param.30, bf16[256,2048]{1,0:T(8,128)(2,1)} %copy-done.1, bf16[2048,256]{1,0:T(8,128)(2,1)} %param.29, f32[256,256]{1,0:T(8,128)S(1)} %fusion.100), kind=kOutput, calls=%fused_computation.20 | convolution fusion | flops 537788416 | bytes 4456448 | tf_op jit(solution)/shard_map/dot_general | solution.py:158
  176.0 12.2 %all-to-all-done = bf16[64,4,2048]{2,1,0:T(4,128)(2,1)} async-done(((bf16[64,4,2048]{2,1,0:T(4,128)(2,1)}), bf16[64,4,2048]{2,1,0:T(4,128)(2,1)}, u32[]{:S(2)}, u32[]{:S(2)}) %all-to-all-start) | async-done | bytes 1048608 | tf_op jit(solution)/shard_map/all_to_all | solution.py:179
  188.2 2.1 reshape.252
  190.3 4.1 %fusion.9 = f32[256,768]{1,0:T(8,128)} fusion(bf16[256,2048]{1,0:T(8,128)(2,1)} %reshape.252, bf16[1,2048,768]{2,1,0:T(8,128)(2,1)} %param.31), kind=kOutput, calls=%fused_computation.10 | convolution fusion | flops 805306368 | bytes 4980736 | tf_op jit(solution)/shard_map/erd,edf->erf/dot_general | solution.py:186
  194.4 5.5 %fusion.14 = bf16[256,2048]{1,0:T(8,128)(2,1)} fusion(bf16[1,768,2048]{2,1,0:T(8,128)(2,1)S(1)} %copy-done, bf16[256,2048]{1,0:T(8,128)(2,1)} %reshape.252, bf16[1,2048,768]{2,1,0:T(8,128)(2,1)} %param.32, f32[256,768]{1,0:T(8,128)} %fusion.9), kind=kOutput, calls=%fused_computation.22 | convolution fusion | flops 1612316672 | bytes 9175040 | tf_op jit(solution)/shard_map/erf,efd->erd/dot_general | solution.py:189
  200.0 2.3 reshape_transpose_reshape.4
  202.3 5.4 %all-to-all-start.1 = ((bf16[64,4,2048]{2,1,0:T(4,128)(2,1)}), bf16[64,4,2048]{2,1,0:T(4,128)(2,1)}, u32[]{:S(2)}, u32[]{:S(2)}) async-start(bf16[64,4,2048]{2,1,0:T(4,128)(2,1)} %reshape_transpose_reshape.4), calls=%async_computation.2 | async-start | bytes 2097152 | tf_op jit(solution)/shard_map/all_to_all | solution.py:197
  207.8 18.3 %all-to-all-done.1 = bf16[64,4,2048]{2,1,0:T(4,128)(2,1)} async-done(((bf16[64,4,2048]{2,1,0:T(4,128)(2,1)}), bf16[64,4,2048]{2,1,0:T(4,128)(2,1)}, u32[]{:S(2)}, u32[]{:S(2)}) %all-to-all-start.1) | async-done | bytes 1048608 | tf_op jit(solution)/shard_map/all_to_all | solution.py:197
  226.1 2.1 reshape.256
  228.2 2.6 %fusion.18 = bf16[1,32,2048]{2,1,0:T(8,128)(2,1)} fusion(f32[32,256]{1,0:T(8,128)S(1)} %select_reduce_fusion.1, bf16[256,2048]{1,0:T(8,128)(2,1)} %reshape.256, bf16[32,2048]{1,0:T(8,128)(2,1)} %reduce-scatter.2.cloned.1.call-done, bf16[256,2048]{1,0:T(8,128)(2,1)} %copy-done.2, s32[]{:T(128)S(6)} %select_n.39), kind=kOutput, calls=%fused_computation.26 | convolution fusion | flops 201654272 | bytes 1474564 | tf_op jit(solution)/shard_map/dot_general | solution.py:200
  (76 shorter events, 16.6 us)
Async XLA Ops:
  6.5 187.9 %copy-start = (bf16[1,768,2048]{2,1,0:T(8,128)(2,1)S(1)}, bf16[1,768,2048]{2,1,0:T(8,128)(2,1)}, u32[]{:S(2)}) copy-start(bf16[1,768,2048]{2,1,0:T(8,128)(2,1)} %param.33) | copy-start | bytes 9437188
  6.5 68.7 %all-gather.2.cloned.1.call-start = ((), (), s32[]{:S(2)}) async-start(), calls=%async_computation.3 | async-start | bytes 2654208 | tf_op jit(solution)/shard_map/all_gather | solution.py:112
  9.2 4.9 %copy-start.11 = (f32[512]{0:T(512)S(1)}, f32[512]{0:T(512)}, u32[]{:S(2)}) copy-start(f32[512]{0:T(512)} %param.24) | copy-start | bytes 6148
  12.1 0.8 copy-start.4
  14.1 4.7 %copy-start.12 = (s32[2,32,6]{1,0,2:T(2,128)S(1)}, s32[2,32,6]{1,0,2:T(2,128)}, u32[]{:S(2)}) copy-start(s32[2,32,6]{1,0,2:T(2,128)} %param.19) | copy-start | bytes 4612
  15.3 5.3 %copy-start.14 = (f32[2048]{0:T(1024)S(1)}, f32[2048]{0:T(1024)}, u32[]{:S(2)}) copy-start(f32[2048]{0:T(1024)} %param.21) | copy-start | bytes 24580
  16.1 134.9 %all-reduce.3.cloned.1.call-start = ((), (), s32[]{:S(2)}) async-start(), calls=%async_computation.4 | async-start | bytes 2097152 | tf_op jit(solution)/shard_map/psum | solution.py:146
  19.8 5.5 %copy-start.10 = (s32[64,3]{0,1:T(4,128)}, s32[64,3]{0,1:T(4,128)S(1)}, u32[]{:S(2)}) copy-start(s32[64,3]{0,1:T(4,128)S(1)} %reduce-window.9) | copy-start | bytes 2308
  23.0 0.7 copy-start.7
  75.3 3.0 %copy-start.8 = (f32[256,2,192]{0,2,1:T(8,128)S(1)}, f32[256,2,192]{0,2,1:T(8,128)}, u32[]{:S(2)}) copy-start(f32[256,2,192]{0,2,1:T(8,128)} %copy-done.7) | copy-start | bytes 1179652
  78.3 1.3 copy-start.6
  79.6 1.8 copy-start.5
  81.4 1.9 copy-start.3
  88.8 2.8 %slice-start = ((s32[64,3]{0,1:T(4,128)}), s32[64,2]{0,1:T(2,128)S(1)}, s32[]{:S(2)}) async-start(s32[64,3]{0,1:T(4,128)} %copy-done.10), calls=%async_computation.6 | async-start | bytes 2048 | tf_op jit(solution)/shard_map/slice.1
  91.5 62.5 %copy-start.9 = (f32[2048]{0:T(1024)S(1)}, f32[2048]{0:T(1024)}, u32[]{:S(2)}) copy-start(f32[2048]{0:T(1024)} %param.27) | copy-start | bytes 24580
  153.0 1.0 copy-start.2
  154.3 1.0 copy-start.1
  159.0 29.2 %all-to-all-start = ((bf16[64,4,2048]{2,1,0:T(4,128)(2,1)}), bf16[64,4,2048]{2,1,0:T(4,128)(2,1)}, u32[]{:S(2)}, u32[]{:S(2)}) async-start(bf16[64,4,2048]{2,1,0:T(4,128)(2,1)} %reshape.251), calls=%async_computation.1 | async-start | bytes 2097152 | tf_op jit(solution)/shard_map/all_to_all | solution.py:179
  169.7 58.5 %reduce-scatter.2.cloned.1.call-start = ((), (), s32[]{:S(2)}) async-start(), calls=%async_computation.5 | async-start | bytes 1179648 | tf_op jit(solution)/shard_map/reduce_scatter | solution.py:157
  200.0 7.7 %copy-start.13 = (f32[2,32,6]{1,0,2:T(2,128)S(1)}, f32[2,32,6]{1,0,2:T(2,128)}, u32[]{:S(2)}) copy-start(f32[2,32,6]{1,0,2:T(2,128)} %param.20) | copy-start | bytes 4612
  202.3 23.8 %all-to-all-start.1 = ((bf16[64,4,2048]{2,1,0:T(4,128)(2,1)}), bf16[64,4,2048]{2,1,0:T(4,128)(2,1)}, u32[]{:S(2)}, u32[]{:S(2)}) async-start(bf16[64,4,2048]{2,1,0:T(4,128)(2,1)} %reshape_transpose_reshape.4), calls=%async_computation.2 | async-start | bytes 2097152 | tf_op jit(solution)/shard_map/all_to_all | solution.py:197
Sparse Core Ops, SparseCore 0:
  16.2 59.0 all-gather.1
  91.6 59.2 all-reduce.2
  176.1 30.7 reduce-scatter.1

commit v2 on v1

--- a/solution.py
+++ b/solution.py
@@ -10,6 +10,7 @@
 VDIM = 128
 LATENT = 512
 SEGS = 4
+LONGEST_SEGMENT = 1024
 
 
 EPS = 1e-06
@@ -19,6 +20,20 @@
     count = lax.axis_size(axis)
     initial, last = (max(0, -steps), min(count, count - steps))
     return lax.ppermute(value, axis, [(source, source + steps) for source in range(initial, last)])
+
+
+def summed_over(parts, axis):
+    count = lax.axis_size(axis)
+    pieces = parts.reshape((count, parts.shape[0] // count) + parts.shape[1:])
+    arrived = lax.all_to_all(pieces, axis, 0, 0, tiled=True)
+    return jnp.sum(arrived.astype(jnp.float32), axis=0)
+
+
+def gathered_over(block, axis):
+    count = lax.axis_size(axis)
+    copies = jnp.broadcast_to(block[None], (count,) + block.shape)
+    arrived = lax.all_to_all(copies, axis, 0, 0, tiled=True)
+    return arrived.reshape((count * block.shape[0],) + block.shape[1:])
 
 
 def rms_scale(values, gain_vec):
@@ -109,10 +124,15 @@
     compressed = jnp.dot(normed, w_kv_down, preferred_element_type=jnp.float32)
     latent = rms_scale(compressed[:, :LATENT], latent_gain).astype(jnp.bfloat16)
     key_rope = rotary(compressed[:, LATENT:], query_pos).astype(jnp.bfloat16)
-    kv_rows = lax.all_gather(
-        jnp.concatenate([latent, key_rope], axis=-1), "tok", axis=0, tiled=True
-    )
+    n_tok = lax.axis_size("tok")
+    reach = LONGEST_SEGMENT // tok_dev
+    kv_own = jnp.concatenate([latent, key_rope], axis=-1)
+    kv_parts = [kv_own]
+    for steps in range(1, min(reach, n_tok - 1) + 1):
+        kv_parts.insert(0, passed_along(kv_own, "tok", steps))
+    kv_rows = jnp.concatenate(kv_parts, axis=0)
     key_count = kv_rows.shape[0]
+    key_start = query_start + tok_dev - key_count
     expanded = (
         jnp.dot(kv_rows[:, :LATENT], w_kv_up, preferred_element_type=jnp.float32)
         .astype(jnp.bfloat16)
@@ -127,9 +147,13 @@
         "qhd,kd->hqk", queries[..., NOPE:], rope_keys, preferred_element_type=jnp.float32
     )
     scores = scores * score_scale
-    key_index = jnp.arange(key_count, dtype=jnp.int32)
-    allowed = (segment_row[None, :] == query_seg[:, None]) & (
-        key_index[None, :] <= query_index[:, None]
+    key_index = key_start + jnp.arange(key_count, dtype=jnp.int32)
+    padded_seg = jnp.concatenate([jnp.full((key_count,), -1, jnp.int32), segment_row])
+    key_seg = lax.dynamic_slice_in_dim(padded_seg, key_start + key_count, key_count)
+    allowed = (
+        (key_seg[None, :] == query_seg[:, None])
+        & (key_index[None, :] <= query_index[:, None])
+        & (key_index[None, :] >= 0)
     )
     allowed = allowed[None, :, :]
     masked = jnp.where(allowed, scores, -1e30)
@@ -143,23 +167,20 @@
     attended = (
         (weighted / totals).astype(jnp.bfloat16).transpose(1, 0, 2).reshape(tok_dev, local_heads * VDIM)
     )
-    mixed_heads = lax.psum(
-        jnp.dot(attended, w_out, preferred_element_type=jnp.float32).astype(jnp.bfloat16), "mdl"
-    ).astype(jnp.float32)
-    residual = (rows_in.astype(jnp.float32) + mixed_heads).astype(jnp.bfloat16)
-    normed_ffn_all = rms_scale(residual, ffn_gain).astype(jnp.bfloat16)
-    own_residual = lax.dynamic_slice_in_dim(residual, mdl_rank * row_dev, row_dev)
-    normed_ffn = lax.dynamic_slice_in_dim(normed_ffn_all, mdl_rank * row_dev, row_dev)
+    head_parts = jnp.dot(attended, w_out, preferred_element_type=jnp.float32).astype(jnp.bfloat16)
+    mixed_heads = summed_over(head_parts, "mdl")
+    own_input = lax.dynamic_slice_in_dim(rows_in, mdl_rank * row_dev, row_dev)
+    own_residual = (own_input.astype(jnp.float32) + mixed_heads).astype(jnp.bfloat16)
+    normed_ffn = rms_scale(own_residual, ffn_gain).astype(jnp.bfloat16)
+    normed_ffn_all = gathered_over(normed_ffn, "mdl")
 
     gate_proj = jnp.dot(normed_ffn_all, w_shared_gate, preferred_element_type=jnp.float32)
     up_proj = jnp.dot(normed_ffn_all, w_shared_up, preferred_element_type=jnp.float32)
     shared_act = (jax.nn.silu(gate_proj) * up_proj).astype(jnp.bfloat16)
-    shared_out = lax.psum_scatter(
+    shared_out = summed_over(
         jnp.dot(shared_act, w_shared_down, preferred_element_type=jnp.float32).astype(jnp.bfloat16),
         "mdl",
-        scatter_dimension=0,
-        tiled=True,
-    ).astype(jnp.float32)
+    )
 
     onehot = (expert_ids[:, None] == expert_labels[None, :]).astype(jnp.int32)
     earlier = jnp.cumsum(onehot, axis=0) - onehot

time: 238 us -> 178 us (0.75)
  waiting for transfers between devices: 139 us -> 54.3 us
  starting transfers between devices: 16.2 us -> 54.5 us
  between operations: 13.4 us -> 0.38 us
  matrix products: 38.8 us -> 33.6 us
  local copies, waits for them, and re-layouts: 18 us -> 20.5 us
    psum x1 -> x0, waiting for transfers between devices: 59 us -> none  [shards(): lax.psum(jnp.dot(attended, w_out, preferred_element_type=jnp.float32).ast...]
    all_gather x1 -> x0, waiting for transfers between devices: 49.9 us -> none  [shards(): lax.all_gather(jnp.concatenate([latent, key_rope], axis=-1), 'tok', axis=...]
    all_to_all x0 -> x3, waiting for transfers between devices: none -> 25.7 us  [the longest x2 14.8 us: summed_over(): arrived = lax.all_to_all(pieces, axis, 0, 0, tiled=True)]
    ppermute x0 -> x4, starting transfers between devices: none -> 17.7 us  [passed_along(): lax.ppermute(value, axis, [(source, source + steps) for source in range(i...]
    all_to_all x0 -> x3, starting transfers between devices: none -> 15.6 us  [the longest x2 10.5 us: summed_over(): arrived = lax.all_to_all(pieces, axis, 0, 0, tiled=True)]
    all_to_all x1, starting transfers between devices: 10.7 us -> 14.3 us  [shards(): lax.all_to_all(outgoing, ('tok', 'mdl'), split_axis=0, concat_axis=0, til...]
    reduce_sum x0 -> x2, other arithmetic: none -> 2.78 us  [summed_over(): return jnp.sum(arrived.astype(jnp.float32), axis=0)]
    unnamed x32 -> x28, local copies, waits for them, and re-layouts: 6.91 us -> 8.31 us
  transfers between devices with their start and end apart: 5 -> 9, of which waited for: 4 -> 5; matrix products, arithmetic and copies ran while one was open for 13% -> 21% of each run, Pallas kernels for 0% -> 0%
where the time goes in v2:
time: 178 us; the launch traced here: 176 us
  starting transfers between devices  54.5 us (31%)
  waiting for transfers between devices  54.3 us (31%)
  matrix products  33.6 us (19%)
  local copies, waits for them, and re-layouts  20.5 us (12%)
  other arithmetic  13 us (7%)
    ppermute x4, starting transfers between devices, passed_along(): lax.ppermute(value, axis, [(source, source + steps) for source in range(i...  17.7 us
    all_to_all x1, waiting for transfers between devices, shards(): lax.all_to_all(processed, ('tok', 'mdl'), split_axis=0, concat_axis=0, ti...  16.3 us
    all_to_all x2, waiting for transfers between devices, summed_over(): arrived = lax.all_to_all(pieces, axis, 0, 0, tiled=True)  14.8 us
    all_to_all x1, starting transfers between devices, shards(): lax.all_to_all(outgoing, ('tok', 'mdl'), split_axis=0, concat_axis=0, til...  14.3 us
    all_to_all x1, waiting for transfers between devices, shards(): lax.all_to_all(outgoing, ('tok', 'mdl'), split_axis=0, concat_axis=0, til...  12.3 us
    all_to_all x1, waiting for transfers between devices, gathered_over(): arrived = lax.all_to_all(copies, axis, 0, 0, tiled=True)  11 us
    all_to_all x2, starting transfers between devices, summed_over(): arrived = lax.all_to_all(pieces, axis, 0, 0, tiled=True)  10.5 us
    unnamed x28, local copies, waits for them, and re-layouts  8.31 us
  transfers between devices with their start and end apart: 9, of which 5 were waited for; matrix products, arithmetic and copies ran while one was open for 21% of the time, Pallas kernels for 0%

profile of v2, /device:TPU:1, one launch (start us, length us, event | category | flops | bytes accessed | tf_op | source)
XLA Modules:
  0.0 176.3 jit_solution(4617869971657149990)
XLA Ops:
  2.7 2.9 %fusion.52 = f32[256,576]{0,1:T(8,128)S(1)} fusion(bf16[2048,576]{0,1:T(8,128)(2,1)} %param.23, f32[2048]{0:T(1024)} %param.21, f32[256]{0:T(256)S(1)} %add_rsqrt_fusion.1, bf16[2,256,2048]{2,1,0:T(8,128)(2,1)} %param.17, s32[]{:T(128)S(6)} %select_n.37), kind=kOutput, calls=%fused_computation.49 | convolution fusion | flops 606076928 | bytes 4006916 | tf_op jit(solution)/shard_map/dot_general | solution.py:124
  9.5 6.2 %collective-permute-start = (bf16[256,576]{0,1:T(8,128)(2,1)}, bf16[256,576]{0,1:T(8,128)(2,1)}, u32[]{:S(2)}, u32[]{:S(2)}) collective-permute-start(bf16[256,576]{0,1:T(8,128)(2,1)} %pad_maximum_fusion), channel_id=1, source_target_pairs={{0,32},{8,40},{16,48},{24,56},{1,33},{9,41},{17,49},{25,57},{2,34}... | collective-permute-start | bytes 884744 | tf_op jit(solution)/shard_map/ppermute | solution.py:22
  15.7 6.4 %collective-permute-start.1 = (bf16[256,576]{0,1:T(8,128)(2,1)}, bf16[256,576]{0,1:T(8,128)(2,1)}, u32[]{:S(2)}, u32[]{:S(2)}) collective-permute-start(bf16[256,576]{0,1:T(8,128)(2,1)} %pad_maximum_fusion), channel_id=1, source_target_pairs={{0,24},{8,32},{16,40},{24,48},{32,56},{1,25},{9,33},{17,41},{25,49... | collective-permute-start | bytes 884744 | tf_op jit(solution)/shard_map/ppermute | solution.py:22
  24.1 3.1 %collective-permute-start.3 = (bf16[256,576]{0,1:T(8,128)(2,1)}, bf16[256,576]{0,1:T(8,128)(2,1)}, u32[]{:S(2)}, u32[]{:S(2)}) collective-permute-start(bf16[256,576]{0,1:T(8,128)(2,1)} %pad_maximum_fusion), channel_id=1, source_target_pairs={{0,8},{8,16},{16,24},{24,32},{32,40},{40,48},{48,56},{1,9},{9,17},... | collective-permute-start | bytes 884744 | tf_op jit(solution)/shard_map/ppermute | solution.py:22
  27.2 2.6 %copy.37 = bf16[2048,384]{0,1:T(8,128)(2,1)} copy(bf16[2048,384]{1,0:T(8,128)(2,1)} %param.22) | data formatting | bytes 3145728 | tf_op args[5]
  31.0 2.5 %fusion.50 = f32[256,2,192]{0,2,1:T(8,128)S(1)} fusion(bf16[2,192,2048]{2,1,0:T(8,128)(2,1)} %bitcast.105, f32[2048]{0:T(1024)S(1)} %copy-done.10, f32[256]{0:T(256)S(1)} %add_rsqrt_fusion.1, bf16[2,256,2048]{2,1,0:T(8,128)(2,1)} %param.17, s32[]{:T(128)S(6)} %select_n.37), kind=kOutput, calls=%fused_computation.48 | convolution fusion | flops 404750336 | bytes 3023876 | tf_op jit(solution)/shard_map/dot_general | solution.py:118
  41.7 3.7 %fusion.46 = bf16[256,2,128]{0,2,1:T(8,128)(2,1)S(1)} fusion(bf16[1280,2,256]{0,2,1:T(8,128)(2,1)} %bitcast.108, f32[2,256,1280]{2,1,0:T(8,128)} %copy-done.1, pred[256,1280]{1,0:T(8,128)(4,1)} %copy-done.4, f32[256,2]{0,1:T(2,128)S(1)} %bitcast.115), kind=kOutput, calls=%fused_computation.46 | convolution fusion | flops 170526464 | bytes 6686720 | tf_op jit(solution)/shard_map/hqk,khd->hqd/dot_general | solution.py:163
  45.5 2.7 %convolution_convert_fusion.2 = bf16[256,2048]{1,0:T(8,128)(2,1)} fusion(bf16[256,256]{0,1:T(8,128)(2,1)S(1)} %bitcast.109, bf16[256,2048]{1,0:T(8,128)(2,1)} %param.26), kind=kOutput, calls=%fused_computation.21 | convolution fusion | flops 268959744 | bytes 2228224 | tf_op jit(solution)/shard_map/dot_general | solution.py:170
  48.2 6.1 %all-to-all-start = ((bf16[8,32,2048]{2,1,0:T(8,128)(2,1)}), bf16[8,32,2048]{2,1,0:T(8,128)(2,1)}, u32[]{:S(2)}, u32[]{:S(2)}) async-start(bf16[8,32,2048]{2,1,0:T(8,128)(2,1)} %bitcast.104), calls=%async_computation | async-start | bytes 2097152 | tf_op jit(solution)/shard_map/all_to_all | solution.py:28
  55.4 14.0 %all-to-all-done = bf16[8,32,2048]{2,1,0:T(8,128)(2,1)} async-done(((bf16[8,32,2048]{2,1,0:T(8,128)(2,1)}), bf16[8,32,2048]{2,1,0:T(8,128)(2,1)}, u32[]{:S(2)}, u32[]{:S(2)}) %all-to-all-start) | async-done | bytes 1048608 | tf_op jit(solution)/shard_map/all_to_all | solution.py:28
  74.1 5.1 %all-to-all-start.1 = ((bf16[8,32,2048]{2,1,0:T(8,128)(2,1)}), bf16[8,32,2048]{2,1,0:T(8,128)(2,1)}, u32[]{:S(2)}, u32[]{:S(2)}) async-start(bf16[8,32,2048]{2,1,0:T(8,128)(2,1)} %broadcast_in_dim.38), calls=%async_computation.1 | async-start | bytes 2097152 | tf_op jit(solution)/shard_map/all_to_all | solution.py:35
  81.0 2.3 %reshape.310 = bf16[64,4,2048]{2,1,0:T(4,128)(2,1)} reshape(bf16[256,2048]{1,0:T(8,128)(2,1)} %convolution_convert_fusion.3) | data formatting | bytes 2097152 | tf_op jit(solution)/shard_map/reshape | solution.py:198
  83.3 11.0 %all-to-all-done.1 = bf16[8,32,2048]{2,1,0:T(8,128)(2,1)} async-done(((bf16[8,32,2048]{2,1,0:T(8,128)(2,1)}), bf16[8,32,2048]{2,1,0:T(8,128)(2,1)}, u32[]{:S(2)}, u32[]{:S(2)}) %all-to-all-start.1) | async-done | bytes 1048608 | tf_op jit(solution)/shard_map/all_to_all | solution.py:35
  94.2 14.3 %all-to-all-start.3 = ((bf16[64,4,2048]{2,1,0:T(4,128)(2,1)}), bf16[64,4,2048]{2,1,0:T(4,128)(2,1)}, u32[]{:S(2)}, u32[]{:S(2)}) async-start(bf16[64,4,2048]{2,1,0:T(4,128)(2,1)} %reshape.310), calls=%async_computation.3 | async-start | bytes 2097152 | tf_op jit(solution)/shard_map/all_to_all | solution.py:200
  110.6 4.2 %convolution_convert_fusion.1 = bf16[256,2048]{1,0:T(8,128)(2,1)} fusion(bf16[256,2048]{1,0:T(8,128)(2,1)} %param.30, bf16[256,2048]{1,0:T(8,128)(2,1)} %bitcast.17, bf16[2048,256]{1,0:T(8,128)(2,1)} %param.29, f32[256,256]{1,0:T(8,128)S(1)} %fusion.106), kind=kOutput, calls=%fused_computation.20 | convolution fusion | flops 537788416 | bytes 4456448 | tf_op jit(solution)/shard_map/dot_general | solution.py:181
  114.7 12.3 %all-to-all-done.3 = bf16[64,4,2048]{2,1,0:T(4,128)(2,1)} async-done(((bf16[64,4,2048]{2,1,0:T(4,128)(2,1)}), bf16[64,4,2048]{2,1,0:T(4,128)(2,1)}, u32[]{:S(2)}, u32[]{:S(2)}) %all-to-all-start.3) | async-done | bytes 1048608 | tf_op jit(solution)/shard_map/all_to_all | solution.py:200
  127.0 4.4 %all-to-all-start.2 = ((bf16[8,32,2048]{2,1,0:T(8,128)(2,1)}), bf16[8,32,2048]{2,1,0:T(8,128)(2,1)}, u32[]{:S(2)}, u32[]{:S(2)}) async-start(bf16[8,32,2048]{2,1,0:T(8,128)(2,1)} %bitcast.106), calls=%async_computation.2 | async-start | bytes 2097152 | tf_op jit(solution)/shard_map/all_to_all | solution.py:28
  133.6 4.1 %fusion.14 = f32[256,768]{1,0:T(8,128)} fusion(bf16[256,2048]{1,0:T(8,128)(2,1)} %reshape.311, bf16[1,2048,768]{2,1,0:T(8,128)(2,1)} %param.31), kind=kOutput, calls=%fused_computation.13 | convolution fusion | flops 805306368 | bytes 4980736 | tf_op jit(solution)/shard_map/erd,edf->erf/dot_general | solution.py:207
  137.7 5.5 %fusion.18 = bf16[256,2048]{1,0:T(8,128)(2,1)} fusion(bf16[1,768,2048]{2,1,0:T(8,128)(2,1)S(1)} %copy-done, bf16[256,2048]{1,0:T(8,128)(2,1)} %reshape.311, bf16[1,2048,768]{2,1,0:T(8,128)(2,1)} %param.32, f32[256,768]{1,0:T(8,128)} %fusion.14), kind=kOutput, calls=%fused_computation.22 | convolution fusion | flops 1612316672 | bytes 9175040 | tf_op jit(solution)/shard_map/erf,efd->erd/dot_general | solution.py:210
  143.2 2.3 %reshape_transpose_reshape.4 = bf16[64,4,2048]{2,1,0:T(4,128)(2,1)} reshape(bf16[256,2048]{1,0:T(8,128)(2,1)} %fusion.18) | data formatting | bytes 2097152 | tf_op jit(solution)/shard_map/reshape;transpose;reshape | solution.py:216
  146.2 6.9 %all-to-all-start.4 = ((bf16[64,4,2048]{2,1,0:T(4,128)(2,1)}), bf16[64,4,2048]{2,1,0:T(4,128)(2,1)}, u32[]{:S(2)}, u32[]{:S(2)}) async-start(bf16[64,4,2048]{2,1,0:T(4,128)(2,1)} %reshape_transpose_reshape.4), calls=%async_computation.4 | async-start | bytes 2097152 | tf_op jit(solution)/shard_map/all_to_all | solution.py:218
  155.3 16.3 %all-to-all-done.4 = bf16[64,4,2048]{2,1,0:T(4,128)(2,1)} async-done(((bf16[64,4,2048]{2,1,0:T(4,128)(2,1)}), bf16[64,4,2048]{2,1,0:T(4,128)(2,1)}, u32[]{:S(2)}, u32[]{:S(2)}) %all-to-all-start.4) | async-done | bytes 1048608 | tf_op jit(solution)/shard_map/all_to_all | solution.py:218
  171.6 2.2 %reshape.315 = bf16[256,2048]{1,0:T(8,128)(2,1)} reshape(bf16[64,4,2048]{2,1,0:T(4,128)(2,1)} %all-to-all-done.4) | data formatting | bytes 2097152 | tf_op jit(solution)/shard_map/reshape | solution.py:223
  173.8 2.5 %fusion.22 = bf16[1,32,2048]{2,1,0:T(8,128)(2,1)} fusion(f32[32,256]{1,0:T(8,128)} %select_reduce_fusion.1, bf16[256,2048]{1,0:T(8,128)(2,1)} %reshape.315, f32[32,2048]{1,0:T(8,128)S(1)} %convert_reduce_fusion, bf16[32,2048]{1,0:T(8,128)(2,1)S(1)} %get-tuple-element.6), kind=kOutput, calls=%fused_computation.26 | convolution fusion | flops 201588736 | bytes 1605632 | tf_op jit(solution)/shard_map/dot_general | solution.py:221
  (82 shorter events, 32.5 us)
Async XLA Ops:
  0.0 137.7 %copy-start = (bf16[1,768,2048]{2,1,0:T(8,128)(2,1)S(1)}, bf16[1,768,2048]{2,1,0:T(8,128)(2,1)}, u32[]{:S(2)}) copy-start(bf16[1,768,2048]{2,1,0:T(8,128)(2,1)} %param.33) | copy-start | bytes 9437188
  2.7 4.9 %copy-start.6 = (f32[512]{0:T(512)S(1)}, f32[512]{0:T(512)}, u32[]{:S(2)}) copy-start(f32[512]{0:T(512)} %param.24) | copy-start | bytes 6148
  5.6 0.8 copy-start.2
  8.7 22.3 %copy-start.10 = (f32[2048]{0:T(1024)S(1)}, f32[2048]{0:T(1024)}, u32[]{:S(2)}) copy-start(f32[2048]{0:T(1024)} %param.21) | copy-start | bytes 24580
  9.5 24.1 %collective-permute-start = (bf16[256,576]{0,1:T(8,128)(2,1)}, bf16[256,576]{0,1:T(8,128)(2,1)}, u32[]{:S(2)}, u32[]{:S(2)}) collective-permute-start(bf16[256,576]{0,1:T(8,128)(2,1)} %pad_maximum_fusion), channel_id=1, source_target_pairs={{0,32},{8,40},{16,48},{24,56},{1,33},{9,41},{17,49},{25,57},{2,34}... | collective-permute-start | bytes 884744 | tf_op jit(solution)/shard_map/ppermute | solution.py:22
  15.7 19.0 %collective-permute-start.1 = (bf16[256,576]{0,1:T(8,128)(2,1)}, bf16[256,576]{0,1:T(8,128)(2,1)}, u32[]{:S(2)}, u32[]{:S(2)}) collective-permute-start(bf16[256,576]{0,1:T(8,128)(2,1)} %pad_maximum_fusion), channel_id=1, source_target_pairs={{0,24},{8,32},{16,40},{24,48},{32,56},{1,25},{9,33},{17,41},{25,49... | collective-permute-start | bytes 884744 | tf_op jit(solution)/shard_map/ppermute | solution.py:22
  22.0 13.6 %collective-permute-start.2 = (bf16[256,576]{0,1:T(8,128)(2,1)}, bf16[256,576]{0,1:T(8,128)(2,1)}, u32[]{:S(2)}, u32[]{:S(2)}) collective-permute-start(bf16[256,576]{0,1:T(8,128)(2,1)} %pad_maximum_fusion), channel_id=1, source_target_pairs={{0,16},{8,24},{16,32},{24,40},{32,48},{40,56},{1,17},{9,25},{17,33... | collective-permute-start | bytes 884744 | tf_op jit(solution)/shard_map/ppermute | solution.py:22
  24.1 12.6 %collective-permute-start.3 = (bf16[256,576]{0,1:T(8,128)(2,1)}, bf16[256,576]{0,1:T(8,128)(2,1)}, u32[]{:S(2)}, u32[]{:S(2)}) collective-permute-start(bf16[256,576]{0,1:T(8,128)(2,1)} %pad_maximum_fusion), channel_id=1, source_target_pairs={{0,8},{8,16},{16,24},{24,32},{32,40},{40,48},{48,56},{1,9},{9,17},... | collective-permute-start | bytes 884744 | tf_op jit(solution)/shard_map/ppermute | solution.py:22
  31.0 9.2 %copy-start.4 = (pred[256,1280]{1,0:T(8,128)(4,1)}, pred[256,1280]{1,0:T(8,128)(4,1)S(1)}, u32[]{:S(2)}) copy-start(pred[256,1280]{1,0:T(8,128)(4,1)S(1)} %and_and_fusion) | copy-start | bytes 983044
  33.5 4.1 %copy-start.9 = (bf16[512,512]{1,0:T(8,128)(2,1)S(1)}, bf16[512,512]{1,0:T(8,128)(2,1)}, u32[]{:S(2)}) copy-start(bf16[512,512]{1,0:T(8,128)(2,1)} %param.25) | copy-start | bytes 1572868
  38.6 1.1 copy-start.3
  40.2 1.5 copy-start.1
  45.5 8.8 %copy-start.7 = (s32[2,32,6]{1,0,2:T(2,128)S(1)}, s32[2,32,6]{1,0,2:T(2,128)}, u32[]{:S(2)}) copy-start(s32[2,32,6]{1,0,2:T(2,128)} %param.19) | copy-start | bytes 4612
  48.2 23.7 %copy-start.5 = (f32[2048]{0:T(1024)S(1)}, f32[2048]{0:T(1024)}, u32[]{:S(2)}) copy-start(f32[2048]{0:T(1024)} %param.27) | copy-start | bytes 24580
  48.2 21.2 %all-to-all-start = ((bf16[8,32,2048]{2,1,0:T(8,128)(2,1)}), bf16[8,32,2048]{2,1,0:T(8,128)(2,1)}, u32[]{:S(2)}, u32[]{:S(2)}) async-start(bf16[8,32,2048]{2,1,0:T(8,128)(2,1)} %bitcast.104), calls=%async_computation | async-start | bytes 2097152 | tf_op jit(solution)/shard_map/all_to_all | solution.py:28
  74.1 20.2 %all-to-all-start.1 = ((bf16[8,32,2048]{2,1,0:T(8,128)(2,1)}), bf16[8,32,2048]{2,1,0:T(8,128)(2,1)}, u32[]{:S(2)}, u32[]{:S(2)}) async-start(bf16[8,32,2048]{2,1,0:T(8,128)(2,1)} %broadcast_in_dim.38), calls=%async_computation.1 | async-start | bytes 2097152 | tf_op jit(solution)/shard_map/all_to_all | solution.py:35
  94.2 32.8 %all-to-all-start.3 = ((bf16[64,4,2048]{2,1,0:T(4,128)(2,1)}), bf16[64,4,2048]{2,1,0:T(4,128)(2,1)}, u32[]{:S(2)}, u32[]{:S(2)}) async-start(bf16[64,4,2048]{2,1,0:T(4,128)(2,1)} %reshape.310), calls=%async_computation.3 | async-start | bytes 2097152 | tf_op jit(solution)/shard_map/all_to_all | solution.py:200
  127.0 19.2 %all-to-all-start.2 = ((bf16[8,32,2048]{2,1,0:T(8,128)(2,1)}), bf16[8,32,2048]{2,1,0:T(8,128)(2,1)}, u32[]{:S(2)}, u32[]{:S(2)}) async-start(bf16[8,32,2048]{2,1,0:T(8,128)(2,1)} %bitcast.106), calls=%async_computation.2 | async-start | bytes 2097152 | tf_op jit(solution)/shard_map/all_to_all | solution.py:28
  143.2 10.0 %copy-start.8 = (f32[2,32,6]{1,0,2:T(2,128)S(1)}, f32[2,32,6]{1,0,2:T(2,128)}, u32[]{:S(2)}) copy-start(f32[2,32,6]{1,0,2:T(2,128)} %param.20) | copy-start | bytes 4612
  146.2 25.4 %all-to-all-start.4 = ((bf16[64,4,2048]{2,1,0:T(4,128)(2,1)}), bf16[64,4,2048]{2,1,0:T(4,128)(2,1)}, u32[]{:S(2)}, u32[]{:S(2)}) async-start(bf16[64,4,2048]{2,1,0:T(4,128)(2,1)} %reshape_transpose_reshape.4), calls=%async_computation.4 | async-start | bytes 2097152 | tf_op jit(solution)/shard_map/all_to_all | solution.py:218

commit v3 on v2

--- a/solution.py
+++ b/solution.py
@@ -22,18 +22,29 @@
     return lax.ppermute(value, axis, [(source, source + steps) for source in range(initial, last)])
 
 
-def summed_over(parts, axis):
+def summed_over(parts, axis, arrival_order=False):
     count = lax.axis_size(axis)
+    rank = lax.axis_index(axis)
     pieces = parts.reshape((count, parts.shape[0] // count) + parts.shape[1:])
-    arrived = lax.all_to_all(pieces, axis, 0, 0, tiled=True)
-    return jnp.sum(arrived.astype(jnp.float32), axis=0)
+
+    def piece_for(steps):
+        if arrival_order:
+            return pieces[(count - steps) % count]
+        return lax.dynamic_index_in_dim(pieces, (rank + steps) % count, 0, keepdims=False)
+
+    total = piece_for(0).astype(jnp.float32)
+    for steps in range(1, count):
+        moved = lax.ppermute(piece_for(steps), axis, [(i, (i + steps) % count) for i in range(count)])
+        total = total + moved.astype(jnp.float32)
+    return total
 
 
 def gathered_over(block, axis):
     count = lax.axis_size(axis)
-    copies = jnp.broadcast_to(block[None], (count,) + block.shape)
-    arrived = lax.all_to_all(copies, axis, 0, 0, tiled=True)
-    return arrived.reshape((count * block.shape[0],) + block.shape[1:])
+    arrived = [block]
+    for steps in range(1, count):
+        arrived.append(lax.ppermute(block, axis, [(i, (i + steps) % count) for i in range(count)]))
+    return jnp.concatenate(arrived, axis=0)
 
 
 def rms_scale(values, gain_vec):
@@ -180,6 +191,7 @@
     shared_out = summed_over(
         jnp.dot(shared_act, w_shared_down, preferred_element_type=jnp.float32).astype(jnp.bfloat16),
         "mdl",
+        arrival_order=True,
     )
 
     onehot = (expert_ids[:, None] == expert_labels[None, :]).astype(jnp.int32)

time: 178 us -> 169 us (0.949)
  waiting for transfers between devices: 54.3 us -> 22 us
  local copies, waits for them, and re-layouts: 20.5 us -> 32.8 us
  starting transfers between devices: 54.5 us -> 66.4 us
    ppermute x0 -> x21, starting transfers between devices: none -> 29.6 us  [the longest x14 19.5 us: summed_over(): lax.ppermute(piece_for(steps), axis, [(i, (i + steps) % count) for i in r...]
    all_to_all x3 -> x0, waiting for transfers between devices: 25.7 us -> none  [the longest x2 14.8 us: summed_over(): arrived = lax.all_to_all(pieces, axis, 0, 0, tiled=True)]
    ppermute x0 -> x21, waiting for transfers between devices: none -> 22 us  [the longest x14 15.1 us: summed_over(): lax.ppermute(piece_for(steps), axis, [(i, (i + steps) % count) for i in r...]
    all_to_all x1, waiting for transfers between devices: 16.3 us -> 0.01 us  [shards(): lax.all_to_all(processed, ('tok', 'mdl'), split_axis=0, concat_axis=0, ti...]
    all_to_all x3 -> x0, starting transfers between devices: 15.6 us -> none  [the longest x2 10.5 us: summed_over(): arrived = lax.all_to_all(pieces, axis, 0, 0, tiled=True)]
    all_to_all x1, waiting for transfers between devices: 12.3 us -> 0.01 us  [shards(): lax.all_to_all(outgoing, ('tok', 'mdl'), split_axis=0, concat_axis=0, til...]
    unnamed x28 -> x58, local copies, waits for them, and re-layouts: 8.31 us -> 18.2 us
    all_to_all x1, starting transfers between devices: 14.3 us -> 9.82 us  [shards(): lax.all_to_all(outgoing, ('tok', 'mdl'), split_axis=0, concat_axis=0, til...]
  transfers between devices with their start and end apart: 9 -> 27, of which waited for: 5 -> 7; matrix products, arithmetic and copies ran while one was open for 21% -> 21% of each run, Pallas kernels for 0% -> 0%
where the time goes in v3:
time: 169 us; the launch traced here: 168 us
  starting transfers between devices  66.4 us (39%)
  matrix products  33.5 us (20%)
  local copies, waits for them, and re-layouts  32.8 us (19%)
  waiting for transfers between devices  22 us (13%)
  other arithmetic  12.7 us (8%)
    ppermute x14, starting transfers between devices, summed_over(): lax.ppermute(piece_for(steps), axis, [(i, (i + steps) % count) for i in r...  19.5 us
    unnamed x58, local copies, waits for them, and re-layouts  18.2 us
    ppermute x4, starting transfers between devices, passed_along(): lax.ppermute(value, axis, [(source, source + steps) for source in range(i...  17.7 us
    ppermute x14, waiting for transfers between devices, summed_over(): lax.ppermute(piece_for(steps), axis, [(i, (i + steps) % count) for i in r...  15.1 us
    ppermute x7, starting transfers between devices, gathered_over(): lax.ppermute(block, axis, [(i, (i + steps) % count) for i in range(count)])  10.1 us
    all_to_all x1, starting transfers between devices, shards(): lax.all_to_all(outgoing, ('tok', 'mdl'), split_axis=0, concat_axis=0, til...  9.82 us
    all_to_all x1, starting transfers between devices, shards(): lax.all_to_all(processed, ('tok', 'mdl'), split_axis=0, concat_axis=0, ti...  9.28 us
    ppermute x7, waiting for transfers between devices, gathered_over(): lax.ppermute(block, axis, [(i, (i + steps) % count) for i in range(count)])  6.91 us
  transfers between devices with their start and end apart: 27, of which 7 were waited for; matrix products, arithmetic and copies ran while one was open for 21% of the time, Pallas kernels for 0%

profile of v3, /device:TPU:1, one launch (start us, length us, event | category | flops | bytes accessed | tf_op | source)
XLA Modules:
  0.0 168.0 jit_solution(14779528050644958980)
XLA Ops:
  2.7 2.9 %fusion.49 = f32[256,576]{0,1:T(8,128)S(1)} fusion(bf16[2048,576]{0,1:T(8,128)(2,1)} %param.23, f32[2048]{0:T(1024)} %param.21, f32[256]{0:T(256)S(1)} %add_rsqrt_fusion.1, bf16[2,256,2048]{2,1,0:T(8,128)(2,1)} %param.17, s32[]{:T(128)S(6)} %select_n.97), kind=kOutput, calls=%fused_computation.42 | convolution fusion | flops 606076928 | bytes 4006916 | tf_op jit(solution)/shard_map/dot_general | solution.py:135
  9.5 6.2 %collective-permute-start = (bf16[256,576]{0,1:T(8,128)(2,1)}, bf16[256,576]{0,1:T(8,128)(2,1)}, u32[]{:S(2)}, u32[]{:S(2)}) collective-permute-start(bf16[256,576]{0,1:T(8,128)(2,1)} %pad_maximum_fusion), channel_id=1, source_target_pairs={{0,32},{8,40},{16,48},{24,56},{1,33},{9,41},{17,49},{25,57},{2,34}... | collective-permute-start | bytes 884744 | tf_op jit(solution)/shard_map/ppermute | solution.py:22
  15.7 6.4 %collective-permute-start.1 = (bf16[256,576]{0,1:T(8,128)(2,1)}, bf16[256,576]{0,1:T(8,128)(2,1)}, u32[]{:S(2)}, u32[]{:S(2)}) collective-permute-start(bf16[256,576]{0,1:T(8,128)(2,1)} %pad_maximum_fusion), channel_id=1, source_target_pairs={{0,24},{8,32},{16,40},{24,48},{32,56},{1,25},{9,33},{17,41},{25,49... | collective-permute-start | bytes 884744 | tf_op jit(solution)/shard_map/ppermute | solution.py:22
  24.1 3.1 %collective-permute-start.3 = (bf16[256,576]{0,1:T(8,128)(2,1)}, bf16[256,576]{0,1:T(8,128)(2,1)}, u32[]{:S(2)}, u32[]{:S(2)}) collective-permute-start(bf16[256,576]{0,1:T(8,128)(2,1)} %pad_maximum_fusion), channel_id=1, source_target_pairs={{0,8},{8,16},{16,24},{24,32},{32,40},{40,48},{48,56},{1,9},{9,17},... | collective-permute-start | bytes 884744 | tf_op jit(solution)/shard_map/ppermute | solution.py:22
  27.2 2.6 %copy.37 = bf16[2048,384]{0,1:T(8,128)(2,1)} copy(bf16[2048,384]{1,0:T(8,128)(2,1)} %param.22) | data formatting | bytes 3145728 | tf_op args[5]
  29.8 3.2 %fusion.47 = f32[256,2,192]{0,2,1:T(8,128)} fusion(bf16[2,192,2048]{2,1,0:T(8,128)(2,1)} %bitcast.114, f32[2048]{0:T(1024)S(1)} %copy-done.22, f32[256]{0:T(256)S(1)} %add_rsqrt_fusion.1, bf16[2,256,2048]{2,1,0:T(8,128)(2,1)} %param.17, s32[]{:T(128)S(6)} %select_n.97), kind=kOutput, calls=%fused_computation.41 | convolution fusion | flops 404750336 | bytes 3023876 | tf_op jit(solution)/shard_map/dot_general | solution.py:129
  46.5 3.7 %fusion.43 = bf16[256,2,128]{0,2,1:T(8,128)(2,1)S(1)} fusion(bf16[1280,2,256]{0,2,1:T(8,128)(2,1)} %bitcast.116, f32[2,256,1280]{2,1,0:T(8,128)} %copy-done.2, pred[256,1280]{1,0:T(8,128)(4,1)} %and_and_fusion, f32[256,2]{0,1:T(2,128)S(1)} %bitcast.123), kind=kOutput, calls=%fused_computation.39 | convolution fusion | flops 170526464 | bytes 6686720 | tf_op jit(solution)/shard_map/hqk,khd->hqd/dot_general | solution.py:174
  61.0 2.6 %collective-permute-start.8 = (bf16[32,2048]{1,0:T(8,128)(2,1)}, bf16[32,2048]{1,0:T(8,128)(2,1)}, u32[]{:S(2)}, u32[]{:S(2)}) collective-permute-start(bf16[32,2048]{1,0:T(8,128)(2,1)} %get-tuple-element.19), channel_id=1, source_target_pairs={{0,5},{1,6},{2,7},{3,0},{4,1},{5,2},{6,3},{7,4},{8,13},{9,14},{10,... | collective-permute-start | bytes 393224 | tf_op jit(solution)/shard_map/ppermute | solution.py:37
  63.8 2.4 %collective-permute-done.5 = bf16[32,2048]{1,0:T(8,128)(2,1)S(1)} collective-permute-done((bf16[32,2048]{1,0:T(8,128)(2,1)}, bf16[32,2048]{1,0:T(8,128)(2,1)S(1)}, u32[]{:S(2)}, u32[]{:S(2)}) %collective-permute-start.5) | collective-permute-done | bytes 131104 | tf_op jit(solution)/shard_map/ppermute | solution.py:37
  66.1 5.8 %collective-permute-done.6 = bf16[32,2048]{1,0:T(8,128)(2,1)} collective-permute-done((bf16[32,2048]{1,0:T(8,128)(2,1)}, bf16[32,2048]{1,0:T(8,128)(2,1)}, u32[]{:S(2)}, u32[]{:S(2)}) %collective-permute-start.6) | collective-permute-done | bytes 131104 | tf_op jit(solution)/shard_map/ppermute | solution.py:37
  83.3 2.3 %reshape.307 = bf16[64,4,2048]{2,1,0:T(4,128)(2,1)} reshape(bf16[256,2048]{1,0:T(8,128)(2,1)} %convolution_convert_fusion.3) | data formatting | bytes 2097152 | tf_op jit(solution)/shard_map/reshape | solution.py:210
  85.6 9.8 %all-to-all-start = ((bf16[64,4,2048]{2,1,0:T(4,128)(2,1)}), bf16[64,4,2048]{2,1,0:T(4,128)(2,1)}, u32[]{:S(2)}, u32[]{:S(2)}) async-start(bf16[64,4,2048]{2,1,0:T(4,128)(2,1)} %reshape.307), calls=%async_computation | async-start | bytes 2097152 | tf_op jit(solution)/shard_map/all_to_all | solution.py:212
  95.4 2.6 %collective-permute-start.16 = (bf16[32,2048]{1,0:T(8,128)(2,1)S(1)}, bf16[32,2048]{1,0:T(8,128)(2,1)S(1)}, u32[]{:S(2)}, u32[]{:S(2)}) collective-permute-start(bf16[32,2048]{1,0:T(8,128)(2,1)S(1)} %get-tuple-element.6), channel_id=1, source_target_pairs={{0,6},{1,7},{2,0},{3,1},{4,2},{5,3},{6,4},{7,5},{8,14},{9,15},{10,... | collective-permute-start | bytes 393224 | tf_op jit(solution)/shard_map/ppermute | solution.py:46
  105.6 5.6 %collective-permute-done.16 = bf16[32,2048]{1,0:T(8,128)(2,1)S(1)} collective-permute-done((bf16[32,2048]{1,0:T(8,128)(2,1)S(1)}, bf16[32,2048]{1,0:T(8,128)(2,1)S(1)}, u32[]{:S(2)}, u32[]{:S(2)}) %collective-permute-start.16) | collective-permute-done | bytes 131104 | tf_op jit(solution)/shard_map/ppermute | solution.py:46
  115.9 2.2 %reshape.308 = bf16[256,2048]{1,0:T(8,128)(2,1)} reshape(bf16[64,4,2048]{2,1,0:T(4,128)(2,1)} %all-to-all-done) | data formatting | bytes 2097152 | tf_op jit(solution)/shard_map/reshape.35
  118.0 4.1 %fusion.14 = f32[256,768]{1,0:T(8,128)} fusion(bf16[256,2048]{1,0:T(8,128)(2,1)} %reshape.308, bf16[1,2048,768]{2,1,0:T(8,128)(2,1)} %param.31), kind=kOutput, calls=%fused_computation.13 | convolution fusion | flops 805306368 | bytes 4980736 | tf_op jit(solution)/shard_map/erd,edf->erf/dot_general | solution.py:219
  122.1 5.5 %fusion.18 = bf16[256,2048]{1,0:T(8,128)(2,1)} fusion(bf16[1,768,2048]{2,1,0:T(8,128)(2,1)S(1)} %copy-done, bf16[256,2048]{1,0:T(8,128)(2,1)} %reshape.308, bf16[1,2048,768]{2,1,0:T(8,128)(2,1)} %param.32, f32[256,768]{1,0:T(8,128)} %fusion.14), kind=kOutput, calls=%fused_computation.22 | convolution fusion | flops 1612316672 | bytes 9175040 | tf_op jit(solution)/shard_map/erf,efd->erd/dot_general | solution.py:222
  127.6 2.2 %reshape_transpose_reshape.4 = bf16[64,4,2048]{2,1,0:T(4,128)(2,1)} reshape(bf16[256,2048]{1,0:T(8,128)(2,1)} %fusion.18) | data formatting | bytes 2097152 | tf_op jit(solution)/shard_map/reshape;transpose;reshape | solution.py:228
  129.8 9.3 %all-to-all-start.1 = ((bf16[64,4,2048]{2,1,0:T(4,128)(2,1)}), bf16[64,4,2048]{2,1,0:T(4,128)(2,1)}, u32[]{:S(2)}, u32[]{:S(2)}) async-start(bf16[64,4,2048]{2,1,0:T(4,128)(2,1)} %reshape_transpose_reshape.4), calls=%async_computation.1 | async-start | bytes 2097152 | tf_op jit(solution)/shard_map/all_to_all | solution.py:230
  139.1 4.1 %convolution_convert_fusion.1 = bf16[256,2048]{1,0:T(8,128)(2,1)} fusion(bf16[256,2048]{1,0:T(8,128)(2,1)} %param.30, f32[256,256]{1,0:T(8,128)S(1)} %fusion.106, bf16[256,2048]{1,0:T(8,128)(2,1)} %constant_dynamic-update-slice_fusion.5, bf16[2048,256]{1,0:T(8,128)(2,1)} %param.29), kind=kOutput, calls=%fused_computation.20 | convolution fusion | flops 537788416 | bytes 4456448 | tf_op jit(solution)/shard_map/dot_general | solution.py:192
  152.2 3.1 %collective-permute-start.23 = (bf16[32,2048]{1,0:T(8,128)(2,1)}, bf16[32,2048]{1,0:T(8,128)(2,1)}, u32[]{:S(2)}, u32[]{:S(2)}) collective-permute-start(bf16[32,2048]{1,0:T(8,128)(2,1)} %get-tuple-element.11), channel_id=1, source_target_pairs={{0,6},{1,7},{2,0},{3,1},{4,2},{5,3},{6,4},{7,5},{8,14},{9,15},{10,... | collective-permute-start | bytes 393224 | tf_op jit(solution)/shard_map/ppermute | solution.py:37
  155.3 4.0 %collective-permute-done.19 = bf16[32,2048]{1,0:T(8,128)(2,1)S(1)} collective-permute-done((bf16[32,2048]{1,0:T(8,128)(2,1)S(1)}, bf16[32,2048]{1,0:T(8,128)(2,1)S(1)}, u32[]{:S(2)}, u32[]{:S(2)}) %collective-permute-start.19) | collective-permute-done | bytes 131104 | tf_op jit(solution)/shard_map/ppermute | solution.py:37
  162.3 2.3 %collective-permute-done.21 = bf16[32,2048]{1,0:T(8,128)(2,1)} collective-permute-done((bf16[32,2048]{1,0:T(8,128)(2,1)}, bf16[32,2048]{1,0:T(8,128)(2,1)}, u32[]{:S(2)}, u32[]{:S(2)}) %collective-permute-start.21) | collective-permute-done | bytes 131104 | tf_op jit(solution)/shard_map/ppermute | solution.py:37
  165.2 2.9 %fusion.80 = bf16[1,32,2048]{2,1,0:T(8,128)(2,1)} fusion(bf16[32,2048]{1,0:T(8,128)(2,1)} %collective-permute-done.24, bf16[32,2048]{1,0:T(8,128)(2,1)} %collective-permute-done.23, bf16[32,2048]{1,0:T(8,128)(2,1)} %collective-permute-done.22, bf16[32,2048]{1,0:T(8,128)(2,1)} %collective-permute-done.21, bf16[32,2048]{1,0:T(8,128)(2,1)} %collective-permute-done.20, ...), kind=kOutput, calls=%fused_computation.87 | convolution fusion | flops 202571776 | bytes 2392064 | tf_op jit(solution)/shard_map/dot_general | solution.py:233
  (149 shorter events, 68.5 us)
Async XLA Ops:
  9.5 28.2 %collective-permute-start = (bf16[256,576]{0,1:T(8,128)(2,1)}, bf16[256,576]{0,1:T(8,128)(2,1)}, u32[]{:S(2)}, u32[]{:S(2)}) collective-permute-start(bf16[256,576]{0,1:T(8,128)(2,1)} %pad_maximum_fusion), channel_id=1, source_target_pairs={{0,32},{8,40},{16,48},{24,56},{1,33},{9,41},{17,49},{25,57},{2,34}... | collective-permute-start | bytes 884744 | tf_op jit(solution)/shard_map/ppermute | solution.py:22
  15.7 23.0 %collective-permute-start.1 = (bf16[256,576]{0,1:T(8,128)(2,1)}, bf16[256,576]{0,1:T(8,128)(2,1)}, u32[]{:S(2)}, u32[]{:S(2)}) collective-permute-start(bf16[256,576]{0,1:T(8,128)(2,1)} %pad_maximum_fusion), channel_id=1, source_target_pairs={{0,24},{8,32},{16,40},{24,48},{32,56},{1,25},{9,33},{17,41},{25,49... | collective-permute-start | bytes 884744 | tf_op jit(solution)/shard_map/ppermute | solution.py:22
  22.1 17.7 %collective-permute-start.2 = (bf16[256,576]{0,1:T(8,128)(2,1)}, bf16[256,576]{0,1:T(8,128)(2,1)}, u32[]{:S(2)}, u32[]{:S(2)}) collective-permute-start(bf16[256,576]{0,1:T(8,128)(2,1)} %pad_maximum_fusion), channel_id=1, source_target_pairs={{0,16},{8,24},{16,32},{24,40},{32,48},{40,56},{1,17},{9,25},{17,33... | collective-permute-start | bytes 884744 | tf_op jit(solution)/shard_map/ppermute | solution.py:22
  24.1 16.7 %collective-permute-start.3 = (bf16[256,576]{0,1:T(8,128)(2,1)}, bf16[256,576]{0,1:T(8,128)(2,1)}, u32[]{:S(2)}, u32[]{:S(2)}) collective-permute-start(bf16[256,576]{0,1:T(8,128)(2,1)} %pad_maximum_fusion), channel_id=1, source_target_pairs={{0,8},{8,16},{16,24},{24,32},{32,40},{40,48},{48,56},{1,9},{9,17},... | collective-permute-start | bytes 884744 | tf_op jit(solution)/shard_map/ppermute | solution.py:22
  55.3 8.3 %collective-permute-start.4 = (bf16[32,2048]{1,0:T(8,128)(2,1)}, bf16[32,2048]{1,0:T(8,128)(2,1)}, u32[]{:S(2)}, u32[]{:S(2)}) collective-permute-start(bf16[32,2048]{1,0:T(8,128)(2,1)} %get-tuple-element.16), channel_id=1, source_target_pairs={{0,1},{1,2},{2,3},{3,4},{4,5},{5,6},{6,7},{7,0},{8,9},{9,10},{10,1... | collective-permute-start | bytes 393224 | tf_op jit(solution)/shard_map/ppermute | solution.py:37
  56.8 9.3 %collective-permute-start.5 = (bf16[32,2048]{1,0:T(8,128)(2,1)}, bf16[32,2048]{1,0:T(8,128)(2,1)S(1)}, u32[]{:S(2)}, u32[]{:S(2)}) collective-permute-start(bf16[32,2048]{1,0:T(8,128)(2,1)} %get-tuple-element.22), channel_id=1, source_target_pairs={{0,2},{1,3},{2,4},{3,5},{4,6},{5,7},{6,0},{7,1},{8,10},{9,11},{10,... | collective-permute-start | bytes 393224 | tf_op jit(solution)/shard_map/ppermute | solution.py:37
  58.1 13.9 %collective-permute-start.6 = (bf16[32,2048]{1,0:T(8,128)(2,1)}, bf16[32,2048]{1,0:T(8,128)(2,1)}, u32[]{:S(2)}, u32[]{:S(2)}) collective-permute-start(bf16[32,2048]{1,0:T(8,128)(2,1)} %get-tuple-element.21), channel_id=1, source_target_pairs={{0,3},{1,4},{2,5},{3,6},{4,7},{5,0},{6,1},{7,2},{8,11},{9,12},{10,... | collective-permute-start | bytes 393224 | tf_op jit(solution)/shard_map/ppermute | solution.py:37
  60.2 11.8 %collective-permute-start.7 = (bf16[32,2048]{1,0:T(8,128)(2,1)}, bf16[32,2048]{1,0:T(8,128)(2,1)}, u32[]{:S(2)}, u32[]{:S(2)}) collective-permute-start(bf16[32,2048]{1,0:T(8,128)(2,1)} %get-tuple-element.20), channel_id=1, source_target_pairs={{0,4},{1,5},{2,6},{3,7},{4,0},{5,1},{6,2},{7,3},{8,12},{9,13},{10,... | collective-permute-start | bytes 393224 | tf_op jit(solution)/shard_map/ppermute | solution.py:37
  61.0 11.0 %collective-permute-start.8 = (bf16[32,2048]{1,0:T(8,128)(2,1)}, bf16[32,2048]{1,0:T(8,128)(2,1)}, u32[]{:S(2)}, u32[]{:S(2)}) collective-permute-start(bf16[32,2048]{1,0:T(8,128)(2,1)} %get-tuple-element.19), channel_id=1, source_target_pairs={{0,5},{1,6},{2,7},{3,0},{4,1},{5,2},{6,3},{7,4},{8,13},{9,14},{10,... | collective-permute-start | bytes 393224 | tf_op jit(solution)/shard_map/ppermute | solution.py:37
  63.6 8.4 %collective-permute-start.9 = (bf16[32,2048]{1,0:T(8,128)(2,1)S(1)}, bf16[32,2048]{1,0:T(8,128)(2,1)}, u32[]{:S(2)}, u32[]{:S(2)}) collective-permute-start(bf16[32,2048]{1,0:T(8,128)(2,1)S(1)} %get-tuple-element.18), channel_id=1, source_target_pairs={{0,6},{1,7},{2,0},{3,1},{4,2},{5,3},{6,4},{7,5},{8,14},{9,15},{10,... | collective-permute-start | bytes 393224 | tf_op jit(solution)/shard_map/ppermute | solution.py:37
  75.0 20.4 %collective-permute-start.11 = (bf16[32,2048]{1,0:T(8,128)(2,1)S(1)}, bf16[32,2048]{1,0:T(8,128)(2,1)}, u32[]{:S(2)}, u32[]{:S(2)}) collective-permute-start(bf16[32,2048]{1,0:T(8,128)(2,1)S(1)} %get-tuple-element.6), channel_id=1, source_target_pairs={{0,1},{1,2},{2,3},{3,4},{4,5},{5,6},{6,7},{7,0},{8,9},{9,10},{10,1... | collective-permute-start | bytes 393224 | tf_op jit(solution)/shard_map/ppermute | solution.py:46
  75.6 24.0 %collective-permute-start.12 = (bf16[32,2048]{1,0:T(8,128)(2,1)S(1)}, bf16[32,2048]{1,0:T(8,128)(2,1)}, u32[]{:S(2)}, u32[]{:S(2)}) collective-permute-start(bf16[32,2048]{1,0:T(8,128)(2,1)S(1)} %get-tuple-element.6), channel_id=1, source_target_pairs={{0,2},{1,3},{2,4},{3,5},{4,6},{5,7},{6,0},{7,1},{8,10},{9,11},{10,... | collective-permute-start | bytes 393224 | tf_op jit(solution)/shard_map/ppermute | solution.py:46
  77.3 24.6 %collective-permute-start.13 = (bf16[32,2048]{1,0:T(8,128)(2,1)S(1)}, bf16[32,2048]{1,0:T(8,128)(2,1)}, u32[]{:S(2)}, u32[]{:S(2)}) collective-permute-start(bf16[32,2048]{1,0:T(8,128)(2,1)S(1)} %get-tuple-element.6), channel_id=1, source_target_pairs={{0,3},{1,4},{2,5},{3,6},{4,7},{5,0},{6,1},{7,2},{8,11},{9,12},{10,... | collective-permute-start | bytes 393224 | tf_op jit(solution)/shard_map/ppermute | solution.py:46
  79.0 24.4 %collective-permute-start.14 = (bf16[32,2048]{1,0:T(8,128)(2,1)S(1)}, bf16[32,2048]{1,0:T(8,128)(2,1)}, u32[]{:S(2)}, u32[]{:S(2)}) collective-permute-start(bf16[32,2048]{1,0:T(8,128)(2,1)S(1)} %get-tuple-element.6), channel_id=1, source_target_pairs={{0,4},{1,5},{2,6},{3,7},{4,0},{5,1},{6,2},{7,3},{8,12},{9,13},{10,... | collective-permute-start | bytes 393224 | tf_op jit(solution)/shard_map/ppermute | solution.py:46
  79.8 25.2 %collective-permute-start.15 = (bf16[32,2048]{1,0:T(8,128)(2,1)S(1)}, bf16[32,2048]{1,0:T(8,128)(2,1)S(1)}, u32[]{:S(2)}, u32[]{:S(2)}) collective-permute-start(bf16[32,2048]{1,0:T(8,128)(2,1)S(1)} %get-tuple-element.6), channel_id=1, source_target_pairs={{0,5},{1,6},{2,7},{3,0},{4,1},{5,2},{6,3},{7,4},{8,13},{9,14},{10,... | collective-permute-start | bytes 393224 | tf_op jit(solution)/shard_map/ppermute | solution.py:46
  85.6 30.3 %all-to-all-start = ((bf16[64,4,2048]{2,1,0:T(4,128)(2,1)}), bf16[64,4,2048]{2,1,0:T(4,128)(2,1)}, u32[]{:S(2)}, u32[]{:S(2)}) async-start(bf16[64,4,2048]{2,1,0:T(4,128)(2,1)} %reshape.307), calls=%async_computation | async-start | bytes 2097152 | tf_op jit(solution)/shard_map/all_to_all | solution.py:212
  95.4 15.8 %collective-permute-start.16 = (bf16[32,2048]{1,0:T(8,128)(2,1)S(1)}, bf16[32,2048]{1,0:T(8,128)(2,1)S(1)}, u32[]{:S(2)}, u32[]{:S(2)}) collective-permute-start(bf16[32,2048]{1,0:T(8,128)(2,1)S(1)} %get-tuple-element.6), channel_id=1, source_target_pairs={{0,6},{1,7},{2,0},{3,1},{4,2},{5,3},{6,4},{7,5},{8,14},{9,15},{10,... | collective-permute-start | bytes 393224 | tf_op jit(solution)/shard_map/ppermute | solution.py:46
  99.6 13.6 %collective-permute-start.17 = (bf16[32,2048]{1,0:T(8,128)(2,1)S(1)}, bf16[32,2048]{1,0:T(8,128)(2,1)S(1)}, u32[]{:S(2)}, u32[]{:S(2)}) collective-permute-start(bf16[32,2048]{1,0:T(8,128)(2,1)S(1)} %get-tuple-element.6), channel_id=1, source_target_pairs={{0,7},{1,0},{2,1},{3,2},{4,3},{5,4},{6,5},{7,6},{8,15},{9,8},{10,9... | collective-permute-start | bytes 393224 | tf_op jit(solution)/shard_map/ppermute | solution.py:46
  129.8 30.3 %all-to-all-start.1 = ((bf16[64,4,2048]{2,1,0:T(4,128)(2,1)}), bf16[64,4,2048]{2,1,0:T(4,128)(2,1)}, u32[]{:S(2)}, u32[]{:S(2)}) async-start(bf16[64,4,2048]{2,1,0:T(4,128)(2,1)} %reshape_transpose_reshape.4), calls=%async_computation.1 | async-start | bytes 2097152 | tf_op jit(solution)/shard_map/all_to_all | solution.py:230
  147.0 12.3 %collective-permute-start.19 = (bf16[32,2048]{1,0:T(8,128)(2,1)S(1)}, bf16[32,2048]{1,0:T(8,128)(2,1)S(1)}, u32[]{:S(2)}, u32[]{:S(2)}) collective-permute-start(bf16[32,2048]{1,0:T(8,128)(2,1)S(1)} %get-tuple-element.15), channel_id=1, source_target_pairs={{0,2},{1,3},{2,4},{3,5},{4,6},{5,7},{6,0},{7,1},{8,10},{9,11},{10,... | collective-permute-start | bytes 393224 | tf_op jit(solution)/shard_map/ppermute | solution.py:37
  148.1 14.1 %collective-permute-start.20 = (bf16[32,2048]{1,0:T(8,128)(2,1)}, bf16[32,2048]{1,0:T(8,128)(2,1)}, u32[]{:S(2)}, u32[]{:S(2)}) collective-permute-start(bf16[32,2048]{1,0:T(8,128)(2,1)} %get-tuple-element.14), channel_id=1, source_target_pairs={{0,3},{1,4},{2,5},{3,6},{4,7},{5,0},{6,1},{7,2},{8,11},{9,12},{10,... | collective-permute-start | bytes 393224 | tf_op jit(solution)/shard_map/ppermute | solution.py:37
  149.8 14.8 %collective-permute-start.21 = (bf16[32,2048]{1,0:T(8,128)(2,1)}, bf16[32,2048]{1,0:T(8,128)(2,1)}, u32[]{:S(2)}, u32[]{:S(2)}) collective-permute-start(bf16[32,2048]{1,0:T(8,128)(2,1)} %get-tuple-element.13), channel_id=1, source_target_pairs={{0,4},{1,5},{2,6},{3,7},{4,0},{5,1},{6,2},{7,3},{8,12},{9,13},{10,... | collective-permute-start | bytes 393224 | tf_op jit(solution)/shard_map/ppermute | solution.py:37
  150.3 14.8 %collective-permute-start.22 = (bf16[32,2048]{1,0:T(8,128)(2,1)}, bf16[32,2048]{1,0:T(8,128)(2,1)}, u32[]{:S(2)}, u32[]{:S(2)}) collective-permute-start(bf16[32,2048]{1,0:T(8,128)(2,1)} %get-tuple-element.12), channel_id=1, source_target_pairs={{0,5},{1,6},{2,7},{3,0},{4,1},{5,2},{6,3},{7,4},{8,13},{9,14},{10,... | collective-permute-start | bytes 393224 | tf_op jit(solution)/shard_map/ppermute | solution.py:37
  152.2 12.9 %collective-permute-start.23 = (bf16[32,2048]{1,0:T(8,128)(2,1)}, bf16[32,2048]{1,0:T(8,128)(2,1)}, u32[]{:S(2)}, u32[]{:S(2)}) collective-permute-start(bf16[32,2048]{1,0:T(8,128)(2,1)} %get-tuple-element.11), channel_id=1, source_target_pairs={{0,6},{1,7},{2,0},{3,1},{4,2},{5,3},{6,4},{7,5},{8,14},{9,15},{10,... | collective-permute-start | bytes 393224 | tf_op jit(solution)/shard_map/ppermute | solution.py:37
  (27 other events, 277.7 us)

commit v4 on v3

--- a/solution.py
+++ b/solution.py
@@ -203,36 +203,30 @@
         .astype(jnp.int32)
         .reshape(slot_total, row_dev, top_count)
     )
-    placing = jnp.sum(placing, axis=2).astype(jnp.bfloat16)
-    outgoing = (
-        jnp.dot(placing, normed_ffn, preferred_element_type=jnp.float32)
+    placing = (
+        jnp.sum(placing, axis=2)
         .astype(jnp.bfloat16)
-        .reshape(expert_total, capacity, model_width)
-    )
+        .reshape(n_wide, expert_dev, capacity, row_dev)
+    )
+    outgoing = jnp.einsum(
+        "sjkr,rd->sjkd", placing, normed_ffn, preferred_element_type=jnp.float32
+    ).astype(jnp.bfloat16)
     buffer = lax.all_to_all(outgoing, ("tok", "mdl"), split_axis=0, concat_axis=0, tiled=True)
-    item_count = buffer.shape[1]
-    grouped = (
-        buffer.reshape(n_wide, expert_dev, item_count, model_width)
-        .transpose(1, 0, 2, 3)
-        .reshape(expert_dev, n_wide * item_count, model_width)
-    )
-    e_gate = jnp.einsum("erd,edf->erf", grouped, w_expert_gate, preferred_element_type=jnp.float32)
-    e_up = jnp.einsum("erd,edf->erf", grouped, w_expert_up, preferred_element_type=jnp.float32)
+    e_gate = jnp.einsum("sjkd,jdf->sjkf", buffer, w_expert_gate, preferred_element_type=jnp.float32)
+    e_up = jnp.einsum("sjkd,jdf->sjkf", buffer, w_expert_up, preferred_element_type=jnp.float32)
     expert_act = (jax.nn.silu(e_gate) * e_up).astype(jnp.bfloat16)
     produced = jnp.einsum(
-        "erf,efd->erd", expert_act, w_expert_down, preferred_element_type=jnp.float32
+        "sjkf,jfd->sjkd", expert_act, w_expert_down, preferred_element_type=jnp.float32
     ).astype(jnp.bfloat16)
-    processed = (
-        produced.reshape(expert_dev, n_wide, item_count, model_width)
-        .transpose(1, 0, 2, 3)
-        .reshape(n_wide * expert_dev, item_count, model_width)
-    )
-    returned = lax.all_to_all(processed, ("tok", "mdl"), split_axis=0, concat_axis=0, tiled=True)
+    returned = lax.all_to_all(produced, ("tok", "mdl"), split_axis=0, concat_axis=0, tiled=True)
     matched = target.reshape(row_dev, top_count)[:, :, None] == slot_ids[None, None, :]
-    combining = jnp.sum(jnp.where(matched, weight_rows[:, :, None], 0.0), axis=1)
-    routed = jnp.dot(
+    combining = jnp.sum(jnp.where(matched, weight_rows[:, :, None], 0.0), axis=1).reshape(
+        row_dev, n_wide, expert_dev, capacity
+    )
+    routed = jnp.einsum(
+        "rsjk,sjkd->rd",
         combining,
-        returned.reshape(slot_total, model_width).astype(jnp.float32),
+        returned.astype(jnp.float32),
         precision=lax.Precision.HIGHEST,
     )
     finished = (own_residual.astype(jnp.float32) + shared_out + routed).astype(jnp.bfloat16)

time: 169 us -> 168 us (level)
  local copies, waits for them, and re-layouts: 32.8 us -> 30.7 us
    convert_element_type x0 -> x3, local copies, waits for them, and re-layouts: none -> 4.94 us  [the longest x1 3.03 us: shards(): produced = jnp.einsum('sjkf,jfd->sjkd', expert_act, w_expert_down, prefer...]
    reshape x2 -> x0, local copies, waits for them, and re-layouts: 4.41 us -> none  [the longest x1 2.27 us: shards(): outgoing = jnp.dot(placing, normed_ffn, preferred_element_type=jnp.float3...]
    another operation x4 -> x2, local copies, waits for them, and re-layouts: 4.4 us -> 0.01 us  [the longest x1 2.24 us: shards(): processed = produced.reshape(expert_dev, n_wide, item_count, model_width)...]
    unnamed x58 -> x60, local copies, waits for them, and re-layouts: 18.2 us -> 19.1 us
where the time goes in v4:
time: 168 us; the launch traced here: 167 us
  starting transfers between devices  66.5 us (40%)
  matrix products  34.8 us (21%)
  local copies, waits for them, and re-layouts  30.7 us (18%)
  waiting for transfers between devices  21.8 us (13%)
  other arithmetic  12.5 us (7%)
    ppermute x14, starting transfers between devices, summed_over(): lax.ppermute(piece_for(steps), axis, [(i, (i + steps) % count) for i in r...  19.5 us
    unnamed x60, local copies, waits for them, and re-layouts  19.1 us
    ppermute x4, starting transfers between devices, passed_along(): lax.ppermute(value, axis, [(source, source + steps) for source in range(i...  17.7 us
    ppermute x14, waiting for transfers between devices, summed_over(): lax.ppermute(piece_for(steps), axis, [(i, (i + steps) % count) for i in r...  15.8 us
    ppermute x7, starting transfers between devices, gathered_over(): lax.ppermute(block, axis, [(i, (i + steps) % count) for i in range(count)])  10.2 us
    all_to_all x1, starting transfers between devices, shards(): lax.all_to_all(outgoing, ('tok', 'mdl'), split_axis=0, concat_axis=0, til...  9.77 us
    all_to_all x1, starting transfers between devices, shards(): lax.all_to_all(produced, ('tok', 'mdl'), split_axis=0, concat_axis=0, til...  9.28 us
    ppermute x7, waiting for transfers between devices, gathered_over(): lax.ppermute(block, axis, [(i, (i + steps) % count) for i in range(count)])  6.01 us
  transfers between devices with their start and end apart: 27, of which 7 were waited for; matrix products, arithmetic and copies ran while one was open for 21% of the time, Pallas kernels for 0%

profile of v4, /device:TPU:1, one launch (start us, length us, event | category | flops | bytes accessed | tf_op | source)
XLA Modules:
  0.0 166.9 jit_solution(12812277653320083177)
XLA Ops:
  2.7 2.9 %fusion.62 = f32[256,576]{0,1:T(8,128)S(1)} fusion(bf16[2048,576]{0,1:T(8,128)(2,1)} %param.23, f32[2048]{0:T(1024)} %param.21, f32[256]{0:T(256)S(1)} %add_rsqrt_fusion.1, bf16[2,256,2048]{2,1,0:T(8,128)(2,1)} %param.17, s32[]{:T(128)S(6)} %select_n.97), kind=kOutput, calls=%fused_computation.48 | convolution fusion | flops 606076928 | bytes 4006916 | tf_op jit(solution)/shard_map/dot_general | solution.py:135
  9.5 6.2 %collective-permute-start = (bf16[256,576]{0,1:T(8,128)(2,1)}, bf16[256,576]{0,1:T(8,128)(2,1)}, u32[]{:S(2)}, u32[]{:S(2)}) collective-permute-start(bf16[256,576]{0,1:T(8,128)(2,1)} %pad_maximum_fusion), channel_id=1, source_target_pairs={{0,32},{8,40},{16,48},{24,56},{1,33},{9,41},{17,49},{25,57},{2,34}... | collective-permute-start | bytes 884744 | tf_op jit(solution)/shard_map/ppermute | solution.py:22
  15.7 6.4 %collective-permute-start.1 = (bf16[256,576]{0,1:T(8,128)(2,1)}, bf16[256,576]{0,1:T(8,128)(2,1)}, u32[]{:S(2)}, u32[]{:S(2)}) collective-permute-start(bf16[256,576]{0,1:T(8,128)(2,1)} %pad_maximum_fusion), channel_id=1, source_target_pairs={{0,24},{8,32},{16,40},{24,48},{32,56},{1,25},{9,33},{17,41},{25,49... | collective-permute-start | bytes 884744 | tf_op jit(solution)/shard_map/ppermute | solution.py:22
  24.1 3.1 %collective-permute-start.3 = (bf16[256,576]{0,1:T(8,128)(2,1)}, bf16[256,576]{0,1:T(8,128)(2,1)}, u32[]{:S(2)}, u32[]{:S(2)}) collective-permute-start(bf16[256,576]{0,1:T(8,128)(2,1)} %pad_maximum_fusion), channel_id=1, source_target_pairs={{0,8},{8,16},{16,24},{24,32},{32,40},{40,48},{48,56},{1,9},{9,17},... | collective-permute-start | bytes 884744 | tf_op jit(solution)/shard_map/ppermute | solution.py:22
  27.2 2.6 %copy.58 = bf16[2048,384]{0,1:T(8,128)(2,1)} copy(bf16[2048,384]{1,0:T(8,128)(2,1)} %param.22) | data formatting | bytes 3145728 | tf_op args[5]
  29.8 3.2 %fusion.60 = f32[256,2,192]{0,2,1:T(8,128)} fusion(bf16[2,192,2048]{2,1,0:T(8,128)(2,1)} %bitcast.177, f32[2048]{0:T(1024)S(1)} %copy-done.23, f32[256]{0:T(256)S(1)} %add_rsqrt_fusion.1, bf16[2,256,2048]{2,1,0:T(8,128)(2,1)} %param.17, s32[]{:T(128)S(6)} %select_n.97), kind=kOutput, calls=%fused_computation.47 | convolution fusion | flops 404750336 | bytes 3023876 | tf_op jit(solution)/shard_map/dot_general | solution.py:129
  46.5 3.7 %fusion.56 = bf16[256,2,128]{0,2,1:T(8,128)(2,1)S(1)} fusion(bf16[1280,2,256]{0,2,1:T(8,128)(2,1)} %bitcast.180, f32[2,256,1280]{2,1,0:T(8,128)} %copy-done.2, pred[256,1280]{1,0:T(8,128)(4,1)} %and_and_fusion, f32[256,2]{0,1:T(2,128)S(1)} %bitcast.188), kind=kOutput, calls=%fused_computation.45 | convolution fusion | flops 170526464 | bytes 6686720 | tf_op jit(solution)/shard_map/hqk,khd->hqd/dot_general | solution.py:174
  58.2 2.1 %collective-permute-start.6 = (bf16[32,2048]{1,0:T(8,128)(2,1)}, bf16[32,2048]{1,0:T(8,128)(2,1)S(1)}, u32[]{:S(2)}, u32[]{:S(2)}) collective-permute-start(bf16[32,2048]{1,0:T(8,128)(2,1)} %get-tuple-element.21), channel_id=1, source_target_pairs={{0,3},{1,4},{2,5},{3,6},{4,7},{5,0},{6,1},{7,2},{8,11},{9,12},{10,... | collective-permute-start | bytes 393224 | tf_op jit(solution)/shard_map/ppermute | solution.py:37
  61.1 2.6 %collective-permute-start.8 = (bf16[32,2048]{1,0:T(8,128)(2,1)}, bf16[32,2048]{1,0:T(8,128)(2,1)S(1)}, u32[]{:S(2)}, u32[]{:S(2)}) collective-permute-start(bf16[32,2048]{1,0:T(8,128)(2,1)} %get-tuple-element.19), channel_id=1, source_target_pairs={{0,5},{1,6},{2,7},{3,0},{4,1},{5,2},{6,3},{7,4},{8,13},{9,14},{10,... | collective-permute-start | bytes 393224 | tf_op jit(solution)/shard_map/ppermute | solution.py:37
  63.8 2.3 %collective-permute-done.5 = bf16[32,2048]{1,0:T(8,128)(2,1)S(1)} collective-permute-done((bf16[32,2048]{1,0:T(8,128)(2,1)}, bf16[32,2048]{1,0:T(8,128)(2,1)S(1)}, u32[]{:S(2)}, u32[]{:S(2)}) %collective-permute-start.5) | collective-permute-done | bytes 131104 | tf_op jit(solution)/shard_map/ppermute | solution.py:37
  66.1 5.9 %collective-permute-done.6 = bf16[32,2048]{1,0:T(8,128)(2,1)S(1)} collective-permute-done((bf16[32,2048]{1,0:T(8,128)(2,1)}, bf16[32,2048]{1,0:T(8,128)(2,1)S(1)}, u32[]{:S(2)}, u32[]{:S(2)}) %collective-permute-start.6) | collective-permute-done | bytes 131104 | tf_op jit(solution)/shard_map/ppermute | solution.py:37
  79.2 2.1 %collective-permute-start.15 = (bf16[32,2048]{1,0:T(8,128)(2,1)S(1)}, bf16[32,2048]{1,0:T(8,128)(2,1)}, u32[]{:S(2)}, u32[]{:S(2)}) collective-permute-start(bf16[32,2048]{1,0:T(8,128)(2,1)S(1)} %get-tuple-element.6), channel_id=1, source_target_pairs={{0,5},{1,6},{2,7},{3,0},{4,1},{5,2},{6,3},{7,4},{8,13},{9,14},{10,... | collective-permute-start | bytes 393224 | tf_op jit(solution)/shard_map/ppermute | solution.py:46
  83.5 9.8 %all-to-all-start = ((bf16[64,1,4,2048]{3,2,1,0:T(4,128)(2,1)}), bf16[64,1,4,2048]{3,2,1,0:T(4,128)(2,1)}, u32[]{:S(2)}, u32[]{:S(2)}) async-start(bf16[64,1,4,2048]{3,2,1,0:T(4,128)(2,1)} %copy.71), calls=%async_computation | async-start | bytes 2097152 | tf_op jit(solution)/shard_map/all_to_all | solution.py:214
  93.3 2.6 %collective-permute-start.16 = (bf16[32,2048]{1,0:T(8,128)(2,1)S(1)}, bf16[32,2048]{1,0:T(8,128)(2,1)S(1)}, u32[]{:S(2)}, u32[]{:S(2)}) collective-permute-start(bf16[32,2048]{1,0:T(8,128)(2,1)S(1)} %get-tuple-element.6), channel_id=1, source_target_pairs={{0,6},{1,7},{2,0},{3,1},{4,2},{5,3},{6,4},{7,5},{8,14},{9,15},{10,... | collective-permute-start | bytes 393224 | tf_op jit(solution)/shard_map/ppermute | solution.py:46
  104.5 4.7 %collective-permute-done.16 = bf16[32,2048]{1,0:T(8,128)(2,1)S(1)} collective-permute-done((bf16[32,2048]{1,0:T(8,128)(2,1)S(1)}, bf16[32,2048]{1,0:T(8,128)(2,1)S(1)}, u32[]{:S(2)}, u32[]{:S(2)}) %collective-permute-start.16) | collective-permute-done | bytes 131104 | tf_op jit(solution)/shard_map/ppermute | solution.py:46
  113.8 5.0 %fusion.35 = f32[64,1,4,768]{3,0,2,1:T(8,128)} fusion(bf16[1,2048,768]{2,1,0:T(8,128)(2,1)} %param.31, bf16[64,1,4,2048]{3,2,1,0:T(4,128)(2,1)} %all-to-all-done), kind=kOutput, calls=%fused_computation.38 | convolution fusion | flops 805306368 | bytes 4980736 | tf_op jit(solution)/shard_map/sjkd,jdf->sjkf/dot_general | solution.py:215
  118.7 5.9 %fusion.22 = bf16[64,1,4,2048]{3,0,2,1:T(8,128)(2,1)} fusion(bf16[1,768,2048]{2,1,0:T(8,128)(2,1)S(1)} %copy-done, bf16[1,2048,768]{2,1,0:T(8,128)(2,1)} %param.32, bf16[64,1,4,2048]{3,2,1,0:T(4,128)(2,1)} %all-to-all-done, f32[64,1,4,768]{3,0,2,1:T(8,128)} %fusion.35), kind=kOutput, calls=%fused_computation.25 | convolution fusion | flops 1612316672 | bytes 9175040 | tf_op jit(solution)/shard_map/sjkf,jfd->sjkd/dot_general | solution.py:218
  124.7 3.0 %copy.73 = bf16[64,1,4,2048]{3,2,1,0:T(4,128)(2,1)} copy(bf16[64,1,4,2048]{3,0,2,1:T(8,128)(2,1)} %fusion.22) | data formatting | bytes 2097152 | tf_op jit(solution)/shard_map/convert_element_type | solution.py:220
  127.7 9.3 %all-to-all-start.1 = ((bf16[64,1,4,2048]{3,2,1,0:T(4,128)(2,1)}), bf16[64,1,4,2048]{3,2,1,0:T(4,128)(2,1)}, u32[]{:S(2)}, u32[]{:S(2)}) async-start(bf16[64,1,4,2048]{3,2,1,0:T(4,128)(2,1)} %copy.73), calls=%async_computation.1 | async-start | bytes 2097152 | tf_op jit(solution)/shard_map/all_to_all | solution.py:221
  137.0 4.1 %convolution_convert_fusion.1 = bf16[256,2048]{1,0:T(8,128)(2,1)} fusion(bf16[256,2048]{1,0:T(8,128)(2,1)} %param.30, f32[256,256]{1,0:T(8,128)S(1)} %fusion.137, bf16[256,2048]{1,0:T(8,128)(2,1)} %constant_dynamic-update-slice_fusion.5, bf16[2048,256]{1,0:T(8,128)(2,1)} %param.29), kind=kOutput, calls=%fused_computation.20 | convolution fusion | flops 537788416 | bytes 4456448 | tf_op jit(solution)/shard_map/dot_general | solution.py:192
  150.1 3.1 %collective-permute-start.23 = (bf16[32,2048]{1,0:T(8,128)(2,1)}, bf16[32,2048]{1,0:T(8,128)(2,1)}, u32[]{:S(2)}, u32[]{:S(2)}) collective-permute-start(bf16[32,2048]{1,0:T(8,128)(2,1)} %get-tuple-element.11), channel_id=1, source_target_pairs={{0,6},{1,7},{2,0},{3,1},{4,2},{5,3},{6,4},{7,5},{8,14},{9,15},{10,... | collective-permute-start | bytes 393224 | tf_op jit(solution)/shard_map/ppermute | solution.py:37
  153.2 4.0 %collective-permute-done.19 = bf16[32,2048]{1,0:T(8,128)(2,1)S(1)} collective-permute-done((bf16[32,2048]{1,0:T(8,128)(2,1)S(1)}, bf16[32,2048]{1,0:T(8,128)(2,1)S(1)}, u32[]{:S(2)}, u32[]{:S(2)}) %collective-permute-start.19) | collective-permute-done | bytes 131104 | tf_op jit(solution)/shard_map/ppermute | solution.py:37
  159.4 3.0 %collective-permute-done.21 = bf16[32,2048]{1,0:T(8,128)(2,1)} collective-permute-done((bf16[32,2048]{1,0:T(8,128)(2,1)}, bf16[32,2048]{1,0:T(8,128)(2,1)}, u32[]{:S(2)}, u32[]{:S(2)}) %collective-permute-start.21) | collective-permute-done | bytes 131104 | tf_op jit(solution)/shard_map/ppermute | solution.py:37
  163.0 3.9 %fusion.106 = bf16[1,32,2048]{2,1,0:T(8,128)(2,1)} fusion(bf16[64,1,4,2048]{3,2,1,0:T(4,128)(2,1)} %all-to-all-done.1, f32[32,64,4]{0,2,1:T(4,128)S(1)} %bitcast.178, bf16[32,2048]{1,0:T(8,128)(2,1)} %collective-permute-done.24, bf16[32,2048]{1,0:T(8,128)(2,1)} %collective-permute-done.23, bf16[32,2048]{1,0:T(8,128)(2,1)} %collective-permute-done.22, ...), kind=kOutput, calls=%fused_computation.93 | convolution fusion | flops 202571776 | bytes 2392064 | tf_op jit(solution)/shard_map/rsjk,sjkd->rd/dot_general | solution.py:226
  (152 shorter events, 64.7 us)
Async XLA Ops:
  9.5 28.2 %collective-permute-start = (bf16[256,576]{0,1:T(8,128)(2,1)}, bf16[256,576]{0,1:T(8,128)(2,1)}, u32[]{:S(2)}, u32[]{:S(2)}) collective-permute-start(bf16[256,576]{0,1:T(8,128)(2,1)} %pad_maximum_fusion), channel_id=1, source_target_pairs={{0,32},{8,40},{16,48},{24,56},{1,33},{9,41},{17,49},{25,57},{2,34}... | collective-permute-start | bytes 884744 | tf_op jit(solution)/shard_map/ppermute | solution.py:22
  15.7 23.1 %collective-permute-start.1 = (bf16[256,576]{0,1:T(8,128)(2,1)}, bf16[256,576]{0,1:T(8,128)(2,1)}, u32[]{:S(2)}, u32[]{:S(2)}) collective-permute-start(bf16[256,576]{0,1:T(8,128)(2,1)} %pad_maximum_fusion), channel_id=1, source_target_pairs={{0,24},{8,32},{16,40},{24,48},{32,56},{1,25},{9,33},{17,41},{25,49... | collective-permute-start | bytes 884744 | tf_op jit(solution)/shard_map/ppermute | solution.py:22
  22.1 17.7 %collective-permute-start.2 = (bf16[256,576]{0,1:T(8,128)(2,1)}, bf16[256,576]{0,1:T(8,128)(2,1)}, u32[]{:S(2)}, u32[]{:S(2)}) collective-permute-start(bf16[256,576]{0,1:T(8,128)(2,1)} %pad_maximum_fusion), channel_id=1, source_target_pairs={{0,16},{8,24},{16,32},{24,40},{32,48},{40,56},{1,17},{9,25},{17,33... | collective-permute-start | bytes 884744 | tf_op jit(solution)/shard_map/ppermute | solution.py:22
  24.1 16.7 %collective-permute-start.3 = (bf16[256,576]{0,1:T(8,128)(2,1)}, bf16[256,576]{0,1:T(8,128)(2,1)}, u32[]{:S(2)}, u32[]{:S(2)}) collective-permute-start(bf16[256,576]{0,1:T(8,128)(2,1)} %pad_maximum_fusion), channel_id=1, source_target_pairs={{0,8},{8,16},{16,24},{24,32},{32,40},{40,48},{48,56},{1,9},{9,17},... | collective-permute-start | bytes 884744 | tf_op jit(solution)/shard_map/ppermute | solution.py:22
  55.4 8.3 %collective-permute-start.4 = (bf16[32,2048]{1,0:T(8,128)(2,1)}, bf16[32,2048]{1,0:T(8,128)(2,1)}, u32[]{:S(2)}, u32[]{:S(2)}) collective-permute-start(bf16[32,2048]{1,0:T(8,128)(2,1)} %get-tuple-element.16), channel_id=1, source_target_pairs={{0,1},{1,2},{2,3},{3,4},{4,5},{5,6},{6,7},{7,0},{8,9},{9,10},{10,1... | collective-permute-start | bytes 393224 | tf_op jit(solution)/shard_map/ppermute | solution.py:37
  56.9 9.2 %collective-permute-start.5 = (bf16[32,2048]{1,0:T(8,128)(2,1)}, bf16[32,2048]{1,0:T(8,128)(2,1)S(1)}, u32[]{:S(2)}, u32[]{:S(2)}) collective-permute-start(bf16[32,2048]{1,0:T(8,128)(2,1)} %get-tuple-element.22), channel_id=1, source_target_pairs={{0,2},{1,3},{2,4},{3,5},{4,6},{5,7},{6,0},{7,1},{8,10},{9,11},{10,... | collective-permute-start | bytes 393224 | tf_op jit(solution)/shard_map/ppermute | solution.py:37
  58.2 13.7 %collective-permute-start.6 = (bf16[32,2048]{1,0:T(8,128)(2,1)}, bf16[32,2048]{1,0:T(8,128)(2,1)S(1)}, u32[]{:S(2)}, u32[]{:S(2)}) collective-permute-start(bf16[32,2048]{1,0:T(8,128)(2,1)} %get-tuple-element.21), channel_id=1, source_target_pairs={{0,3},{1,4},{2,5},{3,6},{4,7},{5,0},{6,1},{7,2},{8,11},{9,12},{10,... | collective-permute-start | bytes 393224 | tf_op jit(solution)/shard_map/ppermute | solution.py:37
  60.3 11.6 %collective-permute-start.7 = (bf16[32,2048]{1,0:T(8,128)(2,1)}, bf16[32,2048]{1,0:T(8,128)(2,1)S(1)}, u32[]{:S(2)}, u32[]{:S(2)}) collective-permute-start(bf16[32,2048]{1,0:T(8,128)(2,1)} %get-tuple-element.20), channel_id=1, source_target_pairs={{0,4},{1,5},{2,6},{3,7},{4,0},{5,1},{6,2},{7,3},{8,12},{9,13},{10,... | collective-permute-start | bytes 393224 | tf_op jit(solution)/shard_map/ppermute | solution.py:37
  61.1 10.9 %collective-permute-start.8 = (bf16[32,2048]{1,0:T(8,128)(2,1)}, bf16[32,2048]{1,0:T(8,128)(2,1)S(1)}, u32[]{:S(2)}, u32[]{:S(2)}) collective-permute-start(bf16[32,2048]{1,0:T(8,128)(2,1)} %get-tuple-element.19), channel_id=1, source_target_pairs={{0,5},{1,6},{2,7},{3,0},{4,1},{5,2},{6,3},{7,4},{8,13},{9,14},{10,... | collective-permute-start | bytes 393224 | tf_op jit(solution)/shard_map/ppermute | solution.py:37
  63.7 8.2 %collective-permute-start.9 = (bf16[32,2048]{1,0:T(8,128)(2,1)S(1)}, bf16[32,2048]{1,0:T(8,128)(2,1)S(1)}, u32[]{:S(2)}, u32[]{:S(2)}) collective-permute-start(bf16[32,2048]{1,0:T(8,128)(2,1)S(1)} %get-tuple-element.18), channel_id=1, source_target_pairs={{0,6},{1,7},{2,0},{3,1},{4,2},{5,3},{6,4},{7,5},{8,14},{9,15},{10,... | collective-permute-start | bytes 393224 | tf_op jit(solution)/shard_map/ppermute | solution.py:37
  74.2 19.1 %collective-permute-start.11 = (bf16[32,2048]{1,0:T(8,128)(2,1)S(1)}, bf16[32,2048]{1,0:T(8,128)(2,1)}, u32[]{:S(2)}, u32[]{:S(2)}) collective-permute-start(bf16[32,2048]{1,0:T(8,128)(2,1)S(1)} %get-tuple-element.6), channel_id=1, source_target_pairs={{0,1},{1,2},{2,3},{3,4},{4,5},{5,6},{6,7},{7,0},{8,9},{9,10},{10,1... | collective-permute-start | bytes 393224 | tf_op jit(solution)/shard_map/ppermute | solution.py:46
  75.0 22.5 %collective-permute-start.12 = (bf16[32,2048]{1,0:T(8,128)(2,1)S(1)}, bf16[32,2048]{1,0:T(8,128)(2,1)}, u32[]{:S(2)}, u32[]{:S(2)}) collective-permute-start(bf16[32,2048]{1,0:T(8,128)(2,1)S(1)} %get-tuple-element.6), channel_id=1, source_target_pairs={{0,2},{1,3},{2,4},{3,5},{4,6},{5,7},{6,0},{7,1},{8,10},{9,11},{10,... | collective-permute-start | bytes 393224 | tf_op jit(solution)/shard_map/ppermute | solution.py:46
  76.7 23.0 %collective-permute-start.13 = (bf16[32,2048]{1,0:T(8,128)(2,1)S(1)}, bf16[32,2048]{1,0:T(8,128)(2,1)}, u32[]{:S(2)}, u32[]{:S(2)}) collective-permute-start(bf16[32,2048]{1,0:T(8,128)(2,1)S(1)} %get-tuple-element.6), channel_id=1, source_target_pairs={{0,3},{1,4},{2,5},{3,6},{4,7},{5,0},{6,1},{7,2},{8,11},{9,12},{10,... | collective-permute-start | bytes 393224 | tf_op jit(solution)/shard_map/ppermute | solution.py:46
  78.5 22.8 %collective-permute-start.14 = (bf16[32,2048]{1,0:T(8,128)(2,1)S(1)}, bf16[32,2048]{1,0:T(8,128)(2,1)}, u32[]{:S(2)}, u32[]{:S(2)}) collective-permute-start(bf16[32,2048]{1,0:T(8,128)(2,1)S(1)} %get-tuple-element.6), channel_id=1, source_target_pairs={{0,4},{1,5},{2,6},{3,7},{4,0},{5,1},{6,2},{7,3},{8,12},{9,13},{10,... | collective-permute-start | bytes 393224 | tf_op jit(solution)/shard_map/ppermute | solution.py:46
  79.2 23.7 %collective-permute-start.15 = (bf16[32,2048]{1,0:T(8,128)(2,1)S(1)}, bf16[32,2048]{1,0:T(8,128)(2,1)}, u32[]{:S(2)}, u32[]{:S(2)}) collective-permute-start(bf16[32,2048]{1,0:T(8,128)(2,1)S(1)} %get-tuple-element.6), channel_id=1, source_target_pairs={{0,5},{1,6},{2,7},{3,0},{4,1},{5,2},{6,3},{7,4},{8,13},{9,14},{10,... | collective-permute-start | bytes 393224 | tf_op jit(solution)/shard_map/ppermute | solution.py:46
  83.5 30.2 %all-to-all-start = ((bf16[64,1,4,2048]{3,2,1,0:T(4,128)(2,1)}), bf16[64,1,4,2048]{3,2,1,0:T(4,128)(2,1)}, u32[]{:S(2)}, u32[]{:S(2)}) async-start(bf16[64,1,4,2048]{3,2,1,0:T(4,128)(2,1)} %copy.71), calls=%async_computation | async-start | bytes 2097152 | tf_op jit(solution)/shard_map/all_to_all | solution.py:214
  93.3 15.8 %collective-permute-start.16 = (bf16[32,2048]{1,0:T(8,128)(2,1)S(1)}, bf16[32,2048]{1,0:T(8,128)(2,1)S(1)}, u32[]{:S(2)}, u32[]{:S(2)}) collective-permute-start(bf16[32,2048]{1,0:T(8,128)(2,1)S(1)} %get-tuple-element.6), channel_id=1, source_target_pairs={{0,6},{1,7},{2,0},{3,1},{4,2},{5,3},{6,4},{7,5},{8,14},{9,15},{10,... | collective-permute-start | bytes 393224 | tf_op jit(solution)/shard_map/ppermute | solution.py:46
  97.5 13.6 %collective-permute-start.17 = (bf16[32,2048]{1,0:T(8,128)(2,1)S(1)}, bf16[32,2048]{1,0:T(8,128)(2,1)S(1)}, u32[]{:S(2)}, u32[]{:S(2)}) collective-permute-start(bf16[32,2048]{1,0:T(8,128)(2,1)S(1)} %get-tuple-element.6), channel_id=1, source_target_pairs={{0,7},{1,0},{2,1},{3,2},{4,3},{5,4},{6,5},{7,6},{8,15},{9,8},{10,9... | collective-permute-start | bytes 393224 | tf_op jit(solution)/shard_map/ppermute | solution.py:46
  127.7 35.3 %all-to-all-start.1 = ((bf16[64,1,4,2048]{3,2,1,0:T(4,128)(2,1)}), bf16[64,1,4,2048]{3,2,1,0:T(4,128)(2,1)}, u32[]{:S(2)}, u32[]{:S(2)}) async-start(bf16[64,1,4,2048]{3,2,1,0:T(4,128)(2,1)} %copy.73), calls=%async_computation.1 | async-start | bytes 2097152 | tf_op jit(solution)/shard_map/all_to_all | solution.py:221
  144.8 12.4 %collective-permute-start.19 = (bf16[32,2048]{1,0:T(8,128)(2,1)S(1)}, bf16[32,2048]{1,0:T(8,128)(2,1)S(1)}, u32[]{:S(2)}, u32[]{:S(2)}) collective-permute-start(bf16[32,2048]{1,0:T(8,128)(2,1)S(1)} %get-tuple-element.15), channel_id=1, source_target_pairs={{0,2},{1,3},{2,4},{3,5},{4,6},{5,7},{6,0},{7,1},{8,10},{9,11},{10,... | collective-permute-start | bytes 393224 | tf_op jit(solution)/shard_map/ppermute | solution.py:37
  146.0 13.4 %collective-permute-start.20 = (bf16[32,2048]{1,0:T(8,128)(2,1)}, bf16[32,2048]{1,0:T(8,128)(2,1)}, u32[]{:S(2)}, u32[]{:S(2)}) collective-permute-start(bf16[32,2048]{1,0:T(8,128)(2,1)} %get-tuple-element.14), channel_id=1, source_target_pairs={{0,3},{1,4},{2,5},{3,6},{4,7},{5,0},{6,1},{7,2},{8,11},{9,12},{10,... | collective-permute-start | bytes 393224 | tf_op jit(solution)/shard_map/ppermute | solution.py:37
  147.6 14.8 %collective-permute-start.21 = (bf16[32,2048]{1,0:T(8,128)(2,1)}, bf16[32,2048]{1,0:T(8,128)(2,1)}, u32[]{:S(2)}, u32[]{:S(2)}) collective-permute-start(bf16[32,2048]{1,0:T(8,128)(2,1)} %get-tuple-element.13), channel_id=1, source_target_pairs={{0,4},{1,5},{2,6},{3,7},{4,0},{5,1},{6,2},{7,3},{8,12},{9,13},{10,... | collective-permute-start | bytes 393224 | tf_op jit(solution)/shard_map/ppermute | solution.py:37
  148.2 14.8 %collective-permute-start.22 = (bf16[32,2048]{1,0:T(8,128)(2,1)}, bf16[32,2048]{1,0:T(8,128)(2,1)}, u32[]{:S(2)}, u32[]{:S(2)}) collective-permute-start(bf16[32,2048]{1,0:T(8,128)(2,1)} %get-tuple-element.12), channel_id=1, source_target_pairs={{0,5},{1,6},{2,7},{3,0},{4,1},{5,2},{6,3},{7,4},{8,13},{9,14},{10,... | collective-permute-start | bytes 393224 | tf_op jit(solution)/shard_map/ppermute | solution.py:37
  150.1 12.9 %collective-permute-start.23 = (bf16[32,2048]{1,0:T(8,128)(2,1)}, bf16[32,2048]{1,0:T(8,128)(2,1)}, u32[]{:S(2)}, u32[]{:S(2)}) collective-permute-start(bf16[32,2048]{1,0:T(8,128)(2,1)} %get-tuple-element.11), channel_id=1, source_target_pairs={{0,6},{1,7},{2,0},{3,1},{4,2},{5,3},{6,4},{7,5},{8,14},{9,15},{10,... | collective-permute-start | bytes 393224 | tf_op jit(solution)/shard_map/ppermute | solution.py:37
  (28 other events, 296.0 us)

commit v5 on v4

--- a/solution.py
+++ b/solution.py
@@ -141,40 +141,54 @@
     kv_parts = [kv_own]
     for steps in range(1, min(reach, n_tok - 1) + 1):
         kv_parts.insert(0, passed_along(kv_own, "tok", steps))
-    kv_rows = jnp.concatenate(kv_parts, axis=0)
-    key_count = kv_rows.shape[0]
-    key_start = query_start + tok_dev - key_count
-    expanded = (
-        jnp.dot(kv_rows[:, :LATENT], w_kv_up, preferred_element_type=jnp.float32)
-        .astype(jnp.bfloat16)
-        .reshape(key_count, local_heads, NOPE + VDIM)
-    )
-    rope_keys = kv_rows[:, LATENT:]
-    scores = jnp.einsum(
-        "qhd,khd->hqk", queries[..., :NOPE], expanded[..., :NOPE],
+    padded_seg = jnp.concatenate([jnp.full((tok_dev * len(kv_parts),), -1, jnp.int32), segment_row])
+
+    def block_scores(kv_rows, first_key):
+        key_count = kv_rows.shape[0]
+        expanded = (
+            jnp.dot(kv_rows[:, :LATENT], w_kv_up, preferred_element_type=jnp.float32)
+            .astype(jnp.bfloat16)
+            .reshape(key_count, local_heads, NOPE + VDIM)
+        )
+        scores = jnp.einsum(
+            "qhd,khd->hqk", queries[..., :NOPE], expanded[..., :NOPE],
+            preferred_element_type=jnp.float32,
+        )
+        scores = scores + jnp.einsum(
+            "qhd,kd->hqk", queries[..., NOPE:], kv_rows[:, LATENT:],
+            preferred_element_type=jnp.float32,
+        )
+        scores = scores * score_scale
+        key_index = first_key + jnp.arange(key_count, dtype=jnp.int32)
+        key_seg = lax.dynamic_slice_in_dim(padded_seg, first_key + padded_seg.shape[0] - segment_row.shape[0], key_count)
+        allowed = (
+            (key_seg[None, :] == query_seg[:, None])
+            & (key_index[None, :] <= query_index[:, None])
+            & (key_index[None, :] >= 0)
+        )
+        return scores, allowed[None, :, :], expanded[..., NOPE:]
+
+    own_scores, own_allowed, own_values = block_scores(kv_own, query_start)
+    running_max = jnp.max(jnp.where(own_allowed, own_scores, -1e30), axis=-1, keepdims=True)
+    own_weights = jnp.where(own_allowed, jnp.exp(own_scores - running_max), 0.0)
+    totals = jnp.sum(own_weights, axis=-1, keepdims=True)
+    weighted = jnp.einsum(
+        "hqk,khd->hqd", own_weights.astype(jnp.bfloat16), own_values,
         preferred_element_type=jnp.float32,
     )
-    scores = scores + jnp.einsum(
-        "qhd,kd->hqk", queries[..., NOPE:], rope_keys, preferred_element_type=jnp.float32
-    )
-    scores = scores * score_scale
-    key_index = key_start + jnp.arange(key_count, dtype=jnp.int32)
-    padded_seg = jnp.concatenate([jnp.full((key_count,), -1, jnp.int32), segment_row])
-    key_seg = lax.dynamic_slice_in_dim(padded_seg, key_start + key_count, key_count)
-    allowed = (
-        (key_seg[None, :] == query_seg[:, None])
-        & (key_index[None, :] <= query_index[:, None])
-        & (key_index[None, :] >= 0)
-    )
-    allowed = allowed[None, :, :]
-    masked = jnp.where(allowed, scores, -1e30)
-    row_max = jnp.max(masked, axis=-1, keepdims=True)
-    weights = jnp.where(allowed, jnp.exp(scores - row_max), 0.0)
-    totals = jnp.sum(weights, axis=-1, keepdims=True)
-    weighted = jnp.einsum(
-        "hqk,khd->hqd", weights.astype(jnp.bfloat16), expanded[..., NOPE:],
-        preferred_element_type=jnp.float32,
-    )
+    if len(kv_parts) > 1:
+        earlier_rows = jnp.concatenate(kv_parts[:-1], axis=0)
+        scores, allowed, values = block_scores(earlier_rows, query_start - earlier_rows.shape[0])
+        new_max = jnp.maximum(
+            running_max, jnp.max(jnp.where(allowed, scores, -1e30), axis=-1, keepdims=True)
+        )
+        weights = jnp.where(allowed, jnp.exp(scores - new_max), 0.0)
+        factor = jnp.exp(running_max - new_max)
+        totals = totals * factor + jnp.sum(weights, axis=-1, keepdims=True)
+        weighted = weighted * factor + jnp.einsum(
+            "hqk,khd->hqd", weights.astype(jnp.bfloat16), values,
+            preferred_element_type=jnp.float32,
+        )
     attended = (
         (weighted / totals).astype(jnp.bfloat16).transpose(1, 0, 2).reshape(tok_dev, local_heads * VDIM)
     )
@@ -227,7 +241,7 @@
         "rsjk,sjkd->rd",
         combining,
         returned.astype(jnp.float32),
-        precision=lax.Precision.HIGHEST,
+        precision=lax.Precision.HIGH,
     )
     finished = (own_residual.astype(jnp.float32) + shared_out + routed).astype(jnp.bfloat16)
     return finished[None]

time: 168 us -> 175 us (1.042)
  the two profiles are of different devices: /device:TPU:1 before, /device:TPU:32 now
where the time goes in v5:
time: 175 us; the launch traced here: 174 us
  starting transfers between devices  54.6 us (31%)
  matrix products  34.8 us (20%)
  local copies, waits for them, and re-layouts  34 us (19%)
  waiting for transfers between devices  33.1 us (19%)
  other arithmetic  16.5 us (9%)
    ppermute x14, waiting for transfers between devices, summed_over(): lax.ppermute(piece_for(steps), axis, [(i, (i + steps) % count) for i in r...  27.8 us
    unnamed x65, local copies, waits for them, and re-layouts  18.2 us
    ppermute x4, starting transfers between devices, passed_along(): lax.ppermute(value, axis, [(source, source + steps) for source in range(i...  15.1 us
    ppermute x14, starting transfers between devices, summed_over(): lax.ppermute(piece_for(steps), axis, [(i, (i + steps) % count) for i in r...  13.4 us
    all_to_all x1, starting transfers between devices, shards(): lax.all_to_all(produced, ('tok', 'mdl'), split_axis=0, concat_axis=0, til...  10.3 us
    ppermute x7, starting transfers between devices, gathered_over(): lax.ppermute(block, axis, [(i, (i + steps) % count) for i in range(count)])  9.8 us
    all_to_all x1, starting transfers between devices, shards(): lax.all_to_all(outgoing, ('tok', 'mdl'), split_axis=0, concat_axis=0, til...  6 us
    dot_general x1, matrix products, shards(): jnp.einsum('sjkf,jfd->sjkd', expert_act, w_expert_down, preferred_element...  5.91 us
  transfers between devices with their start and end apart: 27, of which 10 were waited for; matrix products, arithmetic and copies ran while one was open for 27% of the time, Pallas kernels for 0%

profile of v5, /device:TPU:32, one launch (start us, length us, event | category | flops | bytes accessed | tf_op | source)
XLA Modules:
  0.0 173.7 jit_solution(12352982659507602083)
XLA Ops:
  2.7 2.9 %fusion.48 = f32[256,576]{0,1:T(8,128)S(1)} fusion(bf16[2048,576]{0,1:T(8,128)(2,1)} %param.23, f32[2048]{0:T(1024)} %param.21, f32[256]{0:T(256)S(1)} %add_rsqrt_fusion.1, bf16[2,256,2048]{2,1,0:T(8,128)(2,1)} %param.17, s32[]{:T(128)S(6)} %select_n.107), kind=kOutput, calls=%fused_computation.46 | convolution fusion | flops 606076928 | bytes 4006916 | tf_op jit(solution)/shard_map/dot_general | solution.py:135
  10.1 5.7 %collective-permute-start = (bf16[256,576]{0,1:T(8,128)(2,1)}, bf16[256,576]{0,1:T(8,128)(2,1)}, u32[]{:S(2)}, u32[]{:S(2)}) collective-permute-start(bf16[256,576]{0,1:T(8,128)(2,1)} %pad_maximum_fusion), channel_id=1, source_target_pairs={{0,32},{8,40},{16,48},{24,56},{1,33},{9,41},{17,49},{25,57},{2,34}... | collective-permute-start | bytes 884744 | tf_op jit(solution)/shard_map/ppermute | solution.py:22
  17.8 5.5 %collective-permute-start.2 = (bf16[256,576]{0,1:T(8,128)(2,1)}, bf16[256,576]{0,1:T(8,128)(2,1)}, u32[]{:S(2)}, u32[]{:S(2)}) collective-permute-start(bf16[256,576]{0,1:T(8,128)(2,1)} %pad_maximum_fusion), channel_id=1, source_target_pairs={{0,16},{8,24},{16,32},{24,40},{32,48},{40,56},{1,17},{9,25},{17,33... | collective-permute-start | bytes 884744 | tf_op jit(solution)/shard_map/ppermute | solution.py:22
  27.6 2.6 %copy.70 = bf16[2048,384]{0,1:T(8,128)(2,1)} copy(bf16[2048,384]{1,0:T(8,128)(2,1)} %param.22) | data formatting | bytes 3145728 | tf_op args[5]
  30.2 3.2 %fusion.46 = f32[256,2,192]{0,2,1:T(8,128)} fusion(bf16[2,192,2048]{2,1,0:T(8,128)(2,1)} %bitcast.211, f32[2048]{0:T(1024)S(1)} %copy-done.26, f32[256]{0:T(256)S(1)} %add_rsqrt_fusion.1, bf16[2,256,2048]{2,1,0:T(8,128)(2,1)} %param.17, s32[]{:T(128)S(6)} %select_n.107), kind=kOutput, calls=%fused_computation.45 | convolution fusion | flops 404750336 | bytes 3023876 | tf_op jit(solution)/shard_map/dot_general | solution.py:129
  62.7 2.9 %collective-permute-start.7 = (bf16[32,2048]{1,0:T(8,128)(2,1)}, bf16[32,2048]{1,0:T(8,128)(2,1)S(1)}, u32[]{:S(2)}, u32[]{:S(2)}) collective-permute-start(bf16[32,2048]{1,0:T(8,128)(2,1)} %get-tuple-element.22), channel_id=1, source_target_pairs={{0,4},{1,5},{2,6},{3,7},{4,0},{5,1},{6,2},{7,3},{8,12},{9,13},{10,... | collective-permute-start | bytes 393224 | tf_op jit(solution)/shard_map/ppermute | solution.py:37
  68.2 4.7 %collective-permute-done.7 = bf16[32,2048]{1,0:T(8,128)(2,1)S(1)} collective-permute-done((bf16[32,2048]{1,0:T(8,128)(2,1)}, bf16[32,2048]{1,0:T(8,128)(2,1)S(1)}, u32[]{:S(2)}, u32[]{:S(2)}) %collective-permute-start.7) | collective-permute-done | bytes 131104 | tf_op jit(solution)/shard_map/ppermute | solution.py:37
  73.1 5.4 %collective-permute-done.5 = bf16[32,2048]{1,0:T(8,128)(2,1)S(1)} collective-permute-done((bf16[32,2048]{1,0:T(8,128)(2,1)}, bf16[32,2048]{1,0:T(8,128)(2,1)S(1)}, u32[]{:S(2)}, u32[]{:S(2)}) %collective-permute-start.5) | collective-permute-done | bytes 131104 | tf_op jit(solution)/shard_map/ppermute | solution.py:37
  81.0 3.1 %collective-permute-start.13 = (bf16[32,2048]{1,0:T(8,128)(2,1)S(1)}, bf16[32,2048]{1,0:T(8,128)(2,1)}, u32[]{:S(2)}, u32[]{:S(2)}) collective-permute-start(bf16[32,2048]{1,0:T(8,128)(2,1)S(1)} %get-tuple-element.6), channel_id=1, source_target_pairs={{0,3},{1,4},{2,5},{3,6},{4,7},{5,0},{6,1},{7,2},{8,11},{9,12},{10,... | collective-permute-start | bytes 393224 | tf_op jit(solution)/shard_map/ppermute | solution.py:46
  85.5 2.2 %collective-permute-start.15 = (bf16[32,2048]{1,0:T(8,128)(2,1)S(1)}, bf16[32,2048]{1,0:T(8,128)(2,1)}, u32[]{:S(2)}, u32[]{:S(2)}) collective-permute-start(bf16[32,2048]{1,0:T(8,128)(2,1)S(1)} %get-tuple-element.6), channel_id=1, source_target_pairs={{0,5},{1,6},{2,7},{3,0},{4,1},{5,2},{6,3},{7,4},{8,13},{9,14},{10,... | collective-permute-start | bytes 393224 | tf_op jit(solution)/shard_map/ppermute | solution.py:46
  89.9 6.0 %all-to-all-start = ((bf16[64,1,4,2048]{3,2,1,0:T(4,128)(2,1)}), bf16[64,1,4,2048]{3,2,1,0:T(4,128)(2,1)}, u32[]{:S(2)}, u32[]{:S(2)}) async-start(bf16[64,1,4,2048]{3,2,1,0:T(4,128)(2,1)} %copy.87), calls=%async_computation | async-start | bytes 2097152 | tf_op jit(solution)/shard_map/all_to_all | solution.py:228
  95.9 2.8 %collective-permute-start.16 = (bf16[32,2048]{1,0:T(8,128)(2,1)S(1)}, bf16[32,2048]{1,0:T(8,128)(2,1)S(1)}, u32[]{:S(2)}, u32[]{:S(2)}) collective-permute-start(bf16[32,2048]{1,0:T(8,128)(2,1)S(1)} %get-tuple-element.6), channel_id=1, source_target_pairs={{0,6},{1,7},{2,0},{3,1},{4,2},{5,3},{6,4},{7,5},{8,14},{9,15},{10,... | collective-permute-start | bytes 393224 | tf_op jit(solution)/shard_map/ppermute | solution.py:46
  106.8 5.3 %collective-permute-done.16 = bf16[32,2048]{1,0:T(8,128)(2,1)S(1)} collective-permute-done((bf16[32,2048]{1,0:T(8,128)(2,1)S(1)}, bf16[32,2048]{1,0:T(8,128)(2,1)S(1)}, u32[]{:S(2)}, u32[]{:S(2)}) %collective-permute-start.16) | collective-permute-done | bytes 131104 | tf_op jit(solution)/shard_map/ppermute | solution.py:46
  115.4 5.0 %fusion.23 = f32[64,1,4,768]{3,0,2,1:T(8,128)} fusion(bf16[1,2048,768]{2,1,0:T(8,128)(2,1)} %param.31, bf16[64,1,4,2048]{3,2,1,0:T(4,128)(2,1)} %all-to-all-done), kind=kOutput, calls=%fused_computation.29 | convolution fusion | flops 805306368 | bytes 4980736 | tf_op jit(solution)/shard_map/sjkd,jdf->sjkf/dot_general | solution.py:229
  120.4 5.9 %fusion.12 = bf16[64,1,4,2048]{3,0,2,1:T(8,128)(2,1)} fusion(bf16[1,768,2048]{2,1,0:T(8,128)(2,1)S(1)} %copy-done, bf16[1,2048,768]{2,1,0:T(8,128)(2,1)} %param.32, bf16[64,1,4,2048]{3,2,1,0:T(4,128)(2,1)} %all-to-all-done, f32[64,1,4,768]{3,0,2,1:T(8,128)} %fusion.23), kind=kOutput, calls=%fused_computation.15 | convolution fusion | flops 1612316672 | bytes 9175040 | tf_op jit(solution)/shard_map/sjkf,jfd->sjkd/dot_general | solution.py:232
  126.3 3.0 %copy.89 = bf16[64,1,4,2048]{3,2,1,0:T(4,128)(2,1)} copy(bf16[64,1,4,2048]{3,0,2,1:T(8,128)(2,1)} %fusion.12) | data formatting | bytes 2097152 | tf_op jit(solution)/shard_map/convert_element_type | solution.py:234
  129.3 10.3 %all-to-all-start.1 = ((bf16[64,1,4,2048]{3,2,1,0:T(4,128)(2,1)}), bf16[64,1,4,2048]{3,2,1,0:T(4,128)(2,1)}, u32[]{:S(2)}, u32[]{:S(2)}) async-start(bf16[64,1,4,2048]{3,2,1,0:T(4,128)(2,1)} %copy.89), calls=%async_computation.1 | async-start | bytes 2097152 | tf_op jit(solution)/shard_map/all_to_all | solution.py:235
  139.6 4.1 %convolution_convert_fusion = bf16[256,2048]{1,0:T(8,128)(2,1)} fusion(bf16[256,2048]{1,0:T(8,128)(2,1)} %param.30, f32[256,256]{1,0:T(8,128)S(1)} %fusion.132, bf16[256,2048]{1,0:T(8,128)(2,1)} %constant_dynamic-update-slice_fusion.4, bf16[2048,256]{1,0:T(8,128)(2,1)} %param.29), kind=kOutput, calls=%fused_computation.10 | convolution fusion | flops 537788416 | bytes 4456448 | tf_op jit(solution)/shard_map/dot_general | solution.py:206
  145.8 2.4 %collective-permute-start.24 = (bf16[32,2048]{1,0:T(8,128)(2,1)S(1)}, bf16[32,2048]{1,0:T(8,128)(2,1)S(1)}, u32[]{:S(2)}, u32[]{:S(2)}) collective-permute-start(bf16[32,2048]{1,0:T(8,128)(2,1)S(1)} %get-tuple-element.12), channel_id=1, source_target_pairs={{0,7},{1,0},{2,1},{3,2},{4,3},{5,4},{6,5},{7,6},{8,15},{9,8},{10,9... | collective-permute-start | bytes 393224 | tf_op jit(solution)/shard_map/ppermute | solution.py:37
  149.2 2.7 %collective-permute-start.21 = (bf16[32,2048]{1,0:T(8,128)(2,1)}, bf16[32,2048]{1,0:T(8,128)(2,1)}, u32[]{:S(2)}, u32[]{:S(2)}) collective-permute-start(bf16[32,2048]{1,0:T(8,128)(2,1)} %get-tuple-element.15), channel_id=1, source_target_pairs={{0,4},{1,5},{2,6},{3,7},{4,0},{5,1},{6,2},{7,3},{8,12},{9,13},{10,... | collective-permute-start | bytes 393224 | tf_op jit(solution)/shard_map/ppermute | solution.py:37
  151.9 3.4 %collective-permute-done.24 = bf16[32,2048]{1,0:T(8,128)(2,1)S(1)} collective-permute-done((bf16[32,2048]{1,0:T(8,128)(2,1)S(1)}, bf16[32,2048]{1,0:T(8,128)(2,1)S(1)}, u32[]{:S(2)}, u32[]{:S(2)}) %collective-permute-start.24) | collective-permute-done | bytes 131104 | tf_op jit(solution)/shard_map/ppermute | solution.py:37
  155.9 7.7 %collective-permute-done.23 = bf16[32,2048]{1,0:T(8,128)(2,1)S(1)} collective-permute-done((bf16[32,2048]{1,0:T(8,128)(2,1)S(1)}, bf16[32,2048]{1,0:T(8,128)(2,1)S(1)}, u32[]{:S(2)}, u32[]{:S(2)}) %collective-permute-start.23) | collective-permute-done | bytes 131104 | tf_op jit(solution)/shard_map/ppermute | solution.py:37
  165.9 4.1 %collective-permute-done.18 = bf16[32,2048]{1,0:T(8,128)(2,1)} collective-permute-done((bf16[32,2048]{1,0:T(8,128)(2,1)S(1)}, bf16[32,2048]{1,0:T(8,128)(2,1)}, u32[]{:S(2)}, u32[]{:S(2)}) %collective-permute-start.18) | collective-permute-done | bytes 131104 | tf_op jit(solution)/shard_map/ppermute | solution.py:37
  169.9 3.7 %fusion.102 = bf16[1,32,2048]{2,1,0:T(8,128)(2,1)} fusion(bf16[64,1,4,2048]{3,2,1,0:T(4,128)(2,1)} %all-to-all-done.1, f32[32,64,4]{0,2,1:T(4,128)S(1)} %bitcast.212, bf16[32,2048]{1,0:T(8,128)(2,1)} %copy-done.13, bf16[32,2048]{1,0:T(8,128)(2,1)} %copy-done.14, bf16[32,2048]{1,0:T(8,128)(2,1)} %collective-permute-done.22, ...), kind=kOutput, calls=%fused_computation.108 | convolution fusion | flops 101908480 | bytes 2392064 | tf_op jit(solution)/shard_map/rsjk,sjkd->rd/dot_general | solution.py:240
  (169 shorter events, 68.5 us)
Async XLA Ops:
  10.1 37.8 %collective-permute-start = (bf16[256,576]{0,1:T(8,128)(2,1)}, bf16[256,576]{0,1:T(8,128)(2,1)}, u32[]{:S(2)}, u32[]{:S(2)}) collective-permute-start(bf16[256,576]{0,1:T(8,128)(2,1)} %pad_maximum_fusion), channel_id=1, source_target_pairs={{0,32},{8,40},{16,48},{24,56},{1,33},{9,41},{17,49},{25,57},{2,34}... | collective-permute-start | bytes 884744 | tf_op jit(solution)/shard_map/ppermute | solution.py:22
  15.8 33.2 %collective-permute-start.1 = (bf16[256,576]{0,1:T(8,128)(2,1)}, bf16[256,576]{0,1:T(8,128)(2,1)}, u32[]{:S(2)}, u32[]{:S(2)}) collective-permute-start(bf16[256,576]{0,1:T(8,128)(2,1)} %pad_maximum_fusion), channel_id=1, source_target_pairs={{0,24},{8,32},{16,40},{24,48},{32,56},{1,25},{9,33},{17,41},{25,49... | collective-permute-start | bytes 884744 | tf_op jit(solution)/shard_map/ppermute | solution.py:22
  17.8 32.3 %collective-permute-start.2 = (bf16[256,576]{0,1:T(8,128)(2,1)}, bf16[256,576]{0,1:T(8,128)(2,1)}, u32[]{:S(2)}, u32[]{:S(2)}) collective-permute-start(bf16[256,576]{0,1:T(8,128)(2,1)} %pad_maximum_fusion), channel_id=1, source_target_pairs={{0,16},{8,24},{16,32},{24,40},{32,48},{40,56},{1,17},{9,25},{17,33... | collective-permute-start | bytes 884744 | tf_op jit(solution)/shard_map/ppermute | solution.py:22
  23.3 27.8 %collective-permute-start.3 = (bf16[256,576]{0,1:T(8,128)(2,1)}, bf16[256,576]{0,1:T(8,128)(2,1)}, u32[]{:S(2)}, u32[]{:S(2)}) collective-permute-start(bf16[256,576]{0,1:T(8,128)(2,1)} %pad_maximum_fusion), channel_id=1, source_target_pairs={{0,8},{8,16},{16,24},{24,32},{32,40},{40,48},{48,56},{1,9},{9,17},... | collective-permute-start | bytes 884744 | tf_op jit(solution)/shard_map/ppermute | solution.py:22
  58.9 6.7 %collective-permute-start.10 = (bf16[32,2048]{1,0:T(8,128)(2,1)}, bf16[32,2048]{1,0:T(8,128)(2,1)S(1)}, u32[]{:S(2)}, u32[]{:S(2)}) collective-permute-start(bf16[32,2048]{1,0:T(8,128)(2,1)} %get-tuple-element.19), channel_id=1, source_target_pairs={{0,7},{1,0},{2,1},{3,2},{4,3},{5,4},{6,5},{7,6},{8,15},{9,8},{10,9... | collective-permute-start | bytes 393224 | tf_op jit(solution)/shard_map/ppermute | solution.py:37
  62.7 10.2 %collective-permute-start.7 = (bf16[32,2048]{1,0:T(8,128)(2,1)}, bf16[32,2048]{1,0:T(8,128)(2,1)S(1)}, u32[]{:S(2)}, u32[]{:S(2)}) collective-permute-start(bf16[32,2048]{1,0:T(8,128)(2,1)} %get-tuple-element.22), channel_id=1, source_target_pairs={{0,4},{1,5},{2,6},{3,7},{4,0},{5,1},{6,2},{7,3},{8,12},{9,13},{10,... | collective-permute-start | bytes 393224 | tf_op jit(solution)/shard_map/ppermute | solution.py:37
  65.6 7.6 %collective-permute-start.6 = (bf16[32,2048]{1,0:T(8,128)(2,1)}, bf16[32,2048]{1,0:T(8,128)(2,1)S(1)}, u32[]{:S(2)}, u32[]{:S(2)}) collective-permute-start(bf16[32,2048]{1,0:T(8,128)(2,1)} %get-tuple-element.23), channel_id=1, source_target_pairs={{0,3},{1,4},{2,5},{3,6},{4,7},{5,0},{6,1},{7,2},{8,11},{9,12},{10,... | collective-permute-start | bytes 393224 | tf_op jit(solution)/shard_map/ppermute | solution.py:37
  65.6 12.9 %collective-permute-start.5 = (bf16[32,2048]{1,0:T(8,128)(2,1)}, bf16[32,2048]{1,0:T(8,128)(2,1)S(1)}, u32[]{:S(2)}, u32[]{:S(2)}) collective-permute-start(bf16[32,2048]{1,0:T(8,128)(2,1)} %get-tuple-element.24), channel_id=1, source_target_pairs={{0,2},{1,3},{2,4},{3,5},{4,6},{5,7},{6,0},{7,1},{8,10},{9,11},{10,... | collective-permute-start | bytes 393224 | tf_op jit(solution)/shard_map/ppermute | solution.py:37
  67.5 11.1 %collective-permute-start.4 = (bf16[32,2048]{1,0:T(8,128)(2,1)S(1)}, bf16[32,2048]{1,0:T(8,128)(2,1)S(1)}, u32[]{:S(2)}, u32[]{:S(2)}) collective-permute-start(bf16[32,2048]{1,0:T(8,128)(2,1)S(1)} %get-tuple-element.18), channel_id=1, source_target_pairs={{0,1},{1,2},{2,3},{3,4},{4,5},{5,6},{6,7},{7,0},{8,9},{9,10},{10,1... | collective-permute-start | bytes 393224 | tf_op jit(solution)/shard_map/ppermute | solution.py:37
  80.7 15.2 %collective-permute-start.11 = (bf16[32,2048]{1,0:T(8,128)(2,1)S(1)}, bf16[32,2048]{1,0:T(8,128)(2,1)}, u32[]{:S(2)}, u32[]{:S(2)}) collective-permute-start(bf16[32,2048]{1,0:T(8,128)(2,1)S(1)} %get-tuple-element.6), channel_id=1, source_target_pairs={{0,1},{1,2},{2,3},{3,4},{4,5},{5,6},{6,7},{7,0},{8,9},{9,10},{10,1... | collective-permute-start | bytes 393224 | tf_op jit(solution)/shard_map/ppermute | solution.py:46
  80.9 19.3 %collective-permute-start.12 = (bf16[32,2048]{1,0:T(8,128)(2,1)S(1)}, bf16[32,2048]{1,0:T(8,128)(2,1)}, u32[]{:S(2)}, u32[]{:S(2)}) collective-permute-start(bf16[32,2048]{1,0:T(8,128)(2,1)S(1)} %get-tuple-element.6), channel_id=1, source_target_pairs={{0,2},{1,3},{2,4},{3,5},{4,6},{5,7},{6,0},{7,1},{8,10},{9,11},{10,... | collective-permute-start | bytes 393224 | tf_op jit(solution)/shard_map/ppermute | solution.py:46
  81.0 21.1 %collective-permute-start.13 = (bf16[32,2048]{1,0:T(8,128)(2,1)S(1)}, bf16[32,2048]{1,0:T(8,128)(2,1)}, u32[]{:S(2)}, u32[]{:S(2)}) collective-permute-start(bf16[32,2048]{1,0:T(8,128)(2,1)S(1)} %get-tuple-element.6), channel_id=1, source_target_pairs={{0,3},{1,4},{2,5},{3,6},{4,7},{5,0},{6,1},{7,2},{8,11},{9,12},{10,... | collective-permute-start | bytes 393224 | tf_op jit(solution)/shard_map/ppermute | solution.py:46
  84.1 19.6 %collective-permute-start.14 = (bf16[32,2048]{1,0:T(8,128)(2,1)S(1)}, bf16[32,2048]{1,0:T(8,128)(2,1)}, u32[]{:S(2)}, u32[]{:S(2)}) collective-permute-start(bf16[32,2048]{1,0:T(8,128)(2,1)S(1)} %get-tuple-element.6), channel_id=1, source_target_pairs={{0,4},{1,5},{2,6},{3,7},{4,0},{5,1},{6,2},{7,3},{8,12},{9,13},{10,... | collective-permute-start | bytes 393224 | tf_op jit(solution)/shard_map/ppermute | solution.py:46
  85.5 19.7 %collective-permute-start.15 = (bf16[32,2048]{1,0:T(8,128)(2,1)S(1)}, bf16[32,2048]{1,0:T(8,128)(2,1)}, u32[]{:S(2)}, u32[]{:S(2)}) collective-permute-start(bf16[32,2048]{1,0:T(8,128)(2,1)S(1)} %get-tuple-element.6), channel_id=1, source_target_pairs={{0,5},{1,6},{2,7},{3,0},{4,1},{5,2},{6,3},{7,4},{8,13},{9,14},{10,... | collective-permute-start | bytes 393224 | tf_op jit(solution)/shard_map/ppermute | solution.py:46
  89.9 25.5 %all-to-all-start = ((bf16[64,1,4,2048]{3,2,1,0:T(4,128)(2,1)}), bf16[64,1,4,2048]{3,2,1,0:T(4,128)(2,1)}, u32[]{:S(2)}, u32[]{:S(2)}) async-start(bf16[64,1,4,2048]{3,2,1,0:T(4,128)(2,1)} %copy.87), calls=%async_computation | async-start | bytes 2097152 | tf_op jit(solution)/shard_map/all_to_all | solution.py:228
  95.9 16.2 %collective-permute-start.16 = (bf16[32,2048]{1,0:T(8,128)(2,1)S(1)}, bf16[32,2048]{1,0:T(8,128)(2,1)S(1)}, u32[]{:S(2)}, u32[]{:S(2)}) collective-permute-start(bf16[32,2048]{1,0:T(8,128)(2,1)S(1)} %get-tuple-element.6), channel_id=1, source_target_pairs={{0,6},{1,7},{2,0},{3,1},{4,2},{5,3},{6,4},{7,5},{8,14},{9,15},{10,... | collective-permute-start | bytes 393224 | tf_op jit(solution)/shard_map/ppermute | solution.py:46
  100.2 12.5 %collective-permute-start.17 = (bf16[32,2048]{1,0:T(8,128)(2,1)S(1)}, bf16[32,2048]{1,0:T(8,128)(2,1)S(1)}, u32[]{:S(2)}, u32[]{:S(2)}) collective-permute-start(bf16[32,2048]{1,0:T(8,128)(2,1)S(1)} %get-tuple-element.6), channel_id=1, source_target_pairs={{0,7},{1,0},{2,1},{3,2},{4,3},{5,4},{6,5},{7,6},{8,15},{9,8},{10,9... | collective-permute-start | bytes 393224 | tf_op jit(solution)/shard_map/ppermute | solution.py:46
  129.3 40.6 %all-to-all-start.1 = ((bf16[64,1,4,2048]{3,2,1,0:T(4,128)(2,1)}), bf16[64,1,4,2048]{3,2,1,0:T(4,128)(2,1)}, u32[]{:S(2)}, u32[]{:S(2)}) async-start(bf16[64,1,4,2048]{3,2,1,0:T(4,128)(2,1)} %copy.89), calls=%async_computation.1 | async-start | bytes 2097152 | tf_op jit(solution)/shard_map/all_to_all | solution.py:235
  145.8 9.4 %collective-permute-start.24 = (bf16[32,2048]{1,0:T(8,128)(2,1)S(1)}, bf16[32,2048]{1,0:T(8,128)(2,1)S(1)}, u32[]{:S(2)}, u32[]{:S(2)}) collective-permute-start(bf16[32,2048]{1,0:T(8,128)(2,1)S(1)} %get-tuple-element.12), channel_id=1, source_target_pairs={{0,7},{1,0},{2,1},{3,2},{4,3},{5,4},{6,5},{7,6},{8,15},{9,8},{10,9... | collective-permute-start | bytes 393224 | tf_op jit(solution)/shard_map/ppermute | solution.py:37
  148.2 15.3 %collective-permute-start.23 = (bf16[32,2048]{1,0:T(8,128)(2,1)S(1)}, bf16[32,2048]{1,0:T(8,128)(2,1)S(1)}, u32[]{:S(2)}, u32[]{:S(2)}) collective-permute-start(bf16[32,2048]{1,0:T(8,128)(2,1)S(1)} %get-tuple-element.13), channel_id=1, source_target_pairs={{0,6},{1,7},{2,0},{3,1},{4,2},{5,3},{6,4},{7,5},{8,14},{9,15},{10,... | collective-permute-start | bytes 393224 | tf_op jit(solution)/shard_map/ppermute | solution.py:37
  149.1 16.7 %collective-permute-start.22 = (bf16[32,2048]{1,0:T(8,128)(2,1)}, bf16[32,2048]{1,0:T(8,128)(2,1)}, u32[]{:S(2)}, u32[]{:S(2)}) collective-permute-start(bf16[32,2048]{1,0:T(8,128)(2,1)} %get-tuple-element.14), channel_id=1, source_target_pairs={{0,5},{1,6},{2,7},{3,0},{4,1},{5,2},{6,3},{7,4},{8,13},{9,14},{10,... | collective-permute-start | bytes 393224 | tf_op jit(solution)/shard_map/ppermute | solution.py:37
  149.2 16.6 %collective-permute-start.21 = (bf16[32,2048]{1,0:T(8,128)(2,1)}, bf16[32,2048]{1,0:T(8,128)(2,1)}, u32[]{:S(2)}, u32[]{:S(2)}) collective-permute-start(bf16[32,2048]{1,0:T(8,128)(2,1)} %get-tuple-element.15), channel_id=1, source_target_pairs={{0,4},{1,5},{2,6},{3,7},{4,0},{5,1},{6,2},{7,3},{8,12},{9,13},{10,... | collective-permute-start | bytes 393224 | tf_op jit(solution)/shard_map/ppermute | solution.py:37
  151.9 14.0 %collective-permute-start.20 = (bf16[32,2048]{1,0:T(8,128)(2,1)}, bf16[32,2048]{1,0:T(8,128)(2,1)}, u32[]{:S(2)}, u32[]{:S(2)}) collective-permute-start(bf16[32,2048]{1,0:T(8,128)(2,1)} %get-tuple-element.16), channel_id=1, source_target_pairs={{0,3},{1,4},{2,5},{3,6},{4,7},{5,0},{6,1},{7,2},{8,11},{9,12},{10,... | collective-permute-start | bytes 393224 | tf_op jit(solution)/shard_map/ppermute | solution.py:37
  155.3 10.6 %collective-permute-start.19 = (bf16[32,2048]{1,0:T(8,128)(2,1)}, bf16[32,2048]{1,0:T(8,128)(2,1)}, u32[]{:S(2)}, u32[]{:S(2)}) collective-permute-start(bf16[32,2048]{1,0:T(8,128)(2,1)} %get-tuple-element.17), channel_id=1, source_target_pairs={{0,2},{1,3},{2,4},{3,5},{4,6},{5,7},{6,0},{7,1},{8,10},{9,11},{10,... | collective-permute-start | bytes 393224 | tf_op jit(solution)/shard_map/ppermute | solution.py:37
  (31 other events, 303.5 us)

commit v6 on v4

--- a/solution.py
+++ b/solution.py
@@ -27,23 +27,33 @@
     rank = lax.axis_index(axis)
     pieces = parts.reshape((count, parts.shape[0] // count) + parts.shape[1:])
 
-    def piece_for(steps):
+    def pair_for(steps):
         if arrival_order:
-            return pieces[(count - steps) % count]
-        return lax.dynamic_index_in_dim(pieces, (rank + steps) % count, 0, keepdims=False)
-
-    total = piece_for(0).astype(jnp.float32)
-    for steps in range(1, count):
-        moved = lax.ppermute(piece_for(steps), axis, [(i, (i + steps) % count) for i in range(count)])
-        total = total + moved.astype(jnp.float32)
-    return total
+            return pieces[2 * steps], pieces[2 * steps + 1]
+        owner = (rank - 2 * steps) % count
+        return (
+            lax.dynamic_index_in_dim(pieces, owner, 0, keepdims=False),
+            lax.dynamic_index_in_dim(pieces, owner ^ 1, 0, keepdims=False),
+        )
+
+    mine, partners = pair_for(0)
+    mine = mine.astype(jnp.float32)
+    partners = partners.astype(jnp.float32)
+    for steps in range(1, count // 2):
+        moved = lax.ppermute(
+            jnp.stack(pair_for(steps)), axis, [(i, (i - 2 * steps) % count) for i in range(count)]
+        )
+        mine = mine + moved[0].astype(jnp.float32)
+        partners = partners + moved[1].astype(jnp.float32)
+    return mine + lax.ppermute(partners, axis, [(i, i ^ 1) for i in range(count)])
 
 
 def gathered_over(block, axis):
     count = lax.axis_size(axis)
-    arrived = [block]
-    for steps in range(1, count):
-        arrived.append(lax.ppermute(block, axis, [(i, (i + steps) % count) for i in range(count)]))
+    pair = jnp.concatenate([block, lax.ppermute(block, axis, [(i, i ^ 1) for i in range(count)])])
+    arrived = [pair]
+    for steps in range(1, count // 2):
+        arrived.append(lax.ppermute(pair, axis, [(i, (i + 2 * steps) % count) for i in range(count)]))
     return jnp.concatenate(arrived, axis=0)
 
 
@@ -227,7 +237,7 @@
         "rsjk,sjkd->rd",
         combining,
         returned.astype(jnp.float32),
-        precision=lax.Precision.HIGHEST,
+        precision=lax.Precision.HIGH,
     )
     finished = (own_residual.astype(jnp.float32) + shared_out + routed).astype(jnp.bfloat16)
     return finished[None]

time: 168 us -> 186 us (1.11)
  waiting for transfers between devices: 21.8 us -> 48.6 us
  starting transfers between devices: 66.5 us -> 54.8 us
  other arithmetic: 12.5 us -> 21.2 us
  local copies, waits for them, and re-layouts: 30.7 us -> 24.1 us
    ppermute x21 -> x12, waiting for transfers between devices: 21.8 us -> 48.6 us  [the longest x6 30.8 us: summed_over(): lax.ppermute(jnp.stack(pair_for(steps)), axis, [(i, (i - 2 * steps) % cou...]
    ppermute x21 -> x12, starting transfers between devices: 29.7 us -> 13.7 us  [the longest x6 8.12 us: summed_over(): lax.ppermute(jnp.stack(pair_for(steps)), axis, [(i, (i - 2 * steps) % cou...]
    unnamed x60 -> x41, local copies, waits for them, and re-layouts: 19.1 us -> 13.5 us
    all_to_all x1, starting transfers between devices: 9.77 us -> 13.2 us  [shards(): lax.all_to_all(outgoing, ('tok', 'mdl'), split_axis=0, concat_axis=0, til...]
    another operation x5 -> x11, other arithmetic: 2.24 us -> 5.29 us  [the longest x6 2.99 us: summed_over(): jnp.stack(pair_for(steps))]
    add x0 -> x2, other arithmetic: none -> 3.04 us  [summed_over(): partners = partners + moved[1].astype(jnp.float32)]
    broadcast_in_dim x0 -> x1, other arithmetic: none -> 1.93 us  [shards(): return finished[None]]
  transfers between devices with their start and end apart: 27 -> 18, of which waited for: 7 -> 7; matrix products, arithmetic and copies ran while one was open for 21% -> 28% of each run, Pallas kernels for 0% -> 0%
where the time goes in v6:
time: 186 us; the launch traced here: 185 us
  starting transfers between devices  54.8 us (29%)
  waiting for transfers between devices  48.6 us (26%)
  matrix products  35.7 us (19%)
  local copies, waits for them, and re-layouts  24.1 us (13%)
  other arithmetic  21.2 us (11%)
    ppermute x6, waiting for transfers between devices, summed_over(): lax.ppermute(jnp.stack(pair_for(steps)), axis, [(i, (i - 2 * steps) % cou...  30.8 us
    ppermute x4, starting transfers between devices, passed_along(): lax.ppermute(value, axis, [(source, source + steps) for source in range(i...  17.7 us
    ppermute x3, waiting for transfers between devices, gathered_over(): lax.ppermute(pair, axis, [(i, (i + 2 * steps) % count) for i in range(cou...  17.4 us
    unnamed x41, local copies, waits for them, and re-layouts  13.5 us
    all_to_all x1, starting transfers between devices, shards(): lax.all_to_all(outgoing, ('tok', 'mdl'), split_axis=0, concat_axis=0, til...  13.2 us
    all_to_all x1, starting transfers between devices, shards(): lax.all_to_all(produced, ('tok', 'mdl'), split_axis=0, concat_axis=0, til...  10.3 us
    ppermute x6, starting transfers between devices, summed_over(): lax.ppermute(jnp.stack(pair_for(steps)), axis, [(i, (i - 2 * steps) % cou...  8.12 us
    dot_general x1, matrix products, shards(): jnp.einsum('sjkf,jfd->sjkd', expert_act, w_expert_down, preferred_element...  5.92 us
  transfers between devices with their start and end apart: 18, of which 7 were waited for; matrix products, arithmetic and copies ran while one was open for 28% of the time, Pallas kernels for 0%

profile of v6, /device:TPU:1, one launch (start us, length us, event | category | flops | bytes accessed | tf_op | source)
XLA Modules:
  0.0 185.0 jit_solution(13624426238231338933)
XLA Ops:
  2.7 2.9 %fusion.62 = f32[256,576]{0,1:T(8,128)S(1)} fusion(bf16[2048,576]{0,1:T(8,128)(2,1)} %param.23, f32[2048]{0:T(1024)} %param.21, f32[256]{0:T(256)S(1)} %add_rsqrt_fusion.1, bf16[2,256,2048]{2,1,0:T(8,128)(2,1)} %param.17, s32[]{:T(128)S(6)} %select_n.81), kind=kOutput, calls=%fused_computation.48 | convolution fusion | flops 606076928 | bytes 4006916 | tf_op jit(solution)/shard_map/dot_general | solution.py:145
  10.1 6.2 %collective-permute-start = (bf16[256,576]{0,1:T(8,128)(2,1)}, bf16[256,576]{0,1:T(8,128)(2,1)}, u32[]{:S(2)}, u32[]{:S(2)}) collective-permute-start(bf16[256,576]{0,1:T(8,128)(2,1)} %pad_maximum_fusion), channel_id=1, source_target_pairs={{0,32},{8,40},{16,48},{24,56},{1,33},{9,41},{17,49},{25,57},{2,34}... | collective-permute-start | bytes 884744 | tf_op jit(solution)/shard_map/ppermute | solution.py:22
  16.3 6.4 %collective-permute-start.1 = (bf16[256,576]{0,1:T(8,128)(2,1)}, bf16[256,576]{0,1:T(8,128)(2,1)}, u32[]{:S(2)}, u32[]{:S(2)}) collective-permute-start(bf16[256,576]{0,1:T(8,128)(2,1)} %pad_maximum_fusion), channel_id=1, source_target_pairs={{0,24},{8,32},{16,40},{24,48},{32,56},{1,25},{9,33},{17,41},{25,49... | collective-permute-start | bytes 884744 | tf_op jit(solution)/shard_map/ppermute | solution.py:22
  22.7 2.0 %collective-permute-start.2 = (bf16[256,576]{0,1:T(8,128)(2,1)}, bf16[256,576]{0,1:T(8,128)(2,1)}, u32[]{:S(2)}, u32[]{:S(2)}) collective-permute-start(bf16[256,576]{0,1:T(8,128)(2,1)} %pad_maximum_fusion), channel_id=1, source_target_pairs={{0,16},{8,24},{16,32},{24,40},{32,48},{40,56},{1,17},{9,25},{17,33... | collective-permute-start | bytes 884744 | tf_op jit(solution)/shard_map/ppermute | solution.py:22
  24.7 3.1 %collective-permute-start.3 = (bf16[256,576]{0,1:T(8,128)(2,1)}, bf16[256,576]{0,1:T(8,128)(2,1)}, u32[]{:S(2)}, u32[]{:S(2)}) collective-permute-start(bf16[256,576]{0,1:T(8,128)(2,1)} %pad_maximum_fusion), channel_id=1, source_target_pairs={{0,8},{8,16},{16,24},{24,32},{32,40},{40,48},{48,56},{1,9},{9,17},... | collective-permute-start | bytes 884744 | tf_op jit(solution)/shard_map/ppermute | solution.py:22
  27.8 2.6 %copy.58 = bf16[2048,384]{0,1:T(8,128)(2,1)} copy(bf16[2048,384]{1,0:T(8,128)(2,1)} %param.22) | data formatting | bytes 3145728 | tf_op args[5]
  30.4 3.2 %fusion.60 = f32[256,2,192]{0,2,1:T(8,128)} fusion(bf16[2,192,2048]{2,1,0:T(8,128)(2,1)} %bitcast.201, f32[2048]{0:T(1024)S(1)} %copy-done.15, f32[256]{0:T(256)S(1)} %add_rsqrt_fusion.1, bf16[2,256,2048]{2,1,0:T(8,128)(2,1)} %param.17, s32[]{:T(128)S(6)} %select_n.81), kind=kOutput, calls=%fused_computation.47 | convolution fusion | flops 404750336 | bytes 3023876 | tf_op jit(solution)/shard_map/dot_general | solution.py:139
  45.5 4.2 %fusion.56 = bf16[256,2,128]{0,2,1:T(8,128)(2,1)} fusion(bf16[1280,2,256]{0,2,1:T(8,128)(2,1)} %bitcast.204, f32[2,256,1280]{2,1,0:T(8,128)} %copy-done.2, pred[256,1280]{1,0:T(8,128)(4,1)S(1)} %copy-done.6, f32[256,2]{0,1:T(2,128)S(1)} %bitcast.212), kind=kOutput, calls=%fused_computation.45 | convolution fusion | flops 170526464 | bytes 6686720 | tf_op jit(solution)/shard_map/hqk,khd->hqd/dot_general | solution.py:184
  52.6 2.8 %collective-permute-start.4 = (bf16[2,32,2048]{2,1,0:T(8,128)(2,1)S(1)}, bf16[2,32,2048]{2,1,0:T(8,128)(2,1)}, u32[]{:S(2)}, u32[]{:S(2)}) collective-permute-start(bf16[2,32,2048]{2,1,0:T(8,128)(2,1)S(1)} %pad_maximum_fusion.1), channel_id=1, source_target_pairs={{0,6},{1,7},{2,0},{3,1},{4,2},{5,3},{6,4},{7,5},{8,14},{9,15},{10,... | collective-permute-start | bytes 786440 | tf_op jit(solution)/shard_map/ppermute | solution.py:43
  60.6 3.5 %collective-permute-done.5 = bf16[2,32,2048]{2,1,0:T(8,128)(2,1)} collective-permute-done((bf16[2,32,2048]{2,1,0:T(8,128)(2,1)}, bf16[2,32,2048]{2,1,0:T(8,128)(2,1)}, u32[]{:S(2)}, u32[]{:S(2)}) %collective-permute-start.5) | collective-permute-done | bytes 262176 | tf_op jit(solution)/shard_map/ppermute | solution.py:43
  64.1 7.7 %collective-permute-done.6 = bf16[2,32,2048]{2,1,0:T(8,128)(2,1)} collective-permute-done((bf16[2,32,2048]{2,1,0:T(8,128)(2,1)}, bf16[2,32,2048]{2,1,0:T(8,128)(2,1)}, u32[]{:S(2)}, u32[]{:S(2)}) %collective-permute-start.6) | collective-permute-done | bytes 262176 | tf_op jit(solution)/shard_map/ppermute | solution.py:43
  82.6 13.2 %all-to-all-start = ((bf16[64,1,4,2048]{3,2,1,0:T(4,128)(2,1)}), bf16[64,1,4,2048]{3,2,1,0:T(4,128)(2,1)}, u32[]{:S(2)}, u32[]{:S(2)}) async-start(bf16[64,1,4,2048]{3,2,1,0:T(4,128)(2,1)} %copy.71), calls=%async_computation | async-start | bytes 2097152 | tf_op jit(solution)/shard_map/all_to_all | solution.py:224
  95.8 2.9 %collective-permute-start.10 = (bf16[64,2048]{1,0:T(8,128)(2,1)}, bf16[64,2048]{1,0:T(8,128)(2,1)S(1)}, u32[]{:S(2)}, u32[]{:S(2)}) collective-permute-start(bf16[64,2048]{1,0:T(8,128)(2,1)} %pad_maximum_fusion.4), channel_id=1, source_target_pairs={{0,4},{1,5},{2,6},{3,7},{4,0},{5,1},{6,2},{7,3},{8,12},{9,13},{10,... | collective-permute-start | bytes 786440 | tf_op jit(solution)/shard_map/ppermute | solution.py:56
  101.9 13.9 %collective-permute-done.10 = bf16[64,2048]{1,0:T(8,128)(2,1)S(1)} collective-permute-done((bf16[64,2048]{1,0:T(8,128)(2,1)}, bf16[64,2048]{1,0:T(8,128)(2,1)S(1)}, u32[]{:S(2)}, u32[]{:S(2)}) %collective-permute-start.10) | collective-permute-done | bytes 262176 | tf_op jit(solution)/shard_map/ppermute | solution.py:56
  116.5 3.5 %collective-permute-done.11 = bf16[64,2048]{1,0:T(8,128)(2,1)S(1)} collective-permute-done((bf16[64,2048]{1,0:T(8,128)(2,1)}, bf16[64,2048]{1,0:T(8,128)(2,1)S(1)}, u32[]{:S(2)}, u32[]{:S(2)}) %collective-permute-start.11) | collective-permute-done | bytes 262176 | tf_op jit(solution)/shard_map/ppermute | solution.py:56
  120.8 2.7 %fusion.122 = f32[256,256]{1,0:T(8,128)} fusion(bf16[256,2048]{1,0:T(8,128)(2,1)} %constant_dynamic-update-slice_fusion.5, bf16[2048,256]{1,0:T(8,128)(2,1)} %param.28), kind=kOutput, calls=%fused_computation.184 | convolution fusion | flops 268435456 | bytes 2359296 | tf_op jit(solution)/shard_map/dot_general | solution.py:198
  123.4 4.2 %convolution_convert_fusion.1 = bf16[256,2048]{1,0:T(8,128)(2,1)} fusion(bf16[256,2048]{1,0:T(8,128)(2,1)} %param.30, f32[256,256]{1,0:T(8,128)} %fusion.122, bf16[256,2048]{1,0:T(8,128)(2,1)} %constant_dynamic-update-slice_fusion.5, bf16[2048,256]{1,0:T(8,128)(2,1)} %param.29), kind=kOutput, calls=%fused_computation.20 | convolution fusion | flops 537788416 | bytes 4456448 | tf_op jit(solution)/shard_map/dot_general | solution.py:202
  133.2 5.0 %fusion.35 = f32[64,1,4,768]{3,0,2,1:T(8,128)} fusion(bf16[1,2048,768]{2,1,0:T(8,128)(2,1)} %param.31, bf16[64,1,4,2048]{3,2,1,0:T(4,128)(2,1)} %all-to-all-done), kind=kOutput, calls=%fused_computation.38 | convolution fusion | flops 805306368 | bytes 4980736 | tf_op jit(solution)/shard_map/sjkd,jdf->sjkf/dot_general | solution.py:225
  138.2 5.9 %fusion.22 = bf16[64,1,4,2048]{3,0,2,1:T(8,128)(2,1)} fusion(bf16[1,768,2048]{2,1,0:T(8,128)(2,1)S(1)} %copy-done, bf16[1,2048,768]{2,1,0:T(8,128)(2,1)} %param.32, bf16[64,1,4,2048]{3,2,1,0:T(4,128)(2,1)} %all-to-all-done, f32[64,1,4,768]{3,0,2,1:T(8,128)} %fusion.35), kind=kOutput, calls=%fused_computation.25 | convolution fusion | flops 1612316672 | bytes 9175040 | tf_op jit(solution)/shard_map/sjkf,jfd->sjkd/dot_general | solution.py:228
  144.1 3.1 %copy.73 = bf16[64,1,4,2048]{3,2,1,0:T(4,128)(2,1)} copy(bf16[64,1,4,2048]{3,0,2,1:T(8,128)(2,1)} %fusion.22) | data formatting | bytes 2097152 | tf_op jit(solution)/shard_map/convert_element_type | solution.py:230
  147.2 10.3 %all-to-all-start.1 = ((bf16[64,1,4,2048]{3,2,1,0:T(4,128)(2,1)}), bf16[64,1,4,2048]{3,2,1,0:T(4,128)(2,1)}, u32[]{:S(2)}, u32[]{:S(2)}) async-start(bf16[64,1,4,2048]{3,2,1,0:T(4,128)(2,1)} %copy.73), calls=%async_computation.1 | async-start | bytes 2097152 | tf_op jit(solution)/shard_map/all_to_all | solution.py:231
  159.0 18.4 %collective-permute-done.14 = bf16[2,32,2048]{2,1,0:T(8,128)(2,1)S(1)} collective-permute-done((bf16[2,32,2048]{2,1,0:T(8,128)(2,1)S(1)}, bf16[2,32,2048]{2,1,0:T(8,128)(2,1)S(1)}, u32[]{:S(2)}, u32[]{:S(2)}) %collective-permute-start.14) | collective-permute-done | bytes 262176 | tf_op jit(solution)/shard_map/ppermute | solution.py:43
  180.3 2.7 %convolution_bitcast_fusion.1 = f32[32,2048]{1,0:T(8,128)S(1)} fusion(bf16[64,1,4,2048]{3,2,1,0:T(4,128)(2,1)} %all-to-all-done.1, f32[32,64,4]{0,2,1:T(4,128)S(1)} %bitcast.202), kind=kOutput, calls=%fused_computation.26 | convolution fusion | flops 100663296 | bytes 1343488 | tf_op jit(solution)/shard_map/rsjk,sjkd->rd/dot_general | solution.py:236
  183.0 1.9 %fusion.94 = bf16[1,32,2048]{2,1,0:T(8,128)(2,1)} fusion(f32[32,2048]{1,0:T(8,128)S(1)} %convolution_bitcast_fusion.1, f32[32,2048]{1,0:T(8,128)} %collective-permute-done.15, bf16[32,2048]{1,0:T(8,128)(2,1)S(1)} %get-tuple-element.8, bf16[2,32,2048]{2,1,0:T(8,128)(2,1)} %copy-done.7, bf16[2,32,2048]{2,1,0:T(8,128)(2,1)} %collective-permute-done.13, ...), kind=kLoop, calls=%fused_computation.100 | loop fusion | flops 786432 | bytes 1310720 | tf_op jit(solution)/shard_map/broadcast_in_dim | solution.py:243
  (124 shorter events, 52.2 us)
Async XLA Ops:
  0.0 138.2 %copy-start = (bf16[1,768,2048]{2,1,0:T(8,128)(2,1)S(1)}, bf16[1,768,2048]{2,1,0:T(8,128)(2,1)}, u32[]{:S(2)}) copy-start(bf16[1,768,2048]{2,1,0:T(8,128)(2,1)} %param.33) | copy-start | bytes 9437188
  8.2 22.2 %copy-start.15 = (f32[2048]{0:T(1024)S(1)}, f32[2048]{0:T(1024)}, u32[]{:S(2)}) copy-start(f32[2048]{0:T(1024)} %param.21) | copy-start | bytes 24580
  10.1 26.7 %collective-permute-start = (bf16[256,576]{0,1:T(8,128)(2,1)}, bf16[256,576]{0,1:T(8,128)(2,1)}, u32[]{:S(2)}, u32[]{:S(2)}) collective-permute-start(bf16[256,576]{0,1:T(8,128)(2,1)} %pad_maximum_fusion), channel_id=1, source_target_pairs={{0,32},{8,40},{16,48},{24,56},{1,33},{9,41},{17,49},{25,57},{2,34}... | collective-permute-start | bytes 884744 | tf_op jit(solution)/shard_map/ppermute | solution.py:22
  16.3 21.5 %collective-permute-start.1 = (bf16[256,576]{0,1:T(8,128)(2,1)}, bf16[256,576]{0,1:T(8,128)(2,1)}, u32[]{:S(2)}, u32[]{:S(2)}) collective-permute-start(bf16[256,576]{0,1:T(8,128)(2,1)} %pad_maximum_fusion), channel_id=1, source_target_pairs={{0,24},{8,32},{16,40},{24,48},{32,56},{1,25},{9,33},{17,41},{25,49... | collective-permute-start | bytes 884744 | tf_op jit(solution)/shard_map/ppermute | solution.py:22
  22.7 16.2 %collective-permute-start.2 = (bf16[256,576]{0,1:T(8,128)(2,1)}, bf16[256,576]{0,1:T(8,128)(2,1)}, u32[]{:S(2)}, u32[]{:S(2)}) collective-permute-start(bf16[256,576]{0,1:T(8,128)(2,1)} %pad_maximum_fusion), channel_id=1, source_target_pairs={{0,16},{8,24},{16,32},{24,40},{32,48},{40,56},{1,17},{9,25},{17,33... | collective-permute-start | bytes 884744 | tf_op jit(solution)/shard_map/ppermute | solution.py:22
  24.7 15.2 %collective-permute-start.3 = (bf16[256,576]{0,1:T(8,128)(2,1)}, bf16[256,576]{0,1:T(8,128)(2,1)}, u32[]{:S(2)}, u32[]{:S(2)}) collective-permute-start(bf16[256,576]{0,1:T(8,128)(2,1)} %pad_maximum_fusion), channel_id=1, source_target_pairs={{0,8},{8,16},{16,24},{24,32},{32,40},{40,48},{48,56},{1,9},{9,17},... | collective-permute-start | bytes 884744 | tf_op jit(solution)/shard_map/ppermute | solution.py:22
  30.4 6.0 %copy-start.12 = (s32[2,32,6]{1,0,2:T(2,128)S(1)}, s32[2,32,6]{1,0,2:T(2,128)}, u32[]{:S(2)}) copy-start(s32[2,32,6]{1,0,2:T(2,128)} %param.19) | copy-start | bytes 4612
  52.6 23.7 %copy-start.10 = (f32[2048]{0:T(1024)S(1)}, f32[2048]{0:T(1024)}, u32[]{:S(2)}) copy-start(f32[2048]{0:T(1024)} %param.27) | copy-start | bytes 24580
  52.6 8.0 %collective-permute-start.4 = (bf16[2,32,2048]{2,1,0:T(8,128)(2,1)S(1)}, bf16[2,32,2048]{2,1,0:T(8,128)(2,1)}, u32[]{:S(2)}, u32[]{:S(2)}) collective-permute-start(bf16[2,32,2048]{2,1,0:T(8,128)(2,1)S(1)} %pad_maximum_fusion.1), channel_id=1, source_target_pairs={{0,6},{1,7},{2,0},{3,1},{4,2},{5,3},{6,4},{7,5},{8,14},{9,15},{10,... | collective-permute-start | bytes 786440 | tf_op jit(solution)/shard_map/ppermute | solution.py:43
  56.1 7.9 %collective-permute-start.5 = (bf16[2,32,2048]{2,1,0:T(8,128)(2,1)}, bf16[2,32,2048]{2,1,0:T(8,128)(2,1)}, u32[]{:S(2)}, u32[]{:S(2)}) collective-permute-start(bf16[2,32,2048]{2,1,0:T(8,128)(2,1)} %pad_maximum_fusion.2), channel_id=1, source_target_pairs={{0,4},{1,5},{2,6},{3,7},{4,0},{5,1},{6,2},{7,3},{8,12},{9,13},{10,... | collective-permute-start | bytes 786440 | tf_op jit(solution)/shard_map/ppermute | solution.py:43
  57.2 14.6 %collective-permute-start.6 = (bf16[2,32,2048]{2,1,0:T(8,128)(2,1)}, bf16[2,32,2048]{2,1,0:T(8,128)(2,1)}, u32[]{:S(2)}, u32[]{:S(2)}) collective-permute-start(bf16[2,32,2048]{2,1,0:T(8,128)(2,1)} %pad_maximum_fusion.3), channel_id=1, source_target_pairs={{0,2},{1,3},{2,4},{3,5},{4,6},{5,7},{6,0},{7,1},{8,10},{9,11},{10,... | collective-permute-start | bytes 786440 | tf_op jit(solution)/shard_map/ppermute | solution.py:43
  73.0 1.9 %collective-permute-start.7 = (f32[32,2048]{1,0:T(8,128)S(1)}, f32[32,2048]{1,0:T(8,128)}, u32[]{:S(2)}, u32[]{:S(2)}) collective-permute-start(f32[32,2048]{1,0:T(8,128)S(1)} %add_bitcast_fusion), channel_id=1, source_target_pairs={{0,1},{1,0},{2,3},{3,2},{4,5},{5,4},{6,7},{7,6},{8,9},{9,8},{10,11... | collective-permute-start | bytes 786440 | tf_op jit(solution)/shard_map/ppermute | solution.py:48
  77.0 1.8 collective-permute-start.8
  79.6 20.7 %collective-permute-start.9 = (bf16[64,2048]{1,0:T(8,128)(2,1)}, bf16[64,2048]{1,0:T(8,128)(2,1)}, u32[]{:S(2)}, u32[]{:S(2)}) collective-permute-start(bf16[64,2048]{1,0:T(8,128)(2,1)} %pad_maximum_fusion.4), channel_id=1, source_target_pairs={{0,2},{1,3},{2,4},{3,5},{4,6},{5,7},{6,0},{7,1},{8,10},{9,11},{10,... | collective-permute-start | bytes 786440 | tf_op jit(solution)/shard_map/ppermute | solution.py:56
  82.6 50.6 %all-to-all-start = ((bf16[64,1,4,2048]{3,2,1,0:T(4,128)(2,1)}), bf16[64,1,4,2048]{3,2,1,0:T(4,128)(2,1)}, u32[]{:S(2)}, u32[]{:S(2)}) async-start(bf16[64,1,4,2048]{3,2,1,0:T(4,128)(2,1)} %copy.71), calls=%async_computation | async-start | bytes 2097152 | tf_op jit(solution)/shard_map/all_to_all | solution.py:224
  95.8 20.0 %collective-permute-start.10 = (bf16[64,2048]{1,0:T(8,128)(2,1)}, bf16[64,2048]{1,0:T(8,128)(2,1)S(1)}, u32[]{:S(2)}, u32[]{:S(2)}) collective-permute-start(bf16[64,2048]{1,0:T(8,128)(2,1)} %pad_maximum_fusion.4), channel_id=1, source_target_pairs={{0,4},{1,5},{2,6},{3,7},{4,0},{5,1},{6,2},{7,3},{8,12},{9,13},{10,... | collective-permute-start | bytes 786440 | tf_op jit(solution)/shard_map/ppermute | solution.py:56
  98.7 21.3 %collective-permute-start.11 = (bf16[64,2048]{1,0:T(8,128)(2,1)}, bf16[64,2048]{1,0:T(8,128)(2,1)S(1)}, u32[]{:S(2)}, u32[]{:S(2)}) collective-permute-start(bf16[64,2048]{1,0:T(8,128)(2,1)} %pad_maximum_fusion.4), channel_id=1, source_target_pairs={{0,6},{1,7},{2,0},{3,1},{4,2},{5,3},{6,4},{7,5},{8,14},{9,15},{10,... | collective-permute-start | bytes 786440 | tf_op jit(solution)/shard_map/ppermute | solution.py:56
  129.6 29.3 %collective-permute-start.12 = (bf16[2,32,2048]{2,1,0:T(8,128)(2,1)}, bf16[2,32,2048]{2,1,0:T(8,128)(2,1)}, u32[]{:S(2)}, u32[]{:S(2)}) collective-permute-start(bf16[2,32,2048]{2,1,0:T(8,128)(2,1)} %pad_maximum_fusion.5), channel_id=1, source_target_pairs={{0,6},{1,7},{2,0},{3,1},{4,2},{5,3},{6,4},{7,5},{8,14},{9,15},{10,... | collective-permute-start | bytes 786440 | tf_op jit(solution)/shard_map/ppermute | solution.py:43
  132.1 26.9 %collective-permute-start.13 = (bf16[2,32,2048]{2,1,0:T(8,128)(2,1)}, bf16[2,32,2048]{2,1,0:T(8,128)(2,1)}, u32[]{:S(2)}, u32[]{:S(2)}) collective-permute-start(bf16[2,32,2048]{2,1,0:T(8,128)(2,1)} %pad_maximum_fusion.6), channel_id=1, source_target_pairs={{0,4},{1,5},{2,6},{3,7},{4,0},{5,1},{6,2},{7,3},{8,12},{9,13},{10,... | collective-permute-start | bytes 786440 | tf_op jit(solution)/shard_map/ppermute | solution.py:43
  144.1 14.9 %copy-start.13 = (f32[2,32,6]{1,0,2:T(2,128)S(1)}, f32[2,32,6]{1,0,2:T(2,128)}, u32[]{:S(2)}) copy-start(f32[2,32,6]{1,0,2:T(2,128)} %param.20) | copy-start | bytes 4612
  147.2 32.9 %copy-start.9 = (s32[32,6]{0,1:T(8,128)S(1)}, s32[32,6]{0,1:T(8,128)}, u32[]{:S(2)}) copy-start(s32[32,6]{0,1:T(8,128)} %copy-done.8) | copy-start | bytes 2308
  147.2 33.1 %all-to-all-start.1 = ((bf16[64,1,4,2048]{3,2,1,0:T(4,128)(2,1)}), bf16[64,1,4,2048]{3,2,1,0:T(4,128)(2,1)}, u32[]{:S(2)}, u32[]{:S(2)}) async-start(bf16[64,1,4,2048]{3,2,1,0:T(4,128)(2,1)} %copy.73), calls=%async_computation.1 | async-start | bytes 2097152 | tf_op jit(solution)/shard_map/all_to_all | solution.py:231
  157.5 19.9 %collective-permute-start.14 = (bf16[2,32,2048]{2,1,0:T(8,128)(2,1)S(1)}, bf16[2,32,2048]{2,1,0:T(8,128)(2,1)S(1)}, u32[]{:S(2)}, u32[]{:S(2)}) collective-permute-start(bf16[2,32,2048]{2,1,0:T(8,128)(2,1)S(1)} %pad_maximum_fusion.7), channel_id=1, source_target_pairs={{0,2},{1,3},{2,4},{3,5},{4,6},{5,7},{6,0},{7,1},{8,10},{9,11},{10,... | collective-permute-start | bytes 786440 | tf_op jit(solution)/shard_map/ppermute | solution.py:43
  179.3 3.7 %collective-permute-start.15 = (f32[32,2048]{1,0:T(8,128)}, f32[32,2048]{1,0:T(8,128)}, u32[]{:S(2)}, u32[]{:S(2)}) collective-permute-start(f32[32,2048]{1,0:T(8,128)} %convert_add_fusion.1), channel_id=1, source_target_pairs={{0,1},{1,0},{2,3},{3,2},{4,5},{5,4},{6,7},{7,6},{8,9},{9,8},{10,11... | collective-permute-start | bytes 786440 | tf_op jit(solution)/shard_map/ppermute | solution.py:48
  (10 other events, 19.5 us)

commit v7 on v4

--- a/solution.py
+++ b/solution.py
@@ -223,12 +223,15 @@
     combining = jnp.sum(jnp.where(matched, weight_rows[:, :, None], 0.0), axis=1).reshape(
         row_dev, n_wide, expert_dev, capacity
     )
-    routed = jnp.einsum(
-        "rsjk,sjkd->rd",
-        combining,
-        returned.astype(jnp.float32),
-        precision=lax.Precision.HIGHEST,
-    )
+    weight_high = combining.astype(jnp.bfloat16)
+    weight_low = (combining - weight_high.astype(jnp.float32)).astype(jnp.bfloat16)
+    both_parts = jnp.einsum(
+        "prsjk,sjkd->prd",
+        jnp.stack([weight_high, weight_low]),
+        returned,
+        preferred_element_type=jnp.float32,
+    )
+    routed = both_parts[0] + both_parts[1]
     finished = (own_residual.astype(jnp.float32) + shared_out + routed).astype(jnp.bfloat16)
     return finished[None]
 

time: 168 us -> 171 us (1.018)
  other arithmetic: 12.5 us -> 20.8 us
  starting transfers between devices: 66.5 us -> 60.7 us
  local copies, waits for them, and re-layouts: 30.7 us -> 32.8 us
    all_to_all x1, starting transfers between devices: 9.77 us -> 5.4 us  [shards(): lax.all_to_all(outgoing, ('tok', 'mdl'), split_axis=0, concat_axis=0, til...]
    ppermute x14, waiting for transfers between devices: 15.8 us -> 13.6 us  [summed_over(): lax.ppermute(piece_for(steps), axis, [(i, (i + steps) % count) for i in r...]
    broadcast_in_dim x0 -> x1, other arithmetic: none -> 2.07 us  [shards(): return finished[None]]
    unnamed x60 -> x54, local copies, waits for them, and re-layouts: 19.1 us -> 19.4 us
  transfers between devices with their start and end apart: 27 -> 27, of which waited for: 7 -> 7; matrix products, arithmetic and copies ran while one was open for 21% -> 26% of each run, Pallas kernels for 0% -> 0%
where the time goes in v7:
time: 171 us; the launch traced here: 170 us
  starting transfers between devices  60.7 us (35%)
  matrix products  34.8 us (20%)
  local copies, waits for them, and re-layouts  32.8 us (19%)
  other arithmetic  20.8 us (12%)
  waiting for transfers between devices  20.5 us (12%)
    unnamed x54, local copies, waits for them, and re-layouts  19.4 us
    ppermute x14, starting transfers between devices, summed_over(): lax.ppermute(piece_for(steps), axis, [(i, (i + steps) % count) for i in r...  18 us
    ppermute x4, starting transfers between devices, passed_along(): lax.ppermute(value, axis, [(source, source + steps) for source in range(i...  17.7 us
    ppermute x14, waiting for transfers between devices, summed_over(): lax.ppermute(piece_for(steps), axis, [(i, (i + steps) % count) for i in r...  13.6 us
    ppermute x7, starting transfers between devices, gathered_over(): lax.ppermute(block, axis, [(i, (i + steps) % count) for i in range(count)])  10.1 us
    all_to_all x1, starting transfers between devices, shards(): lax.all_to_all(produced, ('tok', 'mdl'), split_axis=0, concat_axis=0, til...  9.4 us
    ppermute x7, waiting for transfers between devices, gathered_over(): lax.ppermute(block, axis, [(i, (i + steps) % count) for i in range(count)])  6.88 us
    dot_general x1, matrix products, shards(): jnp.einsum('sjkf,jfd->sjkd', expert_act, w_expert_down, preferred_element...  5.9 us
  transfers between devices with their start and end apart: 27, of which 7 were waited for; matrix products, arithmetic and copies ran while one was open for 26% of the time, Pallas kernels for 0%

profile of v7, /device:TPU:1, one launch (start us, length us, event | category | flops | bytes accessed | tf_op | source)
XLA Modules:
  0.0 170.1 jit_solution(3407011696732426740)
XLA Ops:
  2.7 2.9 %fusion.62 = f32[256,576]{0,1:T(8,128)S(1)} fusion(bf16[2048,576]{0,1:T(8,128)(2,1)} %param.23, f32[2048]{0:T(1024)} %param.21, f32[256]{0:T(256)S(1)} %add_rsqrt_fusion.1, bf16[2,256,2048]{2,1,0:T(8,128)(2,1)} %param.17, s32[]{:T(128)S(6)} %select_n.97), kind=kOutput, calls=%fused_computation.48 | convolution fusion | flops 606076928 | bytes 4006916 | tf_op jit(solution)/shard_map/dot_general | solution.py:135
  10.1 6.2 %collective-permute-start = (bf16[256,576]{0,1:T(8,128)(2,1)}, bf16[256,576]{0,1:T(8,128)(2,1)}, u32[]{:S(2)}, u32[]{:S(2)}) collective-permute-start(bf16[256,576]{0,1:T(8,128)(2,1)} %pad_maximum_fusion), channel_id=1, source_target_pairs={{0,32},{8,40},{16,48},{24,56},{1,33},{9,41},{17,49},{25,57},{2,34}... | collective-permute-start | bytes 884744 | tf_op jit(solution)/shard_map/ppermute | solution.py:22
  16.3 6.4 %collective-permute-start.1 = (bf16[256,576]{0,1:T(8,128)(2,1)}, bf16[256,576]{0,1:T(8,128)(2,1)}, u32[]{:S(2)}, u32[]{:S(2)}) collective-permute-start(bf16[256,576]{0,1:T(8,128)(2,1)} %pad_maximum_fusion), channel_id=1, source_target_pairs={{0,24},{8,32},{16,40},{24,48},{32,56},{1,25},{9,33},{17,41},{25,49... | collective-permute-start | bytes 884744 | tf_op jit(solution)/shard_map/ppermute | solution.py:22
  24.7 3.1 %collective-permute-start.3 = (bf16[256,576]{0,1:T(8,128)(2,1)}, bf16[256,576]{0,1:T(8,128)(2,1)}, u32[]{:S(2)}, u32[]{:S(2)}) collective-permute-start(bf16[256,576]{0,1:T(8,128)(2,1)} %pad_maximum_fusion), channel_id=1, source_target_pairs={{0,8},{8,16},{16,24},{24,32},{32,40},{40,48},{48,56},{1,9},{9,17},... | collective-permute-start | bytes 884744 | tf_op jit(solution)/shard_map/ppermute | solution.py:22
  28.4 2.6 %copy.60 = bf16[2048,384]{0,1:T(8,128)(2,1)} copy(bf16[2048,384]{1,0:T(8,128)(2,1)} %param.22) | data formatting | bytes 3145728 | tf_op args[5]
  31.1 3.2 %fusion.60 = f32[256,2,192]{0,2,1:T(8,128)} fusion(bf16[2,192,2048]{2,1,0:T(8,128)(2,1)} %bitcast.180, f32[2048]{0:T(1024)S(1)} %copy-done.20, f32[256]{0:T(256)S(1)} %add_rsqrt_fusion.1, bf16[2,256,2048]{2,1,0:T(8,128)(2,1)} %param.17, s32[]{:T(128)S(6)} %select_n.97), kind=kOutput, calls=%fused_computation.47 | convolution fusion | flops 404750336 | bytes 3023876 | tf_op jit(solution)/shard_map/dot_general | solution.py:129
  51.6 4.2 %fusion.56 = bf16[256,2,128]{0,2,1:T(8,128)(2,1)} fusion(bf16[1280,2,256]{0,2,1:T(8,128)(2,1)} %bitcast.183, f32[2,256,1280]{2,1,0:T(8,128)} %copy-done.2, pred[256,1280]{1,0:T(8,128)(4,1)S(1)} %copy-done.6, f32[256,2]{0,1:T(2,128)S(1)} %bitcast.191), kind=kOutput, calls=%fused_computation.45 | convolution fusion | flops 170526464 | bytes 6686720 | tf_op jit(solution)/shard_map/hqk,khd->hqd/dot_general | solution.py:174
  63.5 2.1 %collective-permute-start.6 = (bf16[32,2048]{1,0:T(8,128)(2,1)}, bf16[32,2048]{1,0:T(8,128)(2,1)}, u32[]{:S(2)}, u32[]{:S(2)}) collective-permute-start(bf16[32,2048]{1,0:T(8,128)(2,1)} %get-tuple-element.23), channel_id=1, source_target_pairs={{0,3},{1,4},{2,5},{3,6},{4,7},{5,0},{6,1},{7,2},{8,11},{9,12},{10,... | collective-permute-start | bytes 393224 | tf_op jit(solution)/shard_map/ppermute | solution.py:37
  66.4 2.6 %collective-permute-start.8 = (bf16[32,2048]{1,0:T(8,128)(2,1)S(1)}, bf16[32,2048]{1,0:T(8,128)(2,1)}, u32[]{:S(2)}, u32[]{:S(2)}) collective-permute-start(bf16[32,2048]{1,0:T(8,128)(2,1)S(1)} %get-tuple-element.21), channel_id=1, source_target_pairs={{0,5},{1,6},{2,7},{3,0},{4,1},{5,2},{6,3},{7,4},{8,13},{9,14},{10,... | collective-permute-start | bytes 393224 | tf_op jit(solution)/shard_map/ppermute | solution.py:37
  71.6 5.8 %collective-permute-done.6 = bf16[32,2048]{1,0:T(8,128)(2,1)} collective-permute-done((bf16[32,2048]{1,0:T(8,128)(2,1)}, bf16[32,2048]{1,0:T(8,128)(2,1)}, u32[]{:S(2)}, u32[]{:S(2)}) %collective-permute-start.6) | collective-permute-done | bytes 131104 | tf_op jit(solution)/shard_map/ppermute | solution.py:37
  87.5 2.2 %collective-permute-start.15 = (bf16[32,2048]{1,0:T(8,128)(2,1)S(1)}, bf16[32,2048]{1,0:T(8,128)(2,1)S(1)}, u32[]{:S(2)}, u32[]{:S(2)}) collective-permute-start(bf16[32,2048]{1,0:T(8,128)(2,1)S(1)} %get-tuple-element.6), channel_id=1, source_target_pairs={{0,5},{1,6},{2,7},{3,0},{4,1},{5,2},{6,3},{7,4},{8,13},{9,14},{10,... | collective-permute-start | bytes 393224 | tf_op jit(solution)/shard_map/ppermute | solution.py:46
  92.8 5.4 %all-to-all-start = ((bf16[64,1,4,2048]{3,2,1,0:T(4,128)(2,1)}), bf16[64,1,4,2048]{3,2,1,0:T(4,128)(2,1)}, u32[]{:S(2)}, u32[]{:S(2)}) async-start(bf16[64,1,4,2048]{3,2,1,0:T(4,128)(2,1)} %copy.75), calls=%async_computation | async-start | bytes 2097152 | tf_op jit(solution)/shard_map/all_to_all | solution.py:214
  98.2 2.7 %collective-permute-start.16 = (bf16[32,2048]{1,0:T(8,128)(2,1)S(1)}, bf16[32,2048]{1,0:T(8,128)(2,1)S(1)}, u32[]{:S(2)}, u32[]{:S(2)}) collective-permute-start(bf16[32,2048]{1,0:T(8,128)(2,1)S(1)} %get-tuple-element.6), channel_id=1, source_target_pairs={{0,6},{1,7},{2,0},{3,1},{4,2},{5,3},{6,4},{7,5},{8,14},{9,15},{10,... | collective-permute-start | bytes 393224 | tf_op jit(solution)/shard_map/ppermute | solution.py:46
  108.4 5.3 %collective-permute-done.16 = bf16[32,2048]{1,0:T(8,128)(2,1)S(1)} collective-permute-done((bf16[32,2048]{1,0:T(8,128)(2,1)S(1)}, bf16[32,2048]{1,0:T(8,128)(2,1)S(1)}, u32[]{:S(2)}, u32[]{:S(2)}) %collective-permute-start.16) | collective-permute-done | bytes 131104 | tf_op jit(solution)/shard_map/ppermute | solution.py:46
  118.6 5.0 %fusion.35 = f32[64,1,4,768]{3,0,2,1:T(8,128)} fusion(bf16[1,2048,768]{2,1,0:T(8,128)(2,1)} %param.31, bf16[64,1,4,2048]{3,2,1,0:T(4,128)(2,1)} %all-to-all-done), kind=kOutput, calls=%fused_computation.38 | convolution fusion | flops 805306368 | bytes 4980736 | tf_op jit(solution)/shard_map/sjkd,jdf->sjkf/dot_general | solution.py:215
  123.7 5.9 %fusion.22 = bf16[64,1,4,2048]{3,0,2,1:T(8,128)(2,1)} fusion(bf16[1,768,2048]{2,1,0:T(8,128)(2,1)S(1)} %copy-done, bf16[1,2048,768]{2,1,0:T(8,128)(2,1)} %param.32, bf16[64,1,4,2048]{3,2,1,0:T(4,128)(2,1)} %all-to-all-done, f32[64,1,4,768]{3,0,2,1:T(8,128)} %fusion.35), kind=kOutput, calls=%fused_computation.25 | convolution fusion | flops 1612316672 | bytes 9175040 | tf_op jit(solution)/shard_map/sjkf,jfd->sjkd/dot_general | solution.py:218
  129.6 3.0 %copy.77 = bf16[64,1,4,2048]{3,2,1,0:T(4,128)(2,1)} copy(bf16[64,1,4,2048]{3,0,2,1:T(8,128)(2,1)} %fusion.22) | data formatting | bytes 2097152 | tf_op jit(solution)/shard_map/convert_element_type | solution.py:220
  132.6 9.4 %all-to-all-start.1 = ((bf16[64,1,4,2048]{3,2,1,0:T(4,128)(2,1)}), bf16[64,1,4,2048]{3,2,1,0:T(4,128)(2,1)}, u32[]{:S(2)}, u32[]{:S(2)}) async-start(bf16[64,1,4,2048]{3,2,1,0:T(4,128)(2,1)} %copy.77), calls=%async_computation.1 | async-start | bytes 2097152 | tf_op jit(solution)/shard_map/all_to_all | solution.py:221
  142.0 4.1 %convolution_convert_fusion.1 = bf16[256,2048]{1,0:T(8,128)(2,1)} fusion(bf16[256,2048]{1,0:T(8,128)(2,1)} %param.30, f32[256,256]{1,0:T(8,128)S(1)} %fusion.132, bf16[256,2048]{1,0:T(8,128)(2,1)} %constant_dynamic-update-slice_fusion.5, bf16[2048,256]{1,0:T(8,128)(2,1)} %param.29), kind=kOutput, calls=%fused_computation.20 | convolution fusion | flops 537788416 | bytes 4456448 | tf_op jit(solution)/shard_map/dot_general | solution.py:192
  146.1 2.1 %fusion.128 = (bf16[32,2048]{1,0:T(8,128)(2,1)S(1)}, bf16[32,2048]{1,0:T(8,128)(2,1)S(1)}, bf16[32,2048]{1,0:T(8,128)(2,1)}, bf16[32,2048]{1,0:T(8,128)(2,1)}, b...) fusion(bf16[256,2048]{1,0:T(8,128)(2,1)} %convolution_convert_fusion.1), kind=kLoop, calls=%fused_computation.171 | loop fusion | bytes 1835008 | tf_op jit(solution)/shard_map/slice | solution.py:32
  158.2 4.0 %collective-permute-done.19 = bf16[32,2048]{1,0:T(8,128)(2,1)S(1)} collective-permute-done((bf16[32,2048]{1,0:T(8,128)(2,1)S(1)}, bf16[32,2048]{1,0:T(8,128)(2,1)S(1)}, u32[]{:S(2)}, u32[]{:S(2)}) %collective-permute-start.19) | collective-permute-done | bytes 131104 | tf_op jit(solution)/shard_map/ppermute | solution.py:37
  162.8 2.5 %convolution_bitcast_fusion.1 = f32[2,32,2048]{2,1,0:T(8,128)S(1)} fusion(bf16[64,1,4,2048]{3,2,1,0:T(4,128)(2,1)} %all-to-all-done.1, bf16[1,32,64,1,4]{2,1,4,0,3:T(8,128)(2,1)} %get-tuple-element.7, bf16[1,32,64,1,4]{2,1,4,0,3:T(8,128)(2,1)} %get-tuple-element.8), kind=kOutput, calls=%fused_computation.26 | convolution fusion | flops 67125248 | bytes 1605632 | tf_op jit(solution)/shard_map/prsjk,sjkd->prd/dot_general | solution.py:228
  165.4 2.1 %collective-permute-done.21 = bf16[32,2048]{1,0:T(8,128)(2,1)} collective-permute-done((bf16[32,2048]{1,0:T(8,128)(2,1)}, bf16[32,2048]{1,0:T(8,128)(2,1)}, u32[]{:S(2)}, u32[]{:S(2)}) %collective-permute-start.21) | collective-permute-done | bytes 131104 | tf_op jit(solution)/shard_map/ppermute | solution.py:37
  168.0 2.1 %fusion.103 = bf16[1,32,2048]{2,1,0:T(8,128)(2,1)} fusion(f32[2,32,2048]{2,1,0:T(8,128)S(1)} %convolution_bitcast_fusion.1, bf16[32,2048]{1,0:T(8,128)(2,1)} %collective-permute-done.24, bf16[32,2048]{1,0:T(8,128)(2,1)} %collective-permute-done.23, bf16[32,2048]{1,0:T(8,128)(2,1)} %collective-permute-done.22, bf16[32,2048]{1,0:T(8,128)(2,1)} %collective-permute-done.21, ...), kind=kLoop, calls=%fused_computation.102 | loop fusion | flops 1310720 | bytes 1835008 | tf_op jit(solution)/shard_map/broadcast_in_dim | solution.py:236
  (148 shorter events, 74.7 us)
Async XLA Ops:
  10.1 32.8 %collective-permute-start = (bf16[256,576]{0,1:T(8,128)(2,1)}, bf16[256,576]{0,1:T(8,128)(2,1)}, u32[]{:S(2)}, u32[]{:S(2)}) collective-permute-start(bf16[256,576]{0,1:T(8,128)(2,1)} %pad_maximum_fusion), channel_id=1, source_target_pairs={{0,32},{8,40},{16,48},{24,56},{1,33},{9,41},{17,49},{25,57},{2,34}... | collective-permute-start | bytes 884744 | tf_op jit(solution)/shard_map/ppermute | solution.py:22
  16.3 27.6 %collective-permute-start.1 = (bf16[256,576]{0,1:T(8,128)(2,1)}, bf16[256,576]{0,1:T(8,128)(2,1)}, u32[]{:S(2)}, u32[]{:S(2)}) collective-permute-start(bf16[256,576]{0,1:T(8,128)(2,1)} %pad_maximum_fusion), channel_id=1, source_target_pairs={{0,24},{8,32},{16,40},{24,48},{32,56},{1,25},{9,33},{17,41},{25,49... | collective-permute-start | bytes 884744 | tf_op jit(solution)/shard_map/ppermute | solution.py:22
  22.7 22.2 %collective-permute-start.2 = (bf16[256,576]{0,1:T(8,128)(2,1)}, bf16[256,576]{0,1:T(8,128)(2,1)}, u32[]{:S(2)}, u32[]{:S(2)}) collective-permute-start(bf16[256,576]{0,1:T(8,128)(2,1)} %pad_maximum_fusion), channel_id=1, source_target_pairs={{0,16},{8,24},{16,32},{24,40},{32,48},{40,56},{1,17},{9,25},{17,33... | collective-permute-start | bytes 884744 | tf_op jit(solution)/shard_map/ppermute | solution.py:22
  24.7 21.2 %collective-permute-start.3 = (bf16[256,576]{0,1:T(8,128)(2,1)}, bf16[256,576]{0,1:T(8,128)(2,1)}, u32[]{:S(2)}, u32[]{:S(2)}) collective-permute-start(bf16[256,576]{0,1:T(8,128)(2,1)} %pad_maximum_fusion), channel_id=1, source_target_pairs={{0,8},{8,16},{16,24},{24,32},{32,40},{40,48},{48,56},{1,9},{9,17},... | collective-permute-start | bytes 884744 | tf_op jit(solution)/shard_map/ppermute | solution.py:22
  62.1 9.5 %collective-permute-start.5 = (bf16[32,2048]{1,0:T(8,128)(2,1)}, bf16[32,2048]{1,0:T(8,128)(2,1)}, u32[]{:S(2)}, u32[]{:S(2)}) collective-permute-start(bf16[32,2048]{1,0:T(8,128)(2,1)} %get-tuple-element.24), channel_id=1, source_target_pairs={{0,2},{1,3},{2,4},{3,5},{4,6},{5,7},{6,0},{7,1},{8,10},{9,11},{10,... | collective-permute-start | bytes 393224 | tf_op jit(solution)/shard_map/ppermute | solution.py:37
  63.5 13.9 %collective-permute-start.6 = (bf16[32,2048]{1,0:T(8,128)(2,1)}, bf16[32,2048]{1,0:T(8,128)(2,1)}, u32[]{:S(2)}, u32[]{:S(2)}) collective-permute-start(bf16[32,2048]{1,0:T(8,128)(2,1)} %get-tuple-element.23), channel_id=1, source_target_pairs={{0,3},{1,4},{2,5},{3,6},{4,7},{5,0},{6,1},{7,2},{8,11},{9,12},{10,... | collective-permute-start | bytes 393224 | tf_op jit(solution)/shard_map/ppermute | solution.py:37
  65.6 11.8 %collective-permute-start.7 = (bf16[32,2048]{1,0:T(8,128)(2,1)}, bf16[32,2048]{1,0:T(8,128)(2,1)}, u32[]{:S(2)}, u32[]{:S(2)}) collective-permute-start(bf16[32,2048]{1,0:T(8,128)(2,1)} %get-tuple-element.22), channel_id=1, source_target_pairs={{0,4},{1,5},{2,6},{3,7},{4,0},{5,1},{6,2},{7,3},{8,12},{9,13},{10,... | collective-permute-start | bytes 393224 | tf_op jit(solution)/shard_map/ppermute | solution.py:37
  66.4 11.0 %collective-permute-start.8 = (bf16[32,2048]{1,0:T(8,128)(2,1)S(1)}, bf16[32,2048]{1,0:T(8,128)(2,1)}, u32[]{:S(2)}, u32[]{:S(2)}) collective-permute-start(bf16[32,2048]{1,0:T(8,128)(2,1)S(1)} %get-tuple-element.21), channel_id=1, source_target_pairs={{0,5},{1,6},{2,7},{3,0},{4,1},{5,2},{6,3},{7,4},{8,13},{9,14},{10,... | collective-permute-start | bytes 393224 | tf_op jit(solution)/shard_map/ppermute | solution.py:37
  69.0 8.4 %collective-permute-start.9 = (bf16[32,2048]{1,0:T(8,128)(2,1)S(1)}, bf16[32,2048]{1,0:T(8,128)(2,1)}, u32[]{:S(2)}, u32[]{:S(2)}) collective-permute-start(bf16[32,2048]{1,0:T(8,128)(2,1)S(1)} %get-tuple-element.20), channel_id=1, source_target_pairs={{0,6},{1,7},{2,0},{3,1},{4,2},{5,3},{6,4},{7,5},{8,14},{9,15},{10,... | collective-permute-start | bytes 393224 | tf_op jit(solution)/shard_map/ppermute | solution.py:37
  80.5 17.7 %collective-permute-start.11 = (bf16[32,2048]{1,0:T(8,128)(2,1)S(1)}, bf16[32,2048]{1,0:T(8,128)(2,1)}, u32[]{:S(2)}, u32[]{:S(2)}) collective-permute-start(bf16[32,2048]{1,0:T(8,128)(2,1)S(1)} %get-tuple-element.6), channel_id=1, source_target_pairs={{0,1},{1,2},{2,3},{3,4},{4,5},{5,6},{6,7},{7,0},{8,9},{9,10},{10,1... | collective-permute-start | bytes 393224 | tf_op jit(solution)/shard_map/ppermute | solution.py:46
  83.4 19.0 %collective-permute-start.12 = (bf16[32,2048]{1,0:T(8,128)(2,1)S(1)}, bf16[32,2048]{1,0:T(8,128)(2,1)}, u32[]{:S(2)}, u32[]{:S(2)}) collective-permute-start(bf16[32,2048]{1,0:T(8,128)(2,1)S(1)} %get-tuple-element.6), channel_id=1, source_target_pairs={{0,2},{1,3},{2,4},{3,5},{4,6},{5,7},{6,0},{7,1},{8,10},{9,11},{10,... | collective-permute-start | bytes 393224 | tf_op jit(solution)/shard_map/ppermute | solution.py:46
  85.1 19.6 %collective-permute-start.13 = (bf16[32,2048]{1,0:T(8,128)(2,1)S(1)}, bf16[32,2048]{1,0:T(8,128)(2,1)}, u32[]{:S(2)}, u32[]{:S(2)}) collective-permute-start(bf16[32,2048]{1,0:T(8,128)(2,1)S(1)} %get-tuple-element.6), channel_id=1, source_target_pairs={{0,3},{1,4},{2,5},{3,6},{4,7},{5,0},{6,1},{7,2},{8,11},{9,12},{10,... | collective-permute-start | bytes 393224 | tf_op jit(solution)/shard_map/ppermute | solution.py:46
  86.9 19.3 %collective-permute-start.14 = (bf16[32,2048]{1,0:T(8,128)(2,1)S(1)}, bf16[32,2048]{1,0:T(8,128)(2,1)}, u32[]{:S(2)}, u32[]{:S(2)}) collective-permute-start(bf16[32,2048]{1,0:T(8,128)(2,1)S(1)} %get-tuple-element.6), channel_id=1, source_target_pairs={{0,4},{1,5},{2,6},{3,7},{4,0},{5,1},{6,2},{7,3},{8,12},{9,13},{10,... | collective-permute-start | bytes 393224 | tf_op jit(solution)/shard_map/ppermute | solution.py:46
  87.5 20.3 %collective-permute-start.15 = (bf16[32,2048]{1,0:T(8,128)(2,1)S(1)}, bf16[32,2048]{1,0:T(8,128)(2,1)S(1)}, u32[]{:S(2)}, u32[]{:S(2)}) collective-permute-start(bf16[32,2048]{1,0:T(8,128)(2,1)S(1)} %get-tuple-element.6), channel_id=1, source_target_pairs={{0,5},{1,6},{2,7},{3,0},{4,1},{5,2},{6,3},{7,4},{8,13},{9,14},{10,... | collective-permute-start | bytes 393224 | tf_op jit(solution)/shard_map/ppermute | solution.py:46
  92.8 25.9 %all-to-all-start = ((bf16[64,1,4,2048]{3,2,1,0:T(4,128)(2,1)}), bf16[64,1,4,2048]{3,2,1,0:T(4,128)(2,1)}, u32[]{:S(2)}, u32[]{:S(2)}) async-start(bf16[64,1,4,2048]{3,2,1,0:T(4,128)(2,1)} %copy.75), calls=%async_computation | async-start | bytes 2097152 | tf_op jit(solution)/shard_map/all_to_all | solution.py:214
  98.2 15.6 %collective-permute-start.16 = (bf16[32,2048]{1,0:T(8,128)(2,1)S(1)}, bf16[32,2048]{1,0:T(8,128)(2,1)S(1)}, u32[]{:S(2)}, u32[]{:S(2)}) collective-permute-start(bf16[32,2048]{1,0:T(8,128)(2,1)S(1)} %get-tuple-element.6), channel_id=1, source_target_pairs={{0,6},{1,7},{2,0},{3,1},{4,2},{5,3},{6,4},{7,5},{8,14},{9,15},{10,... | collective-permute-start | bytes 393224 | tf_op jit(solution)/shard_map/ppermute | solution.py:46
  102.4 13.6 %collective-permute-start.17 = (bf16[32,2048]{1,0:T(8,128)(2,1)S(1)}, bf16[32,2048]{1,0:T(8,128)(2,1)S(1)}, u32[]{:S(2)}, u32[]{:S(2)}) collective-permute-start(bf16[32,2048]{1,0:T(8,128)(2,1)S(1)} %get-tuple-element.6), channel_id=1, source_target_pairs={{0,7},{1,0},{2,1},{3,2},{4,3},{5,4},{6,5},{7,6},{8,15},{9,8},{10,9... | collective-permute-start | bytes 393224 | tf_op jit(solution)/shard_map/ppermute | solution.py:46
  132.6 30.3 %all-to-all-start.1 = ((bf16[64,1,4,2048]{3,2,1,0:T(4,128)(2,1)}), bf16[64,1,4,2048]{3,2,1,0:T(4,128)(2,1)}, u32[]{:S(2)}, u32[]{:S(2)}) async-start(bf16[64,1,4,2048]{3,2,1,0:T(4,128)(2,1)} %copy.77), calls=%async_computation.1 | async-start | bytes 2097152 | tf_op jit(solution)/shard_map/all_to_all | solution.py:221
  148.2 8.5 %collective-permute-start.18 = (bf16[32,2048]{1,0:T(8,128)(2,1)S(1)}, bf16[32,2048]{1,0:T(8,128)(2,1)S(1)}, u32[]{:S(2)}, u32[]{:S(2)}) collective-permute-start(bf16[32,2048]{1,0:T(8,128)(2,1)S(1)} %get-tuple-element.11), channel_id=1, source_target_pairs={{0,1},{1,2},{2,3},{3,4},{4,5},{5,6},{6,7},{7,0},{8,9},{9,10},{10,1... | collective-permute-start | bytes 393224 | tf_op jit(solution)/shard_map/ppermute | solution.py:37
  149.8 12.4 %collective-permute-start.19 = (bf16[32,2048]{1,0:T(8,128)(2,1)S(1)}, bf16[32,2048]{1,0:T(8,128)(2,1)S(1)}, u32[]{:S(2)}, u32[]{:S(2)}) collective-permute-start(bf16[32,2048]{1,0:T(8,128)(2,1)S(1)} %get-tuple-element.17), channel_id=1, source_target_pairs={{0,2},{1,3},{2,4},{3,5},{4,6},{5,7},{6,0},{7,1},{8,10},{9,11},{10,... | collective-permute-start | bytes 393224 | tf_op jit(solution)/shard_map/ppermute | solution.py:37
  152.5 12.8 %collective-permute-start.20 = (bf16[32,2048]{1,0:T(8,128)(2,1)}, bf16[32,2048]{1,0:T(8,128)(2,1)}, u32[]{:S(2)}, u32[]{:S(2)}) collective-permute-start(bf16[32,2048]{1,0:T(8,128)(2,1)} %get-tuple-element.16), channel_id=1, source_target_pairs={{0,3},{1,4},{2,5},{3,6},{4,7},{5,0},{6,1},{7,2},{8,11},{9,12},{10,... | collective-permute-start | bytes 393224 | tf_op jit(solution)/shard_map/ppermute | solution.py:37
  154.1 13.3 %collective-permute-start.21 = (bf16[32,2048]{1,0:T(8,128)(2,1)}, bf16[32,2048]{1,0:T(8,128)(2,1)}, u32[]{:S(2)}, u32[]{:S(2)}) collective-permute-start(bf16[32,2048]{1,0:T(8,128)(2,1)} %get-tuple-element.15), channel_id=1, source_target_pairs={{0,4},{1,5},{2,6},{3,7},{4,0},{5,1},{6,2},{7,3},{8,12},{9,13},{10,... | collective-permute-start | bytes 393224 | tf_op jit(solution)/shard_map/ppermute | solution.py:37
  154.7 13.3 %collective-permute-start.22 = (bf16[32,2048]{1,0:T(8,128)(2,1)}, bf16[32,2048]{1,0:T(8,128)(2,1)}, u32[]{:S(2)}, u32[]{:S(2)}) collective-permute-start(bf16[32,2048]{1,0:T(8,128)(2,1)} %get-tuple-element.14), channel_id=1, source_target_pairs={{0,5},{1,6},{2,7},{3,0},{4,1},{5,2},{6,3},{7,4},{8,13},{9,14},{10,... | collective-permute-start | bytes 393224 | tf_op jit(solution)/shard_map/ppermute | solution.py:37
  156.6 11.4 %collective-permute-start.23 = (bf16[32,2048]{1,0:T(8,128)(2,1)}, bf16[32,2048]{1,0:T(8,128)(2,1)}, u32[]{:S(2)}, u32[]{:S(2)}) collective-permute-start(bf16[32,2048]{1,0:T(8,128)(2,1)} %get-tuple-element.13), channel_id=1, source_target_pairs={{0,6},{1,7},{2,0},{3,1},{4,2},{5,3},{6,4},{7,5},{8,14},{9,15},{10,... | collective-permute-start | bytes 393224 | tf_op jit(solution)/shard_map/ppermute | solution.py:37
  (24 other events, 250.0 us)

commit v8 on v4

--- a/solution.py
+++ b/solution.py
@@ -139,8 +139,22 @@
     reach = LONGEST_SEGMENT // tok_dev
     kv_own = jnp.concatenate([latent, key_rope], axis=-1)
     kv_parts = [kv_own]
-    for steps in range(1, min(reach, n_tok - 1) + 1):
-        kv_parts.insert(0, passed_along(kv_own, "tok", steps))
+    if n_tok == 2 * reach:
+        across = passed_along(kv_own, "tok", reach)
+        place = tok_rank % reach
+        for steps in range(1, reach):
+            wraps = place + steps >= reach
+            sent = jnp.where(wraps, across, kv_own)
+            pairs = [
+                (half * reach + i, half * reach + (i + steps) % reach)
+                for half in range(2)
+                for i in range(reach)
+            ]
+            kv_parts.insert(0, lax.ppermute(sent, "tok", pairs))
+        kv_parts.insert(0, across)
+    else:
+        for steps in range(1, min(reach, n_tok - 1) + 1):
+            kv_parts.insert(0, passed_along(kv_own, "tok", steps))
     kv_rows = jnp.concatenate(kv_parts, axis=0)
     key_count = kv_rows.shape[0]
     key_start = query_start + tok_dev - key_count

time: 168 us -> 175 us (1.042)
  starting transfers between devices: 66.5 us -> 55.3 us
  waiting for transfers between devices: 21.8 us -> 32.3 us
  other arithmetic: 12.5 us -> 17.3 us
  matrix products: 34.8 us -> 37.3 us
    ppermute x4 -> x1, starting transfers between devices: 17.7 us -> 6.18 us  [passed_along(): lax.ppermute(value, axis, [(source, source + steps) for source in range(i...]
    ppermute x0 -> x3, waiting for transfers between devices: none -> 10.5 us  [shards(): kv_parts.insert(0, lax.ppermute(sent, 'tok', pairs))]
    ppermute x0 -> x3, starting transfers between devices: none -> 4.6 us  [shards(): kv_parts.insert(0, lax.ppermute(sent, 'tok', pairs))]
    all_to_all x1, starting transfers between devices: 9.77 us -> 6.06 us  [shards(): lax.all_to_all(outgoing, ('tok', 'mdl'), split_axis=0, concat_axis=0, til...]
    select_n x0 -> x1, other arithmetic: none -> 2.14 us  [shards(): sent = jnp.where(wraps, across, kv_own)]
    unnamed x60 -> x45, local copies, waits for them, and re-layouts: 19.1 us -> 19.6 us
  transfers between devices with their start and end apart: 27 -> 27, of which waited for: 7 -> 9; matrix products, arithmetic and copies ran while one was open for 21% -> 21% of each run, Pallas kernels for 0% -> 0%
where the time goes in v8:
time: 175 us; the launch traced here: 174 us
  starting transfers between devices  55.3 us (32%)
  matrix products  37.3 us (21%)
  waiting for transfers between devices  32.3 us (18%)
  local copies, waits for them, and re-layouts  31.2 us (18%)
  other arithmetic  17.3 us (10%)
    unnamed x45, local copies, waits for them, and re-layouts  19.6 us
    ppermute x14, starting transfers between devices, summed_over(): lax.ppermute(piece_for(steps), axis, [(i, (i + steps) % count) for i in r...  19.5 us
    ppermute x14, waiting for transfers between devices, summed_over(): lax.ppermute(piece_for(steps), axis, [(i, (i + steps) % count) for i in r...  15.8 us
    ppermute x3, waiting for transfers between devices, shards(): kv_parts.insert(0, lax.ppermute(sent, 'tok', pairs))  10.5 us
    ppermute x7, starting transfers between devices, gathered_over(): lax.ppermute(block, axis, [(i, (i + steps) % count) for i in range(count)])  9.59 us
    all_to_all x1, starting transfers between devices, shards(): lax.all_to_all(produced, ('tok', 'mdl'), split_axis=0, concat_axis=0, til...  9.39 us
    ppermute x1, starting transfers between devices, passed_along(): lax.ppermute(value, axis, [(source, source + steps) for source in range(i...  6.18 us
    all_to_all x1, starting transfers between devices, shards(): lax.all_to_all(outgoing, ('tok', 'mdl'), split_axis=0, concat_axis=0, til...  6.06 us
  transfers between devices with their start and end apart: 27, of which 9 were waited for; matrix products, arithmetic and copies ran while one was open for 21% of the time, Pallas kernels for 0%

profile of v8, /device:TPU:1, one launch (start us, length us, event | category | flops | bytes accessed | tf_op | source)
XLA Modules:
  0.0 174.0 jit_solution(16876712535311770615)
XLA Ops:
  2.7 2.9 %fusion.62 = f32[256,576]{0,1:T(8,128)S(1)} fusion(bf16[2048,576]{0,1:T(8,128)(2,1)} %param.23, f32[2048]{0:T(1024)} %param.21, f32[256]{0:T(256)S(1)} %add_rsqrt_fusion.1, bf16[2,256,2048]{2,1,0:T(8,128)(2,1)} %param.17, s32[]{:T(128)S(6)} %select_n.121), kind=kOutput, calls=%fused_computation.48 | convolution fusion | flops 606076928 | bytes 4006916 | tf_op jit(solution)/shard_map/dot_general | solution.py:135
  10.1 6.2 %collective-permute-start = (bf16[256,576]{0,1:T(8,128)(2,1)}, bf16[256,576]{0,1:T(8,128)(2,1)}, u32[]{:S(2)}, u32[]{:S(2)}) collective-permute-start(bf16[256,576]{0,1:T(8,128)(2,1)} %pad_maximum_fusion), channel_id=1, source_target_pairs={{0,32},{8,40},{16,48},{24,56},{1,33},{9,41},{17,49},{25,57},{2,34}... | collective-permute-start | bytes 884744 | tf_op jit(solution)/shard_map/ppermute | solution.py:22
  16.3 2.6 %copy.58 = bf16[2048,384]{0,1:T(8,128)(2,1)} copy(bf16[2048,384]{1,0:T(8,128)(2,1)} %param.22) | data formatting | bytes 3145728 | tf_op args[5]
  18.9 3.2 %fusion.60 = f32[256,2,192]{0,2,1:T(8,128)} fusion(bf16[2,192,2048]{2,1,0:T(8,128)(2,1)} %bitcast.177, f32[2048]{0:T(1024)S(1)} %copy-done.16, f32[256]{0:T(256)S(1)} %add_rsqrt_fusion.1, bf16[2,256,2048]{2,1,0:T(8,128)(2,1)} %param.17, s32[]{:T(128)S(6)} %select_n.121), kind=kOutput, calls=%fused_computation.47 | convolution fusion | flops 404750336 | bytes 3023876 | tf_op jit(solution)/shard_map/dot_general | solution.py:129
  25.8 2.1 %broadcast_select_fusion = (bf16[256,576]{0,1:T(8,128)(2,1)}, bf16[256,576]{0,1:T(8,128)(2,1)}, bf16[256,576]{0,1:T(8,128)(2,1)}, bf16[1280,576]{0,1:T(8,128)(2,1)}) fusion(bf16[256,576]{0,1:T(8,128)(2,1)} %collective-permute-done, pred[]{:T(512)S(6)} %ge.24, bf16[256,32]{0,1:T(8,128)(2,1)S(1)} %get-tuple-element.33, ...), kind=kLoop, calls=%fused_computation.70 | loop fusion | flops 1327103 | bytes 1769475 | tf_op jit(solution)/shard_map/jit(_where)/select_n | solution.py:147
  27.9 3.8 %collective-permute-start.1 = (bf16[256,576]{0,1:T(8,128)(2,1)}, bf16[256,576]{0,1:T(8,128)(2,1)}, u32[]{:S(2)}, u32[]{:S(2)}) collective-permute-start(bf16[256,576]{0,1:T(8,128)(2,1)} %get-tuple-element.27), channel_id=1, source_target_pairs={{0,24},{8,0},{16,8},{24,16},{32,56},{40,32},{48,40},{56,48},{1,25}... | collective-permute-start | bytes 884744 | tf_op jit(solution)/shard_map/ppermute | solution.py:153
  34.9 8.7 %collective-permute-done.1 = bf16[256,576]{0,1:T(8,128)(2,1)} collective-permute-done((bf16[256,576]{0,1:T(8,128)(2,1)}, bf16[256,576]{0,1:T(8,128)(2,1)}, u32[]{:S(2)}, u32[]{:S(2)}) %collective-permute-start.1) | collective-permute-done | bytes 294944 | tf_op jit(solution)/shard_map/ppermute | solution.py:153
  51.3 2.2 %convolution_convert_fusion = bf16[1280,512]{0,1:T(8,128)(2,1)S(1)} fusion(bf16[512,512]{1,0:T(8,128)(2,1)S(1)} %copy-done.15, bf16[1280,576]{0,1:T(8,128)(2,1)} %constant_dynamic-update-slice_fusion), kind=kOutput, calls=%fused_computation.15 | convolution fusion | flops 671744000 | bytes 3145728 | tf_op jit(solution)/shard_map/dot_general | solution.py:162
  57.9 3.7 %fusion.56 = bf16[256,2,128]{0,2,1:T(8,128)(2,1)S(1)} fusion(bf16[1280,2,256]{0,2,1:T(8,128)(2,1)} %bitcast.180, f32[2,256,1280]{2,1,0:T(8,128)} %copy-done.2, pred[256,1280]{1,0:T(8,128)(4,1)} %and_and_fusion, f32[256,2]{0,1:T(2,128)S(1)} %bitcast.188), kind=kOutput, calls=%fused_computation.45 | convolution fusion | flops 170526464 | bytes 6686720 | tf_op jit(solution)/shard_map/hqk,khd->hqd/dot_general | solution.py:188
  72.4 2.6 %collective-permute-start.8 = (bf16[32,2048]{1,0:T(8,128)(2,1)}, bf16[32,2048]{1,0:T(8,128)(2,1)S(1)}, u32[]{:S(2)}, u32[]{:S(2)}) collective-permute-start(bf16[32,2048]{1,0:T(8,128)(2,1)} %get-tuple-element.19), channel_id=1, source_target_pairs={{0,5},{1,6},{2,7},{3,0},{4,1},{5,2},{6,3},{7,4},{8,13},{9,14},{10,... | collective-permute-start | bytes 393224 | tf_op jit(solution)/shard_map/ppermute | solution.py:37
  75.0 7.3 %collective-permute-done.5 = bf16[32,2048]{1,0:T(8,128)(2,1)S(1)} collective-permute-done((bf16[32,2048]{1,0:T(8,128)(2,1)}, bf16[32,2048]{1,0:T(8,128)(2,1)S(1)}, u32[]{:S(2)}, u32[]{:S(2)}) %collective-permute-start.5) | collective-permute-done | bytes 131104 | tf_op jit(solution)/shard_map/ppermute | solution.py:37
  89.8 2.2 %collective-permute-start.15 = (bf16[32,2048]{1,0:T(8,128)(2,1)S(1)}, bf16[32,2048]{1,0:T(8,128)(2,1)}, u32[]{:S(2)}, u32[]{:S(2)}) collective-permute-start(bf16[32,2048]{1,0:T(8,128)(2,1)S(1)} %get-tuple-element.6), channel_id=1, source_target_pairs={{0,5},{1,6},{2,7},{3,0},{4,1},{5,2},{6,3},{7,4},{8,13},{9,14},{10,... | collective-permute-start | bytes 393224 | tf_op jit(solution)/shard_map/ppermute | solution.py:46
  94.2 6.1 %all-to-all-start = ((bf16[64,1,4,2048]{3,2,1,0:T(4,128)(2,1)}), bf16[64,1,4,2048]{3,2,1,0:T(4,128)(2,1)}, u32[]{:S(2)}, u32[]{:S(2)}) async-start(bf16[64,1,4,2048]{3,2,1,0:T(4,128)(2,1)} %copy.71), calls=%async_computation | async-start | bytes 2097152 | tf_op jit(solution)/shard_map/all_to_all | solution.py:228
  100.3 2.7 %collective-permute-start.16 = (bf16[32,2048]{1,0:T(8,128)(2,1)S(1)}, bf16[32,2048]{1,0:T(8,128)(2,1)S(1)}, u32[]{:S(2)}, u32[]{:S(2)}) collective-permute-start(bf16[32,2048]{1,0:T(8,128)(2,1)S(1)} %get-tuple-element.6), channel_id=1, source_target_pairs={{0,6},{1,7},{2,0},{3,1},{4,2},{5,3},{6,4},{7,5},{8,14},{9,15},{10,... | collective-permute-start | bytes 393224 | tf_op jit(solution)/shard_map/ppermute | solution.py:46
  111.4 4.4 %collective-permute-done.16 = bf16[32,2048]{1,0:T(8,128)(2,1)S(1)} collective-permute-done((bf16[32,2048]{1,0:T(8,128)(2,1)S(1)}, bf16[32,2048]{1,0:T(8,128)(2,1)S(1)}, u32[]{:S(2)}, u32[]{:S(2)}) %collective-permute-start.16) | collective-permute-done | bytes 131104 | tf_op jit(solution)/shard_map/ppermute | solution.py:46
  120.7 5.0 %fusion.35 = f32[64,1,4,768]{3,0,2,1:T(8,128)} fusion(bf16[1,2048,768]{2,1,0:T(8,128)(2,1)} %param.31, bf16[64,1,4,2048]{3,2,1,0:T(4,128)(2,1)} %all-to-all-done), kind=kOutput, calls=%fused_computation.38 | convolution fusion | flops 805306368 | bytes 4980736 | tf_op jit(solution)/shard_map/sjkd,jdf->sjkf/dot_general | solution.py:229
  125.7 5.9 %fusion.22 = bf16[64,1,4,2048]{3,0,2,1:T(8,128)(2,1)} fusion(bf16[1,768,2048]{2,1,0:T(8,128)(2,1)S(1)} %copy-done, bf16[1,2048,768]{2,1,0:T(8,128)(2,1)} %param.32, bf16[64,1,4,2048]{3,2,1,0:T(4,128)(2,1)} %all-to-all-done, f32[64,1,4,768]{3,0,2,1:T(8,128)} %fusion.35), kind=kOutput, calls=%fused_computation.25 | convolution fusion | flops 1612316672 | bytes 9175040 | tf_op jit(solution)/shard_map/sjkf,jfd->sjkd/dot_general | solution.py:232
  131.6 3.0 %copy.73 = bf16[64,1,4,2048]{3,2,1,0:T(4,128)(2,1)} copy(bf16[64,1,4,2048]{3,0,2,1:T(8,128)(2,1)} %fusion.22) | data formatting | bytes 2097152 | tf_op jit(solution)/shard_map/convert_element_type | solution.py:234
  134.7 9.4 %all-to-all-start.1 = ((bf16[64,1,4,2048]{3,2,1,0:T(4,128)(2,1)}), bf16[64,1,4,2048]{3,2,1,0:T(4,128)(2,1)}, u32[]{:S(2)}, u32[]{:S(2)}) async-start(bf16[64,1,4,2048]{3,2,1,0:T(4,128)(2,1)} %copy.73), calls=%async_computation.1 | async-start | bytes 2097152 | tf_op jit(solution)/shard_map/all_to_all | solution.py:235
  144.1 4.1 %convolution_convert_fusion.1 = bf16[256,2048]{1,0:T(8,128)(2,1)} fusion(bf16[256,2048]{1,0:T(8,128)(2,1)} %param.30, f32[256,256]{1,0:T(8,128)S(1)} %fusion.137, bf16[256,2048]{1,0:T(8,128)(2,1)} %constant_dynamic-update-slice_fusion.5, bf16[2048,256]{1,0:T(8,128)(2,1)} %param.29), kind=kOutput, calls=%fused_computation.20 | convolution fusion | flops 537788416 | bytes 4456448 | tf_op jit(solution)/shard_map/dot_general | solution.py:206
  157.2 3.1 %collective-permute-start.23 = (bf16[32,2048]{1,0:T(8,128)(2,1)}, bf16[32,2048]{1,0:T(8,128)(2,1)}, u32[]{:S(2)}, u32[]{:S(2)}) collective-permute-start(bf16[32,2048]{1,0:T(8,128)(2,1)} %get-tuple-element.11), channel_id=1, source_target_pairs={{0,6},{1,7},{2,0},{3,1},{4,2},{5,3},{6,4},{7,5},{8,14},{9,15},{10,... | collective-permute-start | bytes 393224 | tf_op jit(solution)/shard_map/ppermute | solution.py:37
  160.3 4.0 %collective-permute-done.19 = bf16[32,2048]{1,0:T(8,128)(2,1)S(1)} collective-permute-done((bf16[32,2048]{1,0:T(8,128)(2,1)S(1)}, bf16[32,2048]{1,0:T(8,128)(2,1)S(1)}, u32[]{:S(2)}, u32[]{:S(2)}) %collective-permute-start.19) | collective-permute-done | bytes 131104 | tf_op jit(solution)/shard_map/ppermute | solution.py:37
  166.5 3.0 %collective-permute-done.21 = bf16[32,2048]{1,0:T(8,128)(2,1)} collective-permute-done((bf16[32,2048]{1,0:T(8,128)(2,1)}, bf16[32,2048]{1,0:T(8,128)(2,1)}, u32[]{:S(2)}, u32[]{:S(2)}) %collective-permute-start.21) | collective-permute-done | bytes 131104 | tf_op jit(solution)/shard_map/ppermute | solution.py:37
  170.1 3.9 %fusion.106 = bf16[1,32,2048]{2,1,0:T(8,128)(2,1)} fusion(bf16[64,1,4,2048]{3,2,1,0:T(4,128)(2,1)} %all-to-all-done.1, f32[32,64,4]{0,2,1:T(4,128)S(1)} %bitcast.178, bf16[32,2048]{1,0:T(8,128)(2,1)} %collective-permute-done.24, bf16[32,2048]{1,0:T(8,128)(2,1)} %collective-permute-done.23, bf16[32,2048]{1,0:T(8,128)(2,1)} %collective-permute-done.22, ...), kind=kOutput, calls=%fused_computation.96 | convolution fusion | flops 202571776 | bytes 2392064 | tf_op jit(solution)/shard_map/rsjk,sjkd->rd/dot_general | solution.py:240
  (138 shorter events, 71.4 us)
Async XLA Ops:
  10.1 15.7 %collective-permute-start = (bf16[256,576]{0,1:T(8,128)(2,1)}, bf16[256,576]{0,1:T(8,128)(2,1)}, u32[]{:S(2)}, u32[]{:S(2)}) collective-permute-start(bf16[256,576]{0,1:T(8,128)(2,1)} %pad_maximum_fusion), channel_id=1, source_target_pairs={{0,32},{8,40},{16,48},{24,56},{1,33},{9,41},{17,49},{25,57},{2,34}... | collective-permute-start | bytes 884744 | tf_op jit(solution)/shard_map/ppermute | solution.py:22
  27.9 15.7 %collective-permute-start.1 = (bf16[256,576]{0,1:T(8,128)(2,1)}, bf16[256,576]{0,1:T(8,128)(2,1)}, u32[]{:S(2)}, u32[]{:S(2)}) collective-permute-start(bf16[256,576]{0,1:T(8,128)(2,1)} %get-tuple-element.27), channel_id=1, source_target_pairs={{0,24},{8,0},{16,8},{24,16},{32,56},{40,32},{48,40},{56,48},{1,25}... | collective-permute-start | bytes 884744 | tf_op jit(solution)/shard_map/ppermute | solution.py:153
  31.7 13.6 %collective-permute-start.2 = (bf16[256,576]{0,1:T(8,128)(2,1)}, bf16[256,576]{0,1:T(8,128)(2,1)}, u32[]{:S(2)}, u32[]{:S(2)}) collective-permute-start(bf16[256,576]{0,1:T(8,128)(2,1)} %get-tuple-element.26), channel_id=1, source_target_pairs={{0,16},{8,24},{16,0},{24,8},{32,48},{40,56},{48,32},{56,40},{1,17}... | collective-permute-start | bytes 884744 | tf_op jit(solution)/shard_map/ppermute | solution.py:153
  33.7 15.1 %collective-permute-start.3 = (bf16[256,576]{0,1:T(8,128)(2,1)}, bf16[256,576]{0,1:T(8,128)(2,1)}, u32[]{:S(2)}, u32[]{:S(2)}) collective-permute-start(bf16[256,576]{0,1:T(8,128)(2,1)} %get-tuple-element.25), channel_id=1, source_target_pairs={{0,8},{8,16},{16,24},{24,0},{32,40},{40,48},{48,56},{56,32},{1,9},... | collective-permute-start | bytes 884744 | tf_op jit(solution)/shard_map/ppermute | solution.py:153
  65.7 9.4 %collective-permute-start.4 = (bf16[32,2048]{1,0:T(8,128)(2,1)}, bf16[32,2048]{1,0:T(8,128)(2,1)}, u32[]{:S(2)}, u32[]{:S(2)}) collective-permute-start(bf16[32,2048]{1,0:T(8,128)(2,1)} %get-tuple-element.16), channel_id=1, source_target_pairs={{0,1},{1,2},{2,3},{3,4},{4,5},{5,6},{6,7},{7,0},{8,9},{9,10},{10,1... | collective-permute-start | bytes 393224 | tf_op jit(solution)/shard_map/ppermute | solution.py:37
  67.2 15.1 %collective-permute-start.5 = (bf16[32,2048]{1,0:T(8,128)(2,1)}, bf16[32,2048]{1,0:T(8,128)(2,1)S(1)}, u32[]{:S(2)}, u32[]{:S(2)}) collective-permute-start(bf16[32,2048]{1,0:T(8,128)(2,1)} %get-tuple-element.22), channel_id=1, source_target_pairs={{0,2},{1,3},{2,4},{3,5},{4,6},{5,7},{6,0},{7,1},{8,10},{9,11},{10,... | collective-permute-start | bytes 393224 | tf_op jit(solution)/shard_map/ppermute | solution.py:37
  68.6 14.7 %collective-permute-start.6 = (bf16[32,2048]{1,0:T(8,128)(2,1)}, bf16[32,2048]{1,0:T(8,128)(2,1)S(1)}, u32[]{:S(2)}, u32[]{:S(2)}) collective-permute-start(bf16[32,2048]{1,0:T(8,128)(2,1)} %get-tuple-element.21), channel_id=1, source_target_pairs={{0,3},{1,4},{2,5},{3,6},{4,7},{5,0},{6,1},{7,2},{8,11},{9,12},{10,... | collective-permute-start | bytes 393224 | tf_op jit(solution)/shard_map/ppermute | solution.py:37
  70.6 12.7 %collective-permute-start.7 = (bf16[32,2048]{1,0:T(8,128)(2,1)}, bf16[32,2048]{1,0:T(8,128)(2,1)S(1)}, u32[]{:S(2)}, u32[]{:S(2)}) collective-permute-start(bf16[32,2048]{1,0:T(8,128)(2,1)} %get-tuple-element.20), channel_id=1, source_target_pairs={{0,4},{1,5},{2,6},{3,7},{4,0},{5,1},{6,2},{7,3},{8,12},{9,13},{10,... | collective-permute-start | bytes 393224 | tf_op jit(solution)/shard_map/ppermute | solution.py:37
  72.4 10.9 %collective-permute-start.8 = (bf16[32,2048]{1,0:T(8,128)(2,1)}, bf16[32,2048]{1,0:T(8,128)(2,1)S(1)}, u32[]{:S(2)}, u32[]{:S(2)}) collective-permute-start(bf16[32,2048]{1,0:T(8,128)(2,1)} %get-tuple-element.19), channel_id=1, source_target_pairs={{0,5},{1,6},{2,7},{3,0},{4,1},{5,2},{6,3},{7,4},{8,13},{9,14},{10,... | collective-permute-start | bytes 393224 | tf_op jit(solution)/shard_map/ppermute | solution.py:37
  75.0 8.2 %collective-permute-start.9 = (bf16[32,2048]{1,0:T(8,128)(2,1)S(1)}, bf16[32,2048]{1,0:T(8,128)(2,1)S(1)}, u32[]{:S(2)}, u32[]{:S(2)}) collective-permute-start(bf16[32,2048]{1,0:T(8,128)(2,1)S(1)} %get-tuple-element.18), channel_id=1, source_target_pairs={{0,6},{1,7},{2,0},{3,1},{4,2},{5,3},{6,4},{7,5},{8,14},{9,15},{10,... | collective-permute-start | bytes 393224 | tf_op jit(solution)/shard_map/ppermute | solution.py:37
  85.5 14.8 %collective-permute-start.11 = (bf16[32,2048]{1,0:T(8,128)(2,1)S(1)}, bf16[32,2048]{1,0:T(8,128)(2,1)}, u32[]{:S(2)}, u32[]{:S(2)}) collective-permute-start(bf16[32,2048]{1,0:T(8,128)(2,1)S(1)} %get-tuple-element.6), channel_id=1, source_target_pairs={{0,1},{1,2},{2,3},{3,4},{4,5},{5,6},{6,7},{7,0},{8,9},{9,10},{10,1... | collective-permute-start | bytes 393224 | tf_op jit(solution)/shard_map/ppermute | solution.py:46
  86.3 18.2 %collective-permute-start.12 = (bf16[32,2048]{1,0:T(8,128)(2,1)S(1)}, bf16[32,2048]{1,0:T(8,128)(2,1)}, u32[]{:S(2)}, u32[]{:S(2)}) collective-permute-start(bf16[32,2048]{1,0:T(8,128)(2,1)S(1)} %get-tuple-element.6), channel_id=1, source_target_pairs={{0,2},{1,3},{2,4},{3,5},{4,6},{5,7},{6,0},{7,1},{8,10},{9,11},{10,... | collective-permute-start | bytes 393224 | tf_op jit(solution)/shard_map/ppermute | solution.py:46
  88.0 18.7 %collective-permute-start.13 = (bf16[32,2048]{1,0:T(8,128)(2,1)S(1)}, bf16[32,2048]{1,0:T(8,128)(2,1)}, u32[]{:S(2)}, u32[]{:S(2)}) collective-permute-start(bf16[32,2048]{1,0:T(8,128)(2,1)S(1)} %get-tuple-element.6), channel_id=1, source_target_pairs={{0,3},{1,4},{2,5},{3,6},{4,7},{5,0},{6,1},{7,2},{8,11},{9,12},{10,... | collective-permute-start | bytes 393224 | tf_op jit(solution)/shard_map/ppermute | solution.py:46
  89.8 18.5 %collective-permute-start.14 = (bf16[32,2048]{1,0:T(8,128)(2,1)S(1)}, bf16[32,2048]{1,0:T(8,128)(2,1)}, u32[]{:S(2)}, u32[]{:S(2)}) collective-permute-start(bf16[32,2048]{1,0:T(8,128)(2,1)S(1)} %get-tuple-element.6), channel_id=1, source_target_pairs={{0,4},{1,5},{2,6},{3,7},{4,0},{5,1},{6,2},{7,3},{8,12},{9,13},{10,... | collective-permute-start | bytes 393224 | tf_op jit(solution)/shard_map/ppermute | solution.py:46
  89.8 20.1 %collective-permute-start.15 = (bf16[32,2048]{1,0:T(8,128)(2,1)S(1)}, bf16[32,2048]{1,0:T(8,128)(2,1)}, u32[]{:S(2)}, u32[]{:S(2)}) collective-permute-start(bf16[32,2048]{1,0:T(8,128)(2,1)S(1)} %get-tuple-element.6), channel_id=1, source_target_pairs={{0,5},{1,6},{2,7},{3,0},{4,1},{5,2},{6,3},{7,4},{8,13},{9,14},{10,... | collective-permute-start | bytes 393224 | tf_op jit(solution)/shard_map/ppermute | solution.py:46
  94.2 26.5 %all-to-all-start = ((bf16[64,1,4,2048]{3,2,1,0:T(4,128)(2,1)}), bf16[64,1,4,2048]{3,2,1,0:T(4,128)(2,1)}, u32[]{:S(2)}, u32[]{:S(2)}) async-start(bf16[64,1,4,2048]{3,2,1,0:T(4,128)(2,1)} %copy.71), calls=%async_computation | async-start | bytes 2097152 | tf_op jit(solution)/shard_map/all_to_all | solution.py:228
  100.3 15.6 %collective-permute-start.16 = (bf16[32,2048]{1,0:T(8,128)(2,1)S(1)}, bf16[32,2048]{1,0:T(8,128)(2,1)S(1)}, u32[]{:S(2)}, u32[]{:S(2)}) collective-permute-start(bf16[32,2048]{1,0:T(8,128)(2,1)S(1)} %get-tuple-element.6), channel_id=1, source_target_pairs={{0,6},{1,7},{2,0},{3,1},{4,2},{5,3},{6,4},{7,5},{8,14},{9,15},{10,... | collective-permute-start | bytes 393224 | tf_op jit(solution)/shard_map/ppermute | solution.py:46
  104.5 13.6 %collective-permute-start.17 = (bf16[32,2048]{1,0:T(8,128)(2,1)S(1)}, bf16[32,2048]{1,0:T(8,128)(2,1)S(1)}, u32[]{:S(2)}, u32[]{:S(2)}) collective-permute-start(bf16[32,2048]{1,0:T(8,128)(2,1)S(1)} %get-tuple-element.6), channel_id=1, source_target_pairs={{0,7},{1,0},{2,1},{3,2},{4,3},{5,4},{6,5},{7,6},{8,15},{9,8},{10,9... | collective-permute-start | bytes 393224 | tf_op jit(solution)/shard_map/ppermute | solution.py:46
  134.7 35.4 %all-to-all-start.1 = ((bf16[64,1,4,2048]{3,2,1,0:T(4,128)(2,1)}), bf16[64,1,4,2048]{3,2,1,0:T(4,128)(2,1)}, u32[]{:S(2)}, u32[]{:S(2)}) async-start(bf16[64,1,4,2048]{3,2,1,0:T(4,128)(2,1)} %copy.73), calls=%async_computation.1 | async-start | bytes 2097152 | tf_op jit(solution)/shard_map/all_to_all | solution.py:235
  151.9 12.4 %collective-permute-start.19 = (bf16[32,2048]{1,0:T(8,128)(2,1)S(1)}, bf16[32,2048]{1,0:T(8,128)(2,1)S(1)}, u32[]{:S(2)}, u32[]{:S(2)}) collective-permute-start(bf16[32,2048]{1,0:T(8,128)(2,1)S(1)} %get-tuple-element.15), channel_id=1, source_target_pairs={{0,2},{1,3},{2,4},{3,5},{4,6},{5,7},{6,0},{7,1},{8,10},{9,11},{10,... | collective-permute-start | bytes 393224 | tf_op jit(solution)/shard_map/ppermute | solution.py:37
  153.1 13.4 %collective-permute-start.20 = (bf16[32,2048]{1,0:T(8,128)(2,1)}, bf16[32,2048]{1,0:T(8,128)(2,1)}, u32[]{:S(2)}, u32[]{:S(2)}) collective-permute-start(bf16[32,2048]{1,0:T(8,128)(2,1)} %get-tuple-element.14), channel_id=1, source_target_pairs={{0,3},{1,4},{2,5},{3,6},{4,7},{5,0},{6,1},{7,2},{8,11},{9,12},{10,... | collective-permute-start | bytes 393224 | tf_op jit(solution)/shard_map/ppermute | solution.py:37
  154.7 14.8 %collective-permute-start.21 = (bf16[32,2048]{1,0:T(8,128)(2,1)}, bf16[32,2048]{1,0:T(8,128)(2,1)}, u32[]{:S(2)}, u32[]{:S(2)}) collective-permute-start(bf16[32,2048]{1,0:T(8,128)(2,1)} %get-tuple-element.13), channel_id=1, source_target_pairs={{0,4},{1,5},{2,6},{3,7},{4,0},{5,1},{6,2},{7,3},{8,12},{9,13},{10,... | collective-permute-start | bytes 393224 | tf_op jit(solution)/shard_map/ppermute | solution.py:37
  155.3 14.8 %collective-permute-start.22 = (bf16[32,2048]{1,0:T(8,128)(2,1)}, bf16[32,2048]{1,0:T(8,128)(2,1)}, u32[]{:S(2)}, u32[]{:S(2)}) collective-permute-start(bf16[32,2048]{1,0:T(8,128)(2,1)} %get-tuple-element.12), channel_id=1, source_target_pairs={{0,5},{1,6},{2,7},{3,0},{4,1},{5,2},{6,3},{7,4},{8,13},{9,14},{10,... | collective-permute-start | bytes 393224 | tf_op jit(solution)/shard_map/ppermute | solution.py:37
  157.2 12.9 %collective-permute-start.23 = (bf16[32,2048]{1,0:T(8,128)(2,1)}, bf16[32,2048]{1,0:T(8,128)(2,1)}, u32[]{:S(2)}, u32[]{:S(2)}) collective-permute-start(bf16[32,2048]{1,0:T(8,128)(2,1)} %get-tuple-element.11), channel_id=1, source_target_pairs={{0,6},{1,7},{2,0},{3,1},{4,2},{5,3},{6,4},{7,5},{8,14},{9,15},{10,... | collective-permute-start | bytes 393224 | tf_op jit(solution)/shard_map/ppermute | solution.py:37
  (21 other events, 267.1 us)

commit v9 on v4

--- a/solution.py
+++ b/solution.py
@@ -139,8 +139,33 @@
     reach = LONGEST_SEGMENT // tok_dev
     kv_own = jnp.concatenate([latent, key_rope], axis=-1)
     kv_parts = [kv_own]
-    for steps in range(1, min(reach, n_tok - 1) + 1):
-        kv_parts.insert(0, passed_along(kv_own, "tok", steps))
+    if micro_count == 2 and lax.axis_size("section") == 2:
+        other_id = 1 - section_id
+        other_rows = lax.dynamic_index_in_dim(layer_input, other_id, 0, keepdims=False)
+        other_seg = lax.dynamic_index_in_dim(segment_ids, other_id, 0, keepdims=False)
+        other_pos = lax.dynamic_slice_in_dim(positions_of(other_seg, SEGS), query_start, tok_dev)
+        other_normed = rms_scale(other_rows, attn_gain).astype(jnp.bfloat16)
+        other_compressed = jnp.dot(other_normed, w_kv_down, preferred_element_type=jnp.float32)
+        kv_other = jnp.concatenate(
+            [
+                rms_scale(other_compressed[:, :LATENT], latent_gain).astype(jnp.bfloat16),
+                rotary(other_compressed[:, LATENT:], other_pos).astype(jnp.bfloat16),
+            ],
+            axis=-1,
+        )
+        half = n_tok // 2
+        for steps in range(1, min(reach, n_tok - 1) + 1):
+            crossing = (tok_rank < half) & (tok_rank + steps >= half)
+            sent = jnp.where(crossing, kv_other, kv_own)
+            pairs = []
+            for sec in range(2):
+                for t in range(n_tok - steps):
+                    source = (1 - sec) if t < half <= t + steps else sec
+                    pairs.append((source * n_tok + t, sec * n_tok + t + steps))
+            kv_parts.insert(0, lax.ppermute(sent, ("section", "tok"), pairs))
+    else:
+        for steps in range(1, min(reach, n_tok - 1) + 1):
+            kv_parts.insert(0, passed_along(kv_own, "tok", steps))
     kv_rows = jnp.concatenate(kv_parts, axis=0)
     key_count = kv_rows.shape[0]
     key_start = query_start + tok_dev - key_count

time: 168 us -> 169 us (level)
  other arithmetic: 12.5 us -> 17.8 us
  starting transfers between devices: 66.5 us -> 62.3 us
    all_to_all x1, starting transfers between devices: 9.77 us -> 6.48 us  [shards(): lax.all_to_all(outgoing, ('tok', 'mdl'), split_axis=0, concat_axis=0, til...]
    select_n x0 -> x2, other arithmetic: none -> 2.84 us  [shards(): sent = jnp.where(crossing, kv_other, kv_own)]
    reduce_sum x3 -> x4, other arithmetic: 3.01 us -> 3.76 us  [rms_scale(): jnp.mean(values * values, axis=-1, keepdims=True) + EPS]
    unnamed x60 -> x58, local copies, waits for them, and re-layouts: 19.1 us -> 19.2 us
  transfers between devices with their start and end apart: 27 -> 27, of which waited for: 7 -> 7; matrix products, arithmetic and copies ran while one was open for 21% -> 22% of each run, Pallas kernels for 0% -> 0%
where the time goes in v9:
time: 169 us; the launch traced here: 167 us
  starting transfers between devices  62.3 us (37%)
  matrix products  35.5 us (21%)
  local copies, waits for them, and re-layouts  29.3 us (17%)
  waiting for transfers between devices  21.8 us (13%)
  other arithmetic  17.8 us (11%)
    ppermute x14, starting transfers between devices, summed_over(): lax.ppermute(piece_for(steps), axis, [(i, (i + steps) % count) for i in r...  19.5 us
    unnamed x58, local copies, waits for them, and re-layouts  19.2 us
    ppermute x4, starting transfers between devices, shards(): kv_parts.insert(0, lax.ppermute(sent, ('section', 'tok'), pairs))  16.8 us
    ppermute x14, waiting for transfers between devices, summed_over(): lax.ppermute(piece_for(steps), axis, [(i, (i + steps) % count) for i in r...  15.8 us
    ppermute x7, starting transfers between devices, gathered_over(): lax.ppermute(block, axis, [(i, (i + steps) % count) for i in range(count)])  10.2 us
    all_to_all x1, starting transfers between devices, shards(): lax.all_to_all(produced, ('tok', 'mdl'), split_axis=0, concat_axis=0, til...  9.28 us
    all_to_all x1, starting transfers between devices, shards(): lax.all_to_all(outgoing, ('tok', 'mdl'), split_axis=0, concat_axis=0, til...  6.48 us
    ppermute x7, waiting for transfers between devices, gathered_over(): lax.ppermute(block, axis, [(i, (i + steps) % count) for i in range(count)])  6.02 us
  transfers between devices with their start and end apart: 27, of which 7 were waited for; matrix products, arithmetic and copies ran while one was open for 22% of the time, Pallas kernels for 0%

profile of v9, /device:TPU:1, one launch (start us, length us, event | category | flops | bytes accessed | tf_op | source)
XLA Modules:
  0.0 167.4 jit_solution(1450001100936167804)
XLA Ops:
  0.0 2.2 %fusion.25 = (f32[256]{0:T(256)S(1)}, f32[256]{0:T(256)S(1)}) fusion(bf16[2,256,2048]{2,1,0:T(8,128)(2,1)} %param.17, s32[]{:T(128)S(6)} %select_n.128, s32[]{:T(128)S(6)} %select_n.136), kind=kLoop, calls=%fused_computation.29 | loop fusion | flops 3145216 | bytes 2099208 | tf_op jit(solution)/shard_map/reduce_sum | solution.py:52
  2.4 2.8 %fusion.67 = f32[256,576]{0,1:T(8,128)S(1)} fusion(bf16[2048,576]{0,1:T(8,128)(2,1)} %param.23, f32[256]{0:T(256)S(1)} %get-tuple-element.48, f32[2048]{0:T(1024)S(1)} %copy-done.22, bf16[2,256,2048]{2,1,0:T(8,128)(2,1)S(1)} %copy-done.3, s32[]{:T(128)S(6)} %select_n.128), kind=kOutput, calls=%fused_computation.54 | convolution fusion | flops 606076928 | bytes 4006916 | tf_op jit(solution)/shard_map/dot_general | solution.py:135
  11.7 7.2 %collective-permute-start.1 = (bf16[256,576]{0,1:T(8,128)(2,1)}, bf16[256,576]{0,1:T(8,128)(2,1)}, u32[]{:S(2)}, u32[]{:S(2)}) collective-permute-start(bf16[256,576]{0,1:T(8,128)(2,1)} %get-tuple-element.30), channel_id=1, source_target_pairs={{0,24},{72,32},{80,40},{88,48},{32,56},{64,88},{8,96},{16,104},{24... | collective-permute-start | bytes 884744 | tf_op jit(solution)/shard_map/ppermute | solution.py:165
  20.8 4.4 %collective-permute-start = (bf16[256,576]{0,1:T(8,128)(2,1)}, bf16[256,576]{0,1:T(8,128)(2,1)}, u32[]{:S(2)}, u32[]{:S(2)}) collective-permute-start(bf16[256,576]{0,1:T(8,128)(2,1)} %get-tuple-element.32), channel_id=1, source_target_pairs={{64,32},{72,40},{80,48},{88,56},{0,96},{8,104},{16,112},{24,120},{... | collective-permute-start | bytes 884744 | tf_op jit(solution)/shard_map/ppermute | solution.py:165
  27.3 3.1 %collective-permute-start.3 = (bf16[256,576]{0,1:T(8,128)(2,1)}, bf16[256,576]{0,1:T(8,128)(2,1)}, u32[]{:S(2)}, u32[]{:S(2)}) collective-permute-start(bf16[256,576]{0,1:T(8,128)(2,1)} %get-tuple-element.29), channel_id=1, source_target_pairs={{0,8},{8,16},{16,24},{88,32},{32,40},{40,48},{48,56},{64,72},{72,8... | collective-permute-start | bytes 884744 | tf_op jit(solution)/shard_map/ppermute | solution.py:165
  30.4 2.6 %copy.58 = bf16[2048,384]{0,1:T(8,128)(2,1)} copy(bf16[2048,384]{1,0:T(8,128)(2,1)} %param.22) | data formatting | bytes 3145728 | tf_op args[5]
  33.0 3.2 %fusion.65 = f32[256,2,192]{0,2,1:T(8,128)} fusion(bf16[2,192,2048]{2,1,0:T(8,128)(2,1)} %bitcast.186, f32[2048]{0:T(1024)S(1)} %copy-done.22, f32[256]{0:T(256)S(1)} %get-tuple-element.48, bf16[2,256,2048]{2,1,0:T(8,128)(2,1)} %param.17, s32[]{:T(128)S(6)} %select_n.128), kind=kOutput, calls=%fused_computation.53 | convolution fusion | flops 404750336 | bytes 3023876 | tf_op jit(solution)/shard_map/dot_general | solution.py:129
  50.3 3.7 %fusion.59 = bf16[256,2,128]{0,2,1:T(8,128)(2,1)S(1)} fusion(bf16[1280,2,256]{0,2,1:T(8,128)(2,1)} %bitcast.189, f32[2,256,1280]{2,1,0:T(8,128)} %copy-done.2, pred[256,1280]{1,0:T(8,128)(4,1)} %and_and_fusion, f32[256,2]{0,1:T(2,128)S(1)} %bitcast.199), kind=kOutput, calls=%fused_computation.50 | convolution fusion | flops 170526464 | bytes 6686720 | tf_op jit(solution)/shard_map/hqk,khd->hqd/dot_general | solution.py:199
  62.0 2.1 %collective-permute-start.6 = (bf16[32,2048]{1,0:T(8,128)(2,1)}, bf16[32,2048]{1,0:T(8,128)(2,1)S(1)}, u32[]{:S(2)}, u32[]{:S(2)}) collective-permute-start(bf16[32,2048]{1,0:T(8,128)(2,1)} %get-tuple-element.23), channel_id=1, source_target_pairs={{0,3},{1,4},{2,5},{3,6},{4,7},{5,0},{6,1},{7,2},{8,11},{9,12},{10,... | collective-permute-start | bytes 393224 | tf_op jit(solution)/shard_map/ppermute | solution.py:37
  64.8 2.6 %collective-permute-start.8 = (bf16[32,2048]{1,0:T(8,128)(2,1)}, bf16[32,2048]{1,0:T(8,128)(2,1)S(1)}, u32[]{:S(2)}, u32[]{:S(2)}) collective-permute-start(bf16[32,2048]{1,0:T(8,128)(2,1)} %get-tuple-element.21), channel_id=1, source_target_pairs={{0,5},{1,6},{2,7},{3,0},{4,1},{5,2},{6,3},{7,4},{8,13},{9,14},{10,... | collective-permute-start | bytes 393224 | tf_op jit(solution)/shard_map/ppermute | solution.py:37
  67.5 2.4 %collective-permute-done.5 = bf16[32,2048]{1,0:T(8,128)(2,1)S(1)} collective-permute-done((bf16[32,2048]{1,0:T(8,128)(2,1)}, bf16[32,2048]{1,0:T(8,128)(2,1)S(1)}, u32[]{:S(2)}, u32[]{:S(2)}) %collective-permute-start.5) | collective-permute-done | bytes 131104 | tf_op jit(solution)/shard_map/ppermute | solution.py:37
  69.8 5.9 %collective-permute-done.6 = bf16[32,2048]{1,0:T(8,128)(2,1)S(1)} collective-permute-done((bf16[32,2048]{1,0:T(8,128)(2,1)}, bf16[32,2048]{1,0:T(8,128)(2,1)S(1)}, u32[]{:S(2)}, u32[]{:S(2)}) %collective-permute-start.6) | collective-permute-done | bytes 131104 | tf_op jit(solution)/shard_map/ppermute | solution.py:37
  87.3 6.5 %all-to-all-start = ((bf16[64,1,4,2048]{3,2,1,0:T(4,128)(2,1)}), bf16[64,1,4,2048]{3,2,1,0:T(4,128)(2,1)}, u32[]{:S(2)}, u32[]{:S(2)}) async-start(bf16[64,1,4,2048]{3,2,1,0:T(4,128)(2,1)} %copy.71), calls=%async_computation | async-start | bytes 2097152 | tf_op jit(solution)/shard_map/all_to_all | solution.py:239
  93.8 2.6 %collective-permute-start.16 = (bf16[32,2048]{1,0:T(8,128)(2,1)S(1)}, bf16[32,2048]{1,0:T(8,128)(2,1)S(1)}, u32[]{:S(2)}, u32[]{:S(2)}) collective-permute-start(bf16[32,2048]{1,0:T(8,128)(2,1)S(1)} %get-tuple-element.8), channel_id=1, source_target_pairs={{0,6},{1,7},{2,0},{3,1},{4,2},{5,3},{6,4},{7,5},{8,14},{9,15},{10,... | collective-permute-start | bytes 393224 | tf_op jit(solution)/shard_map/ppermute | solution.py:46
  104.9 4.7 %collective-permute-done.16 = bf16[32,2048]{1,0:T(8,128)(2,1)S(1)} collective-permute-done((bf16[32,2048]{1,0:T(8,128)(2,1)S(1)}, bf16[32,2048]{1,0:T(8,128)(2,1)S(1)}, u32[]{:S(2)}, u32[]{:S(2)}) %collective-permute-start.16) | collective-permute-done | bytes 131104 | tf_op jit(solution)/shard_map/ppermute | solution.py:46
  114.2 5.0 %fusion.38 = f32[64,1,4,768]{3,0,2,1:T(8,128)} fusion(bf16[1,2048,768]{2,1,0:T(8,128)(2,1)} %param.31, bf16[64,1,4,2048]{3,2,1,0:T(4,128)(2,1)} %all-to-all-done), kind=kOutput, calls=%fused_computation.43 | convolution fusion | flops 805306368 | bytes 4980736 | tf_op jit(solution)/shard_map/sjkd,jdf->sjkf/dot_general | solution.py:240
  119.2 5.9 %fusion.22 = bf16[64,1,4,2048]{3,0,2,1:T(8,128)(2,1)} fusion(bf16[1,768,2048]{2,1,0:T(8,128)(2,1)S(1)} %copy-done, bf16[1,2048,768]{2,1,0:T(8,128)(2,1)} %param.32, bf16[64,1,4,2048]{3,2,1,0:T(4,128)(2,1)} %all-to-all-done, f32[64,1,4,768]{3,0,2,1:T(8,128)} %fusion.38), kind=kOutput, calls=%fused_computation.27 | convolution fusion | flops 1612316672 | bytes 9175040 | tf_op jit(solution)/shard_map/sjkf,jfd->sjkd/dot_general | solution.py:243
  125.2 3.0 %copy.73 = bf16[64,1,4,2048]{3,2,1,0:T(4,128)(2,1)} copy(bf16[64,1,4,2048]{3,0,2,1:T(8,128)(2,1)} %fusion.22) | data formatting | bytes 2097152 | tf_op jit(solution)/shard_map/convert_element_type | solution.py:245
  128.2 9.3 %all-to-all-start.1 = ((bf16[64,1,4,2048]{3,2,1,0:T(4,128)(2,1)}), bf16[64,1,4,2048]{3,2,1,0:T(4,128)(2,1)}, u32[]{:S(2)}, u32[]{:S(2)}) async-start(bf16[64,1,4,2048]{3,2,1,0:T(4,128)(2,1)} %copy.73), calls=%async_computation.1 | async-start | bytes 2097152 | tf_op jit(solution)/shard_map/all_to_all | solution.py:246
  137.5 4.1 %convolution_convert_fusion.1 = bf16[256,2048]{1,0:T(8,128)(2,1)} fusion(bf16[256,2048]{1,0:T(8,128)(2,1)} %param.30, f32[256,256]{1,0:T(8,128)S(1)} %fusion.156, bf16[256,2048]{1,0:T(8,128)(2,1)} %constant_dynamic-update-slice_fusion.5, bf16[2048,256]{1,0:T(8,128)(2,1)} %param.29), kind=kOutput, calls=%fused_computation.22 | convolution fusion | flops 537788416 | bytes 4456448 | tf_op jit(solution)/shard_map/dot_general | solution.py:217
  150.6 3.1 %collective-permute-start.23 = (bf16[32,2048]{1,0:T(8,128)(2,1)}, bf16[32,2048]{1,0:T(8,128)(2,1)}, u32[]{:S(2)}, u32[]{:S(2)}) collective-permute-start(bf16[32,2048]{1,0:T(8,128)(2,1)} %get-tuple-element.13), channel_id=1, source_target_pairs={{0,6},{1,7},{2,0},{3,1},{4,2},{5,3},{6,4},{7,5},{8,14},{9,15},{10,... | collective-permute-start | bytes 393224 | tf_op jit(solution)/shard_map/ppermute | solution.py:37
  153.7 4.0 %collective-permute-done.19 = bf16[32,2048]{1,0:T(8,128)(2,1)S(1)} collective-permute-done((bf16[32,2048]{1,0:T(8,128)(2,1)S(1)}, bf16[32,2048]{1,0:T(8,128)(2,1)S(1)}, u32[]{:S(2)}, u32[]{:S(2)}) %collective-permute-start.19) | collective-permute-done | bytes 131104 | tf_op jit(solution)/shard_map/ppermute | solution.py:37
  159.9 3.0 %collective-permute-done.21 = bf16[32,2048]{1,0:T(8,128)(2,1)} collective-permute-done((bf16[32,2048]{1,0:T(8,128)(2,1)}, bf16[32,2048]{1,0:T(8,128)(2,1)}, u32[]{:S(2)}, u32[]{:S(2)}) %collective-permute-start.21) | collective-permute-done | bytes 131104 | tf_op jit(solution)/shard_map/ppermute | solution.py:37
  163.5 3.9 %fusion.115 = bf16[1,32,2048]{2,1,0:T(8,128)(2,1)} fusion(bf16[64,1,4,2048]{3,2,1,0:T(4,128)(2,1)} %all-to-all-done.1, f32[32,64,4]{0,2,1:T(4,128)S(1)} %bitcast.187, bf16[32,2048]{1,0:T(8,128)(2,1)} %collective-permute-done.24, bf16[32,2048]{1,0:T(8,128)(2,1)} %collective-permute-done.23, bf16[32,2048]{1,0:T(8,128)(2,1)} %collective-permute-done.22, ...), kind=kOutput, calls=%fused_computation.110 | convolution fusion | flops 202571776 | bytes 2392064 | tf_op jit(solution)/shard_map/rsjk,sjkd->rd/dot_general | solution.py:251
  (156 shorter events, 69.5 us)
Async XLA Ops:
  11.7 30.9 %collective-permute-start.1 = (bf16[256,576]{0,1:T(8,128)(2,1)}, bf16[256,576]{0,1:T(8,128)(2,1)}, u32[]{:S(2)}, u32[]{:S(2)}) collective-permute-start(bf16[256,576]{0,1:T(8,128)(2,1)} %get-tuple-element.30), channel_id=1, source_target_pairs={{0,24},{72,32},{80,40},{88,48},{32,56},{64,88},{8,96},{16,104},{24... | collective-permute-start | bytes 884744 | tf_op jit(solution)/shard_map/ppermute | solution.py:165
  20.8 20.7 %collective-permute-start = (bf16[256,576]{0,1:T(8,128)(2,1)}, bf16[256,576]{0,1:T(8,128)(2,1)}, u32[]{:S(2)}, u32[]{:S(2)}) collective-permute-start(bf16[256,576]{0,1:T(8,128)(2,1)} %get-tuple-element.32), channel_id=1, source_target_pairs={{64,32},{72,40},{80,48},{88,56},{0,96},{8,104},{16,112},{24,120},{... | collective-permute-start | bytes 884744 | tf_op jit(solution)/shard_map/ppermute | solution.py:165
  25.2 18.4 %collective-permute-start.2 = (bf16[256,576]{0,1:T(8,128)(2,1)}, bf16[256,576]{0,1:T(8,128)(2,1)}, u32[]{:S(2)}, u32[]{:S(2)}) collective-permute-start(bf16[256,576]{0,1:T(8,128)(2,1)} %get-tuple-element.31), channel_id=1, source_target_pairs={{0,16},{8,24},{80,32},{88,40},{32,48},{40,56},{64,80},{72,88},{16,... | collective-permute-start | bytes 884744 | tf_op jit(solution)/shard_map/ppermute | solution.py:165
  27.3 17.3 %collective-permute-start.3 = (bf16[256,576]{0,1:T(8,128)(2,1)}, bf16[256,576]{0,1:T(8,128)(2,1)}, u32[]{:S(2)}, u32[]{:S(2)}) collective-permute-start(bf16[256,576]{0,1:T(8,128)(2,1)} %get-tuple-element.29), channel_id=1, source_target_pairs={{0,8},{8,16},{16,24},{88,32},{32,40},{40,48},{48,56},{64,72},{72,8... | collective-permute-start | bytes 884744 | tf_op jit(solution)/shard_map/ppermute | solution.py:165
  59.1 8.3 %collective-permute-start.4 = (bf16[32,2048]{1,0:T(8,128)(2,1)}, bf16[32,2048]{1,0:T(8,128)(2,1)}, u32[]{:S(2)}, u32[]{:S(2)}) collective-permute-start(bf16[32,2048]{1,0:T(8,128)(2,1)} %get-tuple-element.18), channel_id=1, source_target_pairs={{0,1},{1,2},{2,3},{3,4},{4,5},{5,6},{6,7},{7,0},{8,9},{9,10},{10,1... | collective-permute-start | bytes 393224 | tf_op jit(solution)/shard_map/ppermute | solution.py:37
  60.6 9.2 %collective-permute-start.5 = (bf16[32,2048]{1,0:T(8,128)(2,1)}, bf16[32,2048]{1,0:T(8,128)(2,1)S(1)}, u32[]{:S(2)}, u32[]{:S(2)}) collective-permute-start(bf16[32,2048]{1,0:T(8,128)(2,1)} %get-tuple-element.24), channel_id=1, source_target_pairs={{0,2},{1,3},{2,4},{3,5},{4,6},{5,7},{6,0},{7,1},{8,10},{9,11},{10,... | collective-permute-start | bytes 393224 | tf_op jit(solution)/shard_map/ppermute | solution.py:37
  62.0 13.8 %collective-permute-start.6 = (bf16[32,2048]{1,0:T(8,128)(2,1)}, bf16[32,2048]{1,0:T(8,128)(2,1)S(1)}, u32[]{:S(2)}, u32[]{:S(2)}) collective-permute-start(bf16[32,2048]{1,0:T(8,128)(2,1)} %get-tuple-element.23), channel_id=1, source_target_pairs={{0,3},{1,4},{2,5},{3,6},{4,7},{5,0},{6,1},{7,2},{8,11},{9,12},{10,... | collective-permute-start | bytes 393224 | tf_op jit(solution)/shard_map/ppermute | solution.py:37
  64.1 11.6 %collective-permute-start.7 = (bf16[32,2048]{1,0:T(8,128)(2,1)}, bf16[32,2048]{1,0:T(8,128)(2,1)S(1)}, u32[]{:S(2)}, u32[]{:S(2)}) collective-permute-start(bf16[32,2048]{1,0:T(8,128)(2,1)} %get-tuple-element.22), channel_id=1, source_target_pairs={{0,4},{1,5},{2,6},{3,7},{4,0},{5,1},{6,2},{7,3},{8,12},{9,13},{10,... | collective-permute-start | bytes 393224 | tf_op jit(solution)/shard_map/ppermute | solution.py:37
  64.8 10.9 %collective-permute-start.8 = (bf16[32,2048]{1,0:T(8,128)(2,1)}, bf16[32,2048]{1,0:T(8,128)(2,1)S(1)}, u32[]{:S(2)}, u32[]{:S(2)}) collective-permute-start(bf16[32,2048]{1,0:T(8,128)(2,1)} %get-tuple-element.21), channel_id=1, source_target_pairs={{0,5},{1,6},{2,7},{3,0},{4,1},{5,2},{6,3},{7,4},{8,13},{9,14},{10,... | collective-permute-start | bytes 393224 | tf_op jit(solution)/shard_map/ppermute | solution.py:37
  67.5 8.2 %collective-permute-start.9 = (bf16[32,2048]{1,0:T(8,128)(2,1)S(1)}, bf16[32,2048]{1,0:T(8,128)(2,1)S(1)}, u32[]{:S(2)}, u32[]{:S(2)}) collective-permute-start(bf16[32,2048]{1,0:T(8,128)(2,1)S(1)} %get-tuple-element.20), channel_id=1, source_target_pairs={{0,6},{1,7},{2,0},{3,1},{4,2},{5,3},{6,4},{7,5},{8,14},{9,15},{10,... | collective-permute-start | bytes 393224 | tf_op jit(solution)/shard_map/ppermute | solution.py:37
  77.9 15.8 %collective-permute-start.11 = (bf16[32,2048]{1,0:T(8,128)(2,1)S(1)}, bf16[32,2048]{1,0:T(8,128)(2,1)}, u32[]{:S(2)}, u32[]{:S(2)}) collective-permute-start(bf16[32,2048]{1,0:T(8,128)(2,1)S(1)} %get-tuple-element.8), channel_id=1, source_target_pairs={{0,1},{1,2},{2,3},{3,4},{4,5},{5,6},{6,7},{7,0},{8,9},{9,10},{10,1... | collective-permute-start | bytes 393224 | tf_op jit(solution)/shard_map/ppermute | solution.py:46
  78.8 19.2 %collective-permute-start.12 = (bf16[32,2048]{1,0:T(8,128)(2,1)S(1)}, bf16[32,2048]{1,0:T(8,128)(2,1)}, u32[]{:S(2)}, u32[]{:S(2)}) collective-permute-start(bf16[32,2048]{1,0:T(8,128)(2,1)S(1)} %get-tuple-element.8), channel_id=1, source_target_pairs={{0,2},{1,3},{2,4},{3,5},{4,6},{5,7},{6,0},{7,1},{8,10},{9,11},{10,... | collective-permute-start | bytes 393224 | tf_op jit(solution)/shard_map/ppermute | solution.py:46
  80.5 19.7 %collective-permute-start.13 = (bf16[32,2048]{1,0:T(8,128)(2,1)S(1)}, bf16[32,2048]{1,0:T(8,128)(2,1)}, u32[]{:S(2)}, u32[]{:S(2)}) collective-permute-start(bf16[32,2048]{1,0:T(8,128)(2,1)S(1)} %get-tuple-element.8), channel_id=1, source_target_pairs={{0,3},{1,4},{2,5},{3,6},{4,7},{5,0},{6,1},{7,2},{8,11},{9,12},{10,... | collective-permute-start | bytes 393224 | tf_op jit(solution)/shard_map/ppermute | solution.py:46
  82.2 19.5 %collective-permute-start.14 = (bf16[32,2048]{1,0:T(8,128)(2,1)S(1)}, bf16[32,2048]{1,0:T(8,128)(2,1)}, u32[]{:S(2)}, u32[]{:S(2)}) collective-permute-start(bf16[32,2048]{1,0:T(8,128)(2,1)S(1)} %get-tuple-element.8), channel_id=1, source_target_pairs={{0,4},{1,5},{2,6},{3,7},{4,0},{5,1},{6,2},{7,3},{8,12},{9,13},{10,... | collective-permute-start | bytes 393224 | tf_op jit(solution)/shard_map/ppermute | solution.py:46
  83.0 20.4 %collective-permute-start.15 = (bf16[32,2048]{1,0:T(8,128)(2,1)S(1)}, bf16[32,2048]{1,0:T(8,128)(2,1)}, u32[]{:S(2)}, u32[]{:S(2)}) collective-permute-start(bf16[32,2048]{1,0:T(8,128)(2,1)S(1)} %get-tuple-element.8), channel_id=1, source_target_pairs={{0,5},{1,6},{2,7},{3,0},{4,1},{5,2},{6,3},{7,4},{8,13},{9,14},{10,... | collective-permute-start | bytes 393224 | tf_op jit(solution)/shard_map/ppermute | solution.py:46
  87.3 26.9 %all-to-all-start = ((bf16[64,1,4,2048]{3,2,1,0:T(4,128)(2,1)}), bf16[64,1,4,2048]{3,2,1,0:T(4,128)(2,1)}, u32[]{:S(2)}, u32[]{:S(2)}) async-start(bf16[64,1,4,2048]{3,2,1,0:T(4,128)(2,1)} %copy.71), calls=%async_computation | async-start | bytes 2097152 | tf_op jit(solution)/shard_map/all_to_all | solution.py:239
  93.8 15.8 %collective-permute-start.16 = (bf16[32,2048]{1,0:T(8,128)(2,1)S(1)}, bf16[32,2048]{1,0:T(8,128)(2,1)S(1)}, u32[]{:S(2)}, u32[]{:S(2)}) collective-permute-start(bf16[32,2048]{1,0:T(8,128)(2,1)S(1)} %get-tuple-element.8), channel_id=1, source_target_pairs={{0,6},{1,7},{2,0},{3,1},{4,2},{5,3},{6,4},{7,5},{8,14},{9,15},{10,... | collective-permute-start | bytes 393224 | tf_op jit(solution)/shard_map/ppermute | solution.py:46
  98.0 13.6 %collective-permute-start.17 = (bf16[32,2048]{1,0:T(8,128)(2,1)S(1)}, bf16[32,2048]{1,0:T(8,128)(2,1)S(1)}, u32[]{:S(2)}, u32[]{:S(2)}) collective-permute-start(bf16[32,2048]{1,0:T(8,128)(2,1)S(1)} %get-tuple-element.8), channel_id=1, source_target_pairs={{0,7},{1,0},{2,1},{3,2},{4,3},{5,4},{6,5},{7,6},{8,15},{9,8},{10,9... | collective-permute-start | bytes 393224 | tf_op jit(solution)/shard_map/ppermute | solution.py:46
  128.2 35.3 %all-to-all-start.1 = ((bf16[64,1,4,2048]{3,2,1,0:T(4,128)(2,1)}), bf16[64,1,4,2048]{3,2,1,0:T(4,128)(2,1)}, u32[]{:S(2)}, u32[]{:S(2)}) async-start(bf16[64,1,4,2048]{3,2,1,0:T(4,128)(2,1)} %copy.73), calls=%async_computation.1 | async-start | bytes 2097152 | tf_op jit(solution)/shard_map/all_to_all | solution.py:246
  145.3 12.3 %collective-permute-start.19 = (bf16[32,2048]{1,0:T(8,128)(2,1)S(1)}, bf16[32,2048]{1,0:T(8,128)(2,1)S(1)}, u32[]{:S(2)}, u32[]{:S(2)}) collective-permute-start(bf16[32,2048]{1,0:T(8,128)(2,1)S(1)} %get-tuple-element.17), channel_id=1, source_target_pairs={{0,2},{1,3},{2,4},{3,5},{4,6},{5,7},{6,0},{7,1},{8,10},{9,11},{10,... | collective-permute-start | bytes 393224 | tf_op jit(solution)/shard_map/ppermute | solution.py:37
  146.5 13.4 %collective-permute-start.20 = (bf16[32,2048]{1,0:T(8,128)(2,1)}, bf16[32,2048]{1,0:T(8,128)(2,1)}, u32[]{:S(2)}, u32[]{:S(2)}) collective-permute-start(bf16[32,2048]{1,0:T(8,128)(2,1)} %get-tuple-element.16), channel_id=1, source_target_pairs={{0,3},{1,4},{2,5},{3,6},{4,7},{5,0},{6,1},{7,2},{8,11},{9,12},{10,... | collective-permute-start | bytes 393224 | tf_op jit(solution)/shard_map/ppermute | solution.py:37
  148.2 14.7 %collective-permute-start.21 = (bf16[32,2048]{1,0:T(8,128)(2,1)}, bf16[32,2048]{1,0:T(8,128)(2,1)}, u32[]{:S(2)}, u32[]{:S(2)}) collective-permute-start(bf16[32,2048]{1,0:T(8,128)(2,1)} %get-tuple-element.15), channel_id=1, source_target_pairs={{0,4},{1,5},{2,6},{3,7},{4,0},{5,1},{6,2},{7,3},{8,12},{9,13},{10,... | collective-permute-start | bytes 393224 | tf_op jit(solution)/shard_map/ppermute | solution.py:37
  148.8 14.7 %collective-permute-start.22 = (bf16[32,2048]{1,0:T(8,128)(2,1)}, bf16[32,2048]{1,0:T(8,128)(2,1)}, u32[]{:S(2)}, u32[]{:S(2)}) collective-permute-start(bf16[32,2048]{1,0:T(8,128)(2,1)} %get-tuple-element.14), channel_id=1, source_target_pairs={{0,5},{1,6},{2,7},{3,0},{4,1},{5,2},{6,3},{7,4},{8,13},{9,14},{10,... | collective-permute-start | bytes 393224 | tf_op jit(solution)/shard_map/ppermute | solution.py:37
  150.6 12.9 %collective-permute-start.23 = (bf16[32,2048]{1,0:T(8,128)(2,1)}, bf16[32,2048]{1,0:T(8,128)(2,1)}, u32[]{:S(2)}, u32[]{:S(2)}) collective-permute-start(bf16[32,2048]{1,0:T(8,128)(2,1)} %get-tuple-element.13), channel_id=1, source_target_pairs={{0,6},{1,7},{2,0},{3,1},{4,2},{5,3},{6,4},{7,5},{8,14},{9,15},{10,... | collective-permute-start | bytes 393224 | tf_op jit(solution)/shard_map/ppermute | solution.py:37
  (27 other events, 232.7 us)

commit v10 on v4

--- a/solution.py
+++ b/solution.py
@@ -198,19 +198,13 @@
     earlier = jnp.cumsum(onehot, axis=0) - onehot
     slot_index = jnp.sum(earlier * onehot, axis=1)
     target = expert_ids * capacity + slot_index
-    placing = (
-        (slot_ids[:, None] == target[None, :])
-        .astype(jnp.int32)
-        .reshape(slot_total, row_dev, top_count)
-    )
-    placing = (
-        jnp.sum(placing, axis=2)
-        .astype(jnp.bfloat16)
-        .reshape(n_wide, expert_dev, capacity, row_dev)
-    )
-    outgoing = jnp.einsum(
-        "sjkr,rd->sjkd", placing, normed_ffn, preferred_element_type=jnp.float32
-    ).astype(jnp.bfloat16)
+    hit = slot_ids[:, None] == target[None, :]
+    pair_row = jnp.arange(row_dev * top_count, dtype=jnp.int32) // top_count
+    slot_row = jnp.where(
+        jnp.any(hit, axis=1), jnp.sum(jnp.where(hit, pair_row[None, :], 0), axis=1), row_dev
+    )
+    padded_rows = jnp.concatenate([normed_ffn, jnp.zeros((1, model_width), normed_ffn.dtype)])
+    outgoing = padded_rows[slot_row].reshape(n_wide, expert_dev, capacity, model_width)
     buffer = lax.all_to_all(outgoing, ("tok", "mdl"), split_axis=0, concat_axis=0, tiled=True)
     e_gate = jnp.einsum("sjkd,jdf->sjkf", buffer, w_expert_gate, preferred_element_type=jnp.float32)
     e_up = jnp.einsum("sjkd,jdf->sjkf", buffer, w_expert_up, preferred_element_type=jnp.float32)
@@ -219,16 +213,8 @@
         "sjkf,jfd->sjkd", expert_act, w_expert_down, preferred_element_type=jnp.float32
     ).astype(jnp.bfloat16)
     returned = lax.all_to_all(produced, ("tok", "mdl"), split_axis=0, concat_axis=0, tiled=True)
-    matched = target.reshape(row_dev, top_count)[:, :, None] == slot_ids[None, None, :]
-    combining = jnp.sum(jnp.where(matched, weight_rows[:, :, None], 0.0), axis=1).reshape(
-        row_dev, n_wide, expert_dev, capacity
-    )
-    routed = jnp.einsum(
-        "rsjk,sjkd->rd",
-        combining,
-        returned.astype(jnp.float32),
-        precision=lax.Precision.HIGHEST,
-    )
+    picked = returned.reshape(slot_total, model_width)[target].reshape(row_dev, top_count, model_width)
+    routed = jnp.sum(picked.astype(jnp.float32) * weight_rows[:, :, None], axis=1)
     finished = (own_residual.astype(jnp.float32) + shared_out + routed).astype(jnp.bfloat16)
     return finished[None]
 

time: 168 us -> 182 us (1.083)
  local copies, waits for them, and re-layouts: 30.7 us -> 43 us
  other arithmetic: 12.5 us -> 23.1 us
  starting transfers between devices: 66.5 us -> 61.8 us
  matrix products: 34.8 us -> 31.8 us
    gather x0 -> x2, local copies, waits for them, and re-layouts: none -> 6.5 us  [the longest x1 4.17 us: shards(): returned.reshape(slot_total, model_width)[target]]
    ppermute x14, waiting for transfers between devices: 15.8 us -> 9.61 us  [summed_over(): lax.ppermute(piece_for(steps), axis, [(i, (i + steps) % count) for i in r...]
    all_to_all x1, waiting for transfers between devices: 0.01 us -> 5.04 us  [shards(): lax.all_to_all(produced, ('tok', 'mdl'), split_axis=0, concat_axis=0, til...]
    reshape x0 -> x3, local copies, waits for them, and re-layouts: none -> 4.52 us  [the longest x1 2.25 us: shards(): padded_rows[slot_row].reshape(n_wide, expert_dev, capacity, model_width)]
    all_to_all x1, starting transfers between devices: 9.77 us -> 5.41 us  [shards(): lax.all_to_all(outgoing, ('tok', 'mdl'), split_axis=0, concat_axis=0, til...]
    dot_general x2 -> x0, matrix products: 4.3 us -> none  [the longest x1 3.9 us: shards(): jnp.einsum('rsjk,sjkd->rd', combining, returned.astype(jnp.float32), prec...]
    select_n x0 -> x4, other arithmetic: none -> 2.5 us  [the longest x1 1.26 us: shards(): pair_row = jnp.arange(row_dev * top_count, dtype=jnp.int32) // top_count]
    broadcast_in_dim x0 -> x1, other arithmetic: none -> 2.03 us  [shards(): return finished[None]]
  transfers between devices with their start and end apart: 27 -> 27, of which waited for: 7 -> 10; matrix products, arithmetic and copies ran while one was open for 21% -> 31% of each run, Pallas kernels for 0% -> 0%
where the time goes in v10:
time: 182 us; the launch traced here: 181 us
  starting transfers between devices  61.8 us (34%)
  local copies, waits for them, and re-layouts  43 us (24%)
  matrix products  31.8 us (17%)
  other arithmetic  23.1 us (13%)
  waiting for transfers between devices  20.6 us (11%)
    unnamed x51, local copies, waits for them, and re-layouts  19 us
    ppermute x14, starting transfers between devices, summed_over(): lax.ppermute(piece_for(steps), axis, [(i, (i + steps) % count) for i in r...  18.9 us
    ppermute x4, starting transfers between devices, passed_along(): lax.ppermute(value, axis, [(source, source + steps) for source in range(i...  17.7 us
    ppermute x7, starting transfers between devices, gathered_over(): lax.ppermute(block, axis, [(i, (i + steps) % count) for i in range(count)])  10.3 us
    ppermute x14, waiting for transfers between devices, summed_over(): lax.ppermute(piece_for(steps), axis, [(i, (i + steps) % count) for i in r...  9.61 us
    all_to_all x1, starting transfers between devices, shards(): lax.all_to_all(produced, ('tok', 'mdl'), split_axis=0, concat_axis=0, til...  9.39 us
    ppermute x7, waiting for transfers between devices, gathered_over(): lax.ppermute(block, axis, [(i, (i + steps) % count) for i in range(count)])  5.97 us
    dot_general x1, matrix products, shards(): jnp.einsum('sjkf,jfd->sjkd', expert_act, w_expert_down, preferred_element...  5.91 us
  transfers between devices with their start and end apart: 27, of which 10 were waited for; matrix products, arithmetic and copies ran while one was open for 31% of the time, Pallas kernels for 0%

profile of v10, /device:TPU:1, one launch (start us, length us, event | category | flops | bytes accessed | tf_op | source)
XLA Modules:
  0.0 180.7 jit_solution(11602726615511596243)
XLA Ops:
  2.7 2.9 %fusion.61 = f32[256,576]{0,1:T(8,128)S(1)} fusion(bf16[2048,576]{0,1:T(8,128)(2,1)} %param.23, f32[2048]{0:T(1024)} %param.21, f32[256]{0:T(256)S(1)} %add_rsqrt_fusion.1, bf16[2,256,2048]{2,1,0:T(8,128)(2,1)} %param.17, s32[]{:T(128)S(6)} %select_n.140), kind=kOutput, calls=%fused_computation.48 | convolution fusion | flops 606076928 | bytes 4006916 | tf_op jit(solution)/shard_map/dot_general | solution.py:135
  10.1 6.2 %collective-permute-start = (bf16[256,576]{0,1:T(8,128)(2,1)}, bf16[256,576]{0,1:T(8,128)(2,1)}, u32[]{:S(2)}, u32[]{:S(2)}) collective-permute-start(bf16[256,576]{0,1:T(8,128)(2,1)} %pad_maximum_fusion), channel_id=1, source_target_pairs={{0,32},{8,40},{16,48},{24,56},{1,33},{9,41},{17,49},{25,57},{2,34}... | collective-permute-start | bytes 884744 | tf_op jit(solution)/shard_map/ppermute | solution.py:22
  16.4 6.4 %collective-permute-start.1 = (bf16[256,576]{0,1:T(8,128)(2,1)}, bf16[256,576]{0,1:T(8,128)(2,1)}, u32[]{:S(2)}, u32[]{:S(2)}) collective-permute-start(bf16[256,576]{0,1:T(8,128)(2,1)} %pad_maximum_fusion), channel_id=1, source_target_pairs={{0,24},{8,32},{16,40},{24,48},{32,56},{1,25},{9,33},{17,41},{25,49... | collective-permute-start | bytes 884744 | tf_op jit(solution)/shard_map/ppermute | solution.py:22
  24.7 3.1 %collective-permute-start.3 = (bf16[256,576]{0,1:T(8,128)(2,1)}, bf16[256,576]{0,1:T(8,128)(2,1)}, u32[]{:S(2)}, u32[]{:S(2)}) collective-permute-start(bf16[256,576]{0,1:T(8,128)(2,1)} %pad_maximum_fusion), channel_id=1, source_target_pairs={{0,8},{8,16},{16,24},{24,32},{32,40},{40,48},{48,56},{1,9},{9,17},... | collective-permute-start | bytes 884744 | tf_op jit(solution)/shard_map/ppermute | solution.py:22
  29.1 2.6 %copy.60 = bf16[2048,384]{0,1:T(8,128)(2,1)} copy(bf16[2048,384]{1,0:T(8,128)(2,1)} %param.22) | data formatting | bytes 3145728 | tf_op args[5]
  31.8 3.2 %fusion.59 = f32[256,2,192]{0,2,1:T(8,128)} fusion(bf16[2,192,2048]{2,1,0:T(8,128)(2,1)} %bitcast.158, f32[2048]{0:T(1024)S(1)} %copy-done.19, f32[256]{0:T(256)S(1)} %add_rsqrt_fusion.1, bf16[2,256,2048]{2,1,0:T(8,128)(2,1)} %param.17, s32[]{:T(128)S(6)} %select_n.140), kind=kOutput, calls=%fused_computation.47 | convolution fusion | flops 404750336 | bytes 3023876 | tf_op jit(solution)/shard_map/dot_general | solution.py:129
  53.5 4.2 %fusion.55 = bf16[256,2,128]{0,2,1:T(8,128)(2,1)} fusion(bf16[1280,2,256]{0,2,1:T(8,128)(2,1)} %bitcast.160, f32[2,256,1280]{2,1,0:T(8,128)} %copy-done.2, pred[256,1280]{1,0:T(8,128)(4,1)S(1)} %copy-done.6, f32[256,2]{0,1:T(2,128)S(1)} %bitcast.171), kind=kOutput, calls=%fused_computation.45 | convolution fusion | flops 170526464 | bytes 6686720 | tf_op jit(solution)/shard_map/hqk,khd->hqd/dot_general | solution.py:174
  69.0 2.6 %collective-permute-start.8 = (bf16[32,2048]{1,0:T(8,128)(2,1)S(1)}, bf16[32,2048]{1,0:T(8,128)(2,1)S(1)}, u32[]{:S(2)}, u32[]{:S(2)}) collective-permute-start(bf16[32,2048]{1,0:T(8,128)(2,1)S(1)} %get-tuple-element.19), channel_id=1, source_target_pairs={{0,5},{1,6},{2,7},{3,0},{4,1},{5,2},{6,3},{7,4},{8,13},{9,14},{10,... | collective-permute-start | bytes 393224 | tf_op jit(solution)/shard_map/ppermute | solution.py:37
  74.8 3.8 %collective-permute-done.7 = bf16[32,2048]{1,0:T(8,128)(2,1)S(1)} collective-permute-done((bf16[32,2048]{1,0:T(8,128)(2,1)}, bf16[32,2048]{1,0:T(8,128)(2,1)S(1)}, u32[]{:S(2)}, u32[]{:S(2)}) %collective-permute-start.7) | collective-permute-done | bytes 131104 | tf_op jit(solution)/shard_map/ppermute | solution.py:37
  90.0 2.3 %gather_fusion = bf16[256,2048]{1,0:T(8,128)(2,1)} fusion(bf16[33,2048]{1,0:T(8,128)(2,1)S(1)} %concatenate.28, s32[1024]{0:T(1024)S(1)} %pad_clamp_fusion.1), kind=kCustom, calls=%fused_computation | custom fusion | bytes 2098176 | tf_op jit(solution)/shard_map/gather | solution.py:207
  92.3 2.3 %reshape.345 = bf16[64,1,4,2048]{3,2,0,1:T(4,128)(2,1)} reshape(bf16[256,2048]{1,0:T(8,128)(2,1)} %gather_fusion) | data formatting | bytes 2097152 | tf_op jit(solution)/shard_map/reshape | solution.py:207
  94.6 5.4 %all-to-all-start = ((bf16[64,1,4,2048]{3,2,1,0:T(4,128)(2,1)}), bf16[64,1,4,2048]{3,2,1,0:T(4,128)(2,1)}, u32[]{:S(2)}, u32[]{:S(2)}) async-start(bf16[64,1,4,2048]{3,2,1,0:T(4,128)(2,1)} %bitcast.157), calls=%async_computation | async-start | bytes 2097152 | tf_op jit(solution)/shard_map/all_to_all | solution.py:208
  100.0 2.7 %collective-permute-start.16 = (bf16[32,2048]{1,0:T(8,128)(2,1)}, bf16[32,2048]{1,0:T(8,128)(2,1)S(1)}, u32[]{:S(2)}, u32[]{:S(2)}) collective-permute-start(bf16[32,2048]{1,0:T(8,128)(2,1)} %get-tuple-element.6), channel_id=1, source_target_pairs={{0,6},{1,7},{2,0},{3,1},{4,2},{5,3},{6,4},{7,5},{8,14},{9,15},{10,... | collective-permute-start | bytes 393224 | tf_op jit(solution)/shard_map/ppermute | solution.py:46
  111.2 4.4 %collective-permute-done.16 = bf16[32,2048]{1,0:T(8,128)(2,1)S(1)} collective-permute-done((bf16[32,2048]{1,0:T(8,128)(2,1)}, bf16[32,2048]{1,0:T(8,128)(2,1)S(1)}, u32[]{:S(2)}, u32[]{:S(2)}) %collective-permute-start.16) | collective-permute-done | bytes 131104 | tf_op jit(solution)/shard_map/ppermute | solution.py:46
  118.5 2.7 %fusion.122 = f32[256,256]{1,0:T(8,128)} fusion(bf16[256,2048]{1,0:T(8,128)(2,1)} %constant_dynamic-update-slice_fusion.5, bf16[2048,256]{1,0:T(8,128)(2,1)} %param.28), kind=kOutput, calls=%fused_computation.169 | convolution fusion | flops 268435456 | bytes 2359296 | tf_op jit(solution)/shard_map/dot_general | solution.py:188
  121.1 5.0 %fusion.34 = f32[64,1,4,768]{3,0,2,1:T(8,128)} fusion(bf16[1,2048,768]{2,1,0:T(8,128)(2,1)} %param.31, bf16[64,1,4,2048]{3,2,1,0:T(4,128)(2,1)} %all-to-all-done), kind=kOutput, calls=%fused_computation.38 | convolution fusion | flops 805306368 | bytes 4980736 | tf_op jit(solution)/shard_map/sjkd,jdf->sjkf/dot_general | solution.py:209
  126.1 5.9 %fusion.21 = bf16[64,1,4,2048]{3,0,2,1:T(8,128)(2,1)} fusion(bf16[1,768,2048]{2,1,0:T(8,128)(2,1)S(1)} %copy-done, bf16[1,2048,768]{2,1,0:T(8,128)(2,1)} %param.32, bf16[64,1,4,2048]{3,2,1,0:T(4,128)(2,1)} %all-to-all-done, f32[64,1,4,768]{3,0,2,1:T(8,128)} %fusion.34), kind=kOutput, calls=%fused_computation.25 | convolution fusion | flops 1612316672 | bytes 9175040 | tf_op jit(solution)/shard_map/sjkf,jfd->sjkd/dot_general | solution.py:212
  132.1 3.0 %copy.70 = bf16[64,1,4,2048]{3,2,1,0:T(4,128)(2,1)} copy(bf16[64,1,4,2048]{3,0,2,1:T(8,128)(2,1)} %fusion.21) | data formatting | bytes 2097152 | tf_op jit(solution)/shard_map/convert_element_type | solution.py:214
  135.1 9.4 %all-to-all-start.1 = ((bf16[64,1,4,2048]{3,2,1,0:T(4,128)(2,1)}), bf16[64,1,4,2048]{3,2,1,0:T(4,128)(2,1)}, u32[]{:S(2)}, u32[]{:S(2)}) async-start(bf16[64,1,4,2048]{3,2,1,0:T(4,128)(2,1)} %copy.70), calls=%async_computation.1 | async-start | bytes 2097152 | tf_op jit(solution)/shard_map/all_to_all | solution.py:215
  144.5 4.2 %convolution_convert_fusion.1 = bf16[256,2048]{1,0:T(8,128)(2,1)} fusion(bf16[256,2048]{1,0:T(8,128)(2,1)} %param.30, f32[256,256]{1,0:T(8,128)} %fusion.122, bf16[256,2048]{1,0:T(8,128)(2,1)} %constant_dynamic-update-slice_fusion.5, bf16[2048,256]{1,0:T(8,128)(2,1)} %param.29), kind=kOutput, calls=%fused_computation.22 | convolution fusion | flops 537788416 | bytes 4456448 | tf_op jit(solution)/shard_map/dot_general | solution.py:192
  157.9 5.0 %all-to-all-done.1 = bf16[64,1,4,2048]{3,2,1,0:T(4,128)(2,1)} async-done(((bf16[64,1,4,2048]{3,2,1,0:T(4,128)(2,1)}), bf16[64,1,4,2048]{3,2,1,0:T(4,128)(2,1)}, u32[]{:S(2)}, u32[]{:S(2)}) %all-to-all-start.1) | async-done | bytes 1048608 | tf_op jit(solution)/shard_map/all_to_all | solution.py:215
  165.1 4.2 %gather_fusion.1 = bf16[192,2048]{1,0:T(8,128)(2,1)} fusion(bf16[256,2048]{1,0:T(8,128)(2,1)} %reshape.351, s32[1024]{0:T(1024)S(1)} %pad_clamp_fusion), kind=kCustom, calls=%fused_computation.1 | custom fusion | bytes 1573632 | tf_op jit(solution)/shard_map/gather | solution.py:216
  169.3 2.5 %reshape.356 = f32[32,6,2048]{2,1,0:T(8,128)} reshape(bf16[192,2048]{1,0:T(8,128)(2,1)} %gather_fusion.1) | data formatting | bytes 2359296 | tf_op jit(solution)/shard_map/convert_element_type | solution.py:217
  174.2 2.3 %multiply_reduce_fusion = f32[32,2048]{1,0:T(8,128)S(1)} fusion(f32[32,6,2048]{2,1,0:T(8,128)} %reshape.356, f32[32,6]{1,0:T(8,128)S(1)} %bitcast.165), kind=kLoop, calls=%fused_computation.31 | loop fusion | flops 720896 | bytes 1835776 | tf_op jit(solution)/shard_map/reduce_sum | solution.py:217
  (151 shorter events, 83.9 us)
Async XLA Ops:
  10.1 34.6 %collective-permute-start = (bf16[256,576]{0,1:T(8,128)(2,1)}, bf16[256,576]{0,1:T(8,128)(2,1)}, u32[]{:S(2)}, u32[]{:S(2)}) collective-permute-start(bf16[256,576]{0,1:T(8,128)(2,1)} %pad_maximum_fusion), channel_id=1, source_target_pairs={{0,32},{8,40},{16,48},{24,56},{1,33},{9,41},{17,49},{25,57},{2,34}... | collective-permute-start | bytes 884744 | tf_op jit(solution)/shard_map/ppermute | solution.py:22
  16.4 29.4 %collective-permute-start.1 = (bf16[256,576]{0,1:T(8,128)(2,1)}, bf16[256,576]{0,1:T(8,128)(2,1)}, u32[]{:S(2)}, u32[]{:S(2)}) collective-permute-start(bf16[256,576]{0,1:T(8,128)(2,1)} %pad_maximum_fusion), channel_id=1, source_target_pairs={{0,24},{8,32},{16,40},{24,48},{32,56},{1,25},{9,33},{17,41},{25,49... | collective-permute-start | bytes 884744 | tf_op jit(solution)/shard_map/ppermute | solution.py:22
  22.7 24.0 %collective-permute-start.2 = (bf16[256,576]{0,1:T(8,128)(2,1)}, bf16[256,576]{0,1:T(8,128)(2,1)}, u32[]{:S(2)}, u32[]{:S(2)}) collective-permute-start(bf16[256,576]{0,1:T(8,128)(2,1)} %pad_maximum_fusion), channel_id=1, source_target_pairs={{0,16},{8,24},{16,32},{24,40},{32,48},{40,56},{1,17},{9,25},{17,33... | collective-permute-start | bytes 884744 | tf_op jit(solution)/shard_map/ppermute | solution.py:22
  24.7 23.0 %collective-permute-start.3 = (bf16[256,576]{0,1:T(8,128)(2,1)}, bf16[256,576]{0,1:T(8,128)(2,1)}, u32[]{:S(2)}, u32[]{:S(2)}) collective-permute-start(bf16[256,576]{0,1:T(8,128)(2,1)} %pad_maximum_fusion), channel_id=1, source_target_pairs={{0,8},{8,16},{16,24},{24,32},{32,40},{40,48},{48,56},{1,9},{9,17},... | collective-permute-start | bytes 884744 | tf_op jit(solution)/shard_map/ppermute | solution.py:22
  62.8 8.9 %collective-permute-start.4 = (bf16[32,2048]{1,0:T(8,128)(2,1)}, bf16[32,2048]{1,0:T(8,128)(2,1)}, u32[]{:S(2)}, u32[]{:S(2)}) collective-permute-start(bf16[32,2048]{1,0:T(8,128)(2,1)} %get-tuple-element.16), channel_id=1, source_target_pairs={{0,1},{1,2},{2,3},{3,4},{4,5},{5,6},{6,7},{7,0},{8,9},{9,10},{10,1... | collective-permute-start | bytes 393224 | tf_op jit(solution)/shard_map/ppermute | solution.py:37
  64.8 7.8 %collective-permute-start.5 = (bf16[32,2048]{1,0:T(8,128)(2,1)}, bf16[32,2048]{1,0:T(8,128)(2,1)S(1)}, u32[]{:S(2)}, u32[]{:S(2)}) collective-permute-start(bf16[32,2048]{1,0:T(8,128)(2,1)} %get-tuple-element.22), channel_id=1, source_target_pairs={{0,2},{1,3},{2,4},{3,5},{4,6},{5,7},{6,0},{7,1},{8,10},{9,11},{10,... | collective-permute-start | bytes 393224 | tf_op jit(solution)/shard_map/ppermute | solution.py:37
  66.1 8.7 %collective-permute-start.6 = (bf16[32,2048]{1,0:T(8,128)(2,1)}, bf16[32,2048]{1,0:T(8,128)(2,1)S(1)}, u32[]{:S(2)}, u32[]{:S(2)}) collective-permute-start(bf16[32,2048]{1,0:T(8,128)(2,1)} %get-tuple-element.21), channel_id=1, source_target_pairs={{0,3},{1,4},{2,5},{3,6},{4,7},{5,0},{6,1},{7,2},{8,11},{9,12},{10,... | collective-permute-start | bytes 393224 | tf_op jit(solution)/shard_map/ppermute | solution.py:37
  68.2 10.3 %collective-permute-start.7 = (bf16[32,2048]{1,0:T(8,128)(2,1)}, bf16[32,2048]{1,0:T(8,128)(2,1)S(1)}, u32[]{:S(2)}, u32[]{:S(2)}) collective-permute-start(bf16[32,2048]{1,0:T(8,128)(2,1)} %get-tuple-element.20), channel_id=1, source_target_pairs={{0,4},{1,5},{2,6},{3,7},{4,0},{5,1},{6,2},{7,3},{8,12},{9,13},{10,... | collective-permute-start | bytes 393224 | tf_op jit(solution)/shard_map/ppermute | solution.py:37
  69.0 10.5 %collective-permute-start.8 = (bf16[32,2048]{1,0:T(8,128)(2,1)S(1)}, bf16[32,2048]{1,0:T(8,128)(2,1)S(1)}, u32[]{:S(2)}, u32[]{:S(2)}) collective-permute-start(bf16[32,2048]{1,0:T(8,128)(2,1)S(1)} %get-tuple-element.19), channel_id=1, source_target_pairs={{0,5},{1,6},{2,7},{3,0},{4,1},{5,2},{6,3},{7,4},{8,13},{9,14},{10,... | collective-permute-start | bytes 393224 | tf_op jit(solution)/shard_map/ppermute | solution.py:37
  71.6 8.2 %collective-permute-start.9 = (bf16[32,2048]{1,0:T(8,128)(2,1)S(1)}, bf16[32,2048]{1,0:T(8,128)(2,1)S(1)}, u32[]{:S(2)}, u32[]{:S(2)}) collective-permute-start(bf16[32,2048]{1,0:T(8,128)(2,1)S(1)} %get-tuple-element.18), channel_id=1, source_target_pairs={{0,6},{1,7},{2,0},{3,1},{4,2},{5,3},{6,4},{7,5},{8,14},{9,15},{10,... | collective-permute-start | bytes 393224 | tf_op jit(solution)/shard_map/ppermute | solution.py:37
  82.0 18.0 %collective-permute-start.11 = (bf16[32,2048]{1,0:T(8,128)(2,1)}, bf16[32,2048]{1,0:T(8,128)(2,1)}, u32[]{:S(2)}, u32[]{:S(2)}) collective-permute-start(bf16[32,2048]{1,0:T(8,128)(2,1)} %get-tuple-element.6), channel_id=1, source_target_pairs={{0,1},{1,2},{2,3},{3,4},{4,5},{5,6},{6,7},{7,0},{8,9},{9,10},{10,1... | collective-permute-start | bytes 393224 | tf_op jit(solution)/shard_map/ppermute | solution.py:46
  82.7 21.5 %collective-permute-start.12 = (bf16[32,2048]{1,0:T(8,128)(2,1)}, bf16[32,2048]{1,0:T(8,128)(2,1)}, u32[]{:S(2)}, u32[]{:S(2)}) collective-permute-start(bf16[32,2048]{1,0:T(8,128)(2,1)} %get-tuple-element.6), channel_id=1, source_target_pairs={{0,2},{1,3},{2,4},{3,5},{4,6},{5,7},{6,0},{7,1},{8,10},{9,11},{10,... | collective-permute-start | bytes 393224 | tf_op jit(solution)/shard_map/ppermute | solution.py:46
  84.4 22.1 %collective-permute-start.13 = (bf16[32,2048]{1,0:T(8,128)(2,1)}, bf16[32,2048]{1,0:T(8,128)(2,1)}, u32[]{:S(2)}, u32[]{:S(2)}) collective-permute-start(bf16[32,2048]{1,0:T(8,128)(2,1)} %get-tuple-element.6), channel_id=1, source_target_pairs={{0,3},{1,4},{2,5},{3,6},{4,7},{5,0},{6,1},{7,2},{8,11},{9,12},{10,... | collective-permute-start | bytes 393224 | tf_op jit(solution)/shard_map/ppermute | solution.py:46
  86.2 21.8 %collective-permute-start.14 = (bf16[32,2048]{1,0:T(8,128)(2,1)}, bf16[32,2048]{1,0:T(8,128)(2,1)}, u32[]{:S(2)}, u32[]{:S(2)}) collective-permute-start(bf16[32,2048]{1,0:T(8,128)(2,1)} %get-tuple-element.6), channel_id=1, source_target_pairs={{0,4},{1,5},{2,6},{3,7},{4,0},{5,1},{6,2},{7,3},{8,12},{9,13},{10,... | collective-permute-start | bytes 393224 | tf_op jit(solution)/shard_map/ppermute | solution.py:46
  86.8 22.8 %collective-permute-start.15 = (bf16[32,2048]{1,0:T(8,128)(2,1)}, bf16[32,2048]{1,0:T(8,128)(2,1)}, u32[]{:S(2)}, u32[]{:S(2)}) collective-permute-start(bf16[32,2048]{1,0:T(8,128)(2,1)} %get-tuple-element.6), channel_id=1, source_target_pairs={{0,5},{1,6},{2,7},{3,0},{4,1},{5,2},{6,3},{7,4},{8,13},{9,14},{10,... | collective-permute-start | bytes 393224 | tf_op jit(solution)/shard_map/ppermute | solution.py:46
  94.6 26.6 %all-to-all-start = ((bf16[64,1,4,2048]{3,2,1,0:T(4,128)(2,1)}), bf16[64,1,4,2048]{3,2,1,0:T(4,128)(2,1)}, u32[]{:S(2)}, u32[]{:S(2)}) async-start(bf16[64,1,4,2048]{3,2,1,0:T(4,128)(2,1)} %bitcast.157), calls=%async_computation | async-start | bytes 2097152 | tf_op jit(solution)/shard_map/all_to_all | solution.py:208
  100.0 15.6 %collective-permute-start.16 = (bf16[32,2048]{1,0:T(8,128)(2,1)}, bf16[32,2048]{1,0:T(8,128)(2,1)S(1)}, u32[]{:S(2)}, u32[]{:S(2)}) collective-permute-start(bf16[32,2048]{1,0:T(8,128)(2,1)} %get-tuple-element.6), channel_id=1, source_target_pairs={{0,6},{1,7},{2,0},{3,1},{4,2},{5,3},{6,4},{7,5},{8,14},{9,15},{10,... | collective-permute-start | bytes 393224 | tf_op jit(solution)/shard_map/ppermute | solution.py:46
  104.2 13.6 %collective-permute-start.17 = (bf16[32,2048]{1,0:T(8,128)(2,1)}, bf16[32,2048]{1,0:T(8,128)(2,1)S(1)}, u32[]{:S(2)}, u32[]{:S(2)}) collective-permute-start(bf16[32,2048]{1,0:T(8,128)(2,1)} %get-tuple-element.6), channel_id=1, source_target_pairs={{0,7},{1,0},{2,1},{3,2},{4,3},{5,4},{6,5},{7,6},{8,15},{9,8},{10,9... | collective-permute-start | bytes 393224 | tf_op jit(solution)/shard_map/ppermute | solution.py:46
  135.1 27.9 %all-to-all-start.1 = ((bf16[64,1,4,2048]{3,2,1,0:T(4,128)(2,1)}), bf16[64,1,4,2048]{3,2,1,0:T(4,128)(2,1)}, u32[]{:S(2)}, u32[]{:S(2)}) async-start(bf16[64,1,4,2048]{3,2,1,0:T(4,128)(2,1)} %copy.70), calls=%async_computation.1 | async-start | bytes 2097152 | tf_op jit(solution)/shard_map/all_to_all | solution.py:215
  150.8 21.0 %collective-permute-start.18 = (bf16[32,2048]{1,0:T(8,128)(2,1)}, bf16[32,2048]{1,0:T(8,128)(2,1)}, u32[]{:S(2)}, u32[]{:S(2)}) collective-permute-start(bf16[32,2048]{1,0:T(8,128)(2,1)} %get-tuple-element.9), channel_id=1, source_target_pairs={{0,1},{1,2},{2,3},{3,4},{4,5},{5,6},{6,7},{7,0},{8,9},{9,10},{10,1... | collective-permute-start | bytes 393224 | tf_op jit(solution)/shard_map/ppermute | solution.py:37
  152.5 21.0 %collective-permute-start.19 = (bf16[32,2048]{1,0:T(8,128)(2,1)}, bf16[32,2048]{1,0:T(8,128)(2,1)}, u32[]{:S(2)}, u32[]{:S(2)}) collective-permute-start(bf16[32,2048]{1,0:T(8,128)(2,1)} %get-tuple-element.15), channel_id=1, source_target_pairs={{0,2},{1,3},{2,4},{3,5},{4,6},{5,7},{6,0},{7,1},{8,10},{9,11},{10,... | collective-permute-start | bytes 393224 | tf_op jit(solution)/shard_map/ppermute | solution.py:37
  153.8 22.8 %collective-permute-start.20 = (bf16[32,2048]{1,0:T(8,128)(2,1)}, bf16[32,2048]{1,0:T(8,128)(2,1)}, u32[]{:S(2)}, u32[]{:S(2)}) collective-permute-start(bf16[32,2048]{1,0:T(8,128)(2,1)} %get-tuple-element.14), channel_id=1, source_target_pairs={{0,3},{1,4},{2,5},{3,6},{4,7},{5,0},{6,1},{7,2},{8,11},{9,12},{10,... | collective-permute-start | bytes 393224 | tf_op jit(solution)/shard_map/ppermute | solution.py:37
  155.4 21.1 %collective-permute-start.21 = (bf16[32,2048]{1,0:T(8,128)(2,1)}, bf16[32,2048]{1,0:T(8,128)(2,1)}, u32[]{:S(2)}, u32[]{:S(2)}) collective-permute-start(bf16[32,2048]{1,0:T(8,128)(2,1)} %get-tuple-element.13), channel_id=1, source_target_pairs={{0,4},{1,5},{2,6},{3,7},{4,0},{5,1},{6,2},{7,3},{8,12},{9,13},{10,... | collective-permute-start | bytes 393224 | tf_op jit(solution)/shard_map/ppermute | solution.py:37
  156.0 20.5 %collective-permute-start.22 = (bf16[32,2048]{1,0:T(8,128)(2,1)}, bf16[32,2048]{1,0:T(8,128)(2,1)}, u32[]{:S(2)}, u32[]{:S(2)}) collective-permute-start(bf16[32,2048]{1,0:T(8,128)(2,1)} %get-tuple-element.12), channel_id=1, source_target_pairs={{0,5},{1,6},{2,7},{3,0},{4,1},{5,2},{6,3},{7,4},{8,13},{9,14},{10,... | collective-permute-start | bytes 393224 | tf_op jit(solution)/shard_map/ppermute | solution.py:37
  (23 other events, 309.2 us)

commit v11 on v4

--- a/solution.py
+++ b/solution.py
@@ -126,11 +126,23 @@
     query_index = query_start + jnp.arange(tok_dev, dtype=jnp.int32)
 
     normed = rms_scale(rows_in, attn_gain).astype(jnp.bfloat16)
-    queries = jnp.dot(normed, w_query, preferred_element_type=jnp.float32).reshape(
-        tok_dev, local_heads, qk_width
-    )
-    queries = jnp.concatenate(
-        [queries[..., :NOPE], rotary(queries[..., NOPE:], query_pos)], axis=-1
+    queries_t = jnp.einsum(
+        "dc,qd->cq", w_query, normed, preferred_element_type=jnp.float32
+    ).reshape(local_heads, qk_width, tok_dev)
+    half_rope = ROPE // 2
+    frequency = 10000.0 ** (-jnp.arange(half_rope, dtype=jnp.float32) / half_rope)
+    angles = frequency[:, None] * query_pos.astype(jnp.float32)[None, :]
+    cosine = jnp.cos(angles)[None]
+    sine_part = jnp.sin(angles)[None]
+    lead_half = queries_t[:, NOPE : NOPE + half_rope]
+    tail_half = queries_t[:, NOPE + half_rope :]
+    queries_t = jnp.concatenate(
+        [
+            queries_t[:, :NOPE],
+            lead_half * cosine - tail_half * sine_part,
+            lead_half * sine_part + tail_half * cosine,
+        ],
+        axis=1,
     ).astype(jnp.bfloat16)
     compressed = jnp.dot(normed, w_kv_down, preferred_element_type=jnp.float32)
     latent = rms_scale(compressed[:, :LATENT], latent_gain).astype(jnp.bfloat16)
@@ -151,11 +163,11 @@
     )
     rope_keys = kv_rows[:, LATENT:]
     scores = jnp.einsum(
-        "qhd,khd->hqk", queries[..., :NOPE], expanded[..., :NOPE],
+        "hdq,khd->hqk", queries_t[:, :NOPE], expanded[..., :NOPE],
         preferred_element_type=jnp.float32,
     )
     scores = scores + jnp.einsum(
-        "qhd,kd->hqk", queries[..., NOPE:], rope_keys, preferred_element_type=jnp.float32
+        "hdq,kd->hqk", queries_t[:, NOPE:], rope_keys, preferred_element_type=jnp.float32
     )
     scores = scores * score_scale
     key_index = key_start + jnp.arange(key_count, dtype=jnp.int32)

time: 168 us -> 168 us (level)
    unnamed x60 -> x59, local copies, waits for them, and re-layouts: 19.1 us -> 16.3 us
    dot_general x0 -> x1, local copies, waits for them, and re-layouts: none -> 1.91 us  [shards(): jnp.einsum('dc,qd->cq', w_query, normed, preferred_element_type=jnp.float32)]
where the time goes in v11:
time: 168 us; the launch traced here: 167 us
  starting transfers between devices  66.9 us (40%)
  matrix products  34.8 us (21%)
  local copies, waits for them, and re-layouts  29.8 us (18%)
  waiting for transfers between devices  21.8 us (13%)
  other arithmetic  12.6 us (8%)
    ppermute x14, starting transfers between devices, summed_over(): lax.ppermute(piece_for(steps), axis, [(i, (i + steps) % count) for i in r...  19.5 us
    ppermute x4, starting transfers between devices, passed_along(): lax.ppermute(value, axis, [(source, source + steps) for source in range(i...  17.7 us
    unnamed x59, local copies, waits for them, and re-layouts  16.3 us
    ppermute x14, waiting for transfers between devices, summed_over(): lax.ppermute(piece_for(steps), axis, [(i, (i + steps) % count) for i in r...  15.8 us
    all_to_all x1, starting transfers between devices, shards(): lax.all_to_all(outgoing, ('tok', 'mdl'), split_axis=0, concat_axis=0, til...  10.2 us
    ppermute x7, starting transfers between devices, gathered_over(): lax.ppermute(block, axis, [(i, (i + steps) % count) for i in range(count)])  10.2 us
    all_to_all x1, starting transfers between devices, shards(): lax.all_to_all(produced, ('tok', 'mdl'), split_axis=0, concat_axis=0, til...  9.28 us
    ppermute x7, waiting for transfers between devices, gathered_over(): lax.ppermute(block, axis, [(i, (i + steps) % count) for i in range(count)])  6.04 us
  transfers between devices with their start and end apart: 27, of which 7 were waited for; matrix products, arithmetic and copies ran while one was open for 21% of the time, Pallas kernels for 0%

profile of v11, /device:TPU:1, one launch (start us, length us, event | category | flops | bytes accessed | tf_op | source)
XLA Modules:
  0.0 166.6 jit_solution(4629691312252953636)
XLA Ops:
  2.7 2.9 %fusion.86 = f32[256,576]{0,1:T(8,128)S(1)} fusion(bf16[2048,576]{0,1:T(8,128)(2,1)} %param.23, f32[2048]{0:T(1024)} %param.21, f32[256]{0:T(256)S(1)} %add_rsqrt_fusion.1, bf16[2,256,2048]{2,1,0:T(8,128)(2,1)} %param.17, s32[]{:T(128)S(6)} %select_n.97), kind=kOutput, calls=%fused_computation.78 | convolution fusion | flops 606076928 | bytes 4006916 | tf_op jit(solution)/shard_map/dot_general | solution.py:147
  9.5 6.2 %collective-permute-start = (bf16[256,576]{0,1:T(8,128)(2,1)}, bf16[256,576]{0,1:T(8,128)(2,1)}, u32[]{:S(2)}, u32[]{:S(2)}) collective-permute-start(bf16[256,576]{0,1:T(8,128)(2,1)} %pad_maximum_fusion), channel_id=1, source_target_pairs={{0,32},{8,40},{16,48},{24,56},{1,33},{9,41},{17,49},{25,57},{2,34}... | collective-permute-start | bytes 884744 | tf_op jit(solution)/shard_map/ppermute | solution.py:22
  15.7 6.4 %collective-permute-start.1 = (bf16[256,576]{0,1:T(8,128)(2,1)}, bf16[256,576]{0,1:T(8,128)(2,1)}, u32[]{:S(2)}, u32[]{:S(2)}) collective-permute-start(bf16[256,576]{0,1:T(8,128)(2,1)} %pad_maximum_fusion), channel_id=1, source_target_pairs={{0,24},{8,32},{16,40},{24,48},{32,56},{1,25},{9,33},{17,41},{25,49... | collective-permute-start | bytes 884744 | tf_op jit(solution)/shard_map/ppermute | solution.py:22
  24.1 3.1 %collective-permute-start.3 = (bf16[256,576]{0,1:T(8,128)(2,1)}, bf16[256,576]{0,1:T(8,128)(2,1)}, u32[]{:S(2)}, u32[]{:S(2)}) collective-permute-start(bf16[256,576]{0,1:T(8,128)(2,1)} %pad_maximum_fusion), channel_id=1, source_target_pairs={{0,8},{8,16},{16,24},{24,32},{32,40},{40,48},{48,56},{1,9},{9,17},... | collective-permute-start | bytes 884744 | tf_op jit(solution)/shard_map/ppermute | solution.py:22
  27.4 3.2 %convolution_bitcast_fusion.1 = f32[384,256]{0,1:T(8,128)} fusion(bf16[2048,384]{1,0:T(8,128)(2,1)} %param.22, f32[2048]{0:T(1024)S(1)} %copy-done.23, f32[256]{0:T(256)S(1)} %add_rsqrt_fusion.1, bf16[2,256,2048]{2,1,0:T(8,128)(2,1)} %param.17, s32[]{:T(128)S(6)} %select_n.97), kind=kOutput, calls=%fused_computation.38 | convolution fusion | flops 404750336 | bytes 3023876 | tf_op jit(solution)/shard_map/dc,qd->cq/dot_general | solution.py:129
  45.8 3.7 %fusion.52 = bf16[256,2,128]{0,2,1:T(8,128)(2,1)S(1)} fusion(bf16[1280,2,256]{0,2,1:T(8,128)(2,1)} %bitcast.168, f32[2,256,1280]{2,1,0:T(8,128)} %copy-done.2, pred[256,1280]{1,0:T(8,128)(4,1)} %and_and_fusion, f32[256,2]{0,1:T(2,128)S(1)} %bitcast.176), kind=kOutput, calls=%fused_computation.41 | convolution fusion | flops 170526464 | bytes 6686720 | tf_op jit(solution)/shard_map/hqk,khd->hqd/dot_general | solution.py:186
  57.5 2.1 %collective-permute-start.6 = (bf16[32,2048]{1,0:T(8,128)(2,1)}, bf16[32,2048]{1,0:T(8,128)(2,1)S(1)}, u32[]{:S(2)}, u32[]{:S(2)}) collective-permute-start(bf16[32,2048]{1,0:T(8,128)(2,1)} %get-tuple-element.21), channel_id=1, source_target_pairs={{0,3},{1,4},{2,5},{3,6},{4,7},{5,0},{6,1},{7,2},{8,11},{9,12},{10,... | collective-permute-start | bytes 393224 | tf_op jit(solution)/shard_map/ppermute | solution.py:37
  60.4 2.6 %collective-permute-start.8 = (bf16[32,2048]{1,0:T(8,128)(2,1)}, bf16[32,2048]{1,0:T(8,128)(2,1)S(1)}, u32[]{:S(2)}, u32[]{:S(2)}) collective-permute-start(bf16[32,2048]{1,0:T(8,128)(2,1)} %get-tuple-element.19), channel_id=1, source_target_pairs={{0,5},{1,6},{2,7},{3,0},{4,1},{5,2},{6,3},{7,4},{8,13},{9,14},{10,... | collective-permute-start | bytes 393224 | tf_op jit(solution)/shard_map/ppermute | solution.py:37
  63.0 2.3 %collective-permute-done.5 = bf16[32,2048]{1,0:T(8,128)(2,1)S(1)} collective-permute-done((bf16[32,2048]{1,0:T(8,128)(2,1)}, bf16[32,2048]{1,0:T(8,128)(2,1)S(1)}, u32[]{:S(2)}, u32[]{:S(2)}) %collective-permute-start.5) | collective-permute-done | bytes 131104 | tf_op jit(solution)/shard_map/ppermute | solution.py:37
  65.3 5.9 %collective-permute-done.6 = bf16[32,2048]{1,0:T(8,128)(2,1)S(1)} collective-permute-done((bf16[32,2048]{1,0:T(8,128)(2,1)}, bf16[32,2048]{1,0:T(8,128)(2,1)S(1)}, u32[]{:S(2)}, u32[]{:S(2)}) %collective-permute-start.6) | collective-permute-done | bytes 131104 | tf_op jit(solution)/shard_map/ppermute | solution.py:37
  78.5 2.1 %collective-permute-start.15 = (bf16[32,2048]{1,0:T(8,128)(2,1)S(1)}, bf16[32,2048]{1,0:T(8,128)(2,1)}, u32[]{:S(2)}, u32[]{:S(2)}) collective-permute-start(bf16[32,2048]{1,0:T(8,128)(2,1)S(1)} %get-tuple-element.6), channel_id=1, source_target_pairs={{0,5},{1,6},{2,7},{3,0},{4,1},{5,2},{6,3},{7,4},{8,13},{9,14},{10,... | collective-permute-start | bytes 393224 | tf_op jit(solution)/shard_map/ppermute | solution.py:46
  82.8 10.2 %all-to-all-start = ((bf16[64,1,4,2048]{3,2,1,0:T(4,128)(2,1)}), bf16[64,1,4,2048]{3,2,1,0:T(4,128)(2,1)}, u32[]{:S(2)}, u32[]{:S(2)}) async-start(bf16[64,1,4,2048]{3,2,1,0:T(4,128)(2,1)} %copy.85), calls=%async_computation | async-start | bytes 2097152 | tf_op jit(solution)/shard_map/all_to_all | solution.py:226
  93.0 2.6 %collective-permute-start.16 = (bf16[32,2048]{1,0:T(8,128)(2,1)S(1)}, bf16[32,2048]{1,0:T(8,128)(2,1)S(1)}, u32[]{:S(2)}, u32[]{:S(2)}) collective-permute-start(bf16[32,2048]{1,0:T(8,128)(2,1)S(1)} %get-tuple-element.6), channel_id=1, source_target_pairs={{0,6},{1,7},{2,0},{3,1},{4,2},{5,3},{6,4},{7,5},{8,14},{9,15},{10,... | collective-permute-start | bytes 393224 | tf_op jit(solution)/shard_map/ppermute | solution.py:46
  104.2 4.7 %collective-permute-done.16 = bf16[32,2048]{1,0:T(8,128)(2,1)S(1)} collective-permute-done((bf16[32,2048]{1,0:T(8,128)(2,1)S(1)}, bf16[32,2048]{1,0:T(8,128)(2,1)S(1)}, u32[]{:S(2)}, u32[]{:S(2)}) %collective-permute-start.16) | collective-permute-done | bytes 131104 | tf_op jit(solution)/shard_map/ppermute | solution.py:46
  113.5 5.0 %fusion.31 = f32[64,1,4,768]{3,0,2,1:T(8,128)} fusion(bf16[1,2048,768]{2,1,0:T(8,128)(2,1)} %param.31, bf16[64,1,4,2048]{3,2,1,0:T(4,128)(2,1)} %all-to-all-done), kind=kOutput, calls=%fused_computation.33 | convolution fusion | flops 805306368 | bytes 4980736 | tf_op jit(solution)/shard_map/sjkd,jdf->sjkf/dot_general | solution.py:227
  118.4 5.9 %fusion.20 = bf16[64,1,4,2048]{3,0,2,1:T(8,128)(2,1)} fusion(bf16[1,768,2048]{2,1,0:T(8,128)(2,1)S(1)} %copy-done, bf16[1,2048,768]{2,1,0:T(8,128)(2,1)} %param.32, bf16[64,1,4,2048]{3,2,1,0:T(4,128)(2,1)} %all-to-all-done, f32[64,1,4,768]{3,0,2,1:T(8,128)} %fusion.31), kind=kOutput, calls=%fused_computation.22 | convolution fusion | flops 1612316672 | bytes 9175040 | tf_op jit(solution)/shard_map/sjkf,jfd->sjkd/dot_general | solution.py:230
  124.4 3.0 %copy.87 = bf16[64,1,4,2048]{3,2,1,0:T(4,128)(2,1)} copy(bf16[64,1,4,2048]{3,0,2,1:T(8,128)(2,1)} %fusion.20) | data formatting | bytes 2097152 | tf_op jit(solution)/shard_map/convert_element_type | solution.py:232
  127.4 9.3 %all-to-all-start.1 = ((bf16[64,1,4,2048]{3,2,1,0:T(4,128)(2,1)}), bf16[64,1,4,2048]{3,2,1,0:T(4,128)(2,1)}, u32[]{:S(2)}, u32[]{:S(2)}) async-start(bf16[64,1,4,2048]{3,2,1,0:T(4,128)(2,1)} %copy.87), calls=%async_computation.1 | async-start | bytes 2097152 | tf_op jit(solution)/shard_map/all_to_all | solution.py:233
  136.7 4.1 %convolution_convert_fusion.1 = bf16[256,2048]{1,0:T(8,128)(2,1)} fusion(bf16[256,2048]{1,0:T(8,128)(2,1)} %param.30, f32[256,256]{1,0:T(8,128)S(1)} %fusion.134, bf16[256,2048]{1,0:T(8,128)(2,1)} %constant_dynamic-update-slice_fusion.5, bf16[2048,256]{1,0:T(8,128)(2,1)} %param.29), kind=kOutput, calls=%fused_computation.17 | convolution fusion | flops 537788416 | bytes 4456448 | tf_op jit(solution)/shard_map/dot_general | solution.py:204
  140.8 2.1 %fusion.130 = (bf16[32,2048]{1,0:T(8,128)(2,1)S(1)}, bf16[32,2048]{1,0:T(8,128)(2,1)S(1)}, bf16[32,2048]{1,0:T(8,128)(2,1)}, bf16[32,2048]{1,0:T(8,128)(2,1)}, b...) fusion(bf16[256,2048]{1,0:T(8,128)(2,1)} %convolution_convert_fusion.1), kind=kLoop, calls=%fused_computation.162 | loop fusion | bytes 1835008 | tf_op jit(solution)/shard_map/slice | solution.py:32
  149.8 3.1 %collective-permute-start.23 = (bf16[32,2048]{1,0:T(8,128)(2,1)}, bf16[32,2048]{1,0:T(8,128)(2,1)}, u32[]{:S(2)}, u32[]{:S(2)}) collective-permute-start(bf16[32,2048]{1,0:T(8,128)(2,1)} %get-tuple-element.11), channel_id=1, source_target_pairs={{0,6},{1,7},{2,0},{3,1},{4,2},{5,3},{6,4},{7,5},{8,14},{9,15},{10,... | collective-permute-start | bytes 393224 | tf_op jit(solution)/shard_map/ppermute | solution.py:37
  152.9 4.0 %collective-permute-done.19 = bf16[32,2048]{1,0:T(8,128)(2,1)S(1)} collective-permute-done((bf16[32,2048]{1,0:T(8,128)(2,1)S(1)}, bf16[32,2048]{1,0:T(8,128)(2,1)S(1)}, u32[]{:S(2)}, u32[]{:S(2)}) %collective-permute-start.19) | collective-permute-done | bytes 131104 | tf_op jit(solution)/shard_map/ppermute | solution.py:37
  159.1 3.0 %collective-permute-done.21 = bf16[32,2048]{1,0:T(8,128)(2,1)} collective-permute-done((bf16[32,2048]{1,0:T(8,128)(2,1)}, bf16[32,2048]{1,0:T(8,128)(2,1)}, u32[]{:S(2)}, u32[]{:S(2)}) %collective-permute-start.21) | collective-permute-done | bytes 131104 | tf_op jit(solution)/shard_map/ppermute | solution.py:37
  162.7 3.9 %fusion.95 = bf16[1,32,2048]{2,1,0:T(8,128)(2,1)} fusion(bf16[64,1,4,2048]{3,2,1,0:T(4,128)(2,1)} %all-to-all-done.1, f32[32,64,4]{0,2,1:T(4,128)S(1)} %bitcast.166, bf16[32,2048]{1,0:T(8,128)(2,1)} %collective-permute-done.24, bf16[32,2048]{1,0:T(8,128)(2,1)} %collective-permute-done.23, bf16[32,2048]{1,0:T(8,128)(2,1)} %collective-permute-done.22, ...), kind=kOutput, calls=%fused_computation.82 | convolution fusion | flops 202571776 | bytes 2392064 | tf_op jit(solution)/shard_map/rsjk,sjkd->rd/dot_general | solution.py:238
  (153 shorter events, 64.4 us)
Async XLA Ops:
  9.5 27.8 %collective-permute-start = (bf16[256,576]{0,1:T(8,128)(2,1)}, bf16[256,576]{0,1:T(8,128)(2,1)}, u32[]{:S(2)}, u32[]{:S(2)}) collective-permute-start(bf16[256,576]{0,1:T(8,128)(2,1)} %pad_maximum_fusion), channel_id=1, source_target_pairs={{0,32},{8,40},{16,48},{24,56},{1,33},{9,41},{17,49},{25,57},{2,34}... | collective-permute-start | bytes 884744 | tf_op jit(solution)/shard_map/ppermute | solution.py:22
  15.7 22.6 %collective-permute-start.1 = (bf16[256,576]{0,1:T(8,128)(2,1)}, bf16[256,576]{0,1:T(8,128)(2,1)}, u32[]{:S(2)}, u32[]{:S(2)}) collective-permute-start(bf16[256,576]{0,1:T(8,128)(2,1)} %pad_maximum_fusion), channel_id=1, source_target_pairs={{0,24},{8,32},{16,40},{24,48},{32,56},{1,25},{9,33},{17,41},{25,49... | collective-permute-start | bytes 884744 | tf_op jit(solution)/shard_map/ppermute | solution.py:22
  22.1 17.2 %collective-permute-start.2 = (bf16[256,576]{0,1:T(8,128)(2,1)}, bf16[256,576]{0,1:T(8,128)(2,1)}, u32[]{:S(2)}, u32[]{:S(2)}) collective-permute-start(bf16[256,576]{0,1:T(8,128)(2,1)} %pad_maximum_fusion), channel_id=1, source_target_pairs={{0,16},{8,24},{16,32},{24,40},{32,48},{40,56},{1,17},{9,25},{17,33... | collective-permute-start | bytes 884744 | tf_op jit(solution)/shard_map/ppermute | solution.py:22
  24.1 16.2 %collective-permute-start.3 = (bf16[256,576]{0,1:T(8,128)(2,1)}, bf16[256,576]{0,1:T(8,128)(2,1)}, u32[]{:S(2)}, u32[]{:S(2)}) collective-permute-start(bf16[256,576]{0,1:T(8,128)(2,1)} %pad_maximum_fusion), channel_id=1, source_target_pairs={{0,8},{8,16},{16,24},{24,32},{32,40},{40,48},{48,56},{1,9},{9,17},... | collective-permute-start | bytes 884744 | tf_op jit(solution)/shard_map/ppermute | solution.py:22
  54.6 8.3 %collective-permute-start.4 = (bf16[32,2048]{1,0:T(8,128)(2,1)}, bf16[32,2048]{1,0:T(8,128)(2,1)}, u32[]{:S(2)}, u32[]{:S(2)}) collective-permute-start(bf16[32,2048]{1,0:T(8,128)(2,1)} %get-tuple-element.16), channel_id=1, source_target_pairs={{0,1},{1,2},{2,3},{3,4},{4,5},{5,6},{6,7},{7,0},{8,9},{9,10},{10,1... | collective-permute-start | bytes 393224 | tf_op jit(solution)/shard_map/ppermute | solution.py:37
  56.2 9.2 %collective-permute-start.5 = (bf16[32,2048]{1,0:T(8,128)(2,1)}, bf16[32,2048]{1,0:T(8,128)(2,1)S(1)}, u32[]{:S(2)}, u32[]{:S(2)}) collective-permute-start(bf16[32,2048]{1,0:T(8,128)(2,1)} %get-tuple-element.22), channel_id=1, source_target_pairs={{0,2},{1,3},{2,4},{3,5},{4,6},{5,7},{6,0},{7,1},{8,10},{9,11},{10,... | collective-permute-start | bytes 393224 | tf_op jit(solution)/shard_map/ppermute | solution.py:37
  57.5 13.7 %collective-permute-start.6 = (bf16[32,2048]{1,0:T(8,128)(2,1)}, bf16[32,2048]{1,0:T(8,128)(2,1)S(1)}, u32[]{:S(2)}, u32[]{:S(2)}) collective-permute-start(bf16[32,2048]{1,0:T(8,128)(2,1)} %get-tuple-element.21), channel_id=1, source_target_pairs={{0,3},{1,4},{2,5},{3,6},{4,7},{5,0},{6,1},{7,2},{8,11},{9,12},{10,... | collective-permute-start | bytes 393224 | tf_op jit(solution)/shard_map/ppermute | solution.py:37
  59.6 11.6 %collective-permute-start.7 = (bf16[32,2048]{1,0:T(8,128)(2,1)}, bf16[32,2048]{1,0:T(8,128)(2,1)S(1)}, u32[]{:S(2)}, u32[]{:S(2)}) collective-permute-start(bf16[32,2048]{1,0:T(8,128)(2,1)} %get-tuple-element.20), channel_id=1, source_target_pairs={{0,4},{1,5},{2,6},{3,7},{4,0},{5,1},{6,2},{7,3},{8,12},{9,13},{10,... | collective-permute-start | bytes 393224 | tf_op jit(solution)/shard_map/ppermute | solution.py:37
  60.4 10.9 %collective-permute-start.8 = (bf16[32,2048]{1,0:T(8,128)(2,1)}, bf16[32,2048]{1,0:T(8,128)(2,1)S(1)}, u32[]{:S(2)}, u32[]{:S(2)}) collective-permute-start(bf16[32,2048]{1,0:T(8,128)(2,1)} %get-tuple-element.19), channel_id=1, source_target_pairs={{0,5},{1,6},{2,7},{3,0},{4,1},{5,2},{6,3},{7,4},{8,13},{9,14},{10,... | collective-permute-start | bytes 393224 | tf_op jit(solution)/shard_map/ppermute | solution.py:37
  63.0 8.2 %collective-permute-start.9 = (bf16[32,2048]{1,0:T(8,128)(2,1)S(1)}, bf16[32,2048]{1,0:T(8,128)(2,1)S(1)}, u32[]{:S(2)}, u32[]{:S(2)}) collective-permute-start(bf16[32,2048]{1,0:T(8,128)(2,1)S(1)} %get-tuple-element.18), channel_id=1, source_target_pairs={{0,6},{1,7},{2,0},{3,1},{4,2},{5,3},{6,4},{7,5},{8,14},{9,15},{10,... | collective-permute-start | bytes 393224 | tf_op jit(solution)/shard_map/ppermute | solution.py:37
  73.4 19.6 %collective-permute-start.11 = (bf16[32,2048]{1,0:T(8,128)(2,1)S(1)}, bf16[32,2048]{1,0:T(8,128)(2,1)}, u32[]{:S(2)}, u32[]{:S(2)}) collective-permute-start(bf16[32,2048]{1,0:T(8,128)(2,1)S(1)} %get-tuple-element.6), channel_id=1, source_target_pairs={{0,1},{1,2},{2,3},{3,4},{4,5},{5,6},{6,7},{7,0},{8,9},{9,10},{10,1... | collective-permute-start | bytes 393224 | tf_op jit(solution)/shard_map/ppermute | solution.py:46
  74.3 23.0 %collective-permute-start.12 = (bf16[32,2048]{1,0:T(8,128)(2,1)S(1)}, bf16[32,2048]{1,0:T(8,128)(2,1)}, u32[]{:S(2)}, u32[]{:S(2)}) collective-permute-start(bf16[32,2048]{1,0:T(8,128)(2,1)S(1)} %get-tuple-element.6), channel_id=1, source_target_pairs={{0,2},{1,3},{2,4},{3,5},{4,6},{5,7},{6,0},{7,1},{8,10},{9,11},{10,... | collective-permute-start | bytes 393224 | tf_op jit(solution)/shard_map/ppermute | solution.py:46
  76.0 23.5 %collective-permute-start.13 = (bf16[32,2048]{1,0:T(8,128)(2,1)S(1)}, bf16[32,2048]{1,0:T(8,128)(2,1)}, u32[]{:S(2)}, u32[]{:S(2)}) collective-permute-start(bf16[32,2048]{1,0:T(8,128)(2,1)S(1)} %get-tuple-element.6), channel_id=1, source_target_pairs={{0,3},{1,4},{2,5},{3,6},{4,7},{5,0},{6,1},{7,2},{8,11},{9,12},{10,... | collective-permute-start | bytes 393224 | tf_op jit(solution)/shard_map/ppermute | solution.py:46
  77.7 23.3 %collective-permute-start.14 = (bf16[32,2048]{1,0:T(8,128)(2,1)S(1)}, bf16[32,2048]{1,0:T(8,128)(2,1)}, u32[]{:S(2)}, u32[]{:S(2)}) collective-permute-start(bf16[32,2048]{1,0:T(8,128)(2,1)S(1)} %get-tuple-element.6), channel_id=1, source_target_pairs={{0,4},{1,5},{2,6},{3,7},{4,0},{5,1},{6,2},{7,3},{8,12},{9,13},{10,... | collective-permute-start | bytes 393224 | tf_op jit(solution)/shard_map/ppermute | solution.py:46
  78.5 24.1 %collective-permute-start.15 = (bf16[32,2048]{1,0:T(8,128)(2,1)S(1)}, bf16[32,2048]{1,0:T(8,128)(2,1)}, u32[]{:S(2)}, u32[]{:S(2)}) collective-permute-start(bf16[32,2048]{1,0:T(8,128)(2,1)S(1)} %get-tuple-element.6), channel_id=1, source_target_pairs={{0,5},{1,6},{2,7},{3,0},{4,1},{5,2},{6,3},{7,4},{8,13},{9,14},{10,... | collective-permute-start | bytes 393224 | tf_op jit(solution)/shard_map/ppermute | solution.py:46
  82.8 30.7 %all-to-all-start = ((bf16[64,1,4,2048]{3,2,1,0:T(4,128)(2,1)}), bf16[64,1,4,2048]{3,2,1,0:T(4,128)(2,1)}, u32[]{:S(2)}, u32[]{:S(2)}) async-start(bf16[64,1,4,2048]{3,2,1,0:T(4,128)(2,1)} %copy.85), calls=%async_computation | async-start | bytes 2097152 | tf_op jit(solution)/shard_map/all_to_all | solution.py:226
  93.0 15.8 %collective-permute-start.16 = (bf16[32,2048]{1,0:T(8,128)(2,1)S(1)}, bf16[32,2048]{1,0:T(8,128)(2,1)S(1)}, u32[]{:S(2)}, u32[]{:S(2)}) collective-permute-start(bf16[32,2048]{1,0:T(8,128)(2,1)S(1)} %get-tuple-element.6), channel_id=1, source_target_pairs={{0,6},{1,7},{2,0},{3,1},{4,2},{5,3},{6,4},{7,5},{8,14},{9,15},{10,... | collective-permute-start | bytes 393224 | tf_op jit(solution)/shard_map/ppermute | solution.py:46
  97.2 13.6 %collective-permute-start.17 = (bf16[32,2048]{1,0:T(8,128)(2,1)S(1)}, bf16[32,2048]{1,0:T(8,128)(2,1)S(1)}, u32[]{:S(2)}, u32[]{:S(2)}) collective-permute-start(bf16[32,2048]{1,0:T(8,128)(2,1)S(1)} %get-tuple-element.6), channel_id=1, source_target_pairs={{0,7},{1,0},{2,1},{3,2},{4,3},{5,4},{6,5},{7,6},{8,15},{9,8},{10,9... | collective-permute-start | bytes 393224 | tf_op jit(solution)/shard_map/ppermute | solution.py:46
  127.4 35.3 %all-to-all-start.1 = ((bf16[64,1,4,2048]{3,2,1,0:T(4,128)(2,1)}), bf16[64,1,4,2048]{3,2,1,0:T(4,128)(2,1)}, u32[]{:S(2)}, u32[]{:S(2)}) async-start(bf16[64,1,4,2048]{3,2,1,0:T(4,128)(2,1)} %copy.87), calls=%async_computation.1 | async-start | bytes 2097152 | tf_op jit(solution)/shard_map/all_to_all | solution.py:233
  144.5 12.4 %collective-permute-start.19 = (bf16[32,2048]{1,0:T(8,128)(2,1)S(1)}, bf16[32,2048]{1,0:T(8,128)(2,1)S(1)}, u32[]{:S(2)}, u32[]{:S(2)}) collective-permute-start(bf16[32,2048]{1,0:T(8,128)(2,1)S(1)} %get-tuple-element.15), channel_id=1, source_target_pairs={{0,2},{1,3},{2,4},{3,5},{4,6},{5,7},{6,0},{7,1},{8,10},{9,11},{10,... | collective-permute-start | bytes 393224 | tf_op jit(solution)/shard_map/ppermute | solution.py:37
  145.7 13.4 %collective-permute-start.20 = (bf16[32,2048]{1,0:T(8,128)(2,1)}, bf16[32,2048]{1,0:T(8,128)(2,1)}, u32[]{:S(2)}, u32[]{:S(2)}) collective-permute-start(bf16[32,2048]{1,0:T(8,128)(2,1)} %get-tuple-element.14), channel_id=1, source_target_pairs={{0,3},{1,4},{2,5},{3,6},{4,7},{5,0},{6,1},{7,2},{8,11},{9,12},{10,... | collective-permute-start | bytes 393224 | tf_op jit(solution)/shard_map/ppermute | solution.py:37
  147.3 14.8 %collective-permute-start.21 = (bf16[32,2048]{1,0:T(8,128)(2,1)}, bf16[32,2048]{1,0:T(8,128)(2,1)}, u32[]{:S(2)}, u32[]{:S(2)}) collective-permute-start(bf16[32,2048]{1,0:T(8,128)(2,1)} %get-tuple-element.13), channel_id=1, source_target_pairs={{0,4},{1,5},{2,6},{3,7},{4,0},{5,1},{6,2},{7,3},{8,12},{9,13},{10,... | collective-permute-start | bytes 393224 | tf_op jit(solution)/shard_map/ppermute | solution.py:37
  147.9 14.8 %collective-permute-start.22 = (bf16[32,2048]{1,0:T(8,128)(2,1)}, bf16[32,2048]{1,0:T(8,128)(2,1)}, u32[]{:S(2)}, u32[]{:S(2)}) collective-permute-start(bf16[32,2048]{1,0:T(8,128)(2,1)} %get-tuple-element.12), channel_id=1, source_target_pairs={{0,5},{1,6},{2,7},{3,0},{4,1},{5,2},{6,3},{7,4},{8,13},{9,14},{10,... | collective-permute-start | bytes 393224 | tf_op jit(solution)/shard_map/ppermute | solution.py:37
  149.8 12.9 %collective-permute-start.23 = (bf16[32,2048]{1,0:T(8,128)(2,1)}, bf16[32,2048]{1,0:T(8,128)(2,1)}, u32[]{:S(2)}, u32[]{:S(2)}) collective-permute-start(bf16[32,2048]{1,0:T(8,128)(2,1)} %get-tuple-element.11), channel_id=1, source_target_pairs={{0,6},{1,7},{2,0},{3,1},{4,2},{5,3},{6,4},{7,5},{8,14},{9,15},{10,... | collective-permute-start | bytes 393224 | tf_op jit(solution)/shard_map/ppermute | solution.py:37
  (28 other events, 300.8 us)

commit v12 on v4

--- a/solution.py
+++ b/solution.py
@@ -227,7 +227,7 @@
         "rsjk,sjkd->rd",
         combining,
         returned.astype(jnp.float32),
-        precision=lax.Precision.HIGHEST,
+        precision=lax.Precision.HIGH,
     )
     finished = (own_residual.astype(jnp.float32) + shared_out + routed).astype(jnp.bfloat16)
     return finished[None]

time: 168 us -> 168 us (level)
  no operation moved by 1% of the time
where the time goes in v12:
time: 168 us; the launch traced here: 167 us
  starting transfers between devices  66.5 us (40%)
  matrix products  34.6 us (21%)
  local copies, waits for them, and re-layouts  30.7 us (18%)
  waiting for transfers between devices  21.8 us (13%)
  other arithmetic  12.5 us (7%)
    ppermute x14, starting transfers between devices, summed_over(): lax.ppermute(piece_for(steps), axis, [(i, (i + steps) % count) for i in r...  19.5 us
    unnamed x60, local copies, waits for them, and re-layouts  19.1 us
    ppermute x4, starting transfers between devices, passed_along(): lax.ppermute(value, axis, [(source, source + steps) for source in range(i...  17.7 us
    ppermute x14, waiting for transfers between devices, summed_over(): lax.ppermute(piece_for(steps), axis, [(i, (i + steps) % count) for i in r...  15.8 us
    ppermute x7, starting transfers between devices, gathered_over(): lax.ppermute(block, axis, [(i, (i + steps) % count) for i in range(count)])  10.2 us
    all_to_all x1, starting transfers between devices, shards(): lax.all_to_all(outgoing, ('tok', 'mdl'), split_axis=0, concat_axis=0, til...  9.77 us
    all_to_all x1, starting transfers between devices, shards(): lax.all_to_all(produced, ('tok', 'mdl'), split_axis=0, concat_axis=0, til...  9.28 us
    ppermute x7, waiting for transfers between devices, gathered_over(): lax.ppermute(block, axis, [(i, (i + steps) % count) for i in range(count)])  6.01 us
  transfers between devices with their start and end apart: 27, of which 7 were waited for; matrix products, arithmetic and copies ran while one was open for 21% of the time, Pallas kernels for 0%

profile of v12, /device:TPU:1, one launch (start us, length us, event | category | flops | bytes accessed | tf_op | source)
XLA Modules:
  0.0 166.8 jit_solution(12691017175555423642)
XLA Ops:
  2.7 2.9 %fusion.62 = f32[256,576]{0,1:T(8,128)S(1)} fusion(bf16[2048,576]{0,1:T(8,128)(2,1)} %param.23, f32[2048]{0:T(1024)} %param.21, f32[256]{0:T(256)S(1)} %add_rsqrt_fusion.1, bf16[2,256,2048]{2,1,0:T(8,128)(2,1)} %param.17, s32[]{:T(128)S(6)} %select_n.97), kind=kOutput, calls=%fused_computation.48 | convolution fusion | flops 606076928 | bytes 4006916 | tf_op jit(solution)/shard_map/dot_general | solution.py:135
  9.5 6.2 %collective-permute-start = (bf16[256,576]{0,1:T(8,128)(2,1)}, bf16[256,576]{0,1:T(8,128)(2,1)}, u32[]{:S(2)}, u32[]{:S(2)}) collective-permute-start(bf16[256,576]{0,1:T(8,128)(2,1)} %pad_maximum_fusion), channel_id=1, source_target_pairs={{0,32},{8,40},{16,48},{24,56},{1,33},{9,41},{17,49},{25,57},{2,34}... | collective-permute-start | bytes 884744 | tf_op jit(solution)/shard_map/ppermute | solution.py:22
  15.7 6.4 %collective-permute-start.1 = (bf16[256,576]{0,1:T(8,128)(2,1)}, bf16[256,576]{0,1:T(8,128)(2,1)}, u32[]{:S(2)}, u32[]{:S(2)}) collective-permute-start(bf16[256,576]{0,1:T(8,128)(2,1)} %pad_maximum_fusion), channel_id=1, source_target_pairs={{0,24},{8,32},{16,40},{24,48},{32,56},{1,25},{9,33},{17,41},{25,49... | collective-permute-start | bytes 884744 | tf_op jit(solution)/shard_map/ppermute | solution.py:22
  24.1 3.1 %collective-permute-start.3 = (bf16[256,576]{0,1:T(8,128)(2,1)}, bf16[256,576]{0,1:T(8,128)(2,1)}, u32[]{:S(2)}, u32[]{:S(2)}) collective-permute-start(bf16[256,576]{0,1:T(8,128)(2,1)} %pad_maximum_fusion), channel_id=1, source_target_pairs={{0,8},{8,16},{16,24},{24,32},{32,40},{40,48},{48,56},{1,9},{9,17},... | collective-permute-start | bytes 884744 | tf_op jit(solution)/shard_map/ppermute | solution.py:22
  27.2 2.6 %copy.58 = bf16[2048,384]{0,1:T(8,128)(2,1)} copy(bf16[2048,384]{1,0:T(8,128)(2,1)} %param.22) | data formatting | bytes 3145728 | tf_op args[5]
  29.8 3.2 %fusion.60 = f32[256,2,192]{0,2,1:T(8,128)} fusion(bf16[2,192,2048]{2,1,0:T(8,128)(2,1)} %bitcast.177, f32[2048]{0:T(1024)S(1)} %copy-done.23, f32[256]{0:T(256)S(1)} %add_rsqrt_fusion.1, bf16[2,256,2048]{2,1,0:T(8,128)(2,1)} %param.17, s32[]{:T(128)S(6)} %select_n.97), kind=kOutput, calls=%fused_computation.47 | convolution fusion | flops 404750336 | bytes 3023876 | tf_op jit(solution)/shard_map/dot_general | solution.py:129
  46.5 3.7 %fusion.56 = bf16[256,2,128]{0,2,1:T(8,128)(2,1)S(1)} fusion(bf16[1280,2,256]{0,2,1:T(8,128)(2,1)} %bitcast.180, f32[2,256,1280]{2,1,0:T(8,128)} %copy-done.2, pred[256,1280]{1,0:T(8,128)(4,1)} %and_and_fusion, f32[256,2]{0,1:T(2,128)S(1)} %bitcast.188), kind=kOutput, calls=%fused_computation.45 | convolution fusion | flops 170526464 | bytes 6686720 | tf_op jit(solution)/shard_map/hqk,khd->hqd/dot_general | solution.py:174
  58.2 2.1 %collective-permute-start.6 = (bf16[32,2048]{1,0:T(8,128)(2,1)}, bf16[32,2048]{1,0:T(8,128)(2,1)S(1)}, u32[]{:S(2)}, u32[]{:S(2)}) collective-permute-start(bf16[32,2048]{1,0:T(8,128)(2,1)} %get-tuple-element.21), channel_id=1, source_target_pairs={{0,3},{1,4},{2,5},{3,6},{4,7},{5,0},{6,1},{7,2},{8,11},{9,12},{10,... | collective-permute-start | bytes 393224 | tf_op jit(solution)/shard_map/ppermute | solution.py:37
  61.1 2.6 %collective-permute-start.8 = (bf16[32,2048]{1,0:T(8,128)(2,1)}, bf16[32,2048]{1,0:T(8,128)(2,1)S(1)}, u32[]{:S(2)}, u32[]{:S(2)}) collective-permute-start(bf16[32,2048]{1,0:T(8,128)(2,1)} %get-tuple-element.19), channel_id=1, source_target_pairs={{0,5},{1,6},{2,7},{3,0},{4,1},{5,2},{6,3},{7,4},{8,13},{9,14},{10,... | collective-permute-start | bytes 393224 | tf_op jit(solution)/shard_map/ppermute | solution.py:37
  63.8 2.3 %collective-permute-done.5 = bf16[32,2048]{1,0:T(8,128)(2,1)S(1)} collective-permute-done((bf16[32,2048]{1,0:T(8,128)(2,1)}, bf16[32,2048]{1,0:T(8,128)(2,1)S(1)}, u32[]{:S(2)}, u32[]{:S(2)}) %collective-permute-start.5) | collective-permute-done | bytes 131104 | tf_op jit(solution)/shard_map/ppermute | solution.py:37
  66.1 5.9 %collective-permute-done.6 = bf16[32,2048]{1,0:T(8,128)(2,1)S(1)} collective-permute-done((bf16[32,2048]{1,0:T(8,128)(2,1)}, bf16[32,2048]{1,0:T(8,128)(2,1)S(1)}, u32[]{:S(2)}, u32[]{:S(2)}) %collective-permute-start.6) | collective-permute-done | bytes 131104 | tf_op jit(solution)/shard_map/ppermute | solution.py:37
  79.2 2.1 %collective-permute-start.15 = (bf16[32,2048]{1,0:T(8,128)(2,1)S(1)}, bf16[32,2048]{1,0:T(8,128)(2,1)}, u32[]{:S(2)}, u32[]{:S(2)}) collective-permute-start(bf16[32,2048]{1,0:T(8,128)(2,1)S(1)} %get-tuple-element.6), channel_id=1, source_target_pairs={{0,5},{1,6},{2,7},{3,0},{4,1},{5,2},{6,3},{7,4},{8,13},{9,14},{10,... | collective-permute-start | bytes 393224 | tf_op jit(solution)/shard_map/ppermute | solution.py:46
  83.5 9.8 %all-to-all-start = ((bf16[64,1,4,2048]{3,2,1,0:T(4,128)(2,1)}), bf16[64,1,4,2048]{3,2,1,0:T(4,128)(2,1)}, u32[]{:S(2)}, u32[]{:S(2)}) async-start(bf16[64,1,4,2048]{3,2,1,0:T(4,128)(2,1)} %copy.71), calls=%async_computation | async-start | bytes 2097152 | tf_op jit(solution)/shard_map/all_to_all | solution.py:214
  93.3 2.6 %collective-permute-start.16 = (bf16[32,2048]{1,0:T(8,128)(2,1)S(1)}, bf16[32,2048]{1,0:T(8,128)(2,1)S(1)}, u32[]{:S(2)}, u32[]{:S(2)}) collective-permute-start(bf16[32,2048]{1,0:T(8,128)(2,1)S(1)} %get-tuple-element.6), channel_id=1, source_target_pairs={{0,6},{1,7},{2,0},{3,1},{4,2},{5,3},{6,4},{7,5},{8,14},{9,15},{10,... | collective-permute-start | bytes 393224 | tf_op jit(solution)/shard_map/ppermute | solution.py:46
  104.5 4.7 %collective-permute-done.16 = bf16[32,2048]{1,0:T(8,128)(2,1)S(1)} collective-permute-done((bf16[32,2048]{1,0:T(8,128)(2,1)S(1)}, bf16[32,2048]{1,0:T(8,128)(2,1)S(1)}, u32[]{:S(2)}, u32[]{:S(2)}) %collective-permute-start.16) | collective-permute-done | bytes 131104 | tf_op jit(solution)/shard_map/ppermute | solution.py:46
  113.8 5.0 %fusion.35 = f32[64,1,4,768]{3,0,2,1:T(8,128)} fusion(bf16[1,2048,768]{2,1,0:T(8,128)(2,1)} %param.31, bf16[64,1,4,2048]{3,2,1,0:T(4,128)(2,1)} %all-to-all-done), kind=kOutput, calls=%fused_computation.38 | convolution fusion | flops 805306368 | bytes 4980736 | tf_op jit(solution)/shard_map/sjkd,jdf->sjkf/dot_general | solution.py:215
  118.7 5.9 %fusion.22 = bf16[64,1,4,2048]{3,0,2,1:T(8,128)(2,1)} fusion(bf16[1,768,2048]{2,1,0:T(8,128)(2,1)S(1)} %copy-done, bf16[1,2048,768]{2,1,0:T(8,128)(2,1)} %param.32, bf16[64,1,4,2048]{3,2,1,0:T(4,128)(2,1)} %all-to-all-done, f32[64,1,4,768]{3,0,2,1:T(8,128)} %fusion.35), kind=kOutput, calls=%fused_computation.25 | convolution fusion | flops 1612316672 | bytes 9175040 | tf_op jit(solution)/shard_map/sjkf,jfd->sjkd/dot_general | solution.py:218
  124.7 3.0 %copy.73 = bf16[64,1,4,2048]{3,2,1,0:T(4,128)(2,1)} copy(bf16[64,1,4,2048]{3,0,2,1:T(8,128)(2,1)} %fusion.22) | data formatting | bytes 2097152 | tf_op jit(solution)/shard_map/convert_element_type | solution.py:220
  127.7 9.3 %all-to-all-start.1 = ((bf16[64,1,4,2048]{3,2,1,0:T(4,128)(2,1)}), bf16[64,1,4,2048]{3,2,1,0:T(4,128)(2,1)}, u32[]{:S(2)}, u32[]{:S(2)}) async-start(bf16[64,1,4,2048]{3,2,1,0:T(4,128)(2,1)} %copy.73), calls=%async_computation.1 | async-start | bytes 2097152 | tf_op jit(solution)/shard_map/all_to_all | solution.py:221
  137.0 4.1 %convolution_convert_fusion.1 = bf16[256,2048]{1,0:T(8,128)(2,1)} fusion(bf16[256,2048]{1,0:T(8,128)(2,1)} %param.30, f32[256,256]{1,0:T(8,128)S(1)} %fusion.137, bf16[256,2048]{1,0:T(8,128)(2,1)} %constant_dynamic-update-slice_fusion.5, bf16[2048,256]{1,0:T(8,128)(2,1)} %param.29), kind=kOutput, calls=%fused_computation.20 | convolution fusion | flops 537788416 | bytes 4456448 | tf_op jit(solution)/shard_map/dot_general | solution.py:192
  150.1 3.1 %collective-permute-start.23 = (bf16[32,2048]{1,0:T(8,128)(2,1)}, bf16[32,2048]{1,0:T(8,128)(2,1)}, u32[]{:S(2)}, u32[]{:S(2)}) collective-permute-start(bf16[32,2048]{1,0:T(8,128)(2,1)} %get-tuple-element.11), channel_id=1, source_target_pairs={{0,6},{1,7},{2,0},{3,1},{4,2},{5,3},{6,4},{7,5},{8,14},{9,15},{10,... | collective-permute-start | bytes 393224 | tf_op jit(solution)/shard_map/ppermute | solution.py:37
  153.2 4.0 %collective-permute-done.19 = bf16[32,2048]{1,0:T(8,128)(2,1)S(1)} collective-permute-done((bf16[32,2048]{1,0:T(8,128)(2,1)S(1)}, bf16[32,2048]{1,0:T(8,128)(2,1)S(1)}, u32[]{:S(2)}, u32[]{:S(2)}) %collective-permute-start.19) | collective-permute-done | bytes 131104 | tf_op jit(solution)/shard_map/ppermute | solution.py:37
  159.4 3.0 %collective-permute-done.21 = bf16[32,2048]{1,0:T(8,128)(2,1)} collective-permute-done((bf16[32,2048]{1,0:T(8,128)(2,1)}, bf16[32,2048]{1,0:T(8,128)(2,1)}, u32[]{:S(2)}, u32[]{:S(2)}) %collective-permute-start.21) | collective-permute-done | bytes 131104 | tf_op jit(solution)/shard_map/ppermute | solution.py:37
  163.0 3.7 %fusion.106 = bf16[1,32,2048]{2,1,0:T(8,128)(2,1)} fusion(bf16[64,1,4,2048]{3,2,1,0:T(4,128)(2,1)} %all-to-all-done.1, f32[32,64,4]{0,2,1:T(4,128)S(1)} %bitcast.178, bf16[32,2048]{1,0:T(8,128)(2,1)} %collective-permute-done.24, bf16[32,2048]{1,0:T(8,128)(2,1)} %collective-permute-done.23, bf16[32,2048]{1,0:T(8,128)(2,1)} %collective-permute-done.22, ...), kind=kOutput, calls=%fused_computation.93 | convolution fusion | flops 101908480 | bytes 2392064 | tf_op jit(solution)/shard_map/rsjk,sjkd->rd/dot_general | solution.py:226
  (152 shorter events, 64.7 us)
Async XLA Ops:
  9.5 28.2 %collective-permute-start = (bf16[256,576]{0,1:T(8,128)(2,1)}, bf16[256,576]{0,1:T(8,128)(2,1)}, u32[]{:S(2)}, u32[]{:S(2)}) collective-permute-start(bf16[256,576]{0,1:T(8,128)(2,1)} %pad_maximum_fusion), channel_id=1, source_target_pairs={{0,32},{8,40},{16,48},{24,56},{1,33},{9,41},{17,49},{25,57},{2,34}... | collective-permute-start | bytes 884744 | tf_op jit(solution)/shard_map/ppermute | solution.py:22
  15.7 23.1 %collective-permute-start.1 = (bf16[256,576]{0,1:T(8,128)(2,1)}, bf16[256,576]{0,1:T(8,128)(2,1)}, u32[]{:S(2)}, u32[]{:S(2)}) collective-permute-start(bf16[256,576]{0,1:T(8,128)(2,1)} %pad_maximum_fusion), channel_id=1, source_target_pairs={{0,24},{8,32},{16,40},{24,48},{32,56},{1,25},{9,33},{17,41},{25,49... | collective-permute-start | bytes 884744 | tf_op jit(solution)/shard_map/ppermute | solution.py:22
  22.1 17.7 %collective-permute-start.2 = (bf16[256,576]{0,1:T(8,128)(2,1)}, bf16[256,576]{0,1:T(8,128)(2,1)}, u32[]{:S(2)}, u32[]{:S(2)}) collective-permute-start(bf16[256,576]{0,1:T(8,128)(2,1)} %pad_maximum_fusion), channel_id=1, source_target_pairs={{0,16},{8,24},{16,32},{24,40},{32,48},{40,56},{1,17},{9,25},{17,33... | collective-permute-start | bytes 884744 | tf_op jit(solution)/shard_map/ppermute | solution.py:22
  24.1 16.7 %collective-permute-start.3 = (bf16[256,576]{0,1:T(8,128)(2,1)}, bf16[256,576]{0,1:T(8,128)(2,1)}, u32[]{:S(2)}, u32[]{:S(2)}) collective-permute-start(bf16[256,576]{0,1:T(8,128)(2,1)} %pad_maximum_fusion), channel_id=1, source_target_pairs={{0,8},{8,16},{16,24},{24,32},{32,40},{40,48},{48,56},{1,9},{9,17},... | collective-permute-start | bytes 884744 | tf_op jit(solution)/shard_map/ppermute | solution.py:22
  55.4 8.3 %collective-permute-start.4 = (bf16[32,2048]{1,0:T(8,128)(2,1)}, bf16[32,2048]{1,0:T(8,128)(2,1)}, u32[]{:S(2)}, u32[]{:S(2)}) collective-permute-start(bf16[32,2048]{1,0:T(8,128)(2,1)} %get-tuple-element.16), channel_id=1, source_target_pairs={{0,1},{1,2},{2,3},{3,4},{4,5},{5,6},{6,7},{7,0},{8,9},{9,10},{10,1... | collective-permute-start | bytes 393224 | tf_op jit(solution)/shard_map/ppermute | solution.py:37
  56.9 9.2 %collective-permute-start.5 = (bf16[32,2048]{1,0:T(8,128)(2,1)}, bf16[32,2048]{1,0:T(8,128)(2,1)S(1)}, u32[]{:S(2)}, u32[]{:S(2)}) collective-permute-start(bf16[32,2048]{1,0:T(8,128)(2,1)} %get-tuple-element.22), channel_id=1, source_target_pairs={{0,2},{1,3},{2,4},{3,5},{4,6},{5,7},{6,0},{7,1},{8,10},{9,11},{10,... | collective-permute-start | bytes 393224 | tf_op jit(solution)/shard_map/ppermute | solution.py:37
  58.2 13.7 %collective-permute-start.6 = (bf16[32,2048]{1,0:T(8,128)(2,1)}, bf16[32,2048]{1,0:T(8,128)(2,1)S(1)}, u32[]{:S(2)}, u32[]{:S(2)}) collective-permute-start(bf16[32,2048]{1,0:T(8,128)(2,1)} %get-tuple-element.21), channel_id=1, source_target_pairs={{0,3},{1,4},{2,5},{3,6},{4,7},{5,0},{6,1},{7,2},{8,11},{9,12},{10,... | collective-permute-start | bytes 393224 | tf_op jit(solution)/shard_map/ppermute | solution.py:37
  60.3 11.6 %collective-permute-start.7 = (bf16[32,2048]{1,0:T(8,128)(2,1)}, bf16[32,2048]{1,0:T(8,128)(2,1)S(1)}, u32[]{:S(2)}, u32[]{:S(2)}) collective-permute-start(bf16[32,2048]{1,0:T(8,128)(2,1)} %get-tuple-element.20), channel_id=1, source_target_pairs={{0,4},{1,5},{2,6},{3,7},{4,0},{5,1},{6,2},{7,3},{8,12},{9,13},{10,... | collective-permute-start | bytes 393224 | tf_op jit(solution)/shard_map/ppermute | solution.py:37
  61.1 10.9 %collective-permute-start.8 = (bf16[32,2048]{1,0:T(8,128)(2,1)}, bf16[32,2048]{1,0:T(8,128)(2,1)S(1)}, u32[]{:S(2)}, u32[]{:S(2)}) collective-permute-start(bf16[32,2048]{1,0:T(8,128)(2,1)} %get-tuple-element.19), channel_id=1, source_target_pairs={{0,5},{1,6},{2,7},{3,0},{4,1},{5,2},{6,3},{7,4},{8,13},{9,14},{10,... | collective-permute-start | bytes 393224 | tf_op jit(solution)/shard_map/ppermute | solution.py:37
  63.7 8.2 %collective-permute-start.9 = (bf16[32,2048]{1,0:T(8,128)(2,1)S(1)}, bf16[32,2048]{1,0:T(8,128)(2,1)S(1)}, u32[]{:S(2)}, u32[]{:S(2)}) collective-permute-start(bf16[32,2048]{1,0:T(8,128)(2,1)S(1)} %get-tuple-element.18), channel_id=1, source_target_pairs={{0,6},{1,7},{2,0},{3,1},{4,2},{5,3},{6,4},{7,5},{8,14},{9,15},{10,... | collective-permute-start | bytes 393224 | tf_op jit(solution)/shard_map/ppermute | solution.py:37
  74.2 19.1 %collective-permute-start.11 = (bf16[32,2048]{1,0:T(8,128)(2,1)S(1)}, bf16[32,2048]{1,0:T(8,128)(2,1)}, u32[]{:S(2)}, u32[]{:S(2)}) collective-permute-start(bf16[32,2048]{1,0:T(8,128)(2,1)S(1)} %get-tuple-element.6), channel_id=1, source_target_pairs={{0,1},{1,2},{2,3},{3,4},{4,5},{5,6},{6,7},{7,0},{8,9},{9,10},{10,1... | collective-permute-start | bytes 393224 | tf_op jit(solution)/shard_map/ppermute | solution.py:46
  75.0 22.5 %collective-permute-start.12 = (bf16[32,2048]{1,0:T(8,128)(2,1)S(1)}, bf16[32,2048]{1,0:T(8,128)(2,1)}, u32[]{:S(2)}, u32[]{:S(2)}) collective-permute-start(bf16[32,2048]{1,0:T(8,128)(2,1)S(1)} %get-tuple-element.6), channel_id=1, source_target_pairs={{0,2},{1,3},{2,4},{3,5},{4,6},{5,7},{6,0},{7,1},{8,10},{9,11},{10,... | collective-permute-start | bytes 393224 | tf_op jit(solution)/shard_map/ppermute | solution.py:46
  76.7 23.0 %collective-permute-start.13 = (bf16[32,2048]{1,0:T(8,128)(2,1)S(1)}, bf16[32,2048]{1,0:T(8,128)(2,1)}, u32[]{:S(2)}, u32[]{:S(2)}) collective-permute-start(bf16[32,2048]{1,0:T(8,128)(2,1)S(1)} %get-tuple-element.6), channel_id=1, source_target_pairs={{0,3},{1,4},{2,5},{3,6},{4,7},{5,0},{6,1},{7,2},{8,11},{9,12},{10,... | collective-permute-start | bytes 393224 | tf_op jit(solution)/shard_map/ppermute | solution.py:46
  78.5 22.8 %collective-permute-start.14 = (bf16[32,2048]{1,0:T(8,128)(2,1)S(1)}, bf16[32,2048]{1,0:T(8,128)(2,1)}, u32[]{:S(2)}, u32[]{:S(2)}) collective-permute-start(bf16[32,2048]{1,0:T(8,128)(2,1)S(1)} %get-tuple-element.6), channel_id=1, source_target_pairs={{0,4},{1,5},{2,6},{3,7},{4,0},{5,1},{6,2},{7,3},{8,12},{9,13},{10,... | collective-permute-start | bytes 393224 | tf_op jit(solution)/shard_map/ppermute | solution.py:46
  79.2 23.7 %collective-permute-start.15 = (bf16[32,2048]{1,0:T(8,128)(2,1)S(1)}, bf16[32,2048]{1,0:T(8,128)(2,1)}, u32[]{:S(2)}, u32[]{:S(2)}) collective-permute-start(bf16[32,2048]{1,0:T(8,128)(2,1)S(1)} %get-tuple-element.6), channel_id=1, source_target_pairs={{0,5},{1,6},{2,7},{3,0},{4,1},{5,2},{6,3},{7,4},{8,13},{9,14},{10,... | collective-permute-start | bytes 393224 | tf_op jit(solution)/shard_map/ppermute | solution.py:46
  83.5 30.2 %all-to-all-start = ((bf16[64,1,4,2048]{3,2,1,0:T(4,128)(2,1)}), bf16[64,1,4,2048]{3,2,1,0:T(4,128)(2,1)}, u32[]{:S(2)}, u32[]{:S(2)}) async-start(bf16[64,1,4,2048]{3,2,1,0:T(4,128)(2,1)} %copy.71), calls=%async_computation | async-start | bytes 2097152 | tf_op jit(solution)/shard_map/all_to_all | solution.py:214
  93.3 15.8 %collective-permute-start.16 = (bf16[32,2048]{1,0:T(8,128)(2,1)S(1)}, bf16[32,2048]{1,0:T(8,128)(2,1)S(1)}, u32[]{:S(2)}, u32[]{:S(2)}) collective-permute-start(bf16[32,2048]{1,0:T(8,128)(2,1)S(1)} %get-tuple-element.6), channel_id=1, source_target_pairs={{0,6},{1,7},{2,0},{3,1},{4,2},{5,3},{6,4},{7,5},{8,14},{9,15},{10,... | collective-permute-start | bytes 393224 | tf_op jit(solution)/shard_map/ppermute | solution.py:46
  97.5 13.6 %collective-permute-start.17 = (bf16[32,2048]{1,0:T(8,128)(2,1)S(1)}, bf16[32,2048]{1,0:T(8,128)(2,1)S(1)}, u32[]{:S(2)}, u32[]{:S(2)}) collective-permute-start(bf16[32,2048]{1,0:T(8,128)(2,1)S(1)} %get-tuple-element.6), channel_id=1, source_target_pairs={{0,7},{1,0},{2,1},{3,2},{4,3},{5,4},{6,5},{7,6},{8,15},{9,8},{10,9... | collective-permute-start | bytes 393224 | tf_op jit(solution)/shard_map/ppermute | solution.py:46
  127.7 35.3 %all-to-all-start.1 = ((bf16[64,1,4,2048]{3,2,1,0:T(4,128)(2,1)}), bf16[64,1,4,2048]{3,2,1,0:T(4,128)(2,1)}, u32[]{:S(2)}, u32[]{:S(2)}) async-start(bf16[64,1,4,2048]{3,2,1,0:T(4,128)(2,1)} %copy.73), calls=%async_computation.1 | async-start | bytes 2097152 | tf_op jit(solution)/shard_map/all_to_all | solution.py:221
  144.8 12.4 %collective-permute-start.19 = (bf16[32,2048]{1,0:T(8,128)(2,1)S(1)}, bf16[32,2048]{1,0:T(8,128)(2,1)S(1)}, u32[]{:S(2)}, u32[]{:S(2)}) collective-permute-start(bf16[32,2048]{1,0:T(8,128)(2,1)S(1)} %get-tuple-element.15), channel_id=1, source_target_pairs={{0,2},{1,3},{2,4},{3,5},{4,6},{5,7},{6,0},{7,1},{8,10},{9,11},{10,... | collective-permute-start | bytes 393224 | tf_op jit(solution)/shard_map/ppermute | solution.py:37
  146.0 13.4 %collective-permute-start.20 = (bf16[32,2048]{1,0:T(8,128)(2,1)}, bf16[32,2048]{1,0:T(8,128)(2,1)}, u32[]{:S(2)}, u32[]{:S(2)}) collective-permute-start(bf16[32,2048]{1,0:T(8,128)(2,1)} %get-tuple-element.14), channel_id=1, source_target_pairs={{0,3},{1,4},{2,5},{3,6},{4,7},{5,0},{6,1},{7,2},{8,11},{9,12},{10,... | collective-permute-start | bytes 393224 | tf_op jit(solution)/shard_map/ppermute | solution.py:37
  147.6 14.8 %collective-permute-start.21 = (bf16[32,2048]{1,0:T(8,128)(2,1)}, bf16[32,2048]{1,0:T(8,128)(2,1)}, u32[]{:S(2)}, u32[]{:S(2)}) collective-permute-start(bf16[32,2048]{1,0:T(8,128)(2,1)} %get-tuple-element.13), channel_id=1, source_target_pairs={{0,4},{1,5},{2,6},{3,7},{4,0},{5,1},{6,2},{7,3},{8,12},{9,13},{10,... | collective-permute-start | bytes 393224 | tf_op jit(solution)/shard_map/ppermute | solution.py:37
  148.2 14.8 %collective-permute-start.22 = (bf16[32,2048]{1,0:T(8,128)(2,1)}, bf16[32,2048]{1,0:T(8,128)(2,1)}, u32[]{:S(2)}, u32[]{:S(2)}) collective-permute-start(bf16[32,2048]{1,0:T(8,128)(2,1)} %get-tuple-element.12), channel_id=1, source_target_pairs={{0,5},{1,6},{2,7},{3,0},{4,1},{5,2},{6,3},{7,4},{8,13},{9,14},{10,... | collective-permute-start | bytes 393224 | tf_op jit(solution)/shard_map/ppermute | solution.py:37
  150.1 12.9 %collective-permute-start.23 = (bf16[32,2048]{1,0:T(8,128)(2,1)}, bf16[32,2048]{1,0:T(8,128)(2,1)}, u32[]{:S(2)}, u32[]{:S(2)}) collective-permute-start(bf16[32,2048]{1,0:T(8,128)(2,1)} %get-tuple-element.11), channel_id=1, source_target_pairs={{0,6},{1,7},{2,0},{3,1},{4,2},{5,3},{6,4},{7,5},{8,14},{9,15},{10,... | collective-permute-start | bytes 393224 | tf_op jit(solution)/shard_map/ppermute | solution.py:37
  (28 other events, 296.0 us)

commit v13 on v11

--- a/solution.py
+++ b/solution.py
@@ -239,7 +239,7 @@
         "rsjk,sjkd->rd",
         combining,
         returned.astype(jnp.float32),
-        precision=lax.Precision.HIGHEST,
+        precision=lax.Precision.HIGH,
     )
     finished = (own_residual.astype(jnp.float32) + shared_out + routed).astype(jnp.bfloat16)
     return finished[None]

time: 168 us -> 168 us (level)
  no operation moved by 1% of the time
where the time goes in v13:
time: 168 us; the launch traced here: 166 us
  starting transfers between devices  66.9 us (40%)
  matrix products  34.6 us (21%)
  local copies, waits for them, and re-layouts  29.8 us (18%)
  waiting for transfers between devices  21.8 us (13%)
  other arithmetic  12.6 us (8%)
    ppermute x14, starting transfers between devices, summed_over(): lax.ppermute(piece_for(steps), axis, [(i, (i + steps) % count) for i in r...  19.5 us
    ppermute x4, starting transfers between devices, passed_along(): lax.ppermute(value, axis, [(source, source + steps) for source in range(i...  17.7 us
    unnamed x59, local copies, waits for them, and re-layouts  16.3 us
    ppermute x14, waiting for transfers between devices, summed_over(): lax.ppermute(piece_for(steps), axis, [(i, (i + steps) % count) for i in r...  15.8 us
    all_to_all x1, starting transfers between devices, shards(): lax.all_to_all(outgoing, ('tok', 'mdl'), split_axis=0, concat_axis=0, til...  10.2 us
    ppermute x7, starting transfers between devices, gathered_over(): lax.ppermute(block, axis, [(i, (i + steps) % count) for i in range(count)])  10.2 us
    all_to_all x1, starting transfers between devices, shards(): lax.all_to_all(produced, ('tok', 'mdl'), split_axis=0, concat_axis=0, til...  9.28 us
    ppermute x7, waiting for transfers between devices, gathered_over(): lax.ppermute(block, axis, [(i, (i + steps) % count) for i in range(count)])  6.04 us
  transfers between devices with their start and end apart: 27, of which 7 were waited for; matrix products, arithmetic and copies ran while one was open for 21% of the time, Pallas kernels for 0%

profile of v13, /device:TPU:1, one launch (start us, length us, event | category | flops | bytes accessed | tf_op | source)
XLA Modules:
  0.0 166.4 jit_solution(15582875429124906390)
XLA Ops:
  2.7 2.9 %fusion.86 = f32[256,576]{0,1:T(8,128)S(1)} fusion(bf16[2048,576]{0,1:T(8,128)(2,1)} %param.23, f32[2048]{0:T(1024)} %param.21, f32[256]{0:T(256)S(1)} %add_rsqrt_fusion.1, bf16[2,256,2048]{2,1,0:T(8,128)(2,1)} %param.17, s32[]{:T(128)S(6)} %select_n.97), kind=kOutput, calls=%fused_computation.78 | convolution fusion | flops 606076928 | bytes 4006916 | tf_op jit(solution)/shard_map/dot_general | solution.py:147
  9.5 6.2 %collective-permute-start = (bf16[256,576]{0,1:T(8,128)(2,1)}, bf16[256,576]{0,1:T(8,128)(2,1)}, u32[]{:S(2)}, u32[]{:S(2)}) collective-permute-start(bf16[256,576]{0,1:T(8,128)(2,1)} %pad_maximum_fusion), channel_id=1, source_target_pairs={{0,32},{8,40},{16,48},{24,56},{1,33},{9,41},{17,49},{25,57},{2,34}... | collective-permute-start | bytes 884744 | tf_op jit(solution)/shard_map/ppermute | solution.py:22
  15.7 6.4 %collective-permute-start.1 = (bf16[256,576]{0,1:T(8,128)(2,1)}, bf16[256,576]{0,1:T(8,128)(2,1)}, u32[]{:S(2)}, u32[]{:S(2)}) collective-permute-start(bf16[256,576]{0,1:T(8,128)(2,1)} %pad_maximum_fusion), channel_id=1, source_target_pairs={{0,24},{8,32},{16,40},{24,48},{32,56},{1,25},{9,33},{17,41},{25,49... | collective-permute-start | bytes 884744 | tf_op jit(solution)/shard_map/ppermute | solution.py:22
  24.1 3.1 %collective-permute-start.3 = (bf16[256,576]{0,1:T(8,128)(2,1)}, bf16[256,576]{0,1:T(8,128)(2,1)}, u32[]{:S(2)}, u32[]{:S(2)}) collective-permute-start(bf16[256,576]{0,1:T(8,128)(2,1)} %pad_maximum_fusion), channel_id=1, source_target_pairs={{0,8},{8,16},{16,24},{24,32},{32,40},{40,48},{48,56},{1,9},{9,17},... | collective-permute-start | bytes 884744 | tf_op jit(solution)/shard_map/ppermute | solution.py:22
  27.4 3.2 %convolution_bitcast_fusion.1 = f32[384,256]{0,1:T(8,128)} fusion(bf16[2048,384]{1,0:T(8,128)(2,1)} %param.22, f32[2048]{0:T(1024)S(1)} %copy-done.23, f32[256]{0:T(256)S(1)} %add_rsqrt_fusion.1, bf16[2,256,2048]{2,1,0:T(8,128)(2,1)} %param.17, s32[]{:T(128)S(6)} %select_n.97), kind=kOutput, calls=%fused_computation.38 | convolution fusion | flops 404750336 | bytes 3023876 | tf_op jit(solution)/shard_map/dc,qd->cq/dot_general | solution.py:129
  45.8 3.7 %fusion.52 = bf16[256,2,128]{0,2,1:T(8,128)(2,1)S(1)} fusion(bf16[1280,2,256]{0,2,1:T(8,128)(2,1)} %bitcast.168, f32[2,256,1280]{2,1,0:T(8,128)} %copy-done.2, pred[256,1280]{1,0:T(8,128)(4,1)} %and_and_fusion, f32[256,2]{0,1:T(2,128)S(1)} %bitcast.176), kind=kOutput, calls=%fused_computation.41 | convolution fusion | flops 170526464 | bytes 6686720 | tf_op jit(solution)/shard_map/hqk,khd->hqd/dot_general | solution.py:186
  57.5 2.1 %collective-permute-start.6 = (bf16[32,2048]{1,0:T(8,128)(2,1)}, bf16[32,2048]{1,0:T(8,128)(2,1)S(1)}, u32[]{:S(2)}, u32[]{:S(2)}) collective-permute-start(bf16[32,2048]{1,0:T(8,128)(2,1)} %get-tuple-element.21), channel_id=1, source_target_pairs={{0,3},{1,4},{2,5},{3,6},{4,7},{5,0},{6,1},{7,2},{8,11},{9,12},{10,... | collective-permute-start | bytes 393224 | tf_op jit(solution)/shard_map/ppermute | solution.py:37
  60.4 2.6 %collective-permute-start.8 = (bf16[32,2048]{1,0:T(8,128)(2,1)}, bf16[32,2048]{1,0:T(8,128)(2,1)S(1)}, u32[]{:S(2)}, u32[]{:S(2)}) collective-permute-start(bf16[32,2048]{1,0:T(8,128)(2,1)} %get-tuple-element.19), channel_id=1, source_target_pairs={{0,5},{1,6},{2,7},{3,0},{4,1},{5,2},{6,3},{7,4},{8,13},{9,14},{10,... | collective-permute-start | bytes 393224 | tf_op jit(solution)/shard_map/ppermute | solution.py:37
  63.0 2.3 %collective-permute-done.5 = bf16[32,2048]{1,0:T(8,128)(2,1)S(1)} collective-permute-done((bf16[32,2048]{1,0:T(8,128)(2,1)}, bf16[32,2048]{1,0:T(8,128)(2,1)S(1)}, u32[]{:S(2)}, u32[]{:S(2)}) %collective-permute-start.5) | collective-permute-done | bytes 131104 | tf_op jit(solution)/shard_map/ppermute | solution.py:37
  65.3 5.9 %collective-permute-done.6 = bf16[32,2048]{1,0:T(8,128)(2,1)S(1)} collective-permute-done((bf16[32,2048]{1,0:T(8,128)(2,1)}, bf16[32,2048]{1,0:T(8,128)(2,1)S(1)}, u32[]{:S(2)}, u32[]{:S(2)}) %collective-permute-start.6) | collective-permute-done | bytes 131104 | tf_op jit(solution)/shard_map/ppermute | solution.py:37
  78.5 2.1 %collective-permute-start.15 = (bf16[32,2048]{1,0:T(8,128)(2,1)S(1)}, bf16[32,2048]{1,0:T(8,128)(2,1)}, u32[]{:S(2)}, u32[]{:S(2)}) collective-permute-start(bf16[32,2048]{1,0:T(8,128)(2,1)S(1)} %get-tuple-element.6), channel_id=1, source_target_pairs={{0,5},{1,6},{2,7},{3,0},{4,1},{5,2},{6,3},{7,4},{8,13},{9,14},{10,... | collective-permute-start | bytes 393224 | tf_op jit(solution)/shard_map/ppermute | solution.py:46
  82.8 10.2 %all-to-all-start = ((bf16[64,1,4,2048]{3,2,1,0:T(4,128)(2,1)}), bf16[64,1,4,2048]{3,2,1,0:T(4,128)(2,1)}, u32[]{:S(2)}, u32[]{:S(2)}) async-start(bf16[64,1,4,2048]{3,2,1,0:T(4,128)(2,1)} %copy.85), calls=%async_computation | async-start | bytes 2097152 | tf_op jit(solution)/shard_map/all_to_all | solution.py:226
  93.0 2.6 %collective-permute-start.16 = (bf16[32,2048]{1,0:T(8,128)(2,1)S(1)}, bf16[32,2048]{1,0:T(8,128)(2,1)S(1)}, u32[]{:S(2)}, u32[]{:S(2)}) collective-permute-start(bf16[32,2048]{1,0:T(8,128)(2,1)S(1)} %get-tuple-element.6), channel_id=1, source_target_pairs={{0,6},{1,7},{2,0},{3,1},{4,2},{5,3},{6,4},{7,5},{8,14},{9,15},{10,... | collective-permute-start | bytes 393224 | tf_op jit(solution)/shard_map/ppermute | solution.py:46
  104.2 4.7 %collective-permute-done.16 = bf16[32,2048]{1,0:T(8,128)(2,1)S(1)} collective-permute-done((bf16[32,2048]{1,0:T(8,128)(2,1)S(1)}, bf16[32,2048]{1,0:T(8,128)(2,1)S(1)}, u32[]{:S(2)}, u32[]{:S(2)}) %collective-permute-start.16) | collective-permute-done | bytes 131104 | tf_op jit(solution)/shard_map/ppermute | solution.py:46
  113.5 5.0 %fusion.31 = f32[64,1,4,768]{3,0,2,1:T(8,128)} fusion(bf16[1,2048,768]{2,1,0:T(8,128)(2,1)} %param.31, bf16[64,1,4,2048]{3,2,1,0:T(4,128)(2,1)} %all-to-all-done), kind=kOutput, calls=%fused_computation.33 | convolution fusion | flops 805306368 | bytes 4980736 | tf_op jit(solution)/shard_map/sjkd,jdf->sjkf/dot_general | solution.py:227
  118.4 5.9 %fusion.20 = bf16[64,1,4,2048]{3,0,2,1:T(8,128)(2,1)} fusion(bf16[1,768,2048]{2,1,0:T(8,128)(2,1)S(1)} %copy-done, bf16[1,2048,768]{2,1,0:T(8,128)(2,1)} %param.32, bf16[64,1,4,2048]{3,2,1,0:T(4,128)(2,1)} %all-to-all-done, f32[64,1,4,768]{3,0,2,1:T(8,128)} %fusion.31), kind=kOutput, calls=%fused_computation.22 | convolution fusion | flops 1612316672 | bytes 9175040 | tf_op jit(solution)/shard_map/sjkf,jfd->sjkd/dot_general | solution.py:230
  124.4 3.0 %copy.87 = bf16[64,1,4,2048]{3,2,1,0:T(4,128)(2,1)} copy(bf16[64,1,4,2048]{3,0,2,1:T(8,128)(2,1)} %fusion.20) | data formatting | bytes 2097152 | tf_op jit(solution)/shard_map/convert_element_type | solution.py:232
  127.4 9.3 %all-to-all-start.1 = ((bf16[64,1,4,2048]{3,2,1,0:T(4,128)(2,1)}), bf16[64,1,4,2048]{3,2,1,0:T(4,128)(2,1)}, u32[]{:S(2)}, u32[]{:S(2)}) async-start(bf16[64,1,4,2048]{3,2,1,0:T(4,128)(2,1)} %copy.87), calls=%async_computation.1 | async-start | bytes 2097152 | tf_op jit(solution)/shard_map/all_to_all | solution.py:233
  136.7 4.1 %convolution_convert_fusion.1 = bf16[256,2048]{1,0:T(8,128)(2,1)} fusion(bf16[256,2048]{1,0:T(8,128)(2,1)} %param.30, f32[256,256]{1,0:T(8,128)S(1)} %fusion.134, bf16[256,2048]{1,0:T(8,128)(2,1)} %constant_dynamic-update-slice_fusion.5, bf16[2048,256]{1,0:T(8,128)(2,1)} %param.29), kind=kOutput, calls=%fused_computation.17 | convolution fusion | flops 537788416 | bytes 4456448 | tf_op jit(solution)/shard_map/dot_general | solution.py:204
  140.8 2.1 %fusion.130 = (bf16[32,2048]{1,0:T(8,128)(2,1)S(1)}, bf16[32,2048]{1,0:T(8,128)(2,1)S(1)}, bf16[32,2048]{1,0:T(8,128)(2,1)}, bf16[32,2048]{1,0:T(8,128)(2,1)}, b...) fusion(bf16[256,2048]{1,0:T(8,128)(2,1)} %convolution_convert_fusion.1), kind=kLoop, calls=%fused_computation.162 | loop fusion | bytes 1835008 | tf_op jit(solution)/shard_map/slice | solution.py:32
  149.8 3.1 %collective-permute-start.23 = (bf16[32,2048]{1,0:T(8,128)(2,1)}, bf16[32,2048]{1,0:T(8,128)(2,1)}, u32[]{:S(2)}, u32[]{:S(2)}) collective-permute-start(bf16[32,2048]{1,0:T(8,128)(2,1)} %get-tuple-element.11), channel_id=1, source_target_pairs={{0,6},{1,7},{2,0},{3,1},{4,2},{5,3},{6,4},{7,5},{8,14},{9,15},{10,... | collective-permute-start | bytes 393224 | tf_op jit(solution)/shard_map/ppermute | solution.py:37
  152.9 4.0 %collective-permute-done.19 = bf16[32,2048]{1,0:T(8,128)(2,1)S(1)} collective-permute-done((bf16[32,2048]{1,0:T(8,128)(2,1)S(1)}, bf16[32,2048]{1,0:T(8,128)(2,1)S(1)}, u32[]{:S(2)}, u32[]{:S(2)}) %collective-permute-start.19) | collective-permute-done | bytes 131104 | tf_op jit(solution)/shard_map/ppermute | solution.py:37
  159.1 3.0 %collective-permute-done.21 = bf16[32,2048]{1,0:T(8,128)(2,1)} collective-permute-done((bf16[32,2048]{1,0:T(8,128)(2,1)}, bf16[32,2048]{1,0:T(8,128)(2,1)}, u32[]{:S(2)}, u32[]{:S(2)}) %collective-permute-start.21) | collective-permute-done | bytes 131104 | tf_op jit(solution)/shard_map/ppermute | solution.py:37
  162.7 3.7 %fusion.95 = bf16[1,32,2048]{2,1,0:T(8,128)(2,1)} fusion(bf16[64,1,4,2048]{3,2,1,0:T(4,128)(2,1)} %all-to-all-done.1, f32[32,64,4]{0,2,1:T(4,128)S(1)} %bitcast.166, bf16[32,2048]{1,0:T(8,128)(2,1)} %collective-permute-done.24, bf16[32,2048]{1,0:T(8,128)(2,1)} %collective-permute-done.23, bf16[32,2048]{1,0:T(8,128)(2,1)} %collective-permute-done.22, ...), kind=kOutput, calls=%fused_computation.82 | convolution fusion | flops 101908480 | bytes 2392064 | tf_op jit(solution)/shard_map/rsjk,sjkd->rd/dot_general | solution.py:238
  (153 shorter events, 64.4 us)
Async XLA Ops:
  9.5 27.8 %collective-permute-start = (bf16[256,576]{0,1:T(8,128)(2,1)}, bf16[256,576]{0,1:T(8,128)(2,1)}, u32[]{:S(2)}, u32[]{:S(2)}) collective-permute-start(bf16[256,576]{0,1:T(8,128)(2,1)} %pad_maximum_fusion), channel_id=1, source_target_pairs={{0,32},{8,40},{16,48},{24,56},{1,33},{9,41},{17,49},{25,57},{2,34}... | collective-permute-start | bytes 884744 | tf_op jit(solution)/shard_map/ppermute | solution.py:22
  15.7 22.6 %collective-permute-start.1 = (bf16[256,576]{0,1:T(8,128)(2,1)}, bf16[256,576]{0,1:T(8,128)(2,1)}, u32[]{:S(2)}, u32[]{:S(2)}) collective-permute-start(bf16[256,576]{0,1:T(8,128)(2,1)} %pad_maximum_fusion), channel_id=1, source_target_pairs={{0,24},{8,32},{16,40},{24,48},{32,56},{1,25},{9,33},{17,41},{25,49... | collective-permute-start | bytes 884744 | tf_op jit(solution)/shard_map/ppermute | solution.py:22
  22.1 17.2 %collective-permute-start.2 = (bf16[256,576]{0,1:T(8,128)(2,1)}, bf16[256,576]{0,1:T(8,128)(2,1)}, u32[]{:S(2)}, u32[]{:S(2)}) collective-permute-start(bf16[256,576]{0,1:T(8,128)(2,1)} %pad_maximum_fusion), channel_id=1, source_target_pairs={{0,16},{8,24},{16,32},{24,40},{32,48},{40,56},{1,17},{9,25},{17,33... | collective-permute-start | bytes 884744 | tf_op jit(solution)/shard_map/ppermute | solution.py:22
  24.1 16.2 %collective-permute-start.3 = (bf16[256,576]{0,1:T(8,128)(2,1)}, bf16[256,576]{0,1:T(8,128)(2,1)}, u32[]{:S(2)}, u32[]{:S(2)}) collective-permute-start(bf16[256,576]{0,1:T(8,128)(2,1)} %pad_maximum_fusion), channel_id=1, source_target_pairs={{0,8},{8,16},{16,24},{24,32},{32,40},{40,48},{48,56},{1,9},{9,17},... | collective-permute-start | bytes 884744 | tf_op jit(solution)/shard_map/ppermute | solution.py:22
  54.6 8.3 %collective-permute-start.4 = (bf16[32,2048]{1,0:T(8,128)(2,1)}, bf16[32,2048]{1,0:T(8,128)(2,1)}, u32[]{:S(2)}, u32[]{:S(2)}) collective-permute-start(bf16[32,2048]{1,0:T(8,128)(2,1)} %get-tuple-element.16), channel_id=1, source_target_pairs={{0,1},{1,2},{2,3},{3,4},{4,5},{5,6},{6,7},{7,0},{8,9},{9,10},{10,1... | collective-permute-start | bytes 393224 | tf_op jit(solution)/shard_map/ppermute | solution.py:37
  56.2 9.2 %collective-permute-start.5 = (bf16[32,2048]{1,0:T(8,128)(2,1)}, bf16[32,2048]{1,0:T(8,128)(2,1)S(1)}, u32[]{:S(2)}, u32[]{:S(2)}) collective-permute-start(bf16[32,2048]{1,0:T(8,128)(2,1)} %get-tuple-element.22), channel_id=1, source_target_pairs={{0,2},{1,3},{2,4},{3,5},{4,6},{5,7},{6,0},{7,1},{8,10},{9,11},{10,... | collective-permute-start | bytes 393224 | tf_op jit(solution)/shard_map/ppermute | solution.py:37
  57.5 13.7 %collective-permute-start.6 = (bf16[32,2048]{1,0:T(8,128)(2,1)}, bf16[32,2048]{1,0:T(8,128)(2,1)S(1)}, u32[]{:S(2)}, u32[]{:S(2)}) collective-permute-start(bf16[32,2048]{1,0:T(8,128)(2,1)} %get-tuple-element.21), channel_id=1, source_target_pairs={{0,3},{1,4},{2,5},{3,6},{4,7},{5,0},{6,1},{7,2},{8,11},{9,12},{10,... | collective-permute-start | bytes 393224 | tf_op jit(solution)/shard_map/ppermute | solution.py:37
  59.6 11.6 %collective-permute-start.7 = (bf16[32,2048]{1,0:T(8,128)(2,1)}, bf16[32,2048]{1,0:T(8,128)(2,1)S(1)}, u32[]{:S(2)}, u32[]{:S(2)}) collective-permute-start(bf16[32,2048]{1,0:T(8,128)(2,1)} %get-tuple-element.20), channel_id=1, source_target_pairs={{0,4},{1,5},{2,6},{3,7},{4,0},{5,1},{6,2},{7,3},{8,12},{9,13},{10,... | collective-permute-start | bytes 393224 | tf_op jit(solution)/shard_map/ppermute | solution.py:37
  60.4 10.9 %collective-permute-start.8 = (bf16[32,2048]{1,0:T(8,128)(2,1)}, bf16[32,2048]{1,0:T(8,128)(2,1)S(1)}, u32[]{:S(2)}, u32[]{:S(2)}) collective-permute-start(bf16[32,2048]{1,0:T(8,128)(2,1)} %get-tuple-element.19), channel_id=1, source_target_pairs={{0,5},{1,6},{2,7},{3,0},{4,1},{5,2},{6,3},{7,4},{8,13},{9,14},{10,... | collective-permute-start | bytes 393224 | tf_op jit(solution)/shard_map/ppermute | solution.py:37
  63.0 8.2 %collective-permute-start.9 = (bf16[32,2048]{1,0:T(8,128)(2,1)S(1)}, bf16[32,2048]{1,0:T(8,128)(2,1)S(1)}, u32[]{:S(2)}, u32[]{:S(2)}) collective-permute-start(bf16[32,2048]{1,0:T(8,128)(2,1)S(1)} %get-tuple-element.18), channel_id=1, source_target_pairs={{0,6},{1,7},{2,0},{3,1},{4,2},{5,3},{6,4},{7,5},{8,14},{9,15},{10,... | collective-permute-start | bytes 393224 | tf_op jit(solution)/shard_map/ppermute | solution.py:37
  73.4 19.6 %collective-permute-start.11 = (bf16[32,2048]{1,0:T(8,128)(2,1)S(1)}, bf16[32,2048]{1,0:T(8,128)(2,1)}, u32[]{:S(2)}, u32[]{:S(2)}) collective-permute-start(bf16[32,2048]{1,0:T(8,128)(2,1)S(1)} %get-tuple-element.6), channel_id=1, source_target_pairs={{0,1},{1,2},{2,3},{3,4},{4,5},{5,6},{6,7},{7,0},{8,9},{9,10},{10,1... | collective-permute-start | bytes 393224 | tf_op jit(solution)/shard_map/ppermute | solution.py:46
  74.3 23.0 %collective-permute-start.12 = (bf16[32,2048]{1,0:T(8,128)(2,1)S(1)}, bf16[32,2048]{1,0:T(8,128)(2,1)}, u32[]{:S(2)}, u32[]{:S(2)}) collective-permute-start(bf16[32,2048]{1,0:T(8,128)(2,1)S(1)} %get-tuple-element.6), channel_id=1, source_target_pairs={{0,2},{1,3},{2,4},{3,5},{4,6},{5,7},{6,0},{7,1},{8,10},{9,11},{10,... | collective-permute-start | bytes 393224 | tf_op jit(solution)/shard_map/ppermute | solution.py:46
  76.0 23.5 %collective-permute-start.13 = (bf16[32,2048]{1,0:T(8,128)(2,1)S(1)}, bf16[32,2048]{1,0:T(8,128)(2,1)}, u32[]{:S(2)}, u32[]{:S(2)}) collective-permute-start(bf16[32,2048]{1,0:T(8,128)(2,1)S(1)} %get-tuple-element.6), channel_id=1, source_target_pairs={{0,3},{1,4},{2,5},{3,6},{4,7},{5,0},{6,1},{7,2},{8,11},{9,12},{10,... | collective-permute-start | bytes 393224 | tf_op jit(solution)/shard_map/ppermute | solution.py:46
  77.7 23.3 %collective-permute-start.14 = (bf16[32,2048]{1,0:T(8,128)(2,1)S(1)}, bf16[32,2048]{1,0:T(8,128)(2,1)}, u32[]{:S(2)}, u32[]{:S(2)}) collective-permute-start(bf16[32,2048]{1,0:T(8,128)(2,1)S(1)} %get-tuple-element.6), channel_id=1, source_target_pairs={{0,4},{1,5},{2,6},{3,7},{4,0},{5,1},{6,2},{7,3},{8,12},{9,13},{10,... | collective-permute-start | bytes 393224 | tf_op jit(solution)/shard_map/ppermute | solution.py:46
  78.5 24.1 %collective-permute-start.15 = (bf16[32,2048]{1,0:T(8,128)(2,1)S(1)}, bf16[32,2048]{1,0:T(8,128)(2,1)}, u32[]{:S(2)}, u32[]{:S(2)}) collective-permute-start(bf16[32,2048]{1,0:T(8,128)(2,1)S(1)} %get-tuple-element.6), channel_id=1, source_target_pairs={{0,5},{1,6},{2,7},{3,0},{4,1},{5,2},{6,3},{7,4},{8,13},{9,14},{10,... | collective-permute-start | bytes 393224 | tf_op jit(solution)/shard_map/ppermute | solution.py:46
  82.8 30.7 %all-to-all-start = ((bf16[64,1,4,2048]{3,2,1,0:T(4,128)(2,1)}), bf16[64,1,4,2048]{3,2,1,0:T(4,128)(2,1)}, u32[]{:S(2)}, u32[]{:S(2)}) async-start(bf16[64,1,4,2048]{3,2,1,0:T(4,128)(2,1)} %copy.85), calls=%async_computation | async-start | bytes 2097152 | tf_op jit(solution)/shard_map/all_to_all | solution.py:226
  93.0 15.8 %collective-permute-start.16 = (bf16[32,2048]{1,0:T(8,128)(2,1)S(1)}, bf16[32,2048]{1,0:T(8,128)(2,1)S(1)}, u32[]{:S(2)}, u32[]{:S(2)}) collective-permute-start(bf16[32,2048]{1,0:T(8,128)(2,1)S(1)} %get-tuple-element.6), channel_id=1, source_target_pairs={{0,6},{1,7},{2,0},{3,1},{4,2},{5,3},{6,4},{7,5},{8,14},{9,15},{10,... | collective-permute-start | bytes 393224 | tf_op jit(solution)/shard_map/ppermute | solution.py:46
  97.2 13.6 %collective-permute-start.17 = (bf16[32,2048]{1,0:T(8,128)(2,1)S(1)}, bf16[32,2048]{1,0:T(8,128)(2,1)S(1)}, u32[]{:S(2)}, u32[]{:S(2)}) collective-permute-start(bf16[32,2048]{1,0:T(8,128)(2,1)S(1)} %get-tuple-element.6), channel_id=1, source_target_pairs={{0,7},{1,0},{2,1},{3,2},{4,3},{5,4},{6,5},{7,6},{8,15},{9,8},{10,9... | collective-permute-start | bytes 393224 | tf_op jit(solution)/shard_map/ppermute | solution.py:46
  127.4 35.3 %all-to-all-start.1 = ((bf16[64,1,4,2048]{3,2,1,0:T(4,128)(2,1)}), bf16[64,1,4,2048]{3,2,1,0:T(4,128)(2,1)}, u32[]{:S(2)}, u32[]{:S(2)}) async-start(bf16[64,1,4,2048]{3,2,1,0:T(4,128)(2,1)} %copy.87), calls=%async_computation.1 | async-start | bytes 2097152 | tf_op jit(solution)/shard_map/all_to_all | solution.py:233
  144.5 12.4 %collective-permute-start.19 = (bf16[32,2048]{1,0:T(8,128)(2,1)S(1)}, bf16[32,2048]{1,0:T(8,128)(2,1)S(1)}, u32[]{:S(2)}, u32[]{:S(2)}) collective-permute-start(bf16[32,2048]{1,0:T(8,128)(2,1)S(1)} %get-tuple-element.15), channel_id=1, source_target_pairs={{0,2},{1,3},{2,4},{3,5},{4,6},{5,7},{6,0},{7,1},{8,10},{9,11},{10,... | collective-permute-start | bytes 393224 | tf_op jit(solution)/shard_map/ppermute | solution.py:37
  145.7 13.4 %collective-permute-start.20 = (bf16[32,2048]{1,0:T(8,128)(2,1)}, bf16[32,2048]{1,0:T(8,128)(2,1)}, u32[]{:S(2)}, u32[]{:S(2)}) collective-permute-start(bf16[32,2048]{1,0:T(8,128)(2,1)} %get-tuple-element.14), channel_id=1, source_target_pairs={{0,3},{1,4},{2,5},{3,6},{4,7},{5,0},{6,1},{7,2},{8,11},{9,12},{10,... | collective-permute-start | bytes 393224 | tf_op jit(solution)/shard_map/ppermute | solution.py:37
  147.3 14.8 %collective-permute-start.21 = (bf16[32,2048]{1,0:T(8,128)(2,1)}, bf16[32,2048]{1,0:T(8,128)(2,1)}, u32[]{:S(2)}, u32[]{:S(2)}) collective-permute-start(bf16[32,2048]{1,0:T(8,128)(2,1)} %get-tuple-element.13), channel_id=1, source_target_pairs={{0,4},{1,5},{2,6},{3,7},{4,0},{5,1},{6,2},{7,3},{8,12},{9,13},{10,... | collective-permute-start | bytes 393224 | tf_op jit(solution)/shard_map/ppermute | solution.py:37
  147.9 14.8 %collective-permute-start.22 = (bf16[32,2048]{1,0:T(8,128)(2,1)}, bf16[32,2048]{1,0:T(8,128)(2,1)}, u32[]{:S(2)}, u32[]{:S(2)}) collective-permute-start(bf16[32,2048]{1,0:T(8,128)(2,1)} %get-tuple-element.12), channel_id=1, source_target_pairs={{0,5},{1,6},{2,7},{3,0},{4,1},{5,2},{6,3},{7,4},{8,13},{9,14},{10,... | collective-permute-start | bytes 393224 | tf_op jit(solution)/shard_map/ppermute | solution.py:37
  149.8 12.9 %collective-permute-start.23 = (bf16[32,2048]{1,0:T(8,128)(2,1)}, bf16[32,2048]{1,0:T(8,128)(2,1)}, u32[]{:S(2)}, u32[]{:S(2)}) collective-permute-start(bf16[32,2048]{1,0:T(8,128)(2,1)} %get-tuple-element.11), channel_id=1, source_target_pairs={{0,6},{1,7},{2,0},{3,1},{4,2},{5,3},{6,4},{7,5},{8,14},{9,15},{10,... | collective-permute-start | bytes 393224 | tf_op jit(solution)/shard_map/ppermute | solution.py:37
  (28 other events, 300.8 us)

commit v14 on v13

--- a/solution.py
+++ b/solution.py
@@ -151,8 +151,11 @@
     reach = LONGEST_SEGMENT // tok_dev
     kv_own = jnp.concatenate([latent, key_rope], axis=-1)
     kv_parts = [kv_own]
+    earlier = {}
+    for steps in range(min(reach, n_tok - 1), 0, -1):
+        earlier[steps] = passed_along(kv_own, "tok", steps)
     for steps in range(1, min(reach, n_tok - 1) + 1):
-        kv_parts.insert(0, passed_along(kv_own, "tok", steps))
+        kv_parts.insert(0, earlier[steps])
     kv_rows = jnp.concatenate(kv_parts, axis=0)
     key_count = kv_rows.shape[0]
     key_start = query_start + tok_dev - key_count

time: 168 us -> 168 us (level)
  no operation moved by 1% of the time
where the time goes in v14:
time: 168 us; the launch traced here: 166 us
  starting transfers between devices  66.9 us (40%)
  matrix products  34.6 us (21%)
  local copies, waits for them, and re-layouts  29.8 us (18%)
  waiting for transfers between devices  21.8 us (13%)
  other arithmetic  12.6 us (8%)
    ppermute x14, starting transfers between devices, summed_over(): lax.ppermute(piece_for(steps), axis, [(i, (i + steps) % count) for i in r...  19.5 us
    ppermute x4, starting transfers between devices, passed_along(): lax.ppermute(value, axis, [(source, source + steps) for source in range(i...  17.7 us
    unnamed x59, local copies, waits for them, and re-layouts  16.3 us
    ppermute x14, waiting for transfers between devices, summed_over(): lax.ppermute(piece_for(steps), axis, [(i, (i + steps) % count) for i in r...  15.8 us
    all_to_all x1, starting transfers between devices, shards(): lax.all_to_all(outgoing, ('tok', 'mdl'), split_axis=0, concat_axis=0, til...  10.2 us
    ppermute x7, starting transfers between devices, gathered_over(): lax.ppermute(block, axis, [(i, (i + steps) % count) for i in range(count)])  10.2 us
    all_to_all x1, starting transfers between devices, shards(): lax.all_to_all(produced, ('tok', 'mdl'), split_axis=0, concat_axis=0, til...  9.28 us
    ppermute x7, waiting for transfers between devices, gathered_over(): lax.ppermute(block, axis, [(i, (i + steps) % count) for i in range(count)])  6.04 us
  transfers between devices with their start and end apart: 27, of which 7 were waited for; matrix products, arithmetic and copies ran while one was open for 21% of the time, Pallas kernels for 0%

profile of v14, /device:TPU:1, one launch (start us, length us, event | category | flops | bytes accessed | tf_op | source)
XLA Modules:
  0.0 166.4 jit_solution(15582875429124906390)
XLA Ops:
  2.7 2.9 %fusion.86 = f32[256,576]{0,1:T(8,128)S(1)} fusion(bf16[2048,576]{0,1:T(8,128)(2,1)} %param.23, f32[2048]{0:T(1024)} %param.21, f32[256]{0:T(256)S(1)} %add_rsqrt_fusion.1, bf16[2,256,2048]{2,1,0:T(8,128)(2,1)} %param.17, s32[]{:T(128)S(6)} %select_n.97), kind=kOutput, calls=%fused_computation.78 | convolution fusion | flops 606076928 | bytes 4006916 | tf_op jit(solution)/shard_map/dot_general | solution.py:147
  9.5 6.2 %collective-permute-start = (bf16[256,576]{0,1:T(8,128)(2,1)}, bf16[256,576]{0,1:T(8,128)(2,1)}, u32[]{:S(2)}, u32[]{:S(2)}) collective-permute-start(bf16[256,576]{0,1:T(8,128)(2,1)} %pad_maximum_fusion), channel_id=1, source_target_pairs={{0,32},{8,40},{16,48},{24,56},{1,33},{9,41},{17,49},{25,57},{2,34}... | collective-permute-start | bytes 884744 | tf_op jit(solution)/shard_map/ppermute | solution.py:22
  15.7 6.4 %collective-permute-start.1 = (bf16[256,576]{0,1:T(8,128)(2,1)}, bf16[256,576]{0,1:T(8,128)(2,1)}, u32[]{:S(2)}, u32[]{:S(2)}) collective-permute-start(bf16[256,576]{0,1:T(8,128)(2,1)} %pad_maximum_fusion), channel_id=1, source_target_pairs={{0,24},{8,32},{16,40},{24,48},{32,56},{1,25},{9,33},{17,41},{25,49... | collective-permute-start | bytes 884744 | tf_op jit(solution)/shard_map/ppermute | solution.py:22
  24.1 3.1 %collective-permute-start.3 = (bf16[256,576]{0,1:T(8,128)(2,1)}, bf16[256,576]{0,1:T(8,128)(2,1)}, u32[]{:S(2)}, u32[]{:S(2)}) collective-permute-start(bf16[256,576]{0,1:T(8,128)(2,1)} %pad_maximum_fusion), channel_id=1, source_target_pairs={{0,8},{8,16},{16,24},{24,32},{32,40},{40,48},{48,56},{1,9},{9,17},... | collective-permute-start | bytes 884744 | tf_op jit(solution)/shard_map/ppermute | solution.py:22
  27.4 3.2 %convolution_bitcast_fusion.1 = f32[384,256]{0,1:T(8,128)} fusion(bf16[2048,384]{1,0:T(8,128)(2,1)} %param.22, f32[2048]{0:T(1024)S(1)} %copy-done.23, f32[256]{0:T(256)S(1)} %add_rsqrt_fusion.1, bf16[2,256,2048]{2,1,0:T(8,128)(2,1)} %param.17, s32[]{:T(128)S(6)} %select_n.97), kind=kOutput, calls=%fused_computation.38 | convolution fusion | flops 404750336 | bytes 3023876 | tf_op jit(solution)/shard_map/dc,qd->cq/dot_general | solution.py:129
  45.8 3.7 %fusion.52 = bf16[256,2,128]{0,2,1:T(8,128)(2,1)S(1)} fusion(bf16[1280,2,256]{0,2,1:T(8,128)(2,1)} %bitcast.168, f32[2,256,1280]{2,1,0:T(8,128)} %copy-done.2, pred[256,1280]{1,0:T(8,128)(4,1)} %and_and_fusion, f32[256,2]{0,1:T(2,128)S(1)} %bitcast.176), kind=kOutput, calls=%fused_computation.41 | convolution fusion | flops 170526464 | bytes 6686720 | tf_op jit(solution)/shard_map/hqk,khd->hqd/dot_general | solution.py:189
  57.5 2.1 %collective-permute-start.6 = (bf16[32,2048]{1,0:T(8,128)(2,1)}, bf16[32,2048]{1,0:T(8,128)(2,1)S(1)}, u32[]{:S(2)}, u32[]{:S(2)}) collective-permute-start(bf16[32,2048]{1,0:T(8,128)(2,1)} %get-tuple-element.21), channel_id=1, source_target_pairs={{0,3},{1,4},{2,5},{3,6},{4,7},{5,0},{6,1},{7,2},{8,11},{9,12},{10,... | collective-permute-start | bytes 393224 | tf_op jit(solution)/shard_map/ppermute | solution.py:37
  60.4 2.6 %collective-permute-start.8 = (bf16[32,2048]{1,0:T(8,128)(2,1)}, bf16[32,2048]{1,0:T(8,128)(2,1)S(1)}, u32[]{:S(2)}, u32[]{:S(2)}) collective-permute-start(bf16[32,2048]{1,0:T(8,128)(2,1)} %get-tuple-element.19), channel_id=1, source_target_pairs={{0,5},{1,6},{2,7},{3,0},{4,1},{5,2},{6,3},{7,4},{8,13},{9,14},{10,... | collective-permute-start | bytes 393224 | tf_op jit(solution)/shard_map/ppermute | solution.py:37
  63.0 2.3 %collective-permute-done.5 = bf16[32,2048]{1,0:T(8,128)(2,1)S(1)} collective-permute-done((bf16[32,2048]{1,0:T(8,128)(2,1)}, bf16[32,2048]{1,0:T(8,128)(2,1)S(1)}, u32[]{:S(2)}, u32[]{:S(2)}) %collective-permute-start.5) | collective-permute-done | bytes 131104 | tf_op jit(solution)/shard_map/ppermute | solution.py:37
  65.3 5.9 %collective-permute-done.6 = bf16[32,2048]{1,0:T(8,128)(2,1)S(1)} collective-permute-done((bf16[32,2048]{1,0:T(8,128)(2,1)}, bf16[32,2048]{1,0:T(8,128)(2,1)S(1)}, u32[]{:S(2)}, u32[]{:S(2)}) %collective-permute-start.6) | collective-permute-done | bytes 131104 | tf_op jit(solution)/shard_map/ppermute | solution.py:37
  78.5 2.1 %collective-permute-start.15 = (bf16[32,2048]{1,0:T(8,128)(2,1)S(1)}, bf16[32,2048]{1,0:T(8,128)(2,1)}, u32[]{:S(2)}, u32[]{:S(2)}) collective-permute-start(bf16[32,2048]{1,0:T(8,128)(2,1)S(1)} %get-tuple-element.6), channel_id=1, source_target_pairs={{0,5},{1,6},{2,7},{3,0},{4,1},{5,2},{6,3},{7,4},{8,13},{9,14},{10,... | collective-permute-start | bytes 393224 | tf_op jit(solution)/shard_map/ppermute | solution.py:46
  82.8 10.2 %all-to-all-start = ((bf16[64,1,4,2048]{3,2,1,0:T(4,128)(2,1)}), bf16[64,1,4,2048]{3,2,1,0:T(4,128)(2,1)}, u32[]{:S(2)}, u32[]{:S(2)}) async-start(bf16[64,1,4,2048]{3,2,1,0:T(4,128)(2,1)} %copy.85), calls=%async_computation | async-start | bytes 2097152 | tf_op jit(solution)/shard_map/all_to_all | solution.py:229
  93.0 2.6 %collective-permute-start.16 = (bf16[32,2048]{1,0:T(8,128)(2,1)S(1)}, bf16[32,2048]{1,0:T(8,128)(2,1)S(1)}, u32[]{:S(2)}, u32[]{:S(2)}) collective-permute-start(bf16[32,2048]{1,0:T(8,128)(2,1)S(1)} %get-tuple-element.6), channel_id=1, source_target_pairs={{0,6},{1,7},{2,0},{3,1},{4,2},{5,3},{6,4},{7,5},{8,14},{9,15},{10,... | collective-permute-start | bytes 393224 | tf_op jit(solution)/shard_map/ppermute | solution.py:46
  104.2 4.7 %collective-permute-done.16 = bf16[32,2048]{1,0:T(8,128)(2,1)S(1)} collective-permute-done((bf16[32,2048]{1,0:T(8,128)(2,1)S(1)}, bf16[32,2048]{1,0:T(8,128)(2,1)S(1)}, u32[]{:S(2)}, u32[]{:S(2)}) %collective-permute-start.16) | collective-permute-done | bytes 131104 | tf_op jit(solution)/shard_map/ppermute | solution.py:46
  113.5 5.0 %fusion.31 = f32[64,1,4,768]{3,0,2,1:T(8,128)} fusion(bf16[1,2048,768]{2,1,0:T(8,128)(2,1)} %param.31, bf16[64,1,4,2048]{3,2,1,0:T(4,128)(2,1)} %all-to-all-done), kind=kOutput, calls=%fused_computation.33 | convolution fusion | flops 805306368 | bytes 4980736 | tf_op jit(solution)/shard_map/sjkd,jdf->sjkf/dot_general | solution.py:230
  118.4 5.9 %fusion.20 = bf16[64,1,4,2048]{3,0,2,1:T(8,128)(2,1)} fusion(bf16[1,768,2048]{2,1,0:T(8,128)(2,1)S(1)} %copy-done, bf16[1,2048,768]{2,1,0:T(8,128)(2,1)} %param.32, bf16[64,1,4,2048]{3,2,1,0:T(4,128)(2,1)} %all-to-all-done, f32[64,1,4,768]{3,0,2,1:T(8,128)} %fusion.31), kind=kOutput, calls=%fused_computation.22 | convolution fusion | flops 1612316672 | bytes 9175040 | tf_op jit(solution)/shard_map/sjkf,jfd->sjkd/dot_general | solution.py:233
  124.4 3.0 %copy.87 = bf16[64,1,4,2048]{3,2,1,0:T(4,128)(2,1)} copy(bf16[64,1,4,2048]{3,0,2,1:T(8,128)(2,1)} %fusion.20) | data formatting | bytes 2097152 | tf_op jit(solution)/shard_map/convert_element_type | solution.py:235
  127.4 9.3 %all-to-all-start.1 = ((bf16[64,1,4,2048]{3,2,1,0:T(4,128)(2,1)}), bf16[64,1,4,2048]{3,2,1,0:T(4,128)(2,1)}, u32[]{:S(2)}, u32[]{:S(2)}) async-start(bf16[64,1,4,2048]{3,2,1,0:T(4,128)(2,1)} %copy.87), calls=%async_computation.1 | async-start | bytes 2097152 | tf_op jit(solution)/shard_map/all_to_all | solution.py:236
  136.7 4.1 %convolution_convert_fusion.1 = bf16[256,2048]{1,0:T(8,128)(2,1)} fusion(bf16[256,2048]{1,0:T(8,128)(2,1)} %param.30, f32[256,256]{1,0:T(8,128)S(1)} %fusion.134, bf16[256,2048]{1,0:T(8,128)(2,1)} %constant_dynamic-update-slice_fusion.5, bf16[2048,256]{1,0:T(8,128)(2,1)} %param.29), kind=kOutput, calls=%fused_computation.17 | convolution fusion | flops 537788416 | bytes 4456448 | tf_op jit(solution)/shard_map/dot_general | solution.py:207
  140.8 2.1 %fusion.130 = (bf16[32,2048]{1,0:T(8,128)(2,1)S(1)}, bf16[32,2048]{1,0:T(8,128)(2,1)S(1)}, bf16[32,2048]{1,0:T(8,128)(2,1)}, bf16[32,2048]{1,0:T(8,128)(2,1)}, b...) fusion(bf16[256,2048]{1,0:T(8,128)(2,1)} %convolution_convert_fusion.1), kind=kLoop, calls=%fused_computation.162 | loop fusion | bytes 1835008 | tf_op jit(solution)/shard_map/slice | solution.py:32
  149.8 3.1 %collective-permute-start.23 = (bf16[32,2048]{1,0:T(8,128)(2,1)}, bf16[32,2048]{1,0:T(8,128)(2,1)}, u32[]{:S(2)}, u32[]{:S(2)}) collective-permute-start(bf16[32,2048]{1,0:T(8,128)(2,1)} %get-tuple-element.11), channel_id=1, source_target_pairs={{0,6},{1,7},{2,0},{3,1},{4,2},{5,3},{6,4},{7,5},{8,14},{9,15},{10,... | collective-permute-start | bytes 393224 | tf_op jit(solution)/shard_map/ppermute | solution.py:37
  152.9 4.0 %collective-permute-done.19 = bf16[32,2048]{1,0:T(8,128)(2,1)S(1)} collective-permute-done((bf16[32,2048]{1,0:T(8,128)(2,1)S(1)}, bf16[32,2048]{1,0:T(8,128)(2,1)S(1)}, u32[]{:S(2)}, u32[]{:S(2)}) %collective-permute-start.19) | collective-permute-done | bytes 131104 | tf_op jit(solution)/shard_map/ppermute | solution.py:37
  159.1 3.0 %collective-permute-done.21 = bf16[32,2048]{1,0:T(8,128)(2,1)} collective-permute-done((bf16[32,2048]{1,0:T(8,128)(2,1)}, bf16[32,2048]{1,0:T(8,128)(2,1)}, u32[]{:S(2)}, u32[]{:S(2)}) %collective-permute-start.21) | collective-permute-done | bytes 131104 | tf_op jit(solution)/shard_map/ppermute | solution.py:37
  162.7 3.7 %fusion.95 = bf16[1,32,2048]{2,1,0:T(8,128)(2,1)} fusion(bf16[64,1,4,2048]{3,2,1,0:T(4,128)(2,1)} %all-to-all-done.1, f32[32,64,4]{0,2,1:T(4,128)S(1)} %bitcast.166, bf16[32,2048]{1,0:T(8,128)(2,1)} %collective-permute-done.24, bf16[32,2048]{1,0:T(8,128)(2,1)} %collective-permute-done.23, bf16[32,2048]{1,0:T(8,128)(2,1)} %collective-permute-done.22, ...), kind=kOutput, calls=%fused_computation.82 | convolution fusion | flops 101908480 | bytes 2392064 | tf_op jit(solution)/shard_map/rsjk,sjkd->rd/dot_general | solution.py:241
  (153 shorter events, 64.4 us)
Async XLA Ops:
  9.5 27.8 %collective-permute-start = (bf16[256,576]{0,1:T(8,128)(2,1)}, bf16[256,576]{0,1:T(8,128)(2,1)}, u32[]{:S(2)}, u32[]{:S(2)}) collective-permute-start(bf16[256,576]{0,1:T(8,128)(2,1)} %pad_maximum_fusion), channel_id=1, source_target_pairs={{0,32},{8,40},{16,48},{24,56},{1,33},{9,41},{17,49},{25,57},{2,34}... | collective-permute-start | bytes 884744 | tf_op jit(solution)/shard_map/ppermute | solution.py:22
  15.7 22.6 %collective-permute-start.1 = (bf16[256,576]{0,1:T(8,128)(2,1)}, bf16[256,576]{0,1:T(8,128)(2,1)}, u32[]{:S(2)}, u32[]{:S(2)}) collective-permute-start(bf16[256,576]{0,1:T(8,128)(2,1)} %pad_maximum_fusion), channel_id=1, source_target_pairs={{0,24},{8,32},{16,40},{24,48},{32,56},{1,25},{9,33},{17,41},{25,49... | collective-permute-start | bytes 884744 | tf_op jit(solution)/shard_map/ppermute | solution.py:22
  22.1 17.2 %collective-permute-start.2 = (bf16[256,576]{0,1:T(8,128)(2,1)}, bf16[256,576]{0,1:T(8,128)(2,1)}, u32[]{:S(2)}, u32[]{:S(2)}) collective-permute-start(bf16[256,576]{0,1:T(8,128)(2,1)} %pad_maximum_fusion), channel_id=1, source_target_pairs={{0,16},{8,24},{16,32},{24,40},{32,48},{40,56},{1,17},{9,25},{17,33... | collective-permute-start | bytes 884744 | tf_op jit(solution)/shard_map/ppermute | solution.py:22
  24.1 16.2 %collective-permute-start.3 = (bf16[256,576]{0,1:T(8,128)(2,1)}, bf16[256,576]{0,1:T(8,128)(2,1)}, u32[]{:S(2)}, u32[]{:S(2)}) collective-permute-start(bf16[256,576]{0,1:T(8,128)(2,1)} %pad_maximum_fusion), channel_id=1, source_target_pairs={{0,8},{8,16},{16,24},{24,32},{32,40},{40,48},{48,56},{1,9},{9,17},... | collective-permute-start | bytes 884744 | tf_op jit(solution)/shard_map/ppermute | solution.py:22
  54.6 8.3 %collective-permute-start.4 = (bf16[32,2048]{1,0:T(8,128)(2,1)}, bf16[32,2048]{1,0:T(8,128)(2,1)}, u32[]{:S(2)}, u32[]{:S(2)}) collective-permute-start(bf16[32,2048]{1,0:T(8,128)(2,1)} %get-tuple-element.16), channel_id=1, source_target_pairs={{0,1},{1,2},{2,3},{3,4},{4,5},{5,6},{6,7},{7,0},{8,9},{9,10},{10,1... | collective-permute-start | bytes 393224 | tf_op jit(solution)/shard_map/ppermute | solution.py:37
  56.2 9.2 %collective-permute-start.5 = (bf16[32,2048]{1,0:T(8,128)(2,1)}, bf16[32,2048]{1,0:T(8,128)(2,1)S(1)}, u32[]{:S(2)}, u32[]{:S(2)}) collective-permute-start(bf16[32,2048]{1,0:T(8,128)(2,1)} %get-tuple-element.22), channel_id=1, source_target_pairs={{0,2},{1,3},{2,4},{3,5},{4,6},{5,7},{6,0},{7,1},{8,10},{9,11},{10,... | collective-permute-start | bytes 393224 | tf_op jit(solution)/shard_map/ppermute | solution.py:37
  57.5 13.7 %collective-permute-start.6 = (bf16[32,2048]{1,0:T(8,128)(2,1)}, bf16[32,2048]{1,0:T(8,128)(2,1)S(1)}, u32[]{:S(2)}, u32[]{:S(2)}) collective-permute-start(bf16[32,2048]{1,0:T(8,128)(2,1)} %get-tuple-element.21), channel_id=1, source_target_pairs={{0,3},{1,4},{2,5},{3,6},{4,7},{5,0},{6,1},{7,2},{8,11},{9,12},{10,... | collective-permute-start | bytes 393224 | tf_op jit(solution)/shard_map/ppermute | solution.py:37
  59.6 11.6 %collective-permute-start.7 = (bf16[32,2048]{1,0:T(8,128)(2,1)}, bf16[32,2048]{1,0:T(8,128)(2,1)S(1)}, u32[]{:S(2)}, u32[]{:S(2)}) collective-permute-start(bf16[32,2048]{1,0:T(8,128)(2,1)} %get-tuple-element.20), channel_id=1, source_target_pairs={{0,4},{1,5},{2,6},{3,7},{4,0},{5,1},{6,2},{7,3},{8,12},{9,13},{10,... | collective-permute-start | bytes 393224 | tf_op jit(solution)/shard_map/ppermute | solution.py:37
  60.4 10.9 %collective-permute-start.8 = (bf16[32,2048]{1,0:T(8,128)(2,1)}, bf16[32,2048]{1,0:T(8,128)(2,1)S(1)}, u32[]{:S(2)}, u32[]{:S(2)}) collective-permute-start(bf16[32,2048]{1,0:T(8,128)(2,1)} %get-tuple-element.19), channel_id=1, source_target_pairs={{0,5},{1,6},{2,7},{3,0},{4,1},{5,2},{6,3},{7,4},{8,13},{9,14},{10,... | collective-permute-start | bytes 393224 | tf_op jit(solution)/shard_map/ppermute | solution.py:37
  63.0 8.2 %collective-permute-start.9 = (bf16[32,2048]{1,0:T(8,128)(2,1)S(1)}, bf16[32,2048]{1,0:T(8,128)(2,1)S(1)}, u32[]{:S(2)}, u32[]{:S(2)}) collective-permute-start(bf16[32,2048]{1,0:T(8,128)(2,1)S(1)} %get-tuple-element.18), channel_id=1, source_target_pairs={{0,6},{1,7},{2,0},{3,1},{4,2},{5,3},{6,4},{7,5},{8,14},{9,15},{10,... | collective-permute-start | bytes 393224 | tf_op jit(solution)/shard_map/ppermute | solution.py:37
  73.4 19.6 %collective-permute-start.11 = (bf16[32,2048]{1,0:T(8,128)(2,1)S(1)}, bf16[32,2048]{1,0:T(8,128)(2,1)}, u32[]{:S(2)}, u32[]{:S(2)}) collective-permute-start(bf16[32,2048]{1,0:T(8,128)(2,1)S(1)} %get-tuple-element.6), channel_id=1, source_target_pairs={{0,1},{1,2},{2,3},{3,4},{4,5},{5,6},{6,7},{7,0},{8,9},{9,10},{10,1... | collective-permute-start | bytes 393224 | tf_op jit(solution)/shard_map/ppermute | solution.py:46
  74.3 23.0 %collective-permute-start.12 = (bf16[32,2048]{1,0:T(8,128)(2,1)S(1)}, bf16[32,2048]{1,0:T(8,128)(2,1)}, u32[]{:S(2)}, u32[]{:S(2)}) collective-permute-start(bf16[32,2048]{1,0:T(8,128)(2,1)S(1)} %get-tuple-element.6), channel_id=1, source_target_pairs={{0,2},{1,3},{2,4},{3,5},{4,6},{5,7},{6,0},{7,1},{8,10},{9,11},{10,... | collective-permute-start | bytes 393224 | tf_op jit(solution)/shard_map/ppermute | solution.py:46
  76.0 23.5 %collective-permute-start.13 = (bf16[32,2048]{1,0:T(8,128)(2,1)S(1)}, bf16[32,2048]{1,0:T(8,128)(2,1)}, u32[]{:S(2)}, u32[]{:S(2)}) collective-permute-start(bf16[32,2048]{1,0:T(8,128)(2,1)S(1)} %get-tuple-element.6), channel_id=1, source_target_pairs={{0,3},{1,4},{2,5},{3,6},{4,7},{5,0},{6,1},{7,2},{8,11},{9,12},{10,... | collective-permute-start | bytes 393224 | tf_op jit(solution)/shard_map/ppermute | solution.py:46
  77.7 23.3 %collective-permute-start.14 = (bf16[32,2048]{1,0:T(8,128)(2,1)S(1)}, bf16[32,2048]{1,0:T(8,128)(2,1)}, u32[]{:S(2)}, u32[]{:S(2)}) collective-permute-start(bf16[32,2048]{1,0:T(8,128)(2,1)S(1)} %get-tuple-element.6), channel_id=1, source_target_pairs={{0,4},{1,5},{2,6},{3,7},{4,0},{5,1},{6,2},{7,3},{8,12},{9,13},{10,... | collective-permute-start | bytes 393224 | tf_op jit(solution)/shard_map/ppermute | solution.py:46
  78.5 24.1 %collective-permute-start.15 = (bf16[32,2048]{1,0:T(8,128)(2,1)S(1)}, bf16[32,2048]{1,0:T(8,128)(2,1)}, u32[]{:S(2)}, u32[]{:S(2)}) collective-permute-start(bf16[32,2048]{1,0:T(8,128)(2,1)S(1)} %get-tuple-element.6), channel_id=1, source_target_pairs={{0,5},{1,6},{2,7},{3,0},{4,1},{5,2},{6,3},{7,4},{8,13},{9,14},{10,... | collective-permute-start | bytes 393224 | tf_op jit(solution)/shard_map/ppermute | solution.py:46
  82.8 30.7 %all-to-all-start = ((bf16[64,1,4,2048]{3,2,1,0:T(4,128)(2,1)}), bf16[64,1,4,2048]{3,2,1,0:T(4,128)(2,1)}, u32[]{:S(2)}, u32[]{:S(2)}) async-start(bf16[64,1,4,2048]{3,2,1,0:T(4,128)(2,1)} %copy.85), calls=%async_computation | async-start | bytes 2097152 | tf_op jit(solution)/shard_map/all_to_all | solution.py:229
  93.0 15.8 %collective-permute-start.16 = (bf16[32,2048]{1,0:T(8,128)(2,1)S(1)}, bf16[32,2048]{1,0:T(8,128)(2,1)S(1)}, u32[]{:S(2)}, u32[]{:S(2)}) collective-permute-start(bf16[32,2048]{1,0:T(8,128)(2,1)S(1)} %get-tuple-element.6), channel_id=1, source_target_pairs={{0,6},{1,7},{2,0},{3,1},{4,2},{5,3},{6,4},{7,5},{8,14},{9,15},{10,... | collective-permute-start | bytes 393224 | tf_op jit(solution)/shard_map/ppermute | solution.py:46
  97.2 13.6 %collective-permute-start.17 = (bf16[32,2048]{1,0:T(8,128)(2,1)S(1)}, bf16[32,2048]{1,0:T(8,128)(2,1)S(1)}, u32[]{:S(2)}, u32[]{:S(2)}) collective-permute-start(bf16[32,2048]{1,0:T(8,128)(2,1)S(1)} %get-tuple-element.6), channel_id=1, source_target_pairs={{0,7},{1,0},{2,1},{3,2},{4,3},{5,4},{6,5},{7,6},{8,15},{9,8},{10,9... | collective-permute-start | bytes 393224 | tf_op jit(solution)/shard_map/ppermute | solution.py:46
  127.4 35.3 %all-to-all-start.1 = ((bf16[64,1,4,2048]{3,2,1,0:T(4,128)(2,1)}), bf16[64,1,4,2048]{3,2,1,0:T(4,128)(2,1)}, u32[]{:S(2)}, u32[]{:S(2)}) async-start(bf16[64,1,4,2048]{3,2,1,0:T(4,128)(2,1)} %copy.87), calls=%async_computation.1 | async-start | bytes 2097152 | tf_op jit(solution)/shard_map/all_to_all | solution.py:236
  144.5 12.4 %collective-permute-start.19 = (bf16[32,2048]{1,0:T(8,128)(2,1)S(1)}, bf16[32,2048]{1,0:T(8,128)(2,1)S(1)}, u32[]{:S(2)}, u32[]{:S(2)}) collective-permute-start(bf16[32,2048]{1,0:T(8,128)(2,1)S(1)} %get-tuple-element.15), channel_id=1, source_target_pairs={{0,2},{1,3},{2,4},{3,5},{4,6},{5,7},{6,0},{7,1},{8,10},{9,11},{10,... | collective-permute-start | bytes 393224 | tf_op jit(solution)/shard_map/ppermute | solution.py:37
  145.7 13.4 %collective-permute-start.20 = (bf16[32,2048]{1,0:T(8,128)(2,1)}, bf16[32,2048]{1,0:T(8,128)(2,1)}, u32[]{:S(2)}, u32[]{:S(2)}) collective-permute-start(bf16[32,2048]{1,0:T(8,128)(2,1)} %get-tuple-element.14), channel_id=1, source_target_pairs={{0,3},{1,4},{2,5},{3,6},{4,7},{5,0},{6,1},{7,2},{8,11},{9,12},{10,... | collective-permute-start | bytes 393224 | tf_op jit(solution)/shard_map/ppermute | solution.py:37
  147.3 14.8 %collective-permute-start.21 = (bf16[32,2048]{1,0:T(8,128)(2,1)}, bf16[32,2048]{1,0:T(8,128)(2,1)}, u32[]{:S(2)}, u32[]{:S(2)}) collective-permute-start(bf16[32,2048]{1,0:T(8,128)(2,1)} %get-tuple-element.13), channel_id=1, source_target_pairs={{0,4},{1,5},{2,6},{3,7},{4,0},{5,1},{6,2},{7,3},{8,12},{9,13},{10,... | collective-permute-start | bytes 393224 | tf_op jit(solution)/shard_map/ppermute | solution.py:37
  147.9 14.8 %collective-permute-start.22 = (bf16[32,2048]{1,0:T(8,128)(2,1)}, bf16[32,2048]{1,0:T(8,128)(2,1)}, u32[]{:S(2)}, u32[]{:S(2)}) collective-permute-start(bf16[32,2048]{1,0:T(8,128)(2,1)} %get-tuple-element.12), channel_id=1, source_target_pairs={{0,5},{1,6},{2,7},{3,0},{4,1},{5,2},{6,3},{7,4},{8,13},{9,14},{10,... | collective-permute-start | bytes 393224 | tf_op jit(solution)/shard_map/ppermute | solution.py:37
  149.8 12.9 %collective-permute-start.23 = (bf16[32,2048]{1,0:T(8,128)(2,1)}, bf16[32,2048]{1,0:T(8,128)(2,1)}, u32[]{:S(2)}, u32[]{:S(2)}) collective-permute-start(bf16[32,2048]{1,0:T(8,128)(2,1)} %get-tuple-element.11), channel_id=1, source_target_pairs={{0,6},{1,7},{2,0},{3,1},{4,2},{5,3},{6,4},{7,5},{8,14},{9,15},{10,... | collective-permute-start | bytes 393224 | tf_op jit(solution)/shard_map/ppermute | solution.py:37
  (28 other events, 300.8 us)
